TPU v7x, 32 devices: a whole 2x2x4 slice. The times are simulated.
32 devices in a mesh: tok: 4 (over y, x), feat: 8 (over z, core).
Axes of the slice: x: 2, y: 2, z: 4, core: 2. Of those that a mesh axis runs over, the one named last changes fastest.
Arguments:
- acts: bfloat16 [512, 8192], P('tok', 'feat'), may hold values from -6 to 6
- grad_out: bfloat16 [512, 28672], P('tok', 'feat'), may hold values from -6 to 6
- weight: bfloat16 [8192, 28672], P('tok', 'feat'), may hold values from -0.03125 to 0.03125
- block_rows: int32 [1024], P('feat'), may hold values from 0 to 63
- block_cols: int32 [1024], P('feat'), may hold values from 0 to 27
- block_count: int32 [8], P('feat'), may hold values from 1 to 128, as said below
Outputs:
- grad_in: bfloat16 [512, 8192], P('feat', 'tok')
- block_grads: bfloat16 [1024, 128, 128], P('feat', 'tok')
Inputs may be any that keep to these rules, and one draw needn't show every extreme that they name: `block_count`: each feat shard lists at most 128 blocks; one shard lists exactly 128; listed blocks of a shard may repeat.
All inputs are finite; a program needn't handle non-finite values.
Results may differ from a plain program's by a relative error of at most 0.001.
Values may be sent and summed in bfloat16 or wider, within the bound.
No kernel may reach another device: no remote copies, remote signals or barrier semaphores. Data moves between devices by JAX's collectives and lax.ppermute only.
A program may use at most 128 MiB of HBM per device.

v0:
```python
import jax
import jax.numpy as jnp
from jax import lax
from jax.sharding import PartitionSpec as P

BLK = 128


def per_device(acts, grad_out, weight, block_rows, block_cols, block_count):
    tok_dev = acts.shape[0]
    slot_count = block_rows.shape[0]
    active = (jnp.arange(slot_count, dtype=jnp.int32) < block_count[0]).astype(jnp.float32)
    full_acts = lax.all_gather(acts, "feat", axis=1, tiled=True)
    row_blocks = full_acts.shape[1] // BLK
    partial_sums = lax.dot_general(
        lax.all_gather(grad_out, "tok", axis=0, tiled=True),
        weight,
        (((1,), (1,)), ((), ())),
        preferred_element_type=jnp.float32,
    )
    act_sel = jnp.take(full_acts.reshape(tok_dev, row_blocks, BLK), block_rows, axis=1)
    grad_sel = jnp.take(grad_out.reshape(tok_dev, -1, BLK), block_cols, axis=1)
    partial_tiles = jnp.einsum(
        "tsa,tsb->sab", act_sel, grad_sel, preferred_element_type=jnp.float32
    )
    partial_tiles = partial_tiles * active[:, None, None]
    block_grads = lax.psum_scatter(partial_tiles, "tok", scatter_dimension=1, tiled=True).astype(
        jnp.bfloat16
    )
    grad_in = lax.psum_scatter(partial_sums, "feat", scatter_dimension=0, tiled=True).astype(
        jnp.bfloat16
    )
    return (grad_in, block_grads)


def solution(mesh):
    in_specs = (
        P("tok", "feat"),
        P("tok", "feat"),
        P("tok", "feat"),
        P("feat"),
        P("feat"),
        P("feat"),
    )
    out_specs = (P("feat", "tok"), P("feat", "tok", None))
    return jax.shard_map(
        per_device, mesh=mesh, in_specs=in_specs, out_specs=out_specs, check_vma=False
    )
```

profile of v0, /device:TPU:0, one launch (start us, length us, event | category | flops | bytes accessed | tf_op | source)
XLA Modules:
  0.0 240.9 jit_solution(17467459685259097102)
XLA Ops:
  7.2 0.0 all-gather.3.cloned.1.call-start
  7.2 0.7 all-gather.3.cloned.1.call-update
  7.9 0.0 all-gather.5.cloned.1.call-start
  7.9 1.8 copy.12
  9.7 0.0 all-gather.5.cloned.1.call-update
  9.8 0.0 reduce-scatter.3.cloned.1.call-start
  9.8 51.1 %all-gather.3.cloned.1.call-done = bf16[512,3584]{1,0:T(8,128)(2,1)} async-done(((bf16[128,3584]{1,0:T(8,128)(2,1)}), bf16[512,3584]{1,0:T(8,128)(2,1)}) %all-gather.3.cloned.1.call-update) | async-done | bytes 3670032 | tf_op jit(solution)/shard_map/all_gather | solution.py:16
  60.9 13.5 %fusion.13 = f32[512,2048]{1,0:T(8,128)} fusion(bf16[512,3584]{1,0:T(8,128)(2,1)} %all-gather.3.cloned.1.call-done, bf16[2048,3584]{1,0:T(8,128)(2,1)} %param.8), kind=kOutput, calls=%fused_computation.19 | convolution fusion | flops 7516192768 | bytes 22544384 | tf_op jit(solution)/shard_map/dot_general | solution.py:15
  74.4 0.0 copy-start
  74.4 0.0 copy-start.1
  74.4 0.0 reduce-scatter.3.cloned.1.call-update
  74.5 0.0 reduce-scatter.5.cloned.1.call-start
  74.5 1.1 copy-done
  75.6 0.6 copy.14
  76.9 0.6 copy.15
  77.5 0.0 copy-done.1
  77.6 0.0 copy-start.2
  77.6 3.0 %gather_fusion.1 = bf16[128,128,128]{2,1,0:T(8,128)(2,1)} fusion(bf16[128,28,128]{2,0,1:T(8,128)(2,1)S(1)} %copy.15, s32[1024]{0:T(1024)S(1)} %pad_clamp_fusion), kind=kCustom, calls=%fused_computation.1 | custom fusion | bytes 8389120 | tf_op jit(solution)/shard_map/jit(_take)/gather | solution.py:22
  80.6 0.0 copy-done.2
  80.7 11.6 %all-gather.5.cloned.1.call-done = bf16[128,8192]{0,1:T(8,128)(2,1)} async-done(((bf16[128,1024]{0,1:T(8,128)(2,1)}), bf16[128,8192]{0,1:T(8,128)(2,1)}) %all-gather.5.cloned.1.call-update) | async-done | bytes 2097168 | tf_op jit(solution)/shard_map/all_gather | solution.py:13
  92.2 3.2 %copy.13 = bf16[128,64,128]{2,0,1:T(8,128)(2,1)S(1)} copy(bf16[128,64,128]{0,2,1:T(8,128)(2,1)} %bitcast.17) | data formatting | bytes 4194304 | tf_op jit(solution)/shard_map/reshape | solution.py:21
  95.4 3.0 %gather_fusion = bf16[128,128,128]{2,1,0:T(8,128)(2,1)} fusion(bf16[128,64,128]{2,0,1:T(8,128)(2,1)S(1)} %copy.13, s32[1024]{0:T(1024)S(1)} %pad_clamp_fusion.1), kind=kCustom, calls=%fused_computation | custom fusion | bytes 8389120 | tf_op jit(solution)/shard_map/jit(_take)/gather | solution.py:21
  98.5 9.4 %broadcast_multiply_fusion = f32[128,128,128]{2,1,0:T(8,128)} fusion(f32[128]{0:T(128)S(1)} %get-tuple-element.2, bf16[128,128,128]{2,1,0:T(8,128)(2,1)} %gather_fusion.1, pred[128]{0:T(512)(128)(4,1)S(1)} %get-tuple-element.3, bf16[128,128,128]{2,1,0:T(8,128)(2,1)} %gather_fusion, pred[128]{0:T(512)(128)(4,1)S(1)} %compare_and_fusion.1), kind=kOutput, calls=%fused_computation.7 | convolution fusion | flops 543162368 | bytes 16777984 | tf_op jit(solution)/shard_map/tsa,tsb->sab/dot_general | solution.py:23
  107.9 0.0 reduce-scatter.5.cloned.1.call-update
  107.9 36.2 %reduce-scatter.3.cloned.1.call-done = f32[64,2048]{1,0:T(8,128)} async-done(((f32[512,2048]{1,0:T(8,128)}), f32[64,2048]{1,0:T(8,128)}) %reduce-scatter.3.cloned.1.call-update) | async-done | bytes 524304 | tf_op jit(solution)/shard_map/reduce_scatter | solution.py:30
  144.1 1.8 convert_element_type.13
  145.8 85.7 %reduce-scatter.5.cloned.1.call-done = f32[128,32,128]{2,1,0:T(8,128)} async-done(((f32[128,128,128]{2,1,0:T(8,128)}), f32[128,32,128]{2,1,0:T(8,128)}) %reduce-scatter.5.cloned.1.call-update) | async-done | bytes 2097168 | tf_op jit(solution)/shard_map/reduce_scatter | solution.py:27
  231.6 2.8 %convert_element_type.15 = bf16[128,32,128]{2,1,0:T(8,128)(2,1)} convert(f32[128,32,128]{2,1,0:T(8,128)} %reduce-scatter.5.cloned.1.call-done) | non-fusion elementwise | flops 524288 | bytes 3145728 | tf_op jit(solution)/shard_map/convert_element_type | solution.py:27
  (6 shorter events, 0.0 us)
Async XLA Ops:
  7.2 53.8 %all-gather.3.cloned.1.call-start = ((), (), s32[]{:S(2)}) async-start(), calls=%async_computation.2 | async-start | bytes 4587520 | tf_op jit(solution)/shard_map/all_gather | solution.py:16
  7.9 84.3 %all-gather.5.cloned.1.call-start = ((), (), s32[]{:S(2)}) async-start(), calls=%async_computation.4 | async-start | bytes 2359296 | tf_op jit(solution)/shard_map/all_gather | solution.py:13
  9.8 134.3 %reduce-scatter.3.cloned.1.call-start = ((), (), s32[]{:S(2)}) async-start(), calls=%async_computation.3 | async-start | bytes 4718592 | tf_op jit(solution)/shard_map/reduce_scatter | solution.py:30
  74.4 1.2 copy-start
  74.4 3.1 %copy-start.1 = (s32[128]{0:T(128)S(1)}, s32[128]{0:T(128)}, u32[]{:S(2)}) copy-start(s32[128]{0:T(128)} %param.10) | copy-start | bytes 1540
  74.5 157.1 %reduce-scatter.5.cloned.1.call-start = ((), (), s32[]{:S(2)}) async-start(), calls=%async_computation.5 | async-start | bytes 10485760 | tf_op jit(solution)/shard_map/reduce_scatter | solution.py:27
  77.6 3.0 %copy-start.2 = (s32[128]{0:T(128)S(1)}, s32[128]{0:T(128)}, u32[]{:S(2)}) copy-start(s32[128]{0:T(128)} %param.9) | copy-start | bytes 1540
Sparse Core Ops, SparseCore 0:
  9.8 51.0 all-gather.2
  63.1 29.0 all-gather.4
  94.5 49.4 reduce-scatter.2
  147.0 84.5 reduce-scatter.4
where the time goes:
time: 241 us
  waiting for transfers between devices  185 us (77%)
  matrix products  22.9 us (10%)
  between operations  14.5 us (6%)
  local copies, waits for them, and re-layouts  13.4 us (6%)
  other arithmetic  4.59 us (2%)
    reduce_scatter x1, waiting for transfers between devices, per_device(): lax.psum_scatter(partial_tiles, 'tok', scatter_dimension=1, tiled=True)  85.7 us
    all_gather x1, waiting for transfers between devices, per_device(): lax.all_gather(grad_out, 'tok', axis=0, tiled=True)  51.1 us
    reduce_scatter x1, waiting for transfers between devices, per_device(): lax.psum_scatter(partial_sums, 'feat', scatter_dimension=0, tiled=True)  36.2 us
    dot_general x1, matrix products, per_device(): lax.dot_general(lax.all_gather(grad_out, 'tok', axis=0, tiled=True), weig...  13.5 us
    all_gather x1, waiting for transfers between devices, per_device(): full_acts = lax.all_gather(acts, 'feat', axis=1, tiled=True)  11.6 us
    dot_general x1, matrix products, per_device(): jnp.einsum('tsa,tsb->sab', act_sel, grad_sel, preferred_element_type=jnp....  9.38 us
  transfers between devices with their start and end apart: 4, of which 4 were waited for; matrix products, arithmetic and copies ran while one was open for 15% of the time, Pallas kernels for 0%

commit v1 on v0

v1 whole, which is shorter than its diff:
```python
import functools

import jax
import jax.numpy as jnp
from jax import lax
from jax.experimental import pallas as pl
from jax.experimental.pallas import tpu as pltpu
from jax.sharding import PartitionSpec as P

BLK = 128
SLOTS_PER_STEP = 8


def xor_exchange(x, axis_name, n):
    out = [x]
    for m in range(1, n):
        out.append(lax.ppermute(x, axis_name, perm=[(a, a ^ m) for a in range(n)]))
    return out


def place_rows(pieces, me, axis=0):
    rows = pieces[0].shape[axis]
    shape = list(pieces[0].shape)
    shape[axis] = rows * len(pieces)
    out = jnp.zeros(shape, pieces[0].dtype)
    for m, piece in enumerate(pieces):
        out = lax.dynamic_update_slice_in_dim(out, piece, (me ^ m) * rows, axis)
    return out


def block_kernel(rows_ref, cols_ref, cnt_ref, a_ref, g_ref, o_ref):
    step = pl.program_id(0)
    for u in range(SLOTS_PER_STEP):
        s = step * SLOTS_PER_STEP + u
        a = a_ref[rows_ref[s]]
        g = g_ref[:, pl.ds(pl.multiple_of(cols_ref[s] * BLK, BLK), BLK)]
        tile = jnp.dot(a, g, preferred_element_type=jnp.float32)
        tile = jnp.where(s < cnt_ref[0], tile, jnp.float32(0.0))
        o_ref[u] = tile.astype(o_ref.dtype)


def block_tiles(rows, cols, count, acts_t, gout):
    n_slots = rows.shape[0]
    sub, tokens = acts_t.shape[1], acts_t.shape[2]
    grid_spec = pltpu.PrefetchScalarGridSpec(
        num_scalar_prefetch=3,
        grid=(n_slots // SLOTS_PER_STEP,),
        in_specs=[
            pl.BlockSpec(acts_t.shape, lambda g, r, c, n: (0, 0, 0)),
            pl.BlockSpec(gout.shape, lambda g, r, c, n: (0, 0)),
        ],
        out_specs=pl.BlockSpec((SLOTS_PER_STEP, sub, BLK), lambda g, r, c, n: (g, 0, 0)),
    )
    return pl.pallas_call(
        block_kernel,
        grid_spec=grid_spec,
        out_shape=jax.ShapeDtypeStruct((n_slots, sub, BLK), jnp.bfloat16),
        cost_estimate=pl.CostEstimate(
            flops=2 * n_slots * sub * tokens * BLK,
            bytes_accessed=acts_t.size * 2 + gout.size * 2 + n_slots * sub * BLK * 2,
            transcendentals=0,
        ),
    )(rows, cols, count, acts_t, gout)


def per_device(n_tok, acts, grad_out, weight, block_rows, block_cols, block_count):
    me = lax.axis_index("tok")
    tok_dev, d_dev = acts.shape
    sub = BLK // n_tok

    acts_pieces = acts.reshape(tok_dev, d_dev // BLK, n_tok, sub)
    send = [
        lax.dynamic_index_in_dim(acts_pieces, me ^ m, axis=2, keepdims=False)
        for m in range(n_tok)
    ]
    got = [send[0]] + [
        lax.ppermute(send[m], "tok", perm=[(a, a ^ m) for a in range(n_tok)])
        for m in range(1, n_tok)
    ]
    acts_sub = place_rows(got, me)
    acts_sub_t = jnp.transpose(acts_sub, (1, 2, 0))
    acts_t = lax.all_gather(acts_sub_t, "feat", axis=0, tiled=True)

    gout = place_rows(xor_exchange(grad_out, "tok", n_tok), me)

    partial_sums = lax.dot_general(
        gout, weight, (((1,), (1,)), ((), ())), preferred_element_type=jnp.float32
    )
    grad_in = lax.psum_scatter(partial_sums, "feat", scatter_dimension=0, tiled=True).astype(
        jnp.bfloat16
    )
    block_grads = block_tiles(block_rows, block_cols, block_count, acts_t, gout)
    return (grad_in, block_grads)


def solution(mesh):
    n_tok = mesh.shape["tok"]
    assert n_tok & (n_tok - 1) == 0
    in_specs = (
        P("tok", "feat"),
        P("tok", "feat"),
        P("tok", "feat"),
        P("feat"),
        P("feat"),
        P("feat"),
    )
    out_specs = (P("feat", "tok"), P("feat", "tok", None))
    return jax.shard_map(
        functools.partial(per_device, n_tok),
        mesh=mesh,
        in_specs=in_specs,
        out_specs=out_specs,
        check_vma=False,
    )
```

time: 241 us -> 149 us (0.62)
  waiting for transfers between devices: 185 us -> 92.2 us
  Pallas kernels: 0 us -> 10.9 us
  starting transfers between devices: 0.16 us -> 10.8 us
  matrix products: 22.9 us -> 12.4 us
  local copies, waits for them, and re-layouts: 13.4 us -> 6.12 us
  other arithmetic: 4.59 us -> 1.77 us
    reduce_scatter x1 -> x0, waiting for transfers between devices: 85.7 us -> none  [per_device(): lax.psum_scatter(partial_tiles, 'tok', scatter_dimension=1, tiled=True)]
    all_gather x2 -> x1, waiting for transfers between devices: 62.7 us -> 14 us  [per_device(): acts_t = lax.all_gather(acts_sub_t, 'feat', axis=0, tiled=True)]
    ppermute x0 -> x6, waiting for transfers between devices: none -> 37.2 us  [the longest x3 37.2 us: per_device(): lax.ppermute(send[m], 'tok', perm=[(a, a ^ m) for a in range(n_tok)])]
    pallas_call x0 -> x1, Pallas kernels: none -> 10.9 us  [block_tiles(): pl.pallas_call(block_kernel, grid_spec=grid_spec, out_shape=jax.ShapeDtyp...]
    ppermute x0 -> x6, starting transfers between devices: none -> 10.7 us  [the longest x3 6.16 us: per_device(): lax.ppermute(send[m], 'tok', perm=[(a, a ^ m) for a in range(n_tok)])]
    dot_general x2 -> x1, matrix products: 22.9 us -> 12.4 us  [per_device(): lax.dot_general(gout, weight, (((1,), (1,)), ((), ())), preferred_element...]
    gather x2 -> x0, local copies, waits for them, and re-layouts: 6.05 us -> none  [the longest x1 3.03 us: per_device(): jnp.take(full_acts.reshape(tok_dev, row_blocks, BLK), block_rows, axis=1)]
    reduce_scatter x1, waiting for transfers between devices: 36.2 us -> 40.9 us  [per_device(): lax.psum_scatter(partial_sums, 'feat', scatter_dimension=0, tiled=True)]
  transfers between devices with their start and end apart: 4 -> 8, of which waited for: 4 -> 4; matrix products, arithmetic and copies ran while one was open for 15% -> 11% of each run, Pallas kernels for 0% -> 7%
where the time goes in v1:
time: 149 us
  waiting for transfers between devices  92.2 us (62%)
  between operations  14.8 us (10%)
  matrix products  12.4 us (8%)
  Pallas kernels  10.9 us (7%)
  starting transfers between devices  10.8 us (7%)
  local copies, waits for them, and re-layouts  6.12 us (4%)
  other arithmetic  1.77 us (1%)
    reduce_scatter x1, waiting for transfers between devices, per_device(): lax.psum_scatter(partial_sums, 'feat', scatter_dimension=0, tiled=True)  40.9 us
    ppermute x3, waiting for transfers between devices, per_device(): lax.ppermute(send[m], 'tok', perm=[(a, a ^ m) for a in range(n_tok)])  37.2 us
    all_gather x1, waiting for transfers between devices, per_device(): acts_t = lax.all_gather(acts_sub_t, 'feat', axis=0, tiled=True)  14 us
    dot_general x1, matrix products, per_device(): lax.dot_general(gout, weight, (((1,), (1,)), ((), ())), preferred_element...  12.4 us
    pallas_call x1, Pallas kernels, block_tiles(): pl.pallas_call(block_kernel, grid_spec=grid_spec, out_shape=jax.ShapeDtyp...  10.9 us
    ppermute x3, starting transfers between devices, per_device(): lax.ppermute(send[m], 'tok', perm=[(a, a ^ m) for a in range(n_tok)])  6.16 us
    ppermute x3, starting transfers between devices, xor_exchange(): out.append(lax.ppermute(x, axis_name, perm=[(a, a ^ m) for a in range(n)]))  4.55 us
    unnamed x7, local copies, waits for them, and re-layouts  3.61 us
  transfers between devices with their start and end apart: 8, of which 4 were waited for; matrix products, arithmetic and copies ran while one was open for 11% of the time, Pallas kernels for 7%

profile of v1, /device:TPU:0, one launch (start us, length us, event | category | flops | bytes accessed | tf_op | source)
XLA Modules:
  0.0 149.0 jit_solution(16370198670482249258)
XLA Ops:
  7.2 0.0 copy-start.2
  7.2 0.0 all-gather.2.cloned.1.call-start
  7.2 3.0 %collective-permute-start = (bf16[128,3584]{1,0:T(8,128)(2,1)}, bf16[128,3584]{1,0:T(8,128)(2,1)}, u32[]{:S(2)}, u32[]{:S(2)}) collective-permute-start(bf16[128,3584]{1,0:T(8,128)(2,1)} %param.7), channel_id=1, source_target_pairs={{0,8},{8,0},{16,24},{24,16},{1,9},{9,1},{17,25},{25,17},{2,10},{10... | collective-permute-start | bytes 2752520 | tf_op jit(solution)/shard_map/ppermute | solution.py:17
  10.2 1.5 %collective-permute-start.1 = (bf16[128,3584]{1,0:T(8,128)(2,1)}, bf16[128,3584]{1,0:T(8,128)(2,1)S(1)}, u32[]{:S(2)}, u32[]{:S(2)}) collective-permute-start(bf16[128,3584]{1,0:T(8,128)(2,1)} %param.7), channel_id=1, source_target_pairs={{0,16},{8,24},{16,0},{24,8},{1,17},{9,25},{17,1},{25,9},{2,18},{10... | collective-permute-start | bytes 2752520 | tf_op jit(solution)/shard_map/ppermute | solution.py:17
  11.7 0.0 collective-permute-start.2
  11.8 1.1 copy.13
  12.9 0.7 dynamic-slice_bitcast_fusion
  13.6 1.9 %collective-permute-start.3 = (bf16[128,8,32]{0,2,1:T(8,128)(2,1)}, bf16[128,8,32]{0,2,1:T(8,128)(2,1)S(1)}, u32[]{:S(2)}, u32[]{:S(2)}) collective-permute-start(bf16[128,8,32]{0,2,1:T(8,128)(2,1)} %get-tuple-element.4), channel_id=1, source_target_pairs={{0,8},{8,0},{16,24},{24,16},{1,9},{9,1},{17,25},{25,17},{2,10},{10... | collective-permute-start | bytes 196616 | tf_op jit(solution)/shard_map/ppermute | solution.py:77
  15.5 1.5 %collective-permute-start.4 = (bf16[128,8,32]{0,2,1:T(8,128)(2,1)S(1)}, bf16[128,8,32]{0,2,1:T(8,128)(2,1)S(1)}, u32[]{:S(2)}, u32[]{:S(2)}) collective-permute-start(bf16[128,8,32]{0,2,1:T(8,128)(2,1)S(1)} %get-tuple-element.3), channel_id=1, source_target_pairs={{0,16},{8,24},{16,0},{24,8},{1,17},{9,25},{17,1},{25,9},{2,18},{10... | collective-permute-start | bytes 196616 | tf_op jit(solution)/shard_map/ppermute | solution.py:77
  17.1 34.8 %collective-permute-done.3 = bf16[128,8,32]{0,2,1:T(8,128)(2,1)S(1)} collective-permute-done((bf16[128,8,32]{0,2,1:T(8,128)(2,1)}, bf16[128,8,32]{0,2,1:T(8,128)(2,1)S(1)}, u32[]{:S(2)}, u32[]{:S(2)}) %collective-permute-start.3) | collective-permute-done | bytes 65568 | tf_op jit(solution)/shard_map/ppermute | solution.py:77
  51.9 2.7 %collective-permute-start.5 = (bf16[128,8,32]{0,2,1:T(8,128)(2,1)S(1)}, bf16[128,8,32]{0,2,1:T(8,128)(2,1)S(1)}, u32[]{:S(2)}, u32[]{:S(2)}) collective-permute-start(bf16[128,8,32]{0,2,1:T(8,128)(2,1)S(1)} %get-tuple-element.2), channel_id=1, source_target_pairs={{0,24},{8,16},{16,8},{24,0},{1,25},{9,17},{17,9},{25,1},{2,26},{10... | collective-permute-start | bytes 196616 | tf_op jit(solution)/shard_map/ppermute | solution.py:77
  54.6 0.0 collective-permute-done.4
  54.7 2.4 %collective-permute-done.5 = bf16[128,8,32]{0,2,1:T(8,128)(2,1)S(1)} collective-permute-done((bf16[128,8,32]{0,2,1:T(8,128)(2,1)S(1)}, bf16[128,8,32]{0,2,1:T(8,128)(2,1)S(1)}, u32[]{:S(2)}, u32[]{:S(2)}) %collective-permute-start.5) | collective-permute-done | bytes 65568 | tf_op jit(solution)/shard_map/ppermute | solution.py:77
  57.1 0.0 copy-start.1
  57.1 0.7 copy-done.1
  57.8 0.0 all-gather.2.cloned.1.call-update
  57.8 0.0 reduce-scatter.2.cloned.1.call-start
  57.9 0.2 broadcast_in_dim.6
  58.1 0.0 copy-done.2
  58.1 0.1 constant_dynamic-update-slice_fusion.6
  58.2 0.0 collective-permute-done
  58.2 1.3 constant_dynamic-update-slice_fusion.5
  59.5 0.0 collective-permute-done.1
  59.5 0.1 constant_dynamic-update-slice_fusion.4
  59.6 0.0 collective-permute-done.2
  59.6 0.1 constant_dynamic-update-slice_fusion.3.g_ref
  59.7 0.0 copy-start
  59.7 1.8 %copy-done = bf16[512,3584]{1,0:T(8,128)(2,1)} copy-done((bf16[512,3584]{1,0:T(8,128)(2,1)}, bf16[512,3584]{1,0:T(8,128)(2,1)S(1)}, u32[]{:S(2)}) %copy-start) | copy-done | bytes 3670040
  61.5 12.4 %fusion = f32[512,2048]{1,0:T(8,128)} fusion(bf16[512,3584]{1,0:T(8,128)(2,1)S(1)} %constant_dynamic-update-slice_fusion.3.g_ref, bf16[2048,3584]{1,0:T(8,128)(2,1)} %param.8), kind=kOutput, calls=%fused_computation.11 | convolution fusion | flops 7516192768 | bytes 22544384 | tf_op jit(solution)/shard_map/dot_general | solution.py:86
  73.9 0.0 reduce-scatter.2.cloned.1.call-update
  74.6 14.0 %all-gather.2.cloned.1.call-done.a_ref = bf16[64,32,512]{2,1,0:T(8,128)(2,1)} async-done(((bf16[8,32,512]{2,1,0:T(8,128)(2,1)}), bf16[64,32,512]{2,1,0:T(8,128)(2,1)}) %all-gather.2.cloned.1.call-update) | async-done | bytes 2097168 | tf_op jit(solution)/shard_map/all_gather | solution.py:82
  88.6 10.9 %shard_map.77 = bf16[128,32,128]{2,1,0:T(8,128)(2,1)} custom-call(s32[128]{0:T(128)} %rows_ref.1, s32[128]{0:T(128)} %cols_ref.1, s32[1]{0:T(128)S(6)} %copy.22.cnt_ref, bf16[64,32,512]{2,1,0:T(8,128)(2,1)} %all-gather.2.cloned.1.call-done.a_ref, bf16[512,3584]{1,0:T(8,128)(2,1)} %copy-done), custom_call_target="tpu_custom_call" | custom-call | flops 536870912 | bytes 6815744 | tf_op jit(solution)/shard_map/pallas_call | solution.py:54
  99.5 40.9 %reduce-scatter.2.cloned.1.call-done = f32[64,2048]{1,0:T(8,128)} async-done(((f32[512,2048]{1,0:T(8,128)}), f32[64,2048]{1,0:T(8,128)}) %reduce-scatter.2.cloned.1.call-update) | async-done | bytes 524304 | tf_op jit(solution)/shard_map/reduce_scatter | solution.py:89
  140.4 1.8 %convert_element_type.3 = bf16[64,2048]{1,0:T(8,128)(2,1)} convert(f32[64,2048]{1,0:T(8,128)} %reduce-scatter.2.cloned.1.call-done) | non-fusion elementwise | flops 131072 | bytes 786432 | tf_op jit(solution)/shard_map/convert_element_type | solution.py:89
  (5 shorter events, 0.1 us)
Async XLA Ops:
  7.2 50.9 %copy-start.2 = (bf16[128,3584]{1,0:T(8,128)(2,1)S(1)}, bf16[128,3584]{1,0:T(8,128)(2,1)}, u32[]{:S(2)}) copy-start(bf16[128,3584]{1,0:T(8,128)(2,1)} %param.7) | copy-start | bytes 2752516
  7.2 81.4 %all-gather.2.cloned.1.call-start = ((), (), s32[]{:S(2)}) async-start(), calls=%async_computation.2 | async-start | bytes 2359296 | tf_op jit(solution)/shard_map/all_gather | solution.py:82
  7.2 51.0 %collective-permute-start = (bf16[128,3584]{1,0:T(8,128)(2,1)}, bf16[128,3584]{1,0:T(8,128)(2,1)}, u32[]{:S(2)}, u32[]{:S(2)}) collective-permute-start(bf16[128,3584]{1,0:T(8,128)(2,1)} %param.7), channel_id=1, source_target_pairs={{0,8},{8,0},{16,24},{24,16},{1,9},{9,1},{17,25},{25,17},{2,10},{10... | collective-permute-start | bytes 2752520 | tf_op jit(solution)/shard_map/ppermute | solution.py:17
  10.2 49.3 %collective-permute-start.1 = (bf16[128,3584]{1,0:T(8,128)(2,1)}, bf16[128,3584]{1,0:T(8,128)(2,1)S(1)}, u32[]{:S(2)}, u32[]{:S(2)}) collective-permute-start(bf16[128,3584]{1,0:T(8,128)(2,1)} %param.7), channel_id=1, source_target_pairs={{0,16},{8,24},{16,0},{24,8},{1,17},{9,25},{17,1},{25,9},{2,18},{10... | collective-permute-start | bytes 2752520 | tf_op jit(solution)/shard_map/ppermute | solution.py:17
  11.7 47.8 %collective-permute-start.2 = (bf16[128,3584]{1,0:T(8,128)(2,1)}, bf16[128,3584]{1,0:T(8,128)(2,1)S(1)}, u32[]{:S(2)}, u32[]{:S(2)}) collective-permute-start(bf16[128,3584]{1,0:T(8,128)(2,1)} %param.7), channel_id=1, source_target_pairs={{0,24},{8,16},{16,8},{24,0},{1,25},{9,17},{17,9},{25,1},{2,26},{10... | collective-permute-start | bytes 2752520 | tf_op jit(solution)/shard_map/ppermute | solution.py:17
  13.6 38.3 %collective-permute-start.3 = (bf16[128,8,32]{0,2,1:T(8,128)(2,1)}, bf16[128,8,32]{0,2,1:T(8,128)(2,1)S(1)}, u32[]{:S(2)}, u32[]{:S(2)}) collective-permute-start(bf16[128,8,32]{0,2,1:T(8,128)(2,1)} %get-tuple-element.4), channel_id=1, source_target_pairs={{0,8},{8,0},{16,24},{24,16},{1,9},{9,1},{17,25},{25,17},{2,10},{10... | collective-permute-start | bytes 196616 | tf_op jit(solution)/shard_map/ppermute | solution.py:77
  15.5 39.1 %collective-permute-start.4 = (bf16[128,8,32]{0,2,1:T(8,128)(2,1)S(1)}, bf16[128,8,32]{0,2,1:T(8,128)(2,1)S(1)}, u32[]{:S(2)}, u32[]{:S(2)}) collective-permute-start(bf16[128,8,32]{0,2,1:T(8,128)(2,1)S(1)} %get-tuple-element.3), channel_id=1, source_target_pairs={{0,16},{8,24},{16,0},{24,8},{1,17},{9,25},{17,1},{25,9},{2,18},{10... | collective-permute-start | bytes 196616 | tf_op jit(solution)/shard_map/ppermute | solution.py:77
  51.9 5.2 %collective-permute-start.5 = (bf16[128,8,32]{0,2,1:T(8,128)(2,1)S(1)}, bf16[128,8,32]{0,2,1:T(8,128)(2,1)S(1)}, u32[]{:S(2)}, u32[]{:S(2)}) collective-permute-start(bf16[128,8,32]{0,2,1:T(8,128)(2,1)S(1)} %get-tuple-element.2), channel_id=1, source_target_pairs={{0,24},{8,16},{16,8},{24,0},{1,25},{9,17},{17,9},{25,1},{2,26},{10... | collective-permute-start | bytes 196616 | tf_op jit(solution)/shard_map/ppermute | solution.py:77
  57.1 0.7 copy-start.1
  57.8 82.6 %reduce-scatter.2.cloned.1.call-start = ((), (), s32[]{:S(2)}) async-start(), calls=%async_computation.1 | async-start | bytes 4718592 | tf_op jit(solution)/shard_map/reduce_scatter | solution.py:89
  59.7 1.8 %copy-start = (bf16[512,3584]{1,0:T(8,128)(2,1)}, bf16[512,3584]{1,0:T(8,128)(2,1)S(1)}, u32[]{:S(2)}) copy-start(bf16[512,3584]{1,0:T(8,128)(2,1)S(1)} %constant_dynamic-update-slice_fusion.3.g_ref) | copy-start | bytes 11010052
Sparse Core Ops, SparseCore 0:
  57.9 30.5 all-gather.1
  90.9 49.4 reduce-scatter.1

commit v2 on v1

--- a/solution.py
+++ b/solution.py
@@ -9,6 +9,7 @@
 
 BLK = 128
 SLOTS_PER_STEP = 8
+CHUNKS = 4
 
 
 def xor_exchange(x, axis_name, n):
@@ -63,39 +64,52 @@
     )(rows, cols, count, acts_t, gout)
 
 
-def per_device(n_tok, acts, grad_out, weight, block_rows, block_cols, block_count):
-    me = lax.axis_index("tok")
+def per_device(n_tok, n_feat, chunks, acts, grad_out, weight, block_rows, block_cols, block_count):
+    me_tok = lax.axis_index("tok")
+    me_feat = lax.axis_index("feat")
     tok_dev, d_dev = acts.shape
+    f_dev = grad_out.shape[1]
+    tokens = tok_dev * n_tok
+    out_rows = tokens // n_feat
+    own = tok_dev // out_rows
+    piece = out_rows // chunks
     sub = BLK // n_tok
 
-    acts_pieces = acts.reshape(tok_dev, d_dev // BLK, n_tok, sub)
-    send = [
-        lax.dynamic_index_in_dim(acts_pieces, me ^ m, axis=2, keepdims=False)
-        for m in range(n_tok)
-    ]
-    got = [send[0]] + [
-        lax.ppermute(send[m], "tok", perm=[(a, a ^ m) for a in range(n_tok)])
-        for m in range(1, n_tok)
-    ]
-    acts_sub = place_rows(got, me)
-    acts_sub_t = jnp.transpose(acts_sub, (1, 2, 0))
-    acts_t = lax.all_gather(acts_sub_t, "feat", axis=0, tiled=True)
+    def chunked(x):
+        x = x.reshape((own, chunks, piece) + x.shape[1:])
+        return jnp.swapaxes(x, 0, 1).reshape((chunks, own * piece) + x.shape[3:])
 
-    gout = place_rows(xor_exchange(grad_out, "tok", n_tok), me)
+    acts_c = chunked(acts).reshape(chunks, own * piece, d_dev // BLK, n_tok, sub)
+    got = []
+    for m in range(n_tok):
+        part = lax.dynamic_index_in_dim(acts_c, me_tok ^ m, axis=3, keepdims=False)
+        if m:
+            part = lax.ppermute(part, "tok", perm=[(a, a ^ m) for a in range(n_tok)])
+        got.append(part)
+    acts_sub = place_rows(got, me_tok, axis=1)
+    acts_sub_t = jnp.transpose(acts_sub.reshape(tokens, d_dev // BLK, sub), (1, 2, 0))
+    acts_t = place_rows(xor_exchange(acts_sub_t, "feat", n_feat), me_feat)
 
-    partial_sums = lax.dot_general(
-        gout, weight, (((1,), (1,)), ((), ())), preferred_element_type=jnp.float32
-    )
-    grad_in = lax.psum_scatter(partial_sums, "feat", scatter_dimension=0, tiled=True).astype(
-        jnp.bfloat16
-    )
+    gout_c = chunked(grad_out)
+    outs = []
+    gathered = []
+    for c in range(chunks):
+        g = place_rows(xor_exchange(gout_c[c], "tok", n_tok), me_tok)
+        gathered.append(g)
+        partial_sums = lax.dot_general(
+            g, weight, (((1,), (1,)), ((), ())), preferred_element_type=jnp.float32
+        )
+        outs.append(lax.psum_scatter(partial_sums, "feat", scatter_dimension=0, tiled=True))
+    grad_in = jnp.concatenate(outs, axis=0).astype(jnp.bfloat16)
+    gout = jnp.concatenate(gathered, axis=0)
     block_grads = block_tiles(block_rows, block_cols, block_count, acts_t, gout)
     return (grad_in, block_grads)
 
 
 def solution(mesh):
     n_tok = mesh.shape["tok"]
-    assert n_tok & (n_tok - 1) == 0
+    n_feat = mesh.shape["feat"]
+    assert n_tok & (n_tok - 1) == 0 and n_feat & (n_feat - 1) == 0
     in_specs = (
         P("tok", "feat"),
         P("tok", "feat"),
@@ -106,7 +120,7 @@
     )
     out_specs = (P("feat", "tok"), P("feat", "tok", None))
     return jax.shard_map(
-        functools.partial(per_device, n_tok),
+        functools.partial(per_device, n_tok, n_feat, CHUNKS),
         mesh=mesh,
         in_specs=in_specs,
         out_specs=out_specs,

time: 149 us -> 305 us (2.05)
  the two profiles are of different devices: /device:TPU:0 before, /device:TPU:17 now
where the time goes in v2:
time: 305 us; the launch traced here: 304 us
  local copies, waits for them, and re-layouts  154 us (50%)
  matrix products  44.8 us (15%)
  waiting for transfers between devices  41.3 us (14%)
  starting transfers between devices  30.4 us (10%)
  between operations  15 us (5%)
  Pallas kernels  10.9 us (4%)
  other arithmetic  7.63 us (3%)
    dynamic_update_slice x28, local copies, waits for them, and re-layouts, place_rows(): out = lax.dynamic_update_slice_in_dim(out, piece, (me ^ m) * rows, axis)  145 us
    dot_general x4, matrix products, per_device(): lax.dot_general(g, weight, (((1,), (1,)), ((), ())), preferred_element_ty...  44.8 us
    ppermute x19, waiting for transfers between devices, xor_exchange(): out.append(lax.ppermute(x, axis_name, perm=[(a, a ^ m) for a in range(n)]))  41.2 us
    ppermute x19, starting transfers between devices, xor_exchange(): out.append(lax.ppermute(x, axis_name, perm=[(a, a ^ m) for a in range(n)]))  27.2 us
    pallas_call x1, Pallas kernels, block_tiles(): pl.pallas_call(block_kernel, grid_spec=grid_spec, out_shape=jax.ShapeDtyp...  10.9 us
  transfers between devices with their start and end apart: 26, of which 7 were waited for; matrix products, arithmetic and copies ran while one was open for 66% of the time, Pallas kernels for 4%

profile of v2, /device:TPU:17, one launch (start us, length us, event | category | flops | bytes accessed | tf_op | source)
XLA Modules:
  0.0 303.9 jit_solution(10059244437212410485)
XLA Ops:
  7.2 1.2 copy.26
  9.2 1.2 collective-permute-start.9
  10.4 1.2 collective-permute-start.10
  11.9 1.2 collective-permute-start.6
  13.1 1.2 collective-permute-start.7
  14.4 1.0 constant_dynamic-update-slice_fusion.11
  16.0 2.2 collective-permute-start.8
  18.2 1.0 constant_dynamic-update-slice_fusion.10
  19.4 1.0 constant_dynamic-update-slice_fusion.9
  20.4 1.5 collective-permute-done.11
  22.1 1.0 constant_dynamic-update-slice_fusion.8
  23.1 10.9 %fusion.4 = f32[128,2048]{1,0:T(8,128)} fusion(bf16[128,3584]{1,0:T(8,128)(2,1)S(1)} %constant_dynamic-update-slice_fusion.8, bf16[2048,3584]{1,0:T(8,128)(2,1)} %param.8), kind=kOutput, calls=%fused_computation.39 | convolution fusion | flops 1879048192 | bytes 16646144 | tf_op jit(solution)/shard_map/dot_general | solution.py:99
  34.1 2.2 collective-permute-start.5
  36.3 1.0 constant_dynamic-update-slice_fusion.14
  37.6 1.0 constant_dynamic-update-slice_fusion.13
  38.9 1.0 constant_dynamic-update-slice_fusion.12
  39.8 11.2 %fusion.3 = f32[128,2048]{1,0:T(8,128)} fusion(bf16[128,3584]{1,0:T(8,128)(2,1)S(1)} %constant_dynamic-update-slice_fusion.12, bf16[2048,3584]{1,0:T(8,128)(2,1)} %param.8), kind=kOutput, calls=%fused_computation.38 | convolution fusion | flops 1879048192 | bytes 16646144 | tf_op jit(solution)/shard_map/dot_general | solution.py:99
  51.1 2.2 collective-permute-start.2
  53.4 1.0 constant_dynamic-update-slice_fusion.18
  54.3 1.0 constant_dynamic-update-slice_fusion.17
  55.3 1.0 constant_dynamic-update-slice_fusion.16
  56.3 11.4 %fusion.2 = f32[128,2048]{1,0:T(8,128)} fusion(bf16[128,3584]{1,0:T(8,128)(2,1)S(1)} %constant_dynamic-update-slice_fusion.16, bf16[2048,3584]{1,0:T(8,128)(2,1)} %param.8), kind=kOutput, calls=%fused_computation.37 | convolution fusion | flops 1879048192 | bytes 16646144 | tf_op jit(solution)/shard_map/dot_general | solution.py:99
  68.0 1.0 constant_dynamic-update-slice_fusion.22
  69.0 1.0 constant_dynamic-update-slice_fusion.20
  70.0 11.2 %fusion.1 = f32[128,2048]{1,0:T(8,128)} fusion(bf16[128,3584]{1,0:T(8,128)(2,1)S(1)} %constant_dynamic-update-slice_fusion.20, bf16[2048,3584]{1,0:T(8,128)(2,1)} %param.8), kind=kOutput, calls=%fused_computation.36 | convolution fusion | flops 1879048192 | bytes 16646144 | tf_op jit(solution)/shard_map/dot_general | solution.py:99
  81.3 0.8 reshape_reshape.3
  82.1 2.4 constant_dynamic-slice_fusion
  85.3 2.2 collective-permute-start.14
  89.0 7.5 %dynamic_update_slice.100 = bf16[4,128,8,32]{1,0,3,2:T(4,128)(2,1)S(1)} dynamic-update-slice(bf16[4,128,8,32]{1,0,3,2:T(4,128)(2,1)S(1)} %broadcast_in_dim.7, bf16[4,32,8,32]{1,0,3,2:T(4,128)(2,1)S(1)} %bitcast.37, s32[]{:T(128)} %constant.18.clone.1, s32[]{:T(128)S(6)} %select_n.65, s32[]{:T(128)} %constant.18.clone.1, s32[]{:T(128)} %constant.18.clone.1) | dynamic-update-slice | bytes 131076 | tf_op jit(solution)/shard_map/dynamic_update_slice | solution.py:28
  96.8 42.0 %dynamic_update_slice.101 = bf16[4,128,8,32]{1,0,3,2:T(4,128)(2,1)S(1)} dynamic-update-slice(bf16[4,128,8,32]{1,0,3,2:T(4,128)(2,1)S(1)} %dynamic_update_slice.100, bf16[4,32,8,32]{1,0,3,2:T(4,128)(2,1)S(1)} %copy.14, s32[]{:T(128)} %constant.18.clone.1, s32[]{:T(128)S(6)} %select_n.66, s32[]{:T(128)} %constant.18.clone.1, s32[]{:T(128)} %constant.18.clone.1) | dynamic-update-slice | bytes 131076 | tf_op jit(solution)/shard_map/dynamic_update_slice | solution.py:28
  139.0 42.0 %dynamic_update_slice.102 = bf16[4,128,8,32]{1,0,3,2:T(4,128)(2,1)S(1)} dynamic-update-slice(bf16[4,128,8,32]{1,0,3,2:T(4,128)(2,1)S(1)} %dynamic_update_slice.101, bf16[4,32,8,32]{1,0,3,2:T(4,128)(2,1)S(1)} %copy.15, s32[]{:T(128)} %constant.18.clone.1, s32[]{:T(128)S(6)} %select_n.67, s32[]{:T(128)} %constant.18.clone.1, s32[]{:T(128)} %constant.18.clone.1) | dynamic-update-slice | bytes 131076 | tf_op jit(solution)/shard_map/dynamic_update_slice | solution.py:28
  181.3 42.0 %dynamic_update_slice.103 = bf16[4,128,8,32]{1,0,3,2:T(4,128)(2,1)S(1)} dynamic-update-slice(bf16[4,128,8,32]{1,0,3,2:T(4,128)(2,1)S(1)} %dynamic_update_slice.102, bf16[4,32,8,32]{1,0,3,2:T(4,128)(2,1)S(1)} %copy.16, s32[]{:T(128)} %constant.18.clone.1, s32[]{:T(128)S(6)} %select_n.68, s32[]{:T(128)} %constant.18.clone.1, s32[]{:T(128)} %constant.18.clone.1) | dynamic-update-slice | bytes 131076 | tf_op jit(solution)/shard_map/dynamic_update_slice | solution.py:28
  223.3 7.3 %collective-permute-start.15 = (bf16[8,32,512]{2,1,0:T(8,128)(2,1)S(1)}, bf16[8,32,512]{2,1,0:T(8,128)(2,1)S(1)}, u32[]{:S(2)}, u32[]{:S(2)}) collective-permute-start(bf16[8,32,512]{2,1,0:T(8,128)(2,1)S(1)} %bitcast.39), channel_id=1, source_target_pairs={{0,1},{1,0},{2,3},{3,2},{4,5},{5,4},{6,7},{7,6},{8,9},{9,8},{10,11... | collective-permute-start | bytes 786440 | tf_op jit(solution)/shard_map/ppermute | solution.py:18
  230.6 1.3 collective-permute-start.16
  232.4 2.7 collective-permute-start.19
  235.3 3.3 %pad_maximum_fusion.g_ref = bf16[512,3584]{1,0:T(8,128)(2,1)} fusion(bf16[128,3584]{1,0:T(8,128)(2,1)S(1)} %constant_dynamic-update-slice_fusion.8, bf16[128,3584]{1,0:T(8,128)(2,1)} %copy-done.1, bf16[128,3584]{1,0:T(8,128)(2,1)} %copy-done.2, bf16[128,3584]{1,0:T(8,128)(2,1)} %copy-done.5), kind=kLoop, calls=%fused_computation | loop fusion | flops 14680064 | bytes 7340032 | tf_op jit(solution)/shard_map/concatenate | solution.py:104
  238.7 7.3 %collective-permute-done.16 = bf16[8,32,512]{2,1,0:T(8,128)(2,1)S(1)} collective-permute-done((bf16[8,32,512]{2,1,0:T(8,128)(2,1)S(1)}, bf16[8,32,512]{2,1,0:T(8,128)(2,1)S(1)}, u32[]{:S(2)}, u32[]{:S(2)}) %collective-permute-start.16) | collective-permute-done | bytes 262176 | tf_op jit(solution)/shard_map/ppermute | solution.py:18
  246.0 2.5 collective-permute-start.21
  248.5 3.1 %collective-permute-done.17 = bf16[8,32,512]{2,1,0:T(8,128)(2,1)S(1)} collective-permute-done((bf16[8,32,512]{2,1,0:T(8,128)(2,1)S(1)}, bf16[8,32,512]{2,1,0:T(8,128)(2,1)S(1)}, u32[]{:S(2)}, u32[]{:S(2)}) %collective-permute-start.17) | collective-permute-done | bytes 262176 | tf_op jit(solution)/shard_map/ppermute | solution.py:18
  251.7 4.2 %collective-permute-done.19 = bf16[8,32,512]{2,1,0:T(8,128)(2,1)S(1)} collective-permute-done((bf16[8,32,512]{2,1,0:T(8,128)(2,1)S(1)}, bf16[8,32,512]{2,1,0:T(8,128)(2,1)S(1)}, u32[]{:S(2)}, u32[]{:S(2)}) %collective-permute-start.19) | collective-permute-done | bytes 262176 | tf_op jit(solution)/shard_map/ppermute | solution.py:18
  255.9 18.9 %collective-permute-done.20 = bf16[8,32,512]{2,1,0:T(8,128)(2,1)S(1)} collective-permute-done((bf16[8,32,512]{2,1,0:T(8,128)(2,1)S(1)}, bf16[8,32,512]{2,1,0:T(8,128)(2,1)S(1)}, u32[]{:S(2)}, u32[]{:S(2)}) %collective-permute-start.20) | collective-permute-done | bytes 262176 | tf_op jit(solution)/shard_map/ppermute | solution.py:18
  274.8 5.9 %collective-permute-done.21 = bf16[8,32,512]{2,1,0:T(8,128)(2,1)S(1)} collective-permute-done((bf16[8,32,512]{2,1,0:T(8,128)(2,1)S(1)}, bf16[8,32,512]{2,1,0:T(8,128)(2,1)S(1)}, u32[]{:S(2)}, u32[]{:S(2)}) %collective-permute-start.21) | collective-permute-done | bytes 262176 | tf_op jit(solution)/shard_map/ppermute | solution.py:18
  280.8 1.3 copy-done
  282.1 10.9 %shard_map.77 = bf16[128,32,128]{2,1,0:T(8,128)(2,1)} custom-call(s32[128]{0:T(128)} %rows_ref.1, s32[128]{0:T(128)} %cols_ref.1, s32[1]{0:T(128)S(6)} %copy.59.cnt_ref, bf16[64,32,512]{2,1,0:T(8,128)(2,1)} %copy-done, bf16[512,3584]{1,0:T(8,128)(2,1)} %pad_maximum_fusion.g_ref), custom_call_target="tpu_custom_call" | custom-call | flops 536870912 | bytes 6815744 | tf_op jit(solution)/shard_map/pallas_call | solution.py:55
  293.0 0.9 convert.15
  293.9 0.9 convert.14
  294.8 0.9 convert.13
  295.8 0.9 convert.12
  (80 shorter events, 7.4 us)
Async XLA Ops:
  7.2 285.8 %reduce-scatter.11.cloned.1.call-start = ((), (), s32[]{:S(2)}) async-start(), calls=%async_computation.7 | async-start | bytes 1179648 | tf_op jit(solution)/shard_map/reduce_scatter | solution.py:102
  9.2 6.8 %collective-permute-start.9 = (bf16[32,3584]{1,0:T(8,128)(2,1)}, bf16[32,3584]{1,0:T(8,128)(2,1)}, u32[]{:S(2)}, u32[]{:S(2)}) collective-permute-start(bf16[32,3584]{1,0:T(8,128)(2,1)} %bitcast.5), channel_id=1, source_target_pairs={{0,8},{8,0},{16,24},{24,16},{1,9},{9,1},{17,25},{25,17},{2,10},{10... | collective-permute-start | bytes 688136 | tf_op jit(solution)/shard_map/ppermute | solution.py:18
  10.4 8.7 %collective-permute-start.10 = (bf16[32,3584]{1,0:T(8,128)(2,1)}, bf16[32,3584]{1,0:T(8,128)(2,1)}, u32[]{:S(2)}, u32[]{:S(2)}) collective-permute-start(bf16[32,3584]{1,0:T(8,128)(2,1)} %bitcast.5), channel_id=1, source_target_pairs={{0,16},{8,24},{16,0},{24,8},{1,17},{9,25},{17,1},{25,9},{2,18},{10... | collective-permute-start | bytes 688136 | tf_op jit(solution)/shard_map/ppermute | solution.py:18
  11.7 10.3 %collective-permute-start.11 = (bf16[32,3584]{1,0:T(8,128)(2,1)}, bf16[32,3584]{1,0:T(8,128)(2,1)}, u32[]{:S(2)}, u32[]{:S(2)}) collective-permute-start(bf16[32,3584]{1,0:T(8,128)(2,1)} %bitcast.5), channel_id=1, source_target_pairs={{0,24},{8,16},{16,8},{24,0},{1,25},{9,17},{17,9},{25,1},{2,26},{10... | collective-permute-start | bytes 688136 | tf_op jit(solution)/shard_map/ppermute | solution.py:18
  11.9 22.2 %collective-permute-start.6 = (bf16[32,3584]{1,0:T(8,128)(2,1)S(1)}, bf16[32,3584]{1,0:T(8,128)(2,1)}, u32[]{:S(2)}, u32[]{:S(2)}) collective-permute-start(bf16[32,3584]{1,0:T(8,128)(2,1)S(1)} %bitcast.55), channel_id=1, source_target_pairs={{0,8},{8,0},{16,24},{24,16},{1,9},{9,1},{17,25},{25,17},{2,10},{10... | collective-permute-start | bytes 688136 | tf_op jit(solution)/shard_map/ppermute | solution.py:18
  13.1 24.2 %collective-permute-start.7 = (bf16[32,3584]{1,0:T(8,128)(2,1)S(1)}, bf16[32,3584]{1,0:T(8,128)(2,1)}, u32[]{:S(2)}, u32[]{:S(2)}) collective-permute-start(bf16[32,3584]{1,0:T(8,128)(2,1)S(1)} %bitcast.56), channel_id=1, source_target_pairs={{0,16},{8,24},{16,0},{24,8},{1,17},{9,25},{17,1},{25,9},{2,18},{10... | collective-permute-start | bytes 688136 | tf_op jit(solution)/shard_map/ppermute | solution.py:18
  15.7 6.3 %copy-start.3 = (bf16[128,3584]{1,0:T(8,128)(2,1)}, bf16[128,3584]{1,0:T(8,128)(2,1)S(1)}, u32[]{:S(2)}) copy-start(bf16[128,3584]{1,0:T(8,128)(2,1)S(1)} %constant_dynamic-update-slice_fusion.23) | copy-start | bytes 2752516
  16.0 22.6 %collective-permute-start.8 = (bf16[32,3584]{1,0:T(8,128)(2,1)S(1)}, bf16[32,3584]{1,0:T(8,128)(2,1)}, u32[]{:S(2)}, u32[]{:S(2)}) collective-permute-start(bf16[32,3584]{1,0:T(8,128)(2,1)S(1)} %bitcast.58), channel_id=1, source_target_pairs={{0,24},{8,16},{16,8},{24,0},{1,25},{9,17},{17,9},{25,1},{2,26},{10... | collective-permute-start | bytes 688136 | tf_op jit(solution)/shard_map/ppermute | solution.py:18
  19.1 32.0 %collective-permute-start.3 = (bf16[32,3584]{1,0:T(8,128)(2,1)S(1)}, bf16[32,3584]{1,0:T(8,128)(2,1)}, u32[]{:S(2)}, u32[]{:S(2)}) collective-permute-start(bf16[32,3584]{1,0:T(8,128)(2,1)S(1)} %bitcast.52), channel_id=1, source_target_pairs={{0,8},{8,0},{16,24},{24,16},{1,9},{9,1},{17,25},{25,17},{2,10},{10... | collective-permute-start | bytes 688136 | tf_op jit(solution)/shard_map/ppermute | solution.py:18
  21.9 32.4 %collective-permute-start.4 = (bf16[32,3584]{1,0:T(8,128)(2,1)S(1)}, bf16[32,3584]{1,0:T(8,128)(2,1)}, u32[]{:S(2)}, u32[]{:S(2)}) collective-permute-start(bf16[32,3584]{1,0:T(8,128)(2,1)S(1)} %bitcast.53), channel_id=1, source_target_pairs={{0,16},{8,24},{16,0},{24,8},{1,17},{9,25},{17,1},{25,9},{2,18},{10... | collective-permute-start | bytes 688136 | tf_op jit(solution)/shard_map/ppermute | solution.py:18
  34.0 259.9 %reduce-scatter.9.cloned.1.call-start = ((), (), s32[]{:S(2)}) async-start(), calls=%async_computation.6 | async-start | bytes 1179648 | tf_op jit(solution)/shard_map/reduce_scatter | solution.py:102
  34.1 21.2 %collective-permute-start.5 = (bf16[32,3584]{1,0:T(8,128)(2,1)S(1)}, bf16[32,3584]{1,0:T(8,128)(2,1)}, u32[]{:S(2)}, u32[]{:S(2)}) collective-permute-start(bf16[32,3584]{1,0:T(8,128)(2,1)S(1)} %bitcast.54), channel_id=1, source_target_pairs={{0,24},{8,16},{16,8},{24,0},{1,25},{9,17},{17,9},{25,1},{2,26},{10... | collective-permute-start | bytes 688136 | tf_op jit(solution)/shard_map/ppermute | solution.py:18
  37.3 30.7 %collective-permute-start = (bf16[32,3584]{1,0:T(8,128)(2,1)S(1)}, bf16[32,3584]{1,0:T(8,128)(2,1)}, u32[]{:S(2)}, u32[]{:S(2)}) collective-permute-start(bf16[32,3584]{1,0:T(8,128)(2,1)S(1)} %bitcast.48), channel_id=1, source_target_pairs={{0,8},{8,0},{16,24},{24,16},{1,9},{9,1},{17,25},{25,17},{2,10},{10... | collective-permute-start | bytes 688136 | tf_op jit(solution)/shard_map/ppermute | solution.py:18
  38.6 30.4 %collective-permute-start.1 = (bf16[32,3584]{1,0:T(8,128)(2,1)S(1)}, bf16[32,3584]{1,0:T(8,128)(2,1)S(1)}, u32[]{:S(2)}, u32[]{:S(2)}) collective-permute-start(bf16[32,3584]{1,0:T(8,128)(2,1)S(1)} %bitcast.49), channel_id=1, source_target_pairs={{0,16},{8,24},{16,0},{24,8},{1,17},{9,25},{17,1},{25,9},{2,18},{10... | collective-permute-start | bytes 688136 | tf_op jit(solution)/shard_map/ppermute | solution.py:18
  39.8 11.2 %copy-start.1 = (bf16[128,3584]{1,0:T(8,128)(2,1)}, bf16[128,3584]{1,0:T(8,128)(2,1)S(1)}, u32[]{:S(2)}) copy-start(bf16[128,3584]{1,0:T(8,128)(2,1)S(1)} %constant_dynamic-update-slice_fusion.12) | copy-start | bytes 2752516
  51.1 243.8 %reduce-scatter.7.cloned.1.call-start = ((), (), s32[]{:S(2)}) async-start(), calls=%async_computation.5 | async-start | bytes 1179648 | tf_op jit(solution)/shard_map/reduce_scatter | solution.py:102
  51.1 17.9 %collective-permute-start.2 = (bf16[32,3584]{1,0:T(8,128)(2,1)S(1)}, bf16[32,3584]{1,0:T(8,128)(2,1)}, u32[]{:S(2)}, u32[]{:S(2)}) collective-permute-start(bf16[32,3584]{1,0:T(8,128)(2,1)S(1)} %bitcast.50), channel_id=1, source_target_pairs={{0,24},{8,16},{16,8},{24,0},{1,25},{9,17},{17,9},{25,1},{2,26},{10... | collective-permute-start | bytes 688136 | tf_op jit(solution)/shard_map/ppermute | solution.py:18
  56.3 11.4 %copy-start.2 = (bf16[128,3584]{1,0:T(8,128)(2,1)}, bf16[128,3584]{1,0:T(8,128)(2,1)S(1)}, u32[]{:S(2)}) copy-start(bf16[128,3584]{1,0:T(8,128)(2,1)S(1)} %constant_dynamic-update-slice_fusion.16) | copy-start | bytes 2752516
  56.3 11.7 %copy-start.4 = (bf16[128,3584]{1,0:T(8,128)(2,1)S(1)}, bf16[128,3584]{1,0:T(8,128)(2,1)}, u32[]{:S(2)}) copy-start(bf16[128,3584]{1,0:T(8,128)(2,1)} %copy-done.3) | copy-start | bytes 2752516
  67.7 228.0 %reduce-scatter.5.cloned.1.call-start = ((), (), s32[]{:S(2)}) async-start(), calls=%async_computation.4 | async-start | bytes 1179648 | tf_op jit(solution)/shard_map/reduce_scatter | solution.py:102
  70.0 11.2 %copy-start.5 = (bf16[128,3584]{1,0:T(8,128)(2,1)}, bf16[128,3584]{1,0:T(8,128)(2,1)S(1)}, u32[]{:S(2)}) copy-start(bf16[128,3584]{1,0:T(8,128)(2,1)S(1)} %constant_dynamic-update-slice_fusion.20) | copy-start | bytes 2752516
  70.0 11.3 %copy-start.6 = (bf16[128,1024]{1,0:T(8,128)(2,1)S(1)}, bf16[128,1024]{1,0:T(8,128)(2,1)}, u32[]{:S(2)}) copy-start(bf16[128,1024]{1,0:T(8,128)(2,1)} %param.6) | copy-start | bytes 786436
  84.6 11.9 %collective-permute-start.12 = (bf16[4,32,8,32]{3,2,1,0:T(8,128)(2,1)S(1)}, bf16[4,32,8,32]{3,2,1,0:T(8,128)(2,1)S(1)}, u32[]{:S(2)}, u32[]{:S(2)}) collective-permute-start(bf16[4,32,8,32]{3,2,1,0:T(8,128)(2,1)S(1)} %bitcast.61), channel_id=1, source_target_pairs={{0,8},{8,0},{16,24},{24,16},{1,9},{9,1},{17,25},{25,17},{2,10},{10... | collective-permute-start | bytes 196616 | tf_op jit(solution)/shard_map/ppermute | solution.py:87
  85.0 53.8 %collective-permute-start.13 = (bf16[4,32,8,32]{3,2,1,0:T(8,128)(2,1)S(1)}, bf16[4,32,8,32]{3,2,1,0:T(8,128)(2,1)S(1)}, u32[]{:S(2)}, u32[]{:S(2)}) collective-permute-start(bf16[4,32,8,32]{3,2,1,0:T(8,128)(2,1)S(1)} %bitcast.60), channel_id=1, source_target_pairs={{0,16},{8,24},{16,0},{24,8},{1,17},{9,25},{17,1},{25,9},{2,18},{10... | collective-permute-start | bytes 196616 | tf_op jit(solution)/shard_map/ppermute | solution.py:87
  85.3 95.7 %collective-permute-start.14 = (bf16[4,32,8,32]{3,2,1,0:T(8,128)(2,1)S(1)}, bf16[4,32,8,32]{3,2,1,0:T(8,128)(2,1)S(1)}, u32[]{:S(2)}, u32[]{:S(2)}) collective-permute-start(bf16[4,32,8,32]{3,2,1,0:T(8,128)(2,1)S(1)} %bitcast.59), channel_id=1, source_target_pairs={{0,24},{8,16},{16,8},{24,0},{1,25},{9,17},{17,9},{25,1},{2,26},{10... | collective-permute-start | bytes 196616 | tf_op jit(solution)/shard_map/ppermute | solution.py:87
  223.3 15.3 %collective-permute-start.15 = (bf16[8,32,512]{2,1,0:T(8,128)(2,1)S(1)}, bf16[8,32,512]{2,1,0:T(8,128)(2,1)S(1)}, u32[]{:S(2)}, u32[]{:S(2)}) collective-permute-start(bf16[8,32,512]{2,1,0:T(8,128)(2,1)S(1)} %bitcast.39), channel_id=1, source_target_pairs={{0,1},{1,0},{2,3},{3,2},{4,5},{5,4},{6,7},{7,6},{8,9},{9,8},{10,11... | collective-permute-start | bytes 786440 | tf_op jit(solution)/shard_map/ppermute | solution.py:18
  230.6 15.4 %collective-permute-start.16 = (bf16[8,32,512]{2,1,0:T(8,128)(2,1)S(1)}, bf16[8,32,512]{2,1,0:T(8,128)(2,1)S(1)}, u32[]{:S(2)}, u32[]{:S(2)}) collective-permute-start(bf16[8,32,512]{2,1,0:T(8,128)(2,1)S(1)} %bitcast.40), channel_id=1, source_target_pairs={{0,2},{1,3},{2,0},{3,1},{4,6},{5,7},{6,4},{7,5},{8,10},{9,11},{10,... | collective-permute-start | bytes 786440 | tf_op jit(solution)/shard_map/ppermute | solution.py:18
  231.9 19.7 %collective-permute-start.17 = (bf16[8,32,512]{2,1,0:T(8,128)(2,1)S(1)}, bf16[8,32,512]{2,1,0:T(8,128)(2,1)S(1)}, u32[]{:S(2)}, u32[]{:S(2)}) collective-permute-start(bf16[8,32,512]{2,1,0:T(8,128)(2,1)S(1)} %bitcast.41), channel_id=1, source_target_pairs={{0,3},{1,2},{2,1},{3,0},{4,7},{5,6},{6,5},{7,4},{8,11},{9,10},{10,... | collective-permute-start | bytes 786440 | tf_op jit(solution)/shard_map/ppermute | solution.py:18
  232.4 19.3 %collective-permute-start.18 = (bf16[8,32,512]{2,1,0:T(8,128)(2,1)S(1)}, bf16[8,32,512]{2,1,0:T(8,128)(2,1)S(1)}, u32[]{:S(2)}, u32[]{:S(2)}) collective-permute-start(bf16[8,32,512]{2,1,0:T(8,128)(2,1)S(1)} %bitcast.42), channel_id=1, source_target_pairs={{0,4},{1,5},{2,6},{3,7},{4,0},{5,1},{6,2},{7,3},{8,12},{9,13},{10,... | collective-permute-start | bytes 786440 | tf_op jit(solution)/shard_map/ppermute | solution.py:18
  232.4 23.6 %collective-permute-start.19 = (bf16[8,32,512]{2,1,0:T(8,128)(2,1)S(1)}, bf16[8,32,512]{2,1,0:T(8,128)(2,1)S(1)}, u32[]{:S(2)}, u32[]{:S(2)}) collective-permute-start(bf16[8,32,512]{2,1,0:T(8,128)(2,1)S(1)} %bitcast.43), channel_id=1, source_target_pairs={{0,5},{1,4},{2,7},{3,6},{4,1},{5,0},{6,3},{7,2},{8,13},{9,12},{10,... | collective-permute-start | bytes 786440 | tf_op jit(solution)/shard_map/ppermute | solution.py:18
  238.6 36.2 %collective-permute-start.20 = (bf16[8,32,512]{2,1,0:T(8,128)(2,1)S(1)}, bf16[8,32,512]{2,1,0:T(8,128)(2,1)S(1)}, u32[]{:S(2)}, u32[]{:S(2)}) collective-permute-start(bf16[8,32,512]{2,1,0:T(8,128)(2,1)S(1)} %bitcast.44), channel_id=1, source_target_pairs={{0,6},{1,7},{2,4},{3,5},{4,2},{5,3},{6,0},{7,1},{8,14},{9,15},{10,... | collective-permute-start | bytes 786440 | tf_op jit(solution)/shard_map/ppermute | solution.py:18
  246.0 34.7 %collective-permute-start.21 = (bf16[8,32,512]{2,1,0:T(8,128)(2,1)S(1)}, bf16[8,32,512]{2,1,0:T(8,128)(2,1)S(1)}, u32[]{:S(2)}, u32[]{:S(2)}) collective-permute-start(bf16[8,32,512]{2,1,0:T(8,128)(2,1)S(1)} %bitcast.45), channel_id=1, source_target_pairs={{0,7},{1,6},{2,5},{3,4},{4,3},{5,2},{6,1},{7,0},{8,15},{9,14},{10,... | collective-permute-start | bytes 786440 | tf_op jit(solution)/shard_map/ppermute | solution.py:18
  280.7 1.3 copy-start
Sparse Core Ops, SparseCore 0:
  34.1 32.4 reduce-scatter.10
  68.9 31.1 reduce-scatter.8
  102.4 30.7 reduce-scatter.6
  135.3 30.8 reduce-scatter.4

commit v3 on v1

--- a/solution.py
+++ b/solution.py
@@ -77,6 +77,7 @@
         lax.ppermute(send[m], "tok", perm=[(a, a ^ m) for a in range(n_tok)])
         for m in range(1, n_tok)
     ]
+    got, grad_out = lax.optimization_barrier((got, grad_out))
     acts_sub = place_rows(got, me)
     acts_sub_t = jnp.transpose(acts_sub, (1, 2, 0))
     acts_t = lax.all_gather(acts_sub_t, "feat", axis=0, tiled=True)

time: 149 us -> 132 us (0.89)
  waiting for transfers between devices: 92.2 us -> 78.6 us
  starting transfers between devices: 10.8 us -> 8.11 us
    ppermute x3, waiting for transfers between devices: 0.01 us -> 34.9 us  [xor_exchange(): out.append(lax.ppermute(x, axis_name, perm=[(a, a ^ m) for a in range(n)]))]
    ppermute x3, waiting for transfers between devices: 37.2 us -> 5.14 us  [per_device(): lax.ppermute(send[m], 'tok', perm=[(a, a ^ m) for a in range(n_tok)])]
    all_gather x1, waiting for transfers between devices: 14 us -> 0.02 us  [per_device(): acts_t = lax.all_gather(acts_sub_t, 'feat', axis=0, tiled=True)]
    reduce_scatter x1, waiting for transfers between devices: 40.9 us -> 38.5 us  [per_device(): lax.psum_scatter(partial_sums, 'feat', scatter_dimension=0, tiled=True)]
    ppermute x3, starting transfers between devices: 6.16 us -> 4.54 us  [per_device(): lax.ppermute(send[m], 'tok', perm=[(a, a ^ m) for a in range(n_tok)])]
  transfers between devices with their start and end apart: 8 -> 8, of which waited for: 4 -> 6; matrix products, arithmetic and copies ran while one was open for 11% -> 11% of each run, Pallas kernels for 7% -> 8%
where the time goes in v3:
time: 132 us
  waiting for transfers between devices  78.6 us (60%)
  between operations  14.8 us (11%)
  matrix products  12.4 us (9%)
  Pallas kernels  10.9 us (8%)
  starting transfers between devices  8.11 us (6%)
  local copies, waits for them, and re-layouts  5.56 us (4%)
  other arithmetic  1.77 us (1%)
    reduce_scatter x1, waiting for transfers between devices, per_device(): lax.psum_scatter(partial_sums, 'feat', scatter_dimension=0, tiled=True)  38.5 us
    ppermute x3, waiting for transfers between devices, xor_exchange(): out.append(lax.ppermute(x, axis_name, perm=[(a, a ^ m) for a in range(n)]))  34.9 us
    dot_general x1, matrix products, per_device(): lax.dot_general(gout, weight, (((1,), (1,)), ((), ())), preferred_element...  12.4 us
    pallas_call x1, Pallas kernels, block_tiles(): pl.pallas_call(block_kernel, grid_spec=grid_spec, out_shape=jax.ShapeDtyp...  10.9 us
    ppermute x3, waiting for transfers between devices, per_device(): lax.ppermute(send[m], 'tok', perm=[(a, a ^ m) for a in range(n_tok)])  5.14 us
    ppermute x3, starting transfers between devices, per_device(): lax.ppermute(send[m], 'tok', perm=[(a, a ^ m) for a in range(n_tok)])  4.54 us
    unnamed x7, local copies, waits for them, and re-layouts  3.68 us
    ppermute x3, starting transfers between devices, xor_exchange(): out.append(lax.ppermute(x, axis_name, perm=[(a, a ^ m) for a in range(n)]))  3.49 us
  transfers between devices with their start and end apart: 8, of which 6 were waited for; matrix products, arithmetic and copies ran while one was open for 11% of the time, Pallas kernels for 8%

profile of v3, /device:TPU:0, one launch (start us, length us, event | category | flops | bytes accessed | tf_op | source)
XLA Modules:
  0.0 132.2 jit_solution(13744609461083952037)
XLA Ops:
  7.2 0.0 copy-start.2
  7.2 0.0 all-gather.2.cloned.1.call-start
  7.2 1.2 copy.13
  8.5 3.0 %collective-permute-start = (bf16[128,8,32]{0,2,1:T(8,128)(2,1)S(1)}, bf16[128,8,32]{0,2,1:T(8,128)(2,1)S(1)}, u32[]{:S(2)}, u32[]{:S(2)}) collective-permute-start(bf16[128,8,32]{0,2,1:T(8,128)(2,1)S(1)} %get-tuple-element.14), channel_id=1, source_target_pairs={{0,8},{8,0},{16,24},{24,16},{1,9},{9,1},{17,25},{25,17},{2,10},{10... | collective-permute-start | bytes 196616 | tf_op jit(solution)/shard_map/ppermute | solution.py:77
  11.5 1.5 %collective-permute-start.1 = (bf16[128,8,32]{0,2,1:T(8,128)(2,1)S(1)}, bf16[128,8,32]{0,2,1:T(8,128)(2,1)S(1)}, u32[]{:S(2)}, u32[]{:S(2)}) collective-permute-start(bf16[128,8,32]{0,2,1:T(8,128)(2,1)S(1)} %get-tuple-element.13), channel_id=1, source_target_pairs={{0,16},{8,24},{16,0},{24,8},{1,17},{9,25},{17,1},{25,9},{2,18},{10... | collective-permute-start | bytes 196616 | tf_op jit(solution)/shard_map/ppermute | solution.py:77
  13.0 0.0 collective-permute-start.2
  13.0 0.8 collective-permute-done
  13.8 1.9 %collective-permute-done.1 = bf16[128,8,32]{0,2,1:T(8,128)(2,1)S(1)} collective-permute-done((bf16[128,8,32]{0,2,1:T(8,128)(2,1)S(1)}, bf16[128,8,32]{0,2,1:T(8,128)(2,1)S(1)}, u32[]{:S(2)}, u32[]{:S(2)}) %collective-permute-start.1) | collective-permute-done | bytes 65568 | tf_op jit(solution)/shard_map/ppermute | solution.py:77
  15.8 2.4 %collective-permute-done.2 = bf16[128,8,32]{0,2,1:T(8,128)(2,1)S(1)} collective-permute-done((bf16[128,8,32]{0,2,1:T(8,128)(2,1)S(1)}, bf16[128,8,32]{0,2,1:T(8,128)(2,1)S(1)}, u32[]{:S(2)}, u32[]{:S(2)}) %collective-permute-start.2) | collective-permute-done | bytes 65568 | tf_op jit(solution)/shard_map/ppermute | solution.py:77
  18.2 0.5 collective-permute-start.3
  18.7 0.3 collective-permute-start.4
  19.0 2.7 %collective-permute-start.5 = (bf16[128,3584]{1,0:T(8,128)(2,1)}, bf16[128,3584]{1,0:T(8,128)(2,1)S(1)}, u32[]{:S(2)}, u32[]{:S(2)}) collective-permute-start(bf16[128,3584]{1,0:T(8,128)(2,1)} %param.7), channel_id=1, source_target_pairs={{0,24},{8,16},{16,8},{24,0},{1,25},{9,17},{17,9},{25,1},{2,26},{10... | collective-permute-start | bytes 2752520 | tf_op jit(solution)/shard_map/ppermute | solution.py:17
  21.8 0.0 copy-start.1
  21.8 0.7 copy-done.1
  22.5 0.0 all-gather.2.cloned.1.call-update
  22.5 0.0 reduce-scatter.2.cloned.1.call-start
  22.6 0.2 broadcast_in_dim.6
  22.8 0.0 copy-done.2
  22.8 0.1 constant_dynamic-update-slice_fusion.7
  22.9 18.8 %collective-permute-done.3 = bf16[128,3584]{1,0:T(8,128)(2,1)} collective-permute-done((bf16[128,3584]{1,0:T(8,128)(2,1)}, bf16[128,3584]{1,0:T(8,128)(2,1)}, u32[]{:S(2)}, u32[]{:S(2)}) %collective-permute-start.3) | collective-permute-done | bytes 917536 | tf_op jit(solution)/shard_map/ppermute | solution.py:17
  41.8 1.3 constant_dynamic-update-slice_fusion.6
  43.0 16.0 %collective-permute-done.4 = bf16[128,3584]{1,0:T(8,128)(2,1)S(1)} collective-permute-done((bf16[128,3584]{1,0:T(8,128)(2,1)}, bf16[128,3584]{1,0:T(8,128)(2,1)S(1)}, u32[]{:S(2)}, u32[]{:S(2)}) %collective-permute-start.4) | collective-permute-done | bytes 917536 | tf_op jit(solution)/shard_map/ppermute | solution.py:17
  59.1 0.1 constant_dynamic-update-slice_fusion.5
  59.2 0.0 collective-permute-done.5
  59.2 0.1 constant_dynamic-update-slice_fusion.4.g_ref
  59.3 0.0 copy-start
  59.3 1.8 %copy-done = bf16[512,3584]{1,0:T(8,128)(2,1)} copy-done((bf16[512,3584]{1,0:T(8,128)(2,1)}, bf16[512,3584]{1,0:T(8,128)(2,1)S(1)}, u32[]{:S(2)}) %copy-start) | copy-done | bytes 3670040
  61.1 12.4 %fusion = f32[512,2048]{1,0:T(8,128)} fusion(bf16[512,3584]{1,0:T(8,128)(2,1)S(1)} %constant_dynamic-update-slice_fusion.4.g_ref, bf16[2048,3584]{1,0:T(8,128)(2,1)} %param.8), kind=kOutput, calls=%fused_computation.12 | convolution fusion | flops 7516192768 | bytes 22544384 | tf_op jit(solution)/shard_map/dot_general | solution.py:87
  73.5 0.0 reduce-scatter.2.cloned.1.call-update
  74.2 0.0 all-gather.2.cloned.1.call-done.a_ref
  74.2 10.9 %shard_map.77 = bf16[128,32,128]{2,1,0:T(8,128)(2,1)} custom-call(s32[128]{0:T(128)} %rows_ref.1, s32[128]{0:T(128)} %cols_ref.1, s32[1]{0:T(128)S(6)} %copy.22.cnt_ref, bf16[64,32,512]{2,1,0:T(8,128)(2,1)} %all-gather.2.cloned.1.call-done.a_ref, bf16[512,3584]{1,0:T(8,128)(2,1)} %copy-done), custom_call_target="tpu_custom_call" | custom-call | flops 536870912 | bytes 6815744 | tf_op jit(solution)/shard_map/pallas_call | solution.py:54
  85.1 38.5 %reduce-scatter.2.cloned.1.call-done = f32[64,2048]{1,0:T(8,128)} async-done(((f32[512,2048]{1,0:T(8,128)}), f32[64,2048]{1,0:T(8,128)}) %reduce-scatter.2.cloned.1.call-update) | async-done | bytes 524304 | tf_op jit(solution)/shard_map/reduce_scatter | solution.py:90
  123.6 1.8 %convert_element_type.3 = bf16[64,2048]{1,0:T(8,128)(2,1)} convert(f32[64,2048]{1,0:T(8,128)} %reduce-scatter.2.cloned.1.call-done) | non-fusion elementwise | flops 131072 | bytes 786432 | tf_op jit(solution)/shard_map/convert_element_type | solution.py:90
  (6 shorter events, 0.1 us)
Async XLA Ops:
  7.2 15.7 %copy-start.2 = (bf16[128,3584]{1,0:T(8,128)(2,1)S(1)}, bf16[128,3584]{1,0:T(8,128)(2,1)}, u32[]{:S(2)}) copy-start(bf16[128,3584]{1,0:T(8,128)(2,1)} %param.7) | copy-start | bytes 2752516
  7.2 67.0 %all-gather.2.cloned.1.call-start = ((), (), s32[]{:S(2)}) async-start(), calls=%async_computation.2 | async-start | bytes 2359296 | tf_op jit(solution)/shard_map/all_gather | solution.py:83
  8.5 5.4 %collective-permute-start = (bf16[128,8,32]{0,2,1:T(8,128)(2,1)S(1)}, bf16[128,8,32]{0,2,1:T(8,128)(2,1)S(1)}, u32[]{:S(2)}, u32[]{:S(2)}) collective-permute-start(bf16[128,8,32]{0,2,1:T(8,128)(2,1)S(1)} %get-tuple-element.14), channel_id=1, source_target_pairs={{0,8},{8,0},{16,24},{24,16},{1,9},{9,1},{17,25},{25,17},{2,10},{10... | collective-permute-start | bytes 196616 | tf_op jit(solution)/shard_map/ppermute | solution.py:77
  11.5 4.3 %collective-permute-start.1 = (bf16[128,8,32]{0,2,1:T(8,128)(2,1)S(1)}, bf16[128,8,32]{0,2,1:T(8,128)(2,1)S(1)}, u32[]{:S(2)}, u32[]{:S(2)}) collective-permute-start(bf16[128,8,32]{0,2,1:T(8,128)(2,1)S(1)} %get-tuple-element.13), channel_id=1, source_target_pairs={{0,16},{8,24},{16,0},{24,8},{1,17},{9,25},{17,1},{25,9},{2,18},{10... | collective-permute-start | bytes 196616 | tf_op jit(solution)/shard_map/ppermute | solution.py:77
  13.0 5.2 %collective-permute-start.2 = (bf16[128,8,32]{0,2,1:T(8,128)(2,1)S(1)}, bf16[128,8,32]{0,2,1:T(8,128)(2,1)S(1)}, u32[]{:S(2)}, u32[]{:S(2)}) collective-permute-start(bf16[128,8,32]{0,2,1:T(8,128)(2,1)S(1)} %get-tuple-element.12), channel_id=1, source_target_pairs={{0,24},{8,16},{16,8},{24,0},{1,25},{9,17},{17,9},{25,1},{2,26},{10... | collective-permute-start | bytes 196616 | tf_op jit(solution)/shard_map/ppermute | solution.py:77
  18.2 23.6 %collective-permute-start.3 = (bf16[128,3584]{1,0:T(8,128)(2,1)}, bf16[128,3584]{1,0:T(8,128)(2,1)}, u32[]{:S(2)}, u32[]{:S(2)}) collective-permute-start(bf16[128,3584]{1,0:T(8,128)(2,1)} %param.7), channel_id=1, source_target_pairs={{0,8},{8,0},{16,24},{24,16},{1,9},{9,1},{17,25},{25,17},{2,10},{10... | collective-permute-start | bytes 2752520 | tf_op jit(solution)/shard_map/ppermute | solution.py:17
  18.7 40.4 %collective-permute-start.4 = (bf16[128,3584]{1,0:T(8,128)(2,1)}, bf16[128,3584]{1,0:T(8,128)(2,1)S(1)}, u32[]{:S(2)}, u32[]{:S(2)}) collective-permute-start(bf16[128,3584]{1,0:T(8,128)(2,1)} %param.7), channel_id=1, source_target_pairs={{0,16},{8,24},{16,0},{24,8},{1,17},{9,25},{17,1},{25,9},{2,18},{10... | collective-permute-start | bytes 2752520 | tf_op jit(solution)/shard_map/ppermute | solution.py:17
  19.0 40.2 %collective-permute-start.5 = (bf16[128,3584]{1,0:T(8,128)(2,1)}, bf16[128,3584]{1,0:T(8,128)(2,1)S(1)}, u32[]{:S(2)}, u32[]{:S(2)}) collective-permute-start(bf16[128,3584]{1,0:T(8,128)(2,1)} %param.7), channel_id=1, source_target_pairs={{0,24},{8,16},{16,8},{24,0},{1,25},{9,17},{17,9},{25,1},{2,26},{10... | collective-permute-start | bytes 2752520 | tf_op jit(solution)/shard_map/ppermute | solution.py:17
  21.8 0.7 copy-start.1
  22.5 101.0 %reduce-scatter.2.cloned.1.call-start = ((), (), s32[]{:S(2)}) async-start(), calls=%async_computation.1 | async-start | bytes 4718592 | tf_op jit(solution)/shard_map/reduce_scatter | solution.py:90
  59.3 1.8 %copy-start = (bf16[512,3584]{1,0:T(8,128)(2,1)}, bf16[512,3584]{1,0:T(8,128)(2,1)S(1)}, u32[]{:S(2)}) copy-start(bf16[512,3584]{1,0:T(8,128)(2,1)S(1)} %constant_dynamic-update-slice_fusion.4.g_ref) | copy-start | bytes 11010052
Sparse Core Ops, SparseCore 0:
  22.7 28.4 all-gather.1
  73.6 49.8 reduce-scatter.1

commit v4 on v1

--- a/solution.py
+++ b/solution.py
@@ -65,30 +65,29 @@
 
 def per_device(n_tok, acts, grad_out, weight, block_rows, block_cols, block_count):
     me = lax.axis_index("tok")
-    tok_dev, d_dev = acts.shape
+    tok_dev = acts.shape[0]
     sub = BLK // n_tok
 
-    acts_pieces = acts.reshape(tok_dev, d_dev // BLK, n_tok, sub)
-    send = [
-        lax.dynamic_index_in_dim(acts_pieces, me ^ m, axis=2, keepdims=False)
-        for m in range(n_tok)
-    ]
-    got = [send[0]] + [
-        lax.ppermute(send[m], "tok", perm=[(a, a ^ m) for a in range(n_tok)])
-        for m in range(1, n_tok)
-    ]
-    acts_sub = place_rows(got, me)
-    acts_sub_t = jnp.transpose(acts_sub, (1, 2, 0))
-    acts_t = lax.all_gather(acts_sub_t, "feat", axis=0, tiled=True)
+    full_acts = lax.all_gather(acts, "feat", axis=1, tiled=True)
+    row_blocks = full_acts.shape[1] // BLK
+    acts_pieces = jnp.transpose(full_acts.reshape(tok_dev, row_blocks, n_tok, sub), (2, 1, 3, 0))
 
     gout = place_rows(xor_exchange(grad_out, "tok", n_tok), me)
-
     partial_sums = lax.dot_general(
         gout, weight, (((1,), (1,)), ((), ())), preferred_element_type=jnp.float32
     )
     grad_in = lax.psum_scatter(partial_sums, "feat", scatter_dimension=0, tiled=True).astype(
         jnp.bfloat16
     )
+
+    acts_pieces, gout = lax.optimization_barrier((acts_pieces, gout))
+    got = []
+    for m in range(n_tok):
+        part = lax.dynamic_index_in_dim(acts_pieces, me ^ m, axis=0, keepdims=False)
+        if m:
+            part = lax.ppermute(part, "tok", perm=[(a, a ^ m) for a in range(n_tok)])
+        got.append(part)
+    acts_t = place_rows(got, me, axis=2)
     block_grads = block_tiles(block_rows, block_cols, block_count, acts_t, gout)
     return (grad_in, block_grads)
 

time: 149 us -> 126 us (0.85)
  waiting for transfers between devices: 92.2 us -> 63.2 us
  local copies, waits for them, and re-layouts: 6.12 us -> 14.1 us
  starting transfers between devices: 10.8 us -> 8.11 us
    ppermute x3, waiting for transfers between devices: 0.01 us -> 36.6 us  [xor_exchange(): out.append(lax.ppermute(x, axis_name, perm=[(a, a ^ m) for a in range(n)]))]
    reduce_scatter x1, waiting for transfers between devices: 40.9 us -> 8.25 us  [per_device(): lax.psum_scatter(partial_sums, 'feat', scatter_dimension=0, tiled=True)]
    ppermute x3, waiting for transfers between devices: 37.2 us -> 18.2 us  [per_device(): part = lax.ppermute(part, 'tok', perm=[(a, a ^ m) for a in range(n_tok)])]
    all_gather x1, waiting for transfers between devices: 14 us -> 0.02 us  [per_device(): full_acts = lax.all_gather(acts, 'feat', axis=1, tiled=True)]
    dynamic_update_slice x8, local copies, waits for them, and re-layouts: 1.6 us -> 6.24 us  [place_rows(): out = lax.dynamic_update_slice_in_dim(out, piece, (me ^ m) * rows, axis)]
    ppermute x3, starting transfers between devices: 6.16 us -> 3.49 us  [per_device(): part = lax.ppermute(part, 'tok', perm=[(a, a ^ m) for a in range(n_tok)])]
    squeeze x1, local copies, waits for them, and re-layouts: 0.65 us -> 2.45 us  [per_device(): part = lax.dynamic_index_in_dim(acts_pieces, me ^ m, axis=0, keepdims=False)]
  transfers between devices with their start and end apart: 8 -> 8, of which waited for: 4 -> 5; matrix products, arithmetic and copies ran while one was open for 11% -> 19% of each run, Pallas kernels for 7% -> 9%
where the time goes in v4:
time: 126 us; the launch traced here: 125 us
  waiting for transfers between devices  63.2 us (50%)
  between operations  14.9 us (12%)
  local copies, waits for them, and re-layouts  14.1 us (11%)
  matrix products  12.4 us (10%)
  Pallas kernels  11 us (9%)
  starting transfers between devices  8.11 us (6%)
  other arithmetic  1.77 us (1%)
    ppermute x3, waiting for transfers between devices, xor_exchange(): out.append(lax.ppermute(x, axis_name, perm=[(a, a ^ m) for a in range(n)]))  36.6 us
    ppermute x3, waiting for transfers between devices, per_device(): part = lax.ppermute(part, 'tok', perm=[(a, a ^ m) for a in range(n_tok)])  18.2 us
    dot_general x1, matrix products, per_device(): lax.dot_general(gout, weight, (((1,), (1,)), ((), ())), preferred_element...  12.4 us
    pallas_call x1, Pallas kernels, block_tiles(): pl.pallas_call(block_kernel, grid_spec=grid_spec, out_shape=jax.ShapeDtyp...  11 us
    reduce_scatter x1, waiting for transfers between devices, per_device(): lax.psum_scatter(partial_sums, 'feat', scatter_dimension=0, tiled=True)  8.25 us
    dynamic_update_slice x8, local copies, waits for them, and re-layouts, place_rows(): out = lax.dynamic_update_slice_in_dim(out, piece, (me ^ m) * rows, axis)  6.24 us
    unnamed x7, local copies, waits for them, and re-layouts  4.96 us
    ppermute x3, starting transfers between devices, xor_exchange(): out.append(lax.ppermute(x, axis_name, perm=[(a, a ^ m) for a in range(n)]))  4.55 us
  transfers between devices with their start and end apart: 8, of which 5 were waited for; matrix products, arithmetic and copies ran while one was open for 19% of the time, Pallas kernels for 9%

profile of v4, /device:TPU:0, one launch (start us, length us, event | category | flops | bytes accessed | tf_op | source)
XLA Modules:
  0.0 125.4 jit_solution(478594861234543250)
XLA Ops:
  7.2 0.0 copy-start.2
  7.2 0.0 all-gather.2.cloned.1.call-start
  7.2 3.0 %collective-permute-start = (bf16[128,3584]{1,0:T(8,128)(2,1)}, bf16[128,3584]{1,0:T(8,128)(2,1)}, u32[]{:S(2)}, u32[]{:S(2)}) collective-permute-start(bf16[128,3584]{1,0:T(8,128)(2,1)} %param.7), channel_id=1, source_target_pairs={{0,8},{8,0},{16,24},{24,16},{1,9},{9,1},{17,25},{25,17},{2,10},{10... | collective-permute-start | bytes 2752520 | tf_op jit(solution)/shard_map/ppermute | solution.py:17
  10.2 1.5 %collective-permute-start.1 = (bf16[128,3584]{1,0:T(8,128)(2,1)}, bf16[128,3584]{1,0:T(8,128)(2,1)S(1)}, u32[]{:S(2)}, u32[]{:S(2)}) collective-permute-start(bf16[128,3584]{1,0:T(8,128)(2,1)} %param.7), channel_id=1, source_target_pairs={{0,16},{8,24},{16,0},{24,8},{1,17},{9,25},{17,1},{25,9},{2,18},{10... | collective-permute-start | bytes 2752520 | tf_op jit(solution)/shard_map/ppermute | solution.py:17
  11.7 0.0 collective-permute-start.2
  11.8 1.8 %copy.9 = bf16[128,1024]{0,1:T(8,128)(2,1)} copy(bf16[128,1024]{1,0:T(8,128)(2,1)} %param.6) | data formatting | bytes 524288 | tf_op args[0]
  13.6 0.0 all-gather.2.cloned.1.call-update
  13.6 0.0 reduce-scatter.2.cloned.1.call-start
  13.7 0.2 broadcast_in_dim.6
  13.9 0.0 copy-done.2
  13.9 0.1 constant_dynamic-update-slice_fusion.6
  14.0 17.7 %collective-permute-done = bf16[128,3584]{1,0:T(8,128)(2,1)} collective-permute-done((bf16[128,3584]{1,0:T(8,128)(2,1)}, bf16[128,3584]{1,0:T(8,128)(2,1)}, u32[]{:S(2)}, u32[]{:S(2)}) %collective-permute-start) | collective-permute-done | bytes 917536 | tf_op jit(solution)/shard_map/ppermute | solution.py:17
  31.7 1.3 %constant_dynamic-update-slice_fusion.5 = bf16[512,3584]{1,0:T(8,128)(2,1)S(1)} fusion(bf16[512,3584]{1,0:T(8,128)(2,1)S(1)} %constant_dynamic-update-slice_fusion.6, bf16[128,3584]{1,0:T(8,128)(2,1)} %collective-permute-done, s32[]{:T(128)S(6)} %select_n.30), kind=kLoop, calls=%fused_computation.9 | loop fusion | bytes 1835012 | tf_op jit(solution)/shard_map/dynamic_update_slice | solution.py:27
  33.0 18.9 %collective-permute-done.1 = bf16[128,3584]{1,0:T(8,128)(2,1)S(1)} collective-permute-done((bf16[128,3584]{1,0:T(8,128)(2,1)}, bf16[128,3584]{1,0:T(8,128)(2,1)S(1)}, u32[]{:S(2)}, u32[]{:S(2)}) %collective-permute-start.1) | collective-permute-done | bytes 917536 | tf_op jit(solution)/shard_map/ppermute | solution.py:17
  51.9 0.1 constant_dynamic-update-slice_fusion.4
  52.0 0.0 collective-permute-done.2
  52.0 0.1 constant_dynamic-update-slice_fusion.3.g_ref
  52.1 0.0 copy-start
  52.1 1.8 %copy-done = bf16[512,3584]{1,0:T(8,128)(2,1)} copy-done((bf16[512,3584]{1,0:T(8,128)(2,1)}, bf16[512,3584]{1,0:T(8,128)(2,1)S(1)}, u32[]{:S(2)}) %copy-start) | copy-done | bytes 3670040
  53.9 12.4 %fusion = f32[512,2048]{1,0:T(8,128)} fusion(bf16[512,3584]{1,0:T(8,128)(2,1)S(1)} %constant_dynamic-update-slice_fusion.3.g_ref, bf16[2048,3584]{1,0:T(8,128)(2,1)} %param.8), kind=kOutput, calls=%fused_computation.11 | convolution fusion | flops 7516192768 | bytes 22544384 | tf_op jit(solution)/shard_map/dot_general | solution.py:76
  66.3 0.0 reduce-scatter.2.cloned.1.call-update
  66.4 0.0 all-gather.2.cloned.1.call-done
  66.4 2.4 %dynamic-slice_bitcast_fusion = (bf16[64,32,128]{2,1,0:T(8,128)(2,1)S(1)}, bf16[64,32,128]{2,1,0:T(8,128)(2,1)S(1)}, bf16[64,32,128]{2,1,0:T(8,128)(2,1)}) fusion(bf16[4,64,32,128]{3,2,0,1:T(8,128)(2,1)} %bitcast.13, s32[]{:T(128)S(6)} %select_n.36, s32[]{:T(128)S(6)} %select_n.35, s32[]{:T(128)S(6)} %select_n.34), kind=kLoop, calls=%fused_computation.1 | loop fusion | bytes 3145740 | tf_op jit(solution)/shard_map/jit(dynamic_index_in_dim)/squeeze | solution.py:86
  68.8 1.1 collective-permute-start.3
  70.0 0.9 collective-permute-start.4
  70.9 1.4 %collective-permute-start.5 = (bf16[64,32,128]{2,1,0:T(8,128)(2,1)S(1)}, bf16[64,32,128]{2,1,0:T(8,128)(2,1)}, u32[]{:S(2)}, u32[]{:S(2)}) collective-permute-start(bf16[64,32,128]{2,1,0:T(8,128)(2,1)S(1)} %get-tuple-element.6), channel_id=1, source_target_pairs={{0,24},{8,16},{16,8},{24,0},{1,25},{9,17},{17,9},{25,1},{2,26},{10... | collective-permute-start | bytes 1572872 | tf_op jit(solution)/shard_map/ppermute | solution.py:88
  73.0 0.2 broadcast_in_dim.7
  73.2 1.2 bitcast_dynamic-update-slice_fusion
  74.4 9.6 %collective-permute-done.3 = bf16[64,32,128]{2,1,0:T(8,128)(2,1)} collective-permute-done((bf16[64,32,128]{2,1,0:T(8,128)(2,1)}, bf16[64,32,128]{2,1,0:T(8,128)(2,1)}, u32[]{:S(2)}, u32[]{:S(2)}) %collective-permute-start.3) | collective-permute-done | bytes 524320 | tf_op jit(solution)/shard_map/ppermute | solution.py:88
  84.0 1.2 constant_dynamic-update-slice_fusion.1
  85.2 8.6 %collective-permute-done.4 = bf16[64,32,128]{2,1,0:T(8,128)(2,1)} collective-permute-done((bf16[64,32,128]{2,1,0:T(8,128)(2,1)S(1)}, bf16[64,32,128]{2,1,0:T(8,128)(2,1)}, u32[]{:S(2)}, u32[]{:S(2)}) %collective-permute-start.4) | collective-permute-done | bytes 524320 | tf_op jit(solution)/shard_map/ppermute | solution.py:88
  93.8 1.2 constant_dynamic-update-slice_fusion
  95.0 0.0 collective-permute-done.5
  95.0 1.2 constant_dynamic-update-slice_fusion.2.a_ref
  96.2 0.0 copy-start.1
  96.2 1.4 %copy-done.1 = bf16[64,32,512]{2,1,0:T(8,128)(2,1)} copy-done((bf16[64,32,512]{2,1,0:T(8,128)(2,1)}, bf16[64,32,512]{2,1,0:T(8,128)(2,1)S(1)}, u32[]{:S(2)}) %copy-start.1) | copy-done | bytes 2097176
  97.6 11.0 %shard_map.77 = bf16[128,32,128]{2,1,0:T(8,128)(2,1)} custom-call(s32[128]{0:T(128)} %rows_ref.1, s32[128]{0:T(128)} %cols_ref.1, s32[1]{0:T(128)S(6)} %copy.18.cnt_ref, bf16[64,32,512]{2,1,0:T(8,128)(2,1)} %copy-done.1, bf16[512,3584]{1,0:T(8,128)(2,1)} %copy-done), custom_call_target="tpu_custom_call" | custom-call | flops 536870912 | bytes 6815744 | tf_op jit(solution)/shard_map/pallas_call | solution.py:54
  108.6 8.3 %reduce-scatter.2.cloned.1.call-done = f32[64,2048]{1,0:T(8,128)} async-done(((f32[512,2048]{1,0:T(8,128)}), f32[64,2048]{1,0:T(8,128)}) %reduce-scatter.2.cloned.1.call-update) | async-done | bytes 524304 | tf_op jit(solution)/shard_map/reduce_scatter | solution.py:79
  116.8 1.8 %convert_element_type.3 = bf16[64,2048]{1,0:T(8,128)(2,1)} convert(f32[64,2048]{1,0:T(8,128)} %reduce-scatter.2.cloned.1.call-done) | non-fusion elementwise | flops 131072 | bytes 786432 | tf_op jit(solution)/shard_map/convert_element_type | solution.py:79
Async XLA Ops:
  7.2 6.7 %copy-start.2 = (bf16[128,3584]{1,0:T(8,128)(2,1)S(1)}, bf16[128,3584]{1,0:T(8,128)(2,1)}, u32[]{:S(2)}) copy-start(bf16[128,3584]{1,0:T(8,128)(2,1)} %param.7) | copy-start | bytes 2752516
  7.2 59.2 %all-gather.2.cloned.1.call-start = ((), (), s32[]{:S(2)}) async-start(), calls=%async_computation.2 | async-start | bytes 2359296 | tf_op jit(solution)/shard_map/all_gather | solution.py:71
  7.2 24.5 %collective-permute-start = (bf16[128,3584]{1,0:T(8,128)(2,1)}, bf16[128,3584]{1,0:T(8,128)(2,1)}, u32[]{:S(2)}, u32[]{:S(2)}) collective-permute-start(bf16[128,3584]{1,0:T(8,128)(2,1)} %param.7), channel_id=1, source_target_pairs={{0,8},{8,0},{16,24},{24,16},{1,9},{9,1},{17,25},{25,17},{2,10},{10... | collective-permute-start | bytes 2752520 | tf_op jit(solution)/shard_map/ppermute | solution.py:17
  10.2 41.7 %collective-permute-start.1 = (bf16[128,3584]{1,0:T(8,128)(2,1)}, bf16[128,3584]{1,0:T(8,128)(2,1)S(1)}, u32[]{:S(2)}, u32[]{:S(2)}) collective-permute-start(bf16[128,3584]{1,0:T(8,128)(2,1)} %param.7), channel_id=1, source_target_pairs={{0,16},{8,24},{16,0},{24,8},{1,17},{9,25},{17,1},{25,9},{2,18},{10... | collective-permute-start | bytes 2752520 | tf_op jit(solution)/shard_map/ppermute | solution.py:17
  11.7 40.2 %collective-permute-start.2 = (bf16[128,3584]{1,0:T(8,128)(2,1)}, bf16[128,3584]{1,0:T(8,128)(2,1)S(1)}, u32[]{:S(2)}, u32[]{:S(2)}) collective-permute-start(bf16[128,3584]{1,0:T(8,128)(2,1)} %param.7), channel_id=1, source_target_pairs={{0,24},{8,16},{16,8},{24,0},{1,25},{9,17},{17,9},{25,1},{2,26},{10... | collective-permute-start | bytes 2752520 | tf_op jit(solution)/shard_map/ppermute | solution.py:17
  13.6 103.2 %reduce-scatter.2.cloned.1.call-start = ((), (), s32[]{:S(2)}) async-start(), calls=%async_computation.1 | async-start | bytes 4718592 | tf_op jit(solution)/shard_map/reduce_scatter | solution.py:79
  52.1 1.8 %copy-start = (bf16[512,3584]{1,0:T(8,128)(2,1)}, bf16[512,3584]{1,0:T(8,128)(2,1)S(1)}, u32[]{:S(2)}) copy-start(bf16[512,3584]{1,0:T(8,128)(2,1)S(1)} %constant_dynamic-update-slice_fusion.3.g_ref) | copy-start | bytes 11010052
  68.8 15.2 %collective-permute-start.3 = (bf16[64,32,128]{2,1,0:T(8,128)(2,1)}, bf16[64,32,128]{2,1,0:T(8,128)(2,1)}, u32[]{:S(2)}, u32[]{:S(2)}) collective-permute-start(bf16[64,32,128]{2,1,0:T(8,128)(2,1)} %get-tuple-element.8), channel_id=1, source_target_pairs={{0,8},{8,0},{16,24},{24,16},{1,9},{9,1},{17,25},{25,17},{2,10},{10... | collective-permute-start | bytes 1572872 | tf_op jit(solution)/shard_map/ppermute | solution.py:88
  70.0 23.9 %collective-permute-start.4 = (bf16[64,32,128]{2,1,0:T(8,128)(2,1)S(1)}, bf16[64,32,128]{2,1,0:T(8,128)(2,1)}, u32[]{:S(2)}, u32[]{:S(2)}) collective-permute-start(bf16[64,32,128]{2,1,0:T(8,128)(2,1)S(1)} %get-tuple-element.7), channel_id=1, source_target_pairs={{0,16},{8,24},{16,0},{24,8},{1,17},{9,25},{17,1},{25,9},{2,18},{10... | collective-permute-start | bytes 1572872 | tf_op jit(solution)/shard_map/ppermute | solution.py:88
  70.9 24.1 %collective-permute-start.5 = (bf16[64,32,128]{2,1,0:T(8,128)(2,1)S(1)}, bf16[64,32,128]{2,1,0:T(8,128)(2,1)}, u32[]{:S(2)}, u32[]{:S(2)}) collective-permute-start(bf16[64,32,128]{2,1,0:T(8,128)(2,1)S(1)} %get-tuple-element.6), channel_id=1, source_target_pairs={{0,24},{8,16},{16,8},{24,0},{1,25},{9,17},{17,9},{25,1},{2,26},{10... | collective-permute-start | bytes 1572872 | tf_op jit(solution)/shard_map/ppermute | solution.py:88
  96.2 1.4 %copy-start.1 = (bf16[64,32,512]{2,1,0:T(8,128)(2,1)}, bf16[64,32,512]{2,1,0:T(8,128)(2,1)S(1)}, u32[]{:S(2)}) copy-start(bf16[64,32,512]{2,1,0:T(8,128)(2,1)S(1)} %constant_dynamic-update-slice_fusion.2.a_ref) | copy-start | bytes 6291460
Sparse Core Ops, SparseCore 0:
  13.7 30.7 all-gather.1
  66.5 50.3 reduce-scatter.1

commit v5 on v4

--- a/solution.py
+++ b/solution.py
@@ -63,22 +63,54 @@
     )(rows, cols, count, acts_t, gout)
 
 
-def per_device(n_tok, acts, grad_out, weight, block_rows, block_cols, block_count):
+def feat_all_gather(x, n_feat, me_feat):
+    core = me_feat % 2
+    zs = [x] + [
+        lax.ppermute(x, "feat", perm=[(a, a ^ m) for a in range(n_feat)])
+        for m in range(2, n_feat, 2)
+    ]
+    mine = place_rows([piece[None] for piece in zs], me_feat // 2, axis=0)
+    other = lax.ppermute(mine, "feat", perm=[(a, a ^ 1) for a in range(n_feat)])
+    both = place_rows([mine[:, None], other[:, None]], core, axis=1)
+    return jnp.transpose(both, (2, 0, 1, 3)).reshape(x.shape[0], -1)
+
+
+def feat_reduce_scatter(h, n_feat, me_feat):
+    core = me_feat % 2
+    z = me_feat // 2
+    h = h.reshape((n_feat // 2, 2, h.shape[0] // n_feat) + h.shape[1:])
+    send = lax.dynamic_index_in_dim(h, 1 - core, axis=1, keepdims=False)
+    keep = lax.dynamic_index_in_dim(h, core, axis=1, keepdims=False)
+    chip = keep + lax.ppermute(send, "feat", perm=[(a, a ^ 1) for a in range(n_feat)])
+    total = lax.dynamic_index_in_dim(chip, z, axis=0, keepdims=False)
+    for m in range(1, n_feat // 2):
+        part = lax.dynamic_index_in_dim(chip, z ^ m, axis=0, keepdims=False)
+        total = total + lax.ppermute(part, "feat", perm=[(a, a ^ (2 * m)) for a in range(n_feat)])
+    return total
+
+
+def per_device(n_tok, n_feat, acts, grad_out, weight, block_rows, block_cols, block_count):
     me = lax.axis_index("tok")
+    me_feat = lax.axis_index("feat")
     tok_dev = acts.shape[0]
     sub = BLK // n_tok
 
-    full_acts = lax.all_gather(acts, "feat", axis=1, tiled=True)
+    full_acts = feat_all_gather(acts, n_feat, me_feat)
     row_blocks = full_acts.shape[1] // BLK
     acts_pieces = jnp.transpose(full_acts.reshape(tok_dev, row_blocks, n_tok, sub), (2, 1, 3, 0))
 
     gout = place_rows(xor_exchange(grad_out, "tok", n_tok), me)
-    partial_sums = lax.dot_general(
-        gout, weight, (((1,), (1,)), ((), ())), preferred_element_type=jnp.float32
-    )
-    grad_in = lax.psum_scatter(partial_sums, "feat", scatter_dimension=0, tiled=True).astype(
-        jnp.bfloat16
-    )
+    halves = []
+    d_half = weight.shape[0] // 2
+    for k in range(2):
+        partial_sums = lax.dot_general(
+            gout,
+            weight[k * d_half : (k + 1) * d_half],
+            (((1,), (1,)), ((), ())),
+            preferred_element_type=jnp.float32,
+        )
+        halves.append(feat_reduce_scatter(partial_sums, n_feat, me_feat))
+    grad_in = jnp.concatenate(halves, axis=1).astype(jnp.bfloat16)
 
     acts_pieces, gout = lax.optimization_barrier((acts_pieces, gout))
     got = []
@@ -94,7 +126,8 @@
 
 def solution(mesh):
     n_tok = mesh.shape["tok"]
-    assert n_tok & (n_tok - 1) == 0
+    n_feat = mesh.shape["feat"]
+    assert n_tok & (n_tok - 1) == 0 and n_feat & (n_feat - 1) == 0
     in_specs = (
         P("tok", "feat"),
         P("tok", "feat"),
@@ -105,7 +138,7 @@
     )
     out_specs = (P("feat", "tok"), P("feat", "tok", None))
     return jax.shard_map(
-        functools.partial(per_device, n_tok),
+        functools.partial(per_device, n_tok, n_feat),
         mesh=mesh,
         in_specs=in_specs,
         out_specs=out_specs,

time: 126 us -> 153 us (1.21)
  starting transfers between devices: 8.11 us -> 24.5 us
  between operations: 14.9 us -> 1.61 us
  waiting for transfers between devices: 63.2 us -> 75.4 us
  local copies, waits for them, and re-layouts: 14.1 us -> 19.8 us
  other arithmetic: 1.77 us -> 6.52 us
    ppermute x0 -> x12, waiting for transfers between devices: none -> 34.4 us  [the longest x6 26 us: feat_reduce_scatter(): lax.ppermute(part, 'feat', perm=[(a, a ^ 2 * m) for a in range(n_feat)])]
    ppermute x3, waiting for transfers between devices: 36.6 us -> 21.2 us  [xor_exchange(): out.append(lax.ppermute(x, axis_name, perm=[(a, a ^ m) for a in range(n)]))]
    ppermute x0 -> x12, starting transfers between devices: none -> 15.1 us  [the longest x6 9.32 us: feat_reduce_scatter(): lax.ppermute(part, 'feat', perm=[(a, a ^ 2 * m) for a in range(n_feat)])]
    reduce_scatter x1 -> x0, waiting for transfers between devices: 8.25 us -> none  [per_device(): lax.psum_scatter(partial_sums, 'feat', scatter_dimension=0, tiled=True)]
    dynamic_update_slice x8 -> x14, local copies, waits for them, and re-layouts: 6.24 us -> 11.6 us  [place_rows(): out = lax.dynamic_update_slice_in_dim(out, piece, (me ^ m) * rows, axis)]
    add x0 -> x2, other arithmetic: none -> 3.54 us  [feat_reduce_scatter(): keep + lax.ppermute(send, 'feat', perm=[(a, a ^ 1) for a in range(n_feat)])]
    unnamed x7 -> x23, local copies, waits for them, and re-layouts: 4.96 us -> 2.12 us
    another operation x0 -> x2, other arithmetic: none -> 2.25 us
  transfers between devices with their start and end apart: 8 -> 18, of which waited for: 5 -> 10; matrix products, arithmetic and copies ran while one was open for 19% -> 24% of each run, Pallas kernels for 9% -> 7%
where the time goes in v5:
time: 153 us; the launch traced here: 152 us
  waiting for transfers between devices  75.4 us (49%)
  starting transfers between devices  24.5 us (16%)
  local copies, waits for them, and re-layouts  19.8 us (13%)
  matrix products  13.5 us (9%)
  Pallas kernels  10.9 us (7%)
  other arithmetic  6.52 us (4%)
  between operations  1.61 us (1%)
    ppermute x6, waiting for transfers between devices, feat_reduce_scatter(): lax.ppermute(part, 'feat', perm=[(a, a ^ 2 * m) for a in range(n_feat)])  26 us
    ppermute x3, waiting for transfers between devices, xor_exchange(): out.append(lax.ppermute(x, axis_name, perm=[(a, a ^ m) for a in range(n)]))  21.2 us
    ppermute x3, waiting for transfers between devices, per_device(): part = lax.ppermute(part, 'tok', perm=[(a, a ^ m) for a in range(n_tok)])  19.8 us
    dot_general x2, matrix products, per_device(): lax.dot_general(gout, weight[k * d_half:(k + 1) * d_half], (((1,), (1,)),...  13.5 us
    dynamic_update_slice x14, local copies, waits for them, and re-layouts, place_rows(): out = lax.dynamic_update_slice_in_dim(out, piece, (me ^ m) * rows, axis)  11.6 us
    pallas_call x1, Pallas kernels, block_tiles(): pl.pallas_call(block_kernel, grid_spec=grid_spec, out_shape=jax.ShapeDtyp...  10.9 us
    ppermute x6, starting transfers between devices, feat_reduce_scatter(): lax.ppermute(part, 'feat', perm=[(a, a ^ 2 * m) for a in range(n_feat)])  9.32 us
    ppermute x3, waiting for transfers between devices, feat_all_gather(): lax.ppermute(x, 'feat', perm=[(a, a ^ m) for a in range(n_feat)])  8.43 us
  transfers between devices with their start and end apart: 18, of which 10 were waited for; matrix products, arithmetic and copies ran while one was open for 24% of the time, Pallas kernels for 7%

profile of v5, /device:TPU:0, one launch (start us, length us, event | category | flops | bytes accessed | tf_op | source)
XLA Modules:
  0.0 152.3 jit_solution(5718514670397116852)
XLA Ops:
  0.6 1.1 copy.8
  1.8 3.1 %collective-permute-start.11 = (bf16[128,1024]{0,1:T(8,128)(2,1)S(1)}, bf16[128,1024]{0,1:T(8,128)(2,1)S(1)}, u32[]{:S(2)}, u32[]{:S(2)}) collective-permute-start(bf16[128,1024]{0,1:T(8,128)(2,1)S(1)} %copy.8), channel_id=1, source_target_pairs={{0,2},{1,3},{2,0},{3,1},{4,6},{5,7},{6,4},{7,5},{8,10},{9,11},{10,... | collective-permute-start | bytes 786440 | tf_op jit(solution)/shard_map/ppermute | solution.py:69
  4.8 2.6 %collective-permute-start.12 = (bf16[128,1024]{0,1:T(8,128)(2,1)S(1)}, bf16[128,1024]{0,1:T(8,128)(2,1)S(1)}, u32[]{:S(2)}, u32[]{:S(2)}) collective-permute-start(bf16[128,1024]{0,1:T(8,128)(2,1)S(1)} %copy.8), channel_id=1, source_target_pairs={{0,4},{1,5},{2,6},{3,7},{4,0},{5,1},{6,2},{7,3},{8,12},{9,13},{10,... | collective-permute-start | bytes 786440 | tf_op jit(solution)/shard_map/ppermute | solution.py:69
  7.4 1.7 %collective-permute-start = (bf16[128,3584]{1,0:T(8,128)(2,1)}, bf16[128,3584]{1,0:T(8,128)(2,1)}, u32[]{:S(2)}, u32[]{:S(2)}) collective-permute-start(bf16[128,3584]{1,0:T(8,128)(2,1)} %param.7), channel_id=1, source_target_pairs={{0,8},{8,0},{16,24},{24,16},{1,9},{9,1},{17,25},{25,17},{2,10},{10... | collective-permute-start | bytes 2752520 | tf_op jit(solution)/shard_map/ppermute | solution.py:17
  9.1 1.5 collective-permute-start.1
  10.7 2.0 %broadcast_in_dim.30 = bf16[512,3584]{1,0:T(8,128)(2,1)} broadcast(bf16[]{:T(256)} %constant.83.clone.1), dimensions={} | broadcast | bytes 3670018 | tf_op jit(solution)/shard_map/broadcast_in_dim | solution.py:25
  12.7 2.2 %constant_dynamic-update-slice_fusion.6 = bf16[512,3584]{1,0:T(8,128)(2,1)} fusion(bf16[512,3584]{1,0:T(8,128)(2,1)} %broadcast_in_dim.30, bf16[128,3584]{1,0:T(8,128)(2,1)} %param.7, s32[]{:T(128)S(6)} %select_n.80), kind=kLoop, calls=%fused_computation.39 | loop fusion | bytes 1835012 | tf_op jit(solution)/shard_map/dynamic_update_slice | solution.py:27
  14.9 0.1 broadcast_in_dim.33
  15.1 0.9 collective-permute-done.11
  16.0 2.6 %collective-permute-start.2 = (bf16[128,3584]{1,0:T(8,128)(2,1)}, bf16[128,3584]{1,0:T(8,128)(2,1)S(1)}, u32[]{:S(2)}, u32[]{:S(2)}) collective-permute-start(bf16[128,3584]{1,0:T(8,128)(2,1)} %param.7), channel_id=1, source_target_pairs={{0,24},{8,16},{16,8},{24,0},{1,25},{9,17},{17,9},{25,1},{2,26},{10... | collective-permute-start | bytes 2752520 | tf_op jit(solution)/shard_map/ppermute | solution.py:17
  18.6 7.6 %collective-permute-done.12 = bf16[128,1024]{0,1:T(8,128)(2,1)S(1)} collective-permute-done((bf16[128,1024]{0,1:T(8,128)(2,1)S(1)}, bf16[128,1024]{0,1:T(8,128)(2,1)S(1)}, u32[]{:S(2)}, u32[]{:S(2)}) %collective-permute-start.12) | collective-permute-done | bytes 262176 | tf_op jit(solution)/shard_map/ppermute | solution.py:69
  26.4 0.3 broadcast_in_dim.32
  26.7 0.1 bitcast_dynamic-update-slice_fusion
  26.8 4.2 %collective-permute-done = bf16[128,3584]{1,0:T(8,128)(2,1)} collective-permute-done((bf16[128,3584]{1,0:T(8,128)(2,1)}, bf16[128,3584]{1,0:T(8,128)(2,1)}, u32[]{:S(2)}, u32[]{:S(2)}) %collective-permute-start) | collective-permute-done | bytes 917536 | tf_op jit(solution)/shard_map/ppermute | solution.py:17
  31.0 2.2 %constant_dynamic-update-slice_fusion.5 = bf16[512,3584]{1,0:T(8,128)(2,1)} fusion(bf16[512,3584]{1,0:T(8,128)(2,1)} %constant_dynamic-update-slice_fusion.6, bf16[128,3584]{1,0:T(8,128)(2,1)} %collective-permute-done, s32[]{:T(128)S(6)} %select_n.81), kind=kLoop, calls=%fused_computation.38 | loop fusion | bytes 1835012 | tf_op jit(solution)/shard_map/dynamic_update_slice | solution.py:27
  33.2 16.9 %collective-permute-done.1 = bf16[128,3584]{1,0:T(8,128)(2,1)} collective-permute-done((bf16[128,3584]{1,0:T(8,128)(2,1)}, bf16[128,3584]{1,0:T(8,128)(2,1)}, u32[]{:S(2)}, u32[]{:S(2)}) %collective-permute-start.1) | collective-permute-done | bytes 917536 | tf_op jit(solution)/shard_map/ppermute | solution.py:17
  50.2 2.2 %constant_dynamic-update-slice_fusion.4 = bf16[512,3584]{1,0:T(8,128)(2,1)} fusion(bf16[512,3584]{1,0:T(8,128)(2,1)} %constant_dynamic-update-slice_fusion.5, bf16[128,3584]{1,0:T(8,128)(2,1)} %collective-permute-done.1, s32[]{:T(128)S(6)} %select_n.82), kind=kLoop, calls=%fused_computation.37 | loop fusion | bytes 1835012 | tf_op jit(solution)/shard_map/dynamic_update_slice | solution.py:27
  52.3 1.0 constant_dynamic-update-slice_fusion.3.g_ref
  53.3 7.5 %fusion.2 = f32[512,1024]{1,0:T(8,128)S(1)} fusion(bf16[512,3584]{1,0:T(8,128)(2,1)} %constant_dynamic-update-slice_fusion.3.g_ref, bf16[2048,3584]{1,0:T(8,128)(2,1)} %param.8), kind=kOutput, calls=%fused_computation.2 | convolution fusion | flops 3758096384 | bytes 13107200 | tf_op jit(solution)/shard_map/dot_general | solution.py:106
  60.9 1.2 dynamic-slice_bitcast_fusion.1
  62.2 0.3 copy-done.1
  62.5 1.3 dynamic-slice_bitcast_fusion.2
  63.8 6.0 %fusion = f32[512,1024]{1,0:T(8,128)S(1)} fusion(bf16[512,3584]{1,0:T(8,128)(2,1)} %constant_dynamic-update-slice_fusion.3.g_ref, bf16[2048,3584]{1,0:T(8,128)(2,1)S(1)} %bitcast.74), kind=kOutput, calls=%fused_computation | convolution fusion | flops 3758096384 | bytes 13107200 | tf_op jit(solution)/shard_map/dot_general | solution.py:106
  69.8 2.1 %collective-permute-start.16 = (bf16[64,32,128]{2,1,0:T(8,128)(2,1)}, bf16[64,32,128]{2,1,0:T(8,128)(2,1)}, u32[]{:S(2)}, u32[]{:S(2)}) collective-permute-start(bf16[64,32,128]{2,1,0:T(8,128)(2,1)} %get-tuple-element.7), channel_id=1, source_target_pairs={{0,16},{8,24},{16,0},{24,8},{1,17},{9,25},{17,1},{25,9},{2,18},{10... | collective-permute-start | bytes 1572872 | tf_op jit(solution)/shard_map/ppermute | solution.py:120
  71.9 1.4 collective-permute-start.17
  74.2 0.2 broadcast_in_dim.31
  74.6 4.3 %collective-permute-done.15 = bf16[64,32,128]{2,1,0:T(8,128)(2,1)} collective-permute-done((bf16[64,32,128]{2,1,0:T(8,128)(2,1)}, bf16[64,32,128]{2,1,0:T(8,128)(2,1)}, u32[]{:S(2)}, u32[]{:S(2)}) %collective-permute-start.15) | collective-permute-done | bytes 524320 | tf_op jit(solution)/shard_map/ppermute | solution.py:120
  78.8 1.2 constant_dynamic-update-slice_fusion.1
  80.0 15.6 %collective-permute-done.16 = bf16[64,32,128]{2,1,0:T(8,128)(2,1)} collective-permute-done((bf16[64,32,128]{2,1,0:T(8,128)(2,1)}, bf16[64,32,128]{2,1,0:T(8,128)(2,1)}, u32[]{:S(2)}, u32[]{:S(2)}) %collective-permute-start.16) | collective-permute-done | bytes 524320 | tf_op jit(solution)/shard_map/ppermute | solution.py:120
  95.6 1.2 constant_dynamic-update-slice_fusion
  96.7 1.2 constant_dynamic-update-slice_fusion.2.a_ref
  98.0 2.1 %bitcast_add_fusion.1 = f32[4,64,1024]{2,1,0:T(8,128)S(1)} fusion(f32[4,64,1024]{2,1,0:T(8,128)} %collective-permute-done.3, f32[4,2,64,1024]{3,2,1,0:T(8,128)S(1)} %bitcast.70, s32[]{:T(128)S(6)} %select_n.85), kind=kLoop, calls=%fused_computation.7 | loop fusion | flops 262144 | bytes 3145732 | tf_op jit(solution)/shard_map/add | solution.py:84
  100.1 0.8 dynamic-slice_bitcast_fusion.10
  100.9 0.6 collective-permute-start.4
  101.5 3.5 %collective-permute-start.5 = (f32[64,1024]{1,0:T(8,128)}, f32[64,1024]{1,0:T(8,128)}, u32[]{:S(2)}, u32[]{:S(2)}) collective-permute-start(f32[64,1024]{1,0:T(8,128)} %get-tuple-element.11), channel_id=1, source_target_pairs={{0,4},{1,5},{2,6},{3,7},{4,0},{5,1},{6,2},{7,3},{8,12},{9,13},{10,... | collective-permute-start | bytes 786440 | tf_op jit(solution)/shard_map/ppermute | solution.py:88
  105.0 0.3 collective-permute-start.6
  105.3 1.4 bitcast_add_fusion
  106.8 3.6 %collective-permute-start.10 = (f32[64,1024]{1,0:T(8,128)S(1)}, f32[64,1024]{1,0:T(8,128)}, u32[]{:S(2)}, u32[]{:S(2)}) collective-permute-start(f32[64,1024]{1,0:T(8,128)S(1)} %get-tuple-element.13), channel_id=1, source_target_pairs={{0,6},{1,7},{2,4},{3,5},{4,2},{5,3},{6,0},{7,1},{8,14},{9,15},{10,... | collective-permute-start | bytes 786440 | tf_op jit(solution)/shard_map/ppermute | solution.py:88
  110.4 4.4 %collective-permute-done.4 = f32[64,1024]{1,0:T(8,128)S(1)} collective-permute-done((f32[64,1024]{1,0:T(8,128)S(1)}, f32[64,1024]{1,0:T(8,128)S(1)}, u32[]{:S(2)}, u32[]{:S(2)}) %collective-permute-start.4) | collective-permute-done | bytes 262176 | tf_op jit(solution)/shard_map/ppermute | solution.py:88
  114.8 0.7 copy-done.5
  115.5 1.3 collective-permute-start.9
  116.8 10.9 %shard_map.77 = bf16[128,32,128]{2,1,0:T(8,128)(2,1)} custom-call(s32[128]{0:T(128)} %rows_ref.1, s32[128]{0:T(128)} %cols_ref.1, s32[1]{0:T(128)S(6)} %copy.27.cnt_ref, bf16[64,32,512]{2,1,0:T(8,128)(2,1)} %copy-done, bf16[512,3584]{1,0:T(8,128)(2,1)} %constant_dynamic-update-slice_fusion.3.g_ref), custom_call_target="tpu_custom_call" | custom-call | flops 536870912 | bytes 6815744 | tf_op jit(solution)/shard_map/pallas_call | solution.py:54
  127.7 1.7 %collective-permute-done.5 = f32[64,1024]{1,0:T(8,128)} collective-permute-done((f32[64,1024]{1,0:T(8,128)}, f32[64,1024]{1,0:T(8,128)}, u32[]{:S(2)}, u32[]{:S(2)}) %collective-permute-start.5) | collective-permute-done | bytes 262176 | tf_op jit(solution)/shard_map/ppermute | solution.py:88
  129.4 1.1 fusion.9
  130.5 0.6 collective-permute-done.8
  131.1 19.2 %collective-permute-done.9 = f32[64,1024]{1,0:T(8,128)} collective-permute-done((f32[64,1024]{1,0:T(8,128)S(1)}, f32[64,1024]{1,0:T(8,128)}, u32[]{:S(2)}, u32[]{:S(2)}) %collective-permute-start.9) | collective-permute-done | bytes 262176 | tf_op jit(solution)/shard_map/ppermute | solution.py:88
  150.4 1.2 fusion.6
  151.6 0.7 pad_maximum_fusion
  (43 shorter events, 0.8 us)
Async XLA Ops:
  1.8 14.2 %collective-permute-start.11 = (bf16[128,1024]{0,1:T(8,128)(2,1)S(1)}, bf16[128,1024]{0,1:T(8,128)(2,1)S(1)}, u32[]{:S(2)}, u32[]{:S(2)}) collective-permute-start(bf16[128,1024]{0,1:T(8,128)(2,1)S(1)} %copy.8), channel_id=1, source_target_pairs={{0,2},{1,3},{2,0},{3,1},{4,6},{5,7},{6,4},{7,5},{8,10},{9,11},{10,... | collective-permute-start | bytes 786440 | tf_op jit(solution)/shard_map/ppermute | solution.py:69
  4.8 21.4 %collective-permute-start.12 = (bf16[128,1024]{0,1:T(8,128)(2,1)S(1)}, bf16[128,1024]{0,1:T(8,128)(2,1)S(1)}, u32[]{:S(2)}, u32[]{:S(2)}) collective-permute-start(bf16[128,1024]{0,1:T(8,128)(2,1)S(1)} %copy.8), channel_id=1, source_target_pairs={{0,4},{1,5},{2,6},{3,7},{4,0},{5,1},{6,2},{7,3},{8,12},{9,13},{10,... | collective-permute-start | bytes 786440 | tf_op jit(solution)/shard_map/ppermute | solution.py:69
  7.4 18.8 %collective-permute-start.13 = (bf16[128,1024]{0,1:T(8,128)(2,1)S(1)}, bf16[128,1024]{0,1:T(8,128)(2,1)S(1)}, u32[]{:S(2)}, u32[]{:S(2)}) collective-permute-start(bf16[128,1024]{0,1:T(8,128)(2,1)S(1)} %copy.8), channel_id=1, source_target_pairs={{0,6},{1,7},{2,4},{3,5},{4,2},{5,3},{6,0},{7,1},{8,14},{9,15},{10,... | collective-permute-start | bytes 786440 | tf_op jit(solution)/shard_map/ppermute | solution.py:69
  7.4 23.6 %collective-permute-start = (bf16[128,3584]{1,0:T(8,128)(2,1)}, bf16[128,3584]{1,0:T(8,128)(2,1)}, u32[]{:S(2)}, u32[]{:S(2)}) collective-permute-start(bf16[128,3584]{1,0:T(8,128)(2,1)} %param.7), channel_id=1, source_target_pairs={{0,8},{8,0},{16,24},{24,16},{1,9},{9,1},{17,25},{25,17},{2,10},{10... | collective-permute-start | bytes 2752520 | tf_op jit(solution)/shard_map/ppermute | solution.py:17
  9.1 41.0 %collective-permute-start.1 = (bf16[128,3584]{1,0:T(8,128)(2,1)}, bf16[128,3584]{1,0:T(8,128)(2,1)}, u32[]{:S(2)}, u32[]{:S(2)}) collective-permute-start(bf16[128,3584]{1,0:T(8,128)(2,1)} %param.7), channel_id=1, source_target_pairs={{0,16},{8,24},{16,0},{24,8},{1,17},{9,25},{17,1},{25,9},{2,18},{10... | collective-permute-start | bytes 2752520 | tf_op jit(solution)/shard_map/ppermute | solution.py:17
  16.0 36.3 %collective-permute-start.2 = (bf16[128,3584]{1,0:T(8,128)(2,1)}, bf16[128,3584]{1,0:T(8,128)(2,1)S(1)}, u32[]{:S(2)}, u32[]{:S(2)}) collective-permute-start(bf16[128,3584]{1,0:T(8,128)(2,1)} %param.7), channel_id=1, source_target_pairs={{0,24},{8,16},{16,8},{24,0},{1,25},{9,17},{17,9},{25,1},{2,26},{10... | collective-permute-start | bytes 2752520 | tf_op jit(solution)/shard_map/ppermute | solution.py:17
  26.3 35.8 %collective-permute-start.14 = (bf16[4,128,1024]{1,2,0:T(8,128)(2,1)S(1)}, bf16[4,128,1024]{1,2,0:T(8,128)(2,1)S(1)}, u32[]{:S(2)}, u32[]{:S(2)}) collective-permute-start(bf16[4,128,1024]{1,2,0:T(8,128)(2,1)S(1)} %bitcast_dynamic-update-slice_fusion.3), channel_id=1, source_target_pairs={{0,1},{1,0},{2,3},{3,2},{4,5},{5,4},{6,7},{7,6},{8,9},{9,8},{10,11... | collective-permute-start | bytes 3145736 | tf_op jit(solution)/shard_map/ppermute | solution.py:73
  52.3 11.4 %slice-start = ((s8[14680064]{0:T(1024)(128)(4,1)}), s8[2097152]{0:T(1024)(128)(4,1)S(1)}, s32[]{:S(2)}) async-start(s8[14680064]{0:T(1024)(128)(4,1)} %bitcast.73), calls=%async_computation | async-start | bytes 4194304
  53.3 10.4 %slice-start.1 = ((s8[14680064]{0:T(1024)(128)(4,1)}), s8[4194304]{0:T(1024)(128)(4,1)S(1)}, s32[]{:S(2)}) async-start(s8[14680064]{0:T(1024)(128)(4,1)} %bitcast.73), calls=%async_computation.1 | async-start | bytes 8388608
  53.3 10.4 %slice-start.2 = ((s8[14680064]{0:T(1024)(128)(4,1)}), s8[4194304]{0:T(1024)(128)(4,1)S(1)}, s32[]{:S(2)}) async-start(s8[14680064]{0:T(1024)(128)(4,1)} %bitcast.73), calls=%async_computation.2 | async-start | bytes 8388608
  53.3 10.4 %slice-start.3 = ((s8[14680064]{0:T(1024)(128)(4,1)}), s8[4194304]{0:T(1024)(128)(4,1)S(1)}, s32[]{:S(2)}) async-start(s8[14680064]{0:T(1024)(128)(4,1)} %bitcast.73), calls=%async_computation.3 | async-start | bytes 8388608
  60.8 1.6 %copy-start.1 = (f32[512,1024]{1,0:T(8,128)}, f32[512,1024]{1,0:T(8,128)S(1)}, u32[]{:S(2)}) copy-start(f32[512,1024]{1,0:T(8,128)S(1)} %fusion.2) | copy-start | bytes 6291460
  62.1 35.9 %collective-permute-start.3 = (f32[4,64,1024]{2,1,0:T(8,128)}, f32[4,64,1024]{2,1,0:T(8,128)}, u32[]{:S(2)}, u32[]{:S(2)}) collective-permute-start(f32[4,64,1024]{2,1,0:T(8,128)} %dynamic-slice_bitcast_fusion.1), channel_id=1, source_target_pairs={{0,1},{1,0},{2,3},{3,2},{4,5},{5,4},{6,7},{7,6},{8,9},{9,8},{10,11... | collective-permute-start | bytes 3145736 | tf_op jit(solution)/shard_map/ppermute | solution.py:84
  63.8 15.1 %collective-permute-start.15 = (bf16[64,32,128]{2,1,0:T(8,128)(2,1)}, bf16[64,32,128]{2,1,0:T(8,128)(2,1)}, u32[]{:S(2)}, u32[]{:S(2)}) collective-permute-start(bf16[64,32,128]{2,1,0:T(8,128)(2,1)} %get-tuple-element.8), channel_id=1, source_target_pairs={{0,8},{8,0},{16,24},{24,16},{1,9},{9,1},{17,25},{25,17},{2,10},{10... | collective-permute-start | bytes 1572872 | tf_op jit(solution)/shard_map/ppermute | solution.py:120
  69.8 3.5 %copy-start.3 = (f32[512,1024]{1,0:T(8,128)}, f32[512,1024]{1,0:T(8,128)S(1)}, u32[]{:S(2)}) copy-start(f32[512,1024]{1,0:T(8,128)S(1)} %fusion) | copy-start | bytes 6291460
  69.8 25.7 %collective-permute-start.16 = (bf16[64,32,128]{2,1,0:T(8,128)(2,1)}, bf16[64,32,128]{2,1,0:T(8,128)(2,1)}, u32[]{:S(2)}, u32[]{:S(2)}) collective-permute-start(bf16[64,32,128]{2,1,0:T(8,128)(2,1)} %get-tuple-element.7), channel_id=1, source_target_pairs={{0,16},{8,24},{16,0},{24,8},{1,17},{9,25},{17,1},{25,9},{2,18},{10... | collective-permute-start | bytes 1572872 | tf_op jit(solution)/shard_map/ppermute | solution.py:120
  71.9 24.8 %collective-permute-start.17 = (bf16[64,32,128]{2,1,0:T(8,128)(2,1)}, bf16[64,32,128]{2,1,0:T(8,128)(2,1)}, u32[]{:S(2)}, u32[]{:S(2)}) collective-permute-start(bf16[64,32,128]{2,1,0:T(8,128)(2,1)} %get-tuple-element.6), channel_id=1, source_target_pairs={{0,24},{8,16},{16,8},{24,0},{1,25},{9,17},{17,9},{25,1},{2,26},{10... | collective-permute-start | bytes 1572872 | tf_op jit(solution)/shard_map/ppermute | solution.py:120
  73.4 31.9 %collective-permute-start.7 = (f32[4,64,1024]{2,1,0:T(8,128)S(1)}, f32[4,64,1024]{2,1,0:T(8,128)}, u32[]{:S(2)}, u32[]{:S(2)}) collective-permute-start(f32[4,64,1024]{2,1,0:T(8,128)S(1)} %dynamic-slice_bitcast_fusion), channel_id=1, source_target_pairs={{0,1},{1,0},{2,3},{3,2},{4,5},{5,4},{6,7},{7,6},{8,9},{9,8},{10,11... | collective-permute-start | bytes 3145736 | tf_op jit(solution)/shard_map/ppermute | solution.py:84
  74.4 23.5 %copy-start.2 = (f32[512,1024]{1,0:T(8,128)S(1)}, f32[512,1024]{1,0:T(8,128)}, u32[]{:S(2)}) copy-start(f32[512,1024]{1,0:T(8,128)} %copy-done.1) | copy-start | bytes 6291460
  97.9 3.0 %copy-start = (bf16[64,32,512]{2,1,0:T(8,128)(2,1)}, bf16[64,32,512]{2,1,0:T(8,128)(2,1)S(1)}, u32[]{:S(2)}) copy-start(bf16[64,32,512]{2,1,0:T(8,128)(2,1)S(1)} %constant_dynamic-update-slice_fusion.2.a_ref) | copy-start | bytes 6291460
  97.9 7.4 %copy-start.4 = (f32[512,1024]{1,0:T(8,128)S(1)}, f32[512,1024]{1,0:T(8,128)}, u32[]{:S(2)}) copy-start(f32[512,1024]{1,0:T(8,128)} %copy-done.3) | copy-start | bytes 6291460
  100.9 13.9 %collective-permute-start.4 = (f32[64,1024]{1,0:T(8,128)S(1)}, f32[64,1024]{1,0:T(8,128)S(1)}, u32[]{:S(2)}, u32[]{:S(2)}) collective-permute-start(f32[64,1024]{1,0:T(8,128)S(1)} %get-tuple-element.9), channel_id=1, source_target_pairs={{0,2},{1,3},{2,0},{3,1},{4,6},{5,7},{6,4},{7,5},{8,10},{9,11},{10,... | collective-permute-start | bytes 786440 | tf_op jit(solution)/shard_map/ppermute | solution.py:88
  101.5 27.9 %collective-permute-start.5 = (f32[64,1024]{1,0:T(8,128)}, f32[64,1024]{1,0:T(8,128)}, u32[]{:S(2)}, u32[]{:S(2)}) collective-permute-start(f32[64,1024]{1,0:T(8,128)} %get-tuple-element.11), channel_id=1, source_target_pairs={{0,4},{1,5},{2,6},{3,7},{4,0},{5,1},{6,2},{7,3},{8,12},{9,13},{10,... | collective-permute-start | bytes 786440 | tf_op jit(solution)/shard_map/ppermute | solution.py:88
  105.0 24.4 %collective-permute-start.6 = (f32[64,1024]{1,0:T(8,128)S(1)}, f32[64,1024]{1,0:T(8,128)}, u32[]{:S(2)}, u32[]{:S(2)}) collective-permute-start(f32[64,1024]{1,0:T(8,128)S(1)} %get-tuple-element.10), channel_id=1, source_target_pairs={{0,6},{1,7},{2,4},{3,5},{4,2},{5,3},{6,0},{7,1},{8,14},{9,15},{10,... | collective-permute-start | bytes 786440 | tf_op jit(solution)/shard_map/ppermute | solution.py:88
  106.8 23.8 %collective-permute-start.10 = (f32[64,1024]{1,0:T(8,128)S(1)}, f32[64,1024]{1,0:T(8,128)}, u32[]{:S(2)}, u32[]{:S(2)}) collective-permute-start(f32[64,1024]{1,0:T(8,128)S(1)} %get-tuple-element.13), channel_id=1, source_target_pairs={{0,6},{1,7},{2,4},{3,5},{4,2},{5,3},{6,0},{7,1},{8,14},{9,15},{10,... | collective-permute-start | bytes 786440 | tf_op jit(solution)/shard_map/ppermute | solution.py:88
  110.4 20.8 %collective-permute-start.8 = (f32[64,1024]{1,0:T(8,128)S(1)}, f32[64,1024]{1,0:T(8,128)}, u32[]{:S(2)}, u32[]{:S(2)}) collective-permute-start(f32[64,1024]{1,0:T(8,128)S(1)} %get-tuple-element.12), channel_id=1, source_target_pairs={{0,2},{1,3},{2,0},{3,1},{4,6},{5,7},{6,4},{7,5},{8,10},{9,11},{10,... | collective-permute-start | bytes 786440 | tf_op jit(solution)/shard_map/ppermute | solution.py:88
  114.8 0.7 copy-start.5
  115.5 14.0 %copy-start.6 = (f32[64,1024]{1,0:T(8,128)S(1)}, f32[64,1024]{1,0:T(8,128)}, u32[]{:S(2)}) copy-start(f32[64,1024]{1,0:T(8,128)} %copy-done.5) | copy-start | bytes 786436
  115.5 34.9 %collective-permute-start.9 = (f32[64,1024]{1,0:T(8,128)S(1)}, f32[64,1024]{1,0:T(8,128)}, u32[]{:S(2)}, u32[]{:S(2)}) collective-permute-start(f32[64,1024]{1,0:T(8,128)S(1)} %get-tuple-element.14), channel_id=1, source_target_pairs={{0,4},{1,5},{2,6},{3,7},{4,0},{5,1},{6,2},{7,3},{8,12},{9,13},{10,... | collective-permute-start | bytes 786440 | tf_op jit(solution)/shard_map/ppermute | solution.py:88

commit v6 on v5

--- a/solution.py
+++ b/solution.py
@@ -110,9 +110,9 @@
             preferred_element_type=jnp.float32,
         )
         halves.append(feat_reduce_scatter(partial_sums, n_feat, me_feat))
+
+    acts_pieces, gout, halves[0] = lax.optimization_barrier((acts_pieces, gout, halves[0]))
     grad_in = jnp.concatenate(halves, axis=1).astype(jnp.bfloat16)
-
-    acts_pieces, gout = lax.optimization_barrier((acts_pieces, gout))
     got = []
     for m in range(n_tok):
         part = lax.dynamic_index_in_dim(acts_pieces, me ^ m, axis=0, keepdims=False)

time: 153 us -> 134 us (0.88)
  waiting for transfers between devices: 75.4 us -> 58 us
  starting transfers between devices: 24.5 us -> 28.2 us
  other arithmetic: 6.52 us -> 3.58 us
  local copies, waits for them, and re-layouts: 19.8 us -> 17.7 us
    ppermute x3, waiting for transfers between devices: 19.8 us -> 6.5 us  [per_device(): part = lax.ppermute(part, 'tok', perm=[(a, a ^ m) for a in range(n_tok)])]
    ppermute x3, waiting for transfers between devices: 21.2 us -> 15.4 us  [xor_exchange(): out.append(lax.ppermute(x, axis_name, perm=[(a, a ^ m) for a in range(n)]))]
    ppermute x6, starting transfers between devices: 9.32 us -> 12.2 us  [feat_reduce_scatter(): lax.ppermute(part, 'feat', perm=[(a, a ^ 2 * m) for a in range(n_feat)])]
    another operation x2 -> x1, other arithmetic: 2.25 us -> 0.06 us
    dynamic_update_slice x14, local copies, waits for them, and re-layouts: 11.6 us -> 9.58 us  [place_rows(): out = lax.dynamic_update_slice_in_dim(out, piece, (me ^ m) * rows, axis)]
    ppermute x3, starting transfers between devices: 5.68 us -> 7.33 us  [feat_all_gather(): lax.ppermute(x, 'feat', perm=[(a, a ^ m) for a in range(n_feat)])]
  transfers between devices with their start and end apart: 18 -> 18, of which waited for: 10 -> 10; matrix products, arithmetic and copies ran while one was open for 24% -> 25% of each run, Pallas kernels for 7% -> 0%
where the time goes in v6:
time: 134 us
  waiting for transfers between devices  58 us (43%)
  starting transfers between devices  28.2 us (21%)
  local copies, waits for them, and re-layouts  17.7 us (13%)
  matrix products  14 us (10%)
  Pallas kernels  10.9 us (8%)
  other arithmetic  3.58 us (3%)
  between operations  1.61 us (1%)
    ppermute x6, waiting for transfers between devices, feat_reduce_scatter(): lax.ppermute(part, 'feat', perm=[(a, a ^ 2 * m) for a in range(n_feat)])  26.3 us
    ppermute x3, waiting for transfers between devices, xor_exchange(): out.append(lax.ppermute(x, axis_name, perm=[(a, a ^ m) for a in range(n)]))  15.4 us
    dot_general x2, matrix products, per_device(): lax.dot_general(gout, weight[k * d_half:(k + 1) * d_half], (((1,), (1,)),...  14 us
    ppermute x6, starting transfers between devices, feat_reduce_scatter(): lax.ppermute(part, 'feat', perm=[(a, a ^ 2 * m) for a in range(n_feat)])  12.2 us
    pallas_call x1, Pallas kernels, block_tiles(): pl.pallas_call(block_kernel, grid_spec=grid_spec, out_shape=jax.ShapeDtyp...  10.9 us
    ppermute x3, waiting for transfers between devices, feat_all_gather(): lax.ppermute(x, 'feat', perm=[(a, a ^ m) for a in range(n_feat)])  9.77 us
    dynamic_update_slice x14, local copies, waits for them, and re-layouts, place_rows(): out = lax.dynamic_update_slice_in_dim(out, piece, (me ^ m) * rows, axis)  9.58 us
    ppermute x3, starting transfers between devices, feat_all_gather(): lax.ppermute(x, 'feat', perm=[(a, a ^ m) for a in range(n_feat)])  7.33 us
  transfers between devices with their start and end apart: 18, of which 10 were waited for; matrix products, arithmetic and copies ran while one was open for 25% of the time, Pallas kernels for 0%

profile of v6, /device:TPU:0, one launch (start us, length us, event | category | flops | bytes accessed | tf_op | source)
XLA Modules:
  0.0 133.9 jit_solution(1371994343844063803)
XLA Ops:
  0.6 3.0 %collective-permute-start.4 = (bf16[128,3584]{1,0:T(8,128)(2,1)}, bf16[128,3584]{1,0:T(8,128)(2,1)}, u32[]{:S(2)}, u32[]{:S(2)}) collective-permute-start(bf16[128,3584]{1,0:T(8,128)(2,1)} %param.7), channel_id=1, source_target_pairs={{0,8},{8,0},{16,24},{24,16},{1,9},{9,1},{17,25},{25,17},{2,10},{10... | collective-permute-start | bytes 2752520 | tf_op jit(solution)/shard_map/ppermute | solution.py:17
  3.6 1.5 %collective-permute-start.5 = (bf16[128,3584]{1,0:T(8,128)(2,1)}, bf16[128,3584]{1,0:T(8,128)(2,1)}, u32[]{:S(2)}, u32[]{:S(2)}) collective-permute-start(bf16[128,3584]{1,0:T(8,128)(2,1)} %param.7), channel_id=1, source_target_pairs={{0,16},{8,24},{16,0},{24,8},{1,17},{9,25},{17,1},{25,9},{2,18},{10... | collective-permute-start | bytes 2752520 | tf_op jit(solution)/shard_map/ppermute | solution.py:17
  5.2 1.1 copy.8
  6.3 2.1 %collective-permute-start = (bf16[128,1024]{0,1:T(8,128)(2,1)S(1)}, bf16[128,1024]{0,1:T(8,128)(2,1)}, u32[]{:S(2)}, u32[]{:S(2)}) collective-permute-start(bf16[128,1024]{0,1:T(8,128)(2,1)S(1)} %copy.8), channel_id=1, source_target_pairs={{0,2},{1,3},{2,0},{3,1},{4,6},{5,7},{6,4},{7,5},{8,10},{9,11},{10,... | collective-permute-start | bytes 786440 | tf_op jit(solution)/shard_map/ppermute | solution.py:69
  8.4 2.6 %collective-permute-start.1 = (bf16[128,1024]{0,1:T(8,128)(2,1)S(1)}, bf16[128,1024]{0,1:T(8,128)(2,1)S(1)}, u32[]{:S(2)}, u32[]{:S(2)}) collective-permute-start(bf16[128,1024]{0,1:T(8,128)(2,1)S(1)} %copy.8), channel_id=1, source_target_pairs={{0,4},{1,5},{2,6},{3,7},{4,0},{5,1},{6,2},{7,3},{8,12},{9,13},{10,... | collective-permute-start | bytes 786440 | tf_op jit(solution)/shard_map/ppermute | solution.py:69
  11.0 2.0 %broadcast_in_dim.38 = bf16[512,3584]{1,0:T(8,128)(2,1)} broadcast(bf16[]{:T(256)} %constant.83.clone.1), dimensions={} | broadcast | bytes 3670018 | tf_op jit(solution)/shard_map/broadcast_in_dim | solution.py:25
  13.0 1.0 constant_dynamic-update-slice_fusion.6
  14.0 0.1 broadcast_in_dim.31
  14.3 5.2 %collective-permute-done = bf16[128,1024]{0,1:T(8,128)(2,1)} collective-permute-done((bf16[128,1024]{0,1:T(8,128)(2,1)S(1)}, bf16[128,1024]{0,1:T(8,128)(2,1)}, u32[]{:S(2)}, u32[]{:S(2)}) %collective-permute-start) | collective-permute-done | bytes 262176 | tf_op jit(solution)/shard_map/ppermute | solution.py:69
  19.5 2.6 %collective-permute-start.2 = (bf16[128,1024]{0,1:T(8,128)(2,1)S(1)}, bf16[128,1024]{0,1:T(8,128)(2,1)S(1)}, u32[]{:S(2)}, u32[]{:S(2)}) collective-permute-start(bf16[128,1024]{0,1:T(8,128)(2,1)S(1)} %copy.8), channel_id=1, source_target_pairs={{0,6},{1,7},{2,4},{3,5},{4,2},{5,3},{6,0},{7,1},{8,14},{9,15},{10,... | collective-permute-start | bytes 786440 | tf_op jit(solution)/shard_map/ppermute | solution.py:69
  22.1 1.0 bitcast_dynamic-update-slice_fusion.5
  23.1 1.6 %collective-permute-done.1 = bf16[128,1024]{0,1:T(8,128)(2,1)S(1)} collective-permute-done((bf16[128,1024]{0,1:T(8,128)(2,1)S(1)}, bf16[128,1024]{0,1:T(8,128)(2,1)S(1)}, u32[]{:S(2)}, u32[]{:S(2)}) %collective-permute-start.1) | collective-permute-done | bytes 262176 | tf_op jit(solution)/shard_map/ppermute | solution.py:69
  24.8 2.9 %collective-permute-done.2 = bf16[128,1024]{0,1:T(8,128)(2,1)S(1)} collective-permute-done((bf16[128,1024]{0,1:T(8,128)(2,1)S(1)}, bf16[128,1024]{0,1:T(8,128)(2,1)S(1)}, u32[]{:S(2)}, u32[]{:S(2)}) %collective-permute-start.2) | collective-permute-done | bytes 262176 | tf_op jit(solution)/shard_map/ppermute | solution.py:69
  27.8 2.2 %constant_dynamic-update-slice_fusion.5 = bf16[512,3584]{1,0:T(8,128)(2,1)} fusion(bf16[512,3584]{1,0:T(8,128)(2,1)} %constant_dynamic-update-slice_fusion.6, bf16[128,3584]{1,0:T(8,128)(2,1)} %collective-permute-done.4, s32[]{:T(128)S(6)} %select_n.89), kind=kLoop, calls=%fused_computation.37 | loop fusion | bytes 1835012 | tf_op jit(solution)/shard_map/dynamic_update_slice | solution.py:27
  30.0 15.4 %collective-permute-done.5 = bf16[128,3584]{1,0:T(8,128)(2,1)} collective-permute-done((bf16[128,3584]{1,0:T(8,128)(2,1)}, bf16[128,3584]{1,0:T(8,128)(2,1)}, u32[]{:S(2)}, u32[]{:S(2)}) %collective-permute-start.5) | collective-permute-done | bytes 917536 | tf_op jit(solution)/shard_map/ppermute | solution.py:17
  45.4 2.2 %constant_dynamic-update-slice_fusion.4 = bf16[512,3584]{1,0:T(8,128)(2,1)} fusion(bf16[512,3584]{1,0:T(8,128)(2,1)} %constant_dynamic-update-slice_fusion.5, bf16[128,3584]{1,0:T(8,128)(2,1)} %collective-permute-done.5, s32[]{:T(128)S(6)} %select_n.90), kind=kLoop, calls=%fused_computation.36 | loop fusion | bytes 1835012 | tf_op jit(solution)/shard_map/dynamic_update_slice | solution.py:27
  47.6 1.0 constant_dynamic-update-slice_fusion.3.g_ref
  48.6 7.9 %fusion.2 = f32[512,1024]{1,0:T(8,128)S(1)} fusion(bf16[512,3584]{1,0:T(8,128)(2,1)} %constant_dynamic-update-slice_fusion.3.g_ref, bf16[2048,3584]{1,0:T(8,128)(2,1)} %param.8), kind=kOutput, calls=%fused_computation.2 | convolution fusion | flops 3758096384 | bytes 13107200 | tf_op jit(solution)/shard_map/dot_general | solution.py:106
  56.6 1.2 dynamic-slice_bitcast_fusion.1
  57.8 6.0 %fusion = f32[512,1024]{1,0:T(8,128)S(1)} fusion(bf16[512,3584]{1,0:T(8,128)(2,1)} %constant_dynamic-update-slice_fusion.3.g_ref, bf16[2048,3584]{1,0:T(8,128)(2,1)S(1)} %bitcast.72), kind=kOutput, calls=%fused_computation | convolution fusion | flops 3758096384 | bytes 13107200 | tf_op jit(solution)/shard_map/dot_general | solution.py:106
  63.8 1.0 dynamic-slice_bitcast_fusion
  64.9 0.5 collective-permute-start.11
  66.0 0.3 broadcast_in_dim.30
  66.3 0.1 bitcast_dynamic-update-slice_fusion
  66.5 1.5 %bitcast_dynamic-update-slice_fusion.1 = bf16[4,2,128,1024]{2,3,1,0:T(8,128)(2,1)S(1)} fusion(bf16[4,2,128,1024]{2,3,1,0:T(8,128)(2,1)S(1)} %bitcast_dynamic-update-slice_fusion, s32[]{:T(128)S(6)} %select_n.87, bf16[4,128,1024]{1,2,0:T(8,128)(2,1)} %collective-permute-done.3), kind=kLoop, calls=%fused_computation.7 | loop fusion | bytes 2097156 | tf_op jit(solution)/shard_map/dynamic_update_slice | solution.py:27
  68.0 0.2 copy-done.2
  68.2 1.4 %bitcast_add_fusion.1 = f32[4,64,1024]{2,1,0:T(8,128)S(1)} fusion(f32[4,64,1024]{2,1,0:T(8,128)} %collective-permute-done.7, f32[4,2,64,1024]{3,2,1,0:T(8,128)S(1)} %bitcast.70, s32[]{:T(128)S(6)} %select_n.86), kind=kLoop, calls=%fused_computation.6 | loop fusion | flops 262144 | bytes 3145732 | tf_op jit(solution)/shard_map/add | solution.py:84
  69.7 3.7 %collective-permute-start.10 = (f32[64,1024]{1,0:T(8,128)S(1)}, f32[64,1024]{1,0:T(8,128)S(1)}, u32[]{:S(2)}, u32[]{:S(2)}) collective-permute-start(f32[64,1024]{1,0:T(8,128)S(1)} %get-tuple-element.12), channel_id=1, source_target_pairs={{0,6},{1,7},{2,4},{3,5},{4,2},{5,3},{6,0},{7,1},{8,14},{9,15},{10,... | collective-permute-start | bytes 786440 | tf_op jit(solution)/shard_map/ppermute | solution.py:88
  73.3 0.8 collective-permute-start.9
  74.1 1.4 %bitcast_add_fusion = f32[4,64,1024]{2,1,0:T(8,128)S(1)} fusion(f32[4,64,1024]{2,1,0:T(8,128)} %collective-permute-done.11, f32[4,2,64,1024]{3,2,1,0:T(8,128)S(1)} %bitcast.68, s32[]{:T(128)S(6)} %select_n.86), kind=kLoop, calls=%fused_computation.5 | loop fusion | flops 262144 | bytes 3145732 | tf_op jit(solution)/shard_map/add | solution.py:84
  75.6 1.3 collective-permute-start.12
  76.9 2.9 %collective-permute-start.13 = (f32[64,1024]{1,0:T(8,128)S(1)}, f32[64,1024]{1,0:T(8,128)S(1)}, u32[]{:S(2)}, u32[]{:S(2)}) collective-permute-start(f32[64,1024]{1,0:T(8,128)S(1)} %get-tuple-element.16), channel_id=1, source_target_pairs={{0,4},{1,5},{2,6},{3,7},{4,0},{5,1},{6,2},{7,3},{8,12},{9,13},{10,... | collective-permute-start | bytes 786440 | tf_op jit(solution)/shard_map/ppermute | solution.py:88
  79.8 1.0 collective-permute-done.10
  80.8 3.6 %collective-permute-start.14 = (f32[64,1024]{1,0:T(8,128)S(1)}, f32[64,1024]{1,0:T(8,128)S(1)}, u32[]{:S(2)}, u32[]{:S(2)}) collective-permute-start(f32[64,1024]{1,0:T(8,128)S(1)} %get-tuple-element.15), channel_id=1, source_target_pairs={{0,6},{1,7},{2,4},{3,5},{4,2},{5,3},{6,0},{7,1},{8,14},{9,15},{10,... | collective-permute-start | bytes 786440 | tf_op jit(solution)/shard_map/ppermute | solution.py:88
  84.3 2.3 %collective-permute-done.8 = f32[64,1024]{1,0:T(8,128)S(1)} collective-permute-done((f32[64,1024]{1,0:T(8,128)S(1)}, f32[64,1024]{1,0:T(8,128)S(1)}, u32[]{:S(2)}, u32[]{:S(2)}) %collective-permute-start.8) | collective-permute-done | bytes 262176 | tf_op jit(solution)/shard_map/ppermute | solution.py:88
  86.7 11.0 %collective-permute-done.9 = f32[64,1024]{1,0:T(8,128)S(1)} collective-permute-done((f32[64,1024]{1,0:T(8,128)S(1)}, f32[64,1024]{1,0:T(8,128)S(1)}, u32[]{:S(2)}, u32[]{:S(2)}) %collective-permute-start.9) | collective-permute-done | bytes 262176 | tf_op jit(solution)/shard_map/ppermute | solution.py:88
  97.7 0.4 dynamic-slice_bitcast_fusion.2
  98.2 2.0 %collective-permute-start.16 = (bf16[64,32,128]{2,1,0:T(8,128)(2,1)S(1)}, bf16[64,32,128]{2,1,0:T(8,128)(2,1)S(1)}, u32[]{:S(2)}, u32[]{:S(2)}) collective-permute-start(bf16[64,32,128]{2,1,0:T(8,128)(2,1)S(1)} %get-tuple-element.9), channel_id=1, source_target_pairs={{0,16},{8,24},{16,0},{24,8},{1,17},{9,25},{17,1},{25,9},{2,18},{10... | collective-permute-start | bytes 1572872 | tf_op jit(solution)/shard_map/ppermute | solution.py:120
  100.2 1.4 %collective-permute-start.17 = (bf16[64,32,128]{2,1,0:T(8,128)(2,1)S(1)}, bf16[64,32,128]{2,1,0:T(8,128)(2,1)S(1)}, u32[]{:S(2)}, u32[]{:S(2)}) collective-permute-start(bf16[64,32,128]{2,1,0:T(8,128)(2,1)S(1)} %get-tuple-element.8), channel_id=1, source_target_pairs={{0,24},{8,16},{16,8},{24,0},{1,25},{9,17},{17,9},{25,1},{2,26},{10... | collective-permute-start | bytes 1572872 | tf_op jit(solution)/shard_map/ppermute | solution.py:120
  101.7 12.0 %collective-permute-done.13 = f32[64,1024]{1,0:T(8,128)S(1)} collective-permute-done((f32[64,1024]{1,0:T(8,128)S(1)}, f32[64,1024]{1,0:T(8,128)S(1)}, u32[]{:S(2)}, u32[]{:S(2)}) %collective-permute-start.13) | collective-permute-done | bytes 262176 | tf_op jit(solution)/shard_map/ppermute | solution.py:88
  113.7 0.2 broadcast_in_dim.39
  114.0 0.1 bitcast_dynamic-update-slice_fusion.2
  114.1 0.7 pad_maximum_fusion
  114.8 0.1 constant_dynamic-update-slice_fusion.1
  115.0 5.0 %collective-permute-done.16 = bf16[64,32,128]{2,1,0:T(8,128)(2,1)S(1)} collective-permute-done((bf16[64,32,128]{2,1,0:T(8,128)(2,1)S(1)}, bf16[64,32,128]{2,1,0:T(8,128)(2,1)S(1)}, u32[]{:S(2)}, u32[]{:S(2)}) %collective-permute-start.16) | collective-permute-done | bytes 524320 | tf_op jit(solution)/shard_map/ppermute | solution.py:120
  120.1 1.5 %collective-permute-done.17 = bf16[64,32,128]{2,1,0:T(8,128)(2,1)S(1)} collective-permute-done((bf16[64,32,128]{2,1,0:T(8,128)(2,1)S(1)}, bf16[64,32,128]{2,1,0:T(8,128)(2,1)S(1)}, u32[]{:S(2)}, u32[]{:S(2)}) %collective-permute-start.17) | collective-permute-done | bytes 524320 | tf_op jit(solution)/shard_map/ppermute | solution.py:120
  121.7 1.3 copy-done
  123.0 10.9 %shard_map.77 = bf16[128,32,128]{2,1,0:T(8,128)(2,1)} custom-call(s32[128]{0:T(128)} %rows_ref.1, s32[128]{0:T(128)} %cols_ref.1, s32[1]{0:T(128)S(6)} %copy.27.cnt_ref, bf16[64,32,512]{2,1,0:T(8,128)(2,1)} %copy-done, bf16[512,3584]{1,0:T(8,128)(2,1)} %constant_dynamic-update-slice_fusion.3.g_ref), custom_call_target="tpu_custom_call" | custom-call | flops 536870912 | bytes 6815744 | tf_op jit(solution)/shard_map/pallas_call | solution.py:54
  (37 shorter events, 0.9 us)
Async XLA Ops:
  0.6 12.4 %copy-start.3 = (bf16[128,3584]{1,0:T(8,128)(2,1)S(1)}, bf16[128,3584]{1,0:T(8,128)(2,1)}, u32[]{:S(2)}) copy-start(bf16[128,3584]{1,0:T(8,128)(2,1)} %param.7) | copy-start | bytes 2752516
  0.6 27.2 %collective-permute-start.4 = (bf16[128,3584]{1,0:T(8,128)(2,1)}, bf16[128,3584]{1,0:T(8,128)(2,1)}, u32[]{:S(2)}, u32[]{:S(2)}) collective-permute-start(bf16[128,3584]{1,0:T(8,128)(2,1)} %param.7), channel_id=1, source_target_pairs={{0,8},{8,0},{16,24},{24,16},{1,9},{9,1},{17,25},{25,17},{2,10},{10... | collective-permute-start | bytes 2752520 | tf_op jit(solution)/shard_map/ppermute | solution.py:17
  3.6 41.8 %collective-permute-start.5 = (bf16[128,3584]{1,0:T(8,128)(2,1)}, bf16[128,3584]{1,0:T(8,128)(2,1)}, u32[]{:S(2)}, u32[]{:S(2)}) collective-permute-start(bf16[128,3584]{1,0:T(8,128)(2,1)} %param.7), channel_id=1, source_target_pairs={{0,16},{8,24},{16,0},{24,8},{1,17},{9,25},{17,1},{25,9},{2,18},{10... | collective-permute-start | bytes 2752520 | tf_op jit(solution)/shard_map/ppermute | solution.py:17
  5.2 42.4 %collective-permute-start.6 = (bf16[128,3584]{1,0:T(8,128)(2,1)}, bf16[128,3584]{1,0:T(8,128)(2,1)S(1)}, u32[]{:S(2)}, u32[]{:S(2)}) collective-permute-start(bf16[128,3584]{1,0:T(8,128)(2,1)} %param.7), channel_id=1, source_target_pairs={{0,24},{8,16},{16,8},{24,0},{1,25},{9,17},{17,9},{25,1},{2,26},{10... | collective-permute-start | bytes 2752520 | tf_op jit(solution)/shard_map/ppermute | solution.py:17
  6.3 13.2 %collective-permute-start = (bf16[128,1024]{0,1:T(8,128)(2,1)S(1)}, bf16[128,1024]{0,1:T(8,128)(2,1)}, u32[]{:S(2)}, u32[]{:S(2)}) collective-permute-start(bf16[128,1024]{0,1:T(8,128)(2,1)S(1)} %copy.8), channel_id=1, source_target_pairs={{0,2},{1,3},{2,0},{3,1},{4,6},{5,7},{6,4},{7,5},{8,10},{9,11},{10,... | collective-permute-start | bytes 786440 | tf_op jit(solution)/shard_map/ppermute | solution.py:69
  8.4 16.3 %collective-permute-start.1 = (bf16[128,1024]{0,1:T(8,128)(2,1)S(1)}, bf16[128,1024]{0,1:T(8,128)(2,1)S(1)}, u32[]{:S(2)}, u32[]{:S(2)}) collective-permute-start(bf16[128,1024]{0,1:T(8,128)(2,1)S(1)} %copy.8), channel_id=1, source_target_pairs={{0,4},{1,5},{2,6},{3,7},{4,0},{5,1},{6,2},{7,3},{8,12},{9,13},{10,... | collective-permute-start | bytes 786440 | tf_op jit(solution)/shard_map/ppermute | solution.py:69
  19.5 8.2 %collective-permute-start.2 = (bf16[128,1024]{0,1:T(8,128)(2,1)S(1)}, bf16[128,1024]{0,1:T(8,128)(2,1)S(1)}, u32[]{:S(2)}, u32[]{:S(2)}) collective-permute-start(bf16[128,1024]{0,1:T(8,128)(2,1)S(1)} %copy.8), channel_id=1, source_target_pairs={{0,6},{1,7},{2,4},{3,5},{4,2},{5,3},{6,0},{7,1},{8,14},{9,15},{10,... | collective-permute-start | bytes 786440 | tf_op jit(solution)/shard_map/ppermute | solution.py:69
  27.7 38.7 %collective-permute-start.3 = (bf16[4,128,1024]{1,2,0:T(8,128)(2,1)S(1)}, bf16[4,128,1024]{1,2,0:T(8,128)(2,1)}, u32[]{:S(2)}, u32[]{:S(2)}) collective-permute-start(bf16[4,128,1024]{1,2,0:T(8,128)(2,1)S(1)} %bitcast_dynamic-update-slice_fusion.3), channel_id=1, source_target_pairs={{0,1},{1,0},{2,3},{3,2},{4,5},{5,4},{6,7},{7,6},{8,9},{9,8},{10,11... | collective-permute-start | bytes 3145736 | tf_op jit(solution)/shard_map/ppermute | solution.py:73
  47.6 10.2 %slice-start = ((s8[14680064]{0:T(1024)(128)(4,1)}), s8[4194304]{0:T(1024)(128)(4,1)S(1)}, s32[]{:S(2)}) async-start(s8[14680064]{0:T(1024)(128)(4,1)} %bitcast.71), calls=%async_computation | async-start | bytes 8388608
  48.6 9.2 %slice-start.1 = ((s8[14680064]{0:T(1024)(128)(4,1)}), s8[4194304]{0:T(1024)(128)(4,1)S(1)}, s32[]{:S(2)}) async-start(s8[14680064]{0:T(1024)(128)(4,1)} %bitcast.71), calls=%async_computation.1 | async-start | bytes 8388608
  48.6 9.2 %slice-start.2 = ((s8[14680064]{0:T(1024)(128)(4,1)}), s8[4194304]{0:T(1024)(128)(4,1)S(1)}, s32[]{:S(2)}) async-start(s8[14680064]{0:T(1024)(128)(4,1)} %bitcast.71), calls=%async_computation.2 | async-start | bytes 8388608
  48.6 9.2 %slice-start.3 = ((s8[14680064]{0:T(1024)(128)(4,1)}), s8[2097152]{0:T(1024)(128)(4,1)S(1)}, s32[]{:S(2)}) async-start(s8[14680064]{0:T(1024)(128)(4,1)} %bitcast.71), calls=%async_computation.3 | async-start | bytes 4194304
  56.6 7.2 %copy-start.1 = (f32[512,1024]{1,0:T(8,128)}, f32[512,1024]{1,0:T(8,128)S(1)}, u32[]{:S(2)}) copy-start(f32[512,1024]{1,0:T(8,128)S(1)} %fusion.2) | copy-start | bytes 6291460
  57.8 10.2 %collective-permute-start.7 = (f32[4,64,1024]{2,1,0:T(8,128)}, f32[4,64,1024]{2,1,0:T(8,128)}, u32[]{:S(2)}, u32[]{:S(2)}) collective-permute-start(f32[4,64,1024]{2,1,0:T(8,128)} %dynamic-slice_bitcast_fusion.1), channel_id=1, source_target_pairs={{0,1},{1,0},{2,3},{3,2},{4,5},{5,4},{6,7},{7,6},{8,9},{9,8},{10,11... | collective-permute-start | bytes 3145736 | tf_op jit(solution)/shard_map/ppermute | solution.py:84
  64.9 9.3 %collective-permute-start.11 = (f32[4,64,1024]{2,1,0:T(8,128)}, f32[4,64,1024]{2,1,0:T(8,128)}, u32[]{:S(2)}, u32[]{:S(2)}) collective-permute-start(f32[4,64,1024]{2,1,0:T(8,128)} %dynamic-slice_bitcast_fusion), channel_id=1, source_target_pairs={{0,1},{1,0},{2,3},{3,2},{4,5},{5,4},{6,7},{7,6},{8,9},{9,8},{10,11... | collective-permute-start | bytes 3145736 | tf_op jit(solution)/shard_map/ppermute | solution.py:84
  66.3 1.9 %copy-start.2 = (f32[512,1024]{1,0:T(8,128)S(1)}, f32[512,1024]{1,0:T(8,128)}, u32[]{:S(2)}) copy-start(f32[512,1024]{1,0:T(8,128)} %copy-done.1) | copy-start | bytes 6291460
  69.7 11.1 %collective-permute-start.10 = (f32[64,1024]{1,0:T(8,128)S(1)}, f32[64,1024]{1,0:T(8,128)S(1)}, u32[]{:S(2)}, u32[]{:S(2)}) collective-permute-start(f32[64,1024]{1,0:T(8,128)S(1)} %get-tuple-element.12), channel_id=1, source_target_pairs={{0,6},{1,7},{2,4},{3,5},{4,2},{5,3},{6,0},{7,1},{8,14},{9,15},{10,... | collective-permute-start | bytes 786440 | tf_op jit(solution)/shard_map/ppermute | solution.py:88
  73.3 13.3 %collective-permute-start.8 = (f32[64,1024]{1,0:T(8,128)S(1)}, f32[64,1024]{1,0:T(8,128)S(1)}, u32[]{:S(2)}, u32[]{:S(2)}) collective-permute-start(f32[64,1024]{1,0:T(8,128)S(1)} %get-tuple-element.11), channel_id=1, source_target_pairs={{0,2},{1,3},{2,0},{3,1},{4,6},{5,7},{6,4},{7,5},{8,10},{9,11},{10,... | collective-permute-start | bytes 786440 | tf_op jit(solution)/shard_map/ppermute | solution.py:88
  73.3 24.3 %collective-permute-start.9 = (f32[64,1024]{1,0:T(8,128)S(1)}, f32[64,1024]{1,0:T(8,128)S(1)}, u32[]{:S(2)}, u32[]{:S(2)}) collective-permute-start(f32[64,1024]{1,0:T(8,128)S(1)} %get-tuple-element.13), channel_id=1, source_target_pairs={{0,4},{1,5},{2,6},{3,7},{4,0},{5,1},{6,2},{7,3},{8,12},{9,13},{10,... | collective-permute-start | bytes 786440 | tf_op jit(solution)/shard_map/ppermute | solution.py:88
  75.6 24.7 %collective-permute-start.12 = (f32[64,1024]{1,0:T(8,128)S(1)}, f32[64,1024]{1,0:T(8,128)S(1)}, u32[]{:S(2)}, u32[]{:S(2)}) collective-permute-start(f32[64,1024]{1,0:T(8,128)S(1)} %get-tuple-element.14), channel_id=1, source_target_pairs={{0,2},{1,3},{2,0},{3,1},{4,6},{5,7},{6,4},{7,5},{8,10},{9,11},{10,... | collective-permute-start | bytes 786440 | tf_op jit(solution)/shard_map/ppermute | solution.py:88
  76.9 36.8 %collective-permute-start.13 = (f32[64,1024]{1,0:T(8,128)S(1)}, f32[64,1024]{1,0:T(8,128)S(1)}, u32[]{:S(2)}, u32[]{:S(2)}) collective-permute-start(f32[64,1024]{1,0:T(8,128)S(1)} %get-tuple-element.16), channel_id=1, source_target_pairs={{0,4},{1,5},{2,6},{3,7},{4,0},{5,1},{6,2},{7,3},{8,12},{9,13},{10,... | collective-permute-start | bytes 786440 | tf_op jit(solution)/shard_map/ppermute | solution.py:88
  80.8 32.9 %collective-permute-start.14 = (f32[64,1024]{1,0:T(8,128)S(1)}, f32[64,1024]{1,0:T(8,128)S(1)}, u32[]{:S(2)}, u32[]{:S(2)}) collective-permute-start(f32[64,1024]{1,0:T(8,128)S(1)} %get-tuple-element.15), channel_id=1, source_target_pairs={{0,6},{1,7},{2,4},{3,5},{4,2},{5,3},{6,0},{7,1},{8,14},{9,15},{10,... | collective-permute-start | bytes 786440 | tf_op jit(solution)/shard_map/ppermute | solution.py:88
  98.1 16.7 %collective-permute-start.15 = (bf16[64,32,128]{2,1,0:T(8,128)(2,1)S(1)}, bf16[64,32,128]{2,1,0:T(8,128)(2,1)S(1)}, u32[]{:S(2)}, u32[]{:S(2)}) collective-permute-start(bf16[64,32,128]{2,1,0:T(8,128)(2,1)S(1)} %get-tuple-element.10), channel_id=1, source_target_pairs={{0,8},{8,0},{16,24},{24,16},{1,9},{9,1},{17,25},{25,17},{2,10},{10... | collective-permute-start | bytes 1572872 | tf_op jit(solution)/shard_map/ppermute | solution.py:120
  98.2 21.8 %collective-permute-start.16 = (bf16[64,32,128]{2,1,0:T(8,128)(2,1)S(1)}, bf16[64,32,128]{2,1,0:T(8,128)(2,1)S(1)}, u32[]{:S(2)}, u32[]{:S(2)}) collective-permute-start(bf16[64,32,128]{2,1,0:T(8,128)(2,1)S(1)} %get-tuple-element.9), channel_id=1, source_target_pairs={{0,16},{8,24},{16,0},{24,8},{1,17},{9,25},{17,1},{25,9},{2,18},{10... | collective-permute-start | bytes 1572872 | tf_op jit(solution)/shard_map/ppermute | solution.py:120
  100.2 21.4 %collective-permute-start.17 = (bf16[64,32,128]{2,1,0:T(8,128)(2,1)S(1)}, bf16[64,32,128]{2,1,0:T(8,128)(2,1)S(1)}, u32[]{:S(2)}, u32[]{:S(2)}) collective-permute-start(bf16[64,32,128]{2,1,0:T(8,128)(2,1)S(1)} %get-tuple-element.8), channel_id=1, source_target_pairs={{0,24},{8,16},{16,8},{24,0},{1,25},{9,17},{17,9},{25,1},{2,26},{10... | collective-permute-start | bytes 1572872 | tf_op jit(solution)/shard_map/ppermute | solution.py:120
  121.7 1.3 copy-start

commit v7 on v4

--- a/solution.py
+++ b/solution.py
@@ -9,6 +9,7 @@
 
 BLK = 128
 SLOTS_PER_STEP = 8
+F_CHUNKS = 2
 
 
 def xor_exchange(x, axis_name, n):
@@ -63,6 +64,45 @@
     )(rows, cols, count, acts_t, gout)
 
 
+def matmul_kernel(*refs):
+    if len(refs) == 4:
+        g_ref, w_ref, acc_ref, o_ref = refs
+    else:
+        (g_ref, w_ref, o_ref), acc_ref = refs, None
+    out = lax.dot_general(
+        g_ref[...], w_ref[...], (((1,), (1,)), ((), ())), preferred_element_type=jnp.float32
+    )
+    if acc_ref is not None:
+        out = out + acc_ref[...]
+    o_ref[...] = out
+
+
+def matmul_nt(g, w, acc):
+    rows, depth = g.shape
+    cols = w.shape[0]
+    tile = min(cols, 512)
+    in_specs = [
+        pl.BlockSpec((rows, depth), lambda j: (0, 0)),
+        pl.BlockSpec((tile, depth), lambda j: (j, 0)),
+    ]
+    args = [g, w]
+    if acc is not None:
+        in_specs.append(pl.BlockSpec((rows, tile), lambda j: (0, j)))
+        args.append(acc)
+    return pl.pallas_call(
+        matmul_kernel,
+        grid=(cols // tile,),
+        in_specs=in_specs,
+        out_specs=pl.BlockSpec((rows, tile), lambda j: (0, j)),
+        out_shape=jax.ShapeDtypeStruct((rows, cols), jnp.float32),
+        cost_estimate=pl.CostEstimate(
+            flops=2 * rows * depth * cols,
+            bytes_accessed=g.size * 2 + w.size * 2 + rows * cols * 4 * (2 if acc is not None else 1),
+            transcendentals=0,
+        ),
+    )(*args)
+
+
 def per_device(n_tok, acts, grad_out, weight, block_rows, block_cols, block_count):
     me = lax.axis_index("tok")
     tok_dev = acts.shape[0]
@@ -72,10 +112,19 @@
     row_blocks = full_acts.shape[1] // BLK
     acts_pieces = jnp.transpose(full_acts.reshape(tok_dev, row_blocks, n_tok, sub), (2, 1, 3, 0))
 
-    gout = place_rows(xor_exchange(grad_out, "tok", n_tok), me)
-    partial_sums = lax.dot_general(
-        gout, weight, (((1,), (1,)), ((), ())), preferred_element_type=jnp.float32
-    )
+    f_chunk = grad_out.shape[1] // F_CHUNKS
+    gathered = []
+    partial_sums = None
+    for k in range(F_CHUNKS):
+        cols = slice(k * f_chunk, (k + 1) * f_chunk)
+        piece = grad_out[:, cols]
+        if gathered:
+            piece, gathered[-1] = lax.optimization_barrier((piece, gathered[-1]))
+        gathered.append(place_rows(xor_exchange(piece, "tok", n_tok), me))
+    for k in range(F_CHUNKS):
+        cols = slice(k * f_chunk, (k + 1) * f_chunk)
+        partial_sums = matmul_nt(gathered[k], weight[:, cols], partial_sums)
+    gout = jnp.concatenate(gathered, axis=1)
     grad_in = lax.psum_scatter(partial_sums, "feat", scatter_dimension=0, tiled=True).astype(
         jnp.bfloat16
     )

time: 126 us -> 127 us (level)
  waiting for transfers between devices: 63.2 us -> 37.8 us
  Pallas kernels: 11 us -> 29.4 us
  local copies, waits for them, and re-layouts: 14.1 us -> 27.5 us
  matrix products: 12.4 us -> 0 us
  other arithmetic: 1.77 us -> 5.32 us
  starting transfers between devices: 8.11 us -> 11.6 us
    ppermute x3 -> x6, waiting for transfers between devices: 36.6 us -> 17 us  [xor_exchange(): out.append(lax.ppermute(x, axis_name, perm=[(a, a ^ m) for a in range(n)]))]
    pallas_call x0 -> x2, Pallas kernels: none -> 18.4 us  [matmul_nt(): pl.pallas_call(matmul_kernel, grid=(cols // tile,), in_specs=in_specs, ou...]
    dot_general x1 -> x0, matrix products: 12.4 us -> none  [per_device(): lax.dot_general(gout, weight, (((1,), (1,)), ((), ())), preferred_element...]
    slice x0 -> x2, local copies, waits for them, and re-layouts: none -> 11.3 us  [the longest x1 10.5 us: per_device(): partial_sums = matmul_nt(gathered[k], weight[:, cols], partial_sums)]
    concatenate x0 -> x1, other arithmetic: none -> 3.55 us  [per_device(): gout = jnp.concatenate(gathered, axis=1)]
    ppermute x3 -> x6, starting transfers between devices: 4.55 us -> 8.01 us  [xor_exchange(): out.append(lax.ppermute(x, axis_name, perm=[(a, a ^ m) for a in range(n)]))]
    ppermute x3, waiting for transfers between devices: 18.2 us -> 15.1 us  [per_device(): part = lax.ppermute(part, 'tok', perm=[(a, a ^ m) for a in range(n_tok)])]
    reduce_scatter x1, waiting for transfers between devices: 8.25 us -> 5.7 us  [per_device(): lax.psum_scatter(partial_sums, 'feat', scatter_dimension=0, tiled=True)]
  transfers between devices with their start and end apart: 8 -> 11, of which waited for: 5 -> 6; matrix products, arithmetic and copies ran while one was open for 19% -> 20% of each run, Pallas kernels for 9% -> 23%
where the time goes in v7:
time: 127 us; the launch traced here: 126 us
  waiting for transfers between devices  37.8 us (30%)
  Pallas kernels  29.4 us (23%)
  local copies, waits for them, and re-layouts  27.5 us (22%)
  between operations  14.9 us (12%)
  starting transfers between devices  11.6 us (9%)
  other arithmetic  5.32 us (4%)
    pallas_call x2, Pallas kernels, matmul_nt(): pl.pallas_call(matmul_kernel, grid=(cols // tile,), in_specs=in_specs, ou...  18.4 us
    ppermute x6, waiting for transfers between devices, xor_exchange(): out.append(lax.ppermute(x, axis_name, perm=[(a, a ^ m) for a in range(n)]))  17 us
    ppermute x3, waiting for transfers between devices, per_device(): part = lax.ppermute(part, 'tok', perm=[(a, a ^ m) for a in range(n_tok)])  15.1 us
    pallas_call x1, Pallas kernels, block_tiles(): pl.pallas_call(block_kernel, grid_spec=grid_spec, out_shape=jax.ShapeDtyp...  11 us
    slice x1, local copies, waits for them, and re-layouts, per_device(): partial_sums = matmul_nt(gathered[k], weight[:, cols], partial_sums)  10.5 us
    ppermute x6, starting transfers between devices, xor_exchange(): out.append(lax.ppermute(x, axis_name, perm=[(a, a ^ m) for a in range(n)]))  8.01 us
    dynamic_update_slice x11, local copies, waits for them, and re-layouts, place_rows(): out = lax.dynamic_update_slice_in_dim(out, piece, (me ^ m) * rows, axis)  6.99 us
    unnamed x13, local copies, waits for them, and re-layouts  5.94 us
  transfers between devices with their start and end apart: 11, of which 6 were waited for; matrix products, arithmetic and copies ran while one was open for 20% of the time, Pallas kernels for 23%

profile of v7, /device:TPU:0, one launch (start us, length us, event | category | flops | bytes accessed | tf_op | source)
XLA Modules:
  0.0 126.5 jit_solution(4286327233370358251)
XLA Ops:
  7.2 0.0 copy-start.4
  7.2 0.0 all-gather.2.cloned.1.call-start
  7.2 0.1 broadcast.3.clone
  7.4 1.0 copy-done.4
  8.3 0.9 fusion.1
  9.2 2.9 %collective-permute-start = (bf16[128,1792]{1,0:T(8,128)(2,1)}, bf16[128,1792]{1,0:T(8,128)(2,1)}, u32[]{:S(2)}, u32[]{:S(2)}) collective-permute-start(bf16[128,1792]{1,0:T(8,128)(2,1)} %get-tuple-element.15), channel_id=1, source_target_pairs={{0,8},{8,0},{16,24},{24,16},{1,9},{9,1},{17,25},{25,17},{2,10},{10... | collective-permute-start | bytes 1376264 | tf_op jit(solution)/shard_map/ppermute | solution.py:18
  12.1 1.5 %collective-permute-start.1 = (bf16[128,1792]{1,0:T(8,128)(2,1)}, bf16[128,1792]{1,0:T(8,128)(2,1)S(1)}, u32[]{:S(2)}, u32[]{:S(2)}) collective-permute-start(bf16[128,1792]{1,0:T(8,128)(2,1)} %get-tuple-element.15), channel_id=1, source_target_pairs={{0,16},{8,24},{16,0},{24,8},{1,17},{9,25},{17,1},{25,9},{2,18},{10... | collective-permute-start | bytes 1376264 | tf_op jit(solution)/shard_map/ppermute | solution.py:18
  13.7 0.0 collective-permute-start.2
  13.7 0.8 copy.9
  14.5 0.0 all-gather.2.cloned.1.call-update
  14.5 0.0 reduce-scatter.2.cloned.1.call-start
  14.6 10.5 %fusion = (bf16[2048,1792]{1,0:T(8,128)(2,1)}, bf16[2048,1792]{1,0:T(8,128)(2,1)}) fusion(bf16[2048,3584]{1,0:T(8,128)(2,1)} %param.8), kind=kLoop, calls=%fused_computation.16 | loop fusion | bytes 29360128 | tf_op jit(solution)/shard_map/slice | solution.py:126
  25.0 0.0 collective-permute-done
  25.0 1.1 constant_dynamic-update-slice_fusion.9
  26.1 8.1 %collective-permute-done.1 = bf16[128,1792]{1,0:T(8,128)(2,1)S(1)} collective-permute-done((bf16[128,1792]{1,0:T(8,128)(2,1)}, bf16[128,1792]{1,0:T(8,128)(2,1)S(1)}, u32[]{:S(2)}, u32[]{:S(2)}) %collective-permute-start.1) | collective-permute-done | bytes 458784 | tf_op jit(solution)/shard_map/ppermute | solution.py:18
  34.2 0.0 collective-permute-done.2
  34.3 0.0 copy-start.3
  34.3 1.2 collective-permute-start.3
  35.5 0.9 collective-permute-start.4
  36.4 1.4 %collective-permute-start.5 = (bf16[128,1792]{1,0:T(8,128)(2,1)S(1)}, bf16[128,1792]{1,0:T(8,128)(2,1)S(1)}, u32[]{:S(2)}, u32[]{:S(2)}) collective-permute-start(bf16[128,1792]{1,0:T(8,128)(2,1)S(1)} %get-tuple-element.6), channel_id=1, source_target_pairs={{0,24},{8,16},{16,8},{24,0},{1,25},{9,17},{17,9},{25,1},{2,26},{10... | collective-permute-start | bytes 1376264 | tf_op jit(solution)/shard_map/ppermute | solution.py:18
  37.8 0.0 copy-done.3
  37.8 8.6 %shard_map.77.refs_2_ = f32[512,2048]{1,0:T(8,128)} custom-call(bf16[512,1792]{1,0:T(8,128)(2,1)} %copy-done.3, bf16[2048,1792]{1,0:T(8,128)(2,1)} %get-tuple-element.10.refs_1_), custom_call_target="tpu_custom_call" | custom-call | flops 3758096384 | bytes 13369344 | tf_op jit(solution)/shard_map/pallas_call | solution.py:92
  46.4 0.1 broadcast.3
  46.5 1.3 %collective-permute-done.3 = bf16[128,1792]{1,0:T(8,128)(2,1)} collective-permute-done((bf16[128,1792]{1,0:T(8,128)(2,1)S(1)}, bf16[128,1792]{1,0:T(8,128)(2,1)}, u32[]{:S(2)}, u32[]{:S(2)}) %collective-permute-start.3) | collective-permute-done | bytes 458784 | tf_op jit(solution)/shard_map/ppermute | solution.py:18
  47.9 1.0 constant_dynamic-update-slice_fusion.5
  48.9 7.6 %collective-permute-done.4 = bf16[128,1792]{1,0:T(8,128)(2,1)S(1)} collective-permute-done((bf16[128,1792]{1,0:T(8,128)(2,1)S(1)}, bf16[128,1792]{1,0:T(8,128)(2,1)S(1)}, u32[]{:S(2)}, u32[]{:S(2)}) %collective-permute-start.4) | collective-permute-done | bytes 458784 | tf_op jit(solution)/shard_map/ppermute | solution.py:18
  56.6 0.0 collective-permute-done.5
  56.7 1.3 %copy-done = bf16[512,1792]{1,0:T(8,128)(2,1)} copy-done((bf16[512,1792]{1,0:T(8,128)(2,1)}, bf16[512,1792]{1,0:T(8,128)(2,1)S(1)}, u32[]{:S(2)}) %copy-start) | copy-done | bytes 1835032
  58.0 9.8 %shard_map.78 = f32[512,2048]{1,0:T(8,128)} custom-call(bf16[512,1792]{1,0:T(8,128)(2,1)} %copy-done, bf16[2048,1792]{1,0:T(8,128)(2,1)} %get-tuple-element.11.refs_1_, f32[512,2048]{1,0:T(8,128)} %shard_map.77.refs_2_), custom_call_target="tpu_custom_call" | custom-call | flops 3758096384 | bytes 17563648 | tf_op jit(solution)/shard_map/pallas_call | solution.py:92
  67.8 0.0 reduce-scatter.2.cloned.1.call-update
  67.9 1.4 %copy-done.1 = bf16[512,1792]{1,0:T(8,128)(2,1)S(1)} copy-done((bf16[512,1792]{1,0:T(8,128)(2,1)S(1)}, bf16[512,1792]{1,0:T(8,128)(2,1)}, u32[]{:S(2)}) %copy-start.1) | copy-done | bytes 1835032
  69.3 3.6 %pad_maximum_fusion.g_ref = bf16[512,3584]{1,0:T(8,128)(2,1)} fusion(bf16[512,1792]{1,0:T(8,128)(2,1)S(1)} %copy-done.1, bf16[512,1792]{1,0:T(8,128)(2,1)} %copy-done.3), kind=kLoop, calls=%fused_computation | loop fusion | flops 7340032 | bytes 7340032 | tf_op jit(solution)/shard_map/concatenate | solution.py:127
  72.9 2.7 %dynamic-slice_bitcast_fusion = (bf16[64,32,128]{2,1,0:T(8,128)(2,1)S(1)}, bf16[64,32,128]{2,1,0:T(8,128)(2,1)S(1)}, bf16[64,32,128]{2,1,0:T(8,128)(2,1)}) fusion(bf16[4,64,32,128]{3,2,0,1:T(8,128)(2,1)} %bitcast.11, s32[]{:T(128)S(6)} %select_n.40, s32[]{:T(128)S(6)} %select_n.39, s32[]{:T(128)S(6)} %select_n.38), kind=kLoop, calls=%fused_computation.2 | loop fusion | bytes 3145740 | tf_op jit(solution)/shard_map/jit(dynamic_index_in_dim)/squeeze | solution.py:135
  75.6 0.3 collective-permute-start.6
  75.9 1.1 collective-permute-start.7
  77.0 2.1 %collective-permute-start.8 = (bf16[64,32,128]{2,1,0:T(8,128)(2,1)S(1)}, bf16[64,32,128]{2,1,0:T(8,128)(2,1)}, u32[]{:S(2)}, u32[]{:S(2)}) collective-permute-start(bf16[64,32,128]{2,1,0:T(8,128)(2,1)S(1)} %get-tuple-element.12), channel_id=1, source_target_pairs={{0,24},{8,16},{16,8},{24,0},{1,25},{9,17},{17,9},{25,1},{2,26},{10... | collective-permute-start | bytes 1572872 | tf_op jit(solution)/shard_map/ppermute | solution.py:137
  79.8 0.2 broadcast_in_dim.3
  80.0 1.2 bitcast_dynamic-update-slice_fusion
  81.2 9.6 %collective-permute-done.6 = bf16[64,32,128]{2,1,0:T(8,128)(2,1)} collective-permute-done((bf16[64,32,128]{2,1,0:T(8,128)(2,1)}, bf16[64,32,128]{2,1,0:T(8,128)(2,1)}, u32[]{:S(2)}, u32[]{:S(2)}) %collective-permute-start.6) | collective-permute-done | bytes 524320 | tf_op jit(solution)/shard_map/ppermute | solution.py:137
  90.8 1.2 constant_dynamic-update-slice_fusion.1
  92.0 5.5 %collective-permute-done.7 = bf16[64,32,128]{2,1,0:T(8,128)(2,1)} collective-permute-done((bf16[64,32,128]{2,1,0:T(8,128)(2,1)S(1)}, bf16[64,32,128]{2,1,0:T(8,128)(2,1)}, u32[]{:S(2)}, u32[]{:S(2)}) %collective-permute-start.7) | collective-permute-done | bytes 524320 | tf_op jit(solution)/shard_map/ppermute | solution.py:137
  97.4 1.2 constant_dynamic-update-slice_fusion
  98.6 0.0 collective-permute-done.8
  98.6 1.2 constant_dynamic-update-slice_fusion.2.a_ref
  99.8 1.3 %copy-done.2 = bf16[64,32,512]{2,1,0:T(8,128)(2,1)} copy-done((bf16[64,32,512]{2,1,0:T(8,128)(2,1)}, bf16[64,32,512]{2,1,0:T(8,128)(2,1)S(1)}, u32[]{:S(2)}) %copy-start.2) | copy-done | bytes 2097176
  101.2 11.0 %shard_map.79 = bf16[128,32,128]{2,1,0:T(8,128)(2,1)} custom-call(s32[128]{0:T(128)} %rows_ref.1, s32[128]{0:T(128)} %cols_ref.1, s32[1]{0:T(128)S(6)} %copy.22.cnt_ref, bf16[64,32,512]{2,1,0:T(8,128)(2,1)} %copy-done.2, bf16[512,3584]{1,0:T(8,128)(2,1)} %pad_maximum_fusion.g_ref), custom_call_target="tpu_custom_call" | custom-call | flops 536870912 | bytes 6815744 | tf_op jit(solution)/shard_map/pallas_call | solution.py:55
  112.1 5.7 %reduce-scatter.2.cloned.1.call-done = f32[64,2048]{1,0:T(8,128)} async-done(((f32[512,2048]{1,0:T(8,128)}), f32[64,2048]{1,0:T(8,128)}) %reduce-scatter.2.cloned.1.call-update) | async-done | bytes 524304 | tf_op jit(solution)/shard_map/reduce_scatter | solution.py:128
  117.8 1.8 %convert_element_type.3 = bf16[64,2048]{1,0:T(8,128)(2,1)} convert(f32[64,2048]{1,0:T(8,128)} %reduce-scatter.2.cloned.1.call-done) | non-fusion elementwise | flops 131072 | bytes 786432 | tf_op jit(solution)/shard_map/convert_element_type | solution.py:128
  (11 shorter events, 0.2 us)
Async XLA Ops:
  7.2 1.2 copy-start.4
  7.2 6.5 %copy-start.5 = (bf16[128,1024]{1,0:T(8,128)(2,1)S(1)}, bf16[128,1024]{1,0:T(8,128)(2,1)}, u32[]{:S(2)}) copy-start(bf16[128,1024]{1,0:T(8,128)(2,1)} %param.6) | copy-start | bytes 786436
  7.2 65.7 %all-gather.2.cloned.1.call-start = ((), (), s32[]{:S(2)}) async-start(), calls=%async_computation.2 | async-start | bytes 2359296 | tf_op jit(solution)/shard_map/all_gather | solution.py:111
  9.2 15.8 %collective-permute-start = (bf16[128,1792]{1,0:T(8,128)(2,1)}, bf16[128,1792]{1,0:T(8,128)(2,1)}, u32[]{:S(2)}, u32[]{:S(2)}) collective-permute-start(bf16[128,1792]{1,0:T(8,128)(2,1)} %get-tuple-element.15), channel_id=1, source_target_pairs={{0,8},{8,0},{16,24},{24,16},{1,9},{9,1},{17,25},{25,17},{2,10},{10... | collective-permute-start | bytes 1376264 | tf_op jit(solution)/shard_map/ppermute | solution.py:18
  12.1 22.0 %collective-permute-start.1 = (bf16[128,1792]{1,0:T(8,128)(2,1)}, bf16[128,1792]{1,0:T(8,128)(2,1)S(1)}, u32[]{:S(2)}, u32[]{:S(2)}) collective-permute-start(bf16[128,1792]{1,0:T(8,128)(2,1)} %get-tuple-element.15), channel_id=1, source_target_pairs={{0,16},{8,24},{16,0},{24,8},{1,17},{9,25},{17,1},{25,9},{2,18},{10... | collective-permute-start | bytes 1376264 | tf_op jit(solution)/shard_map/ppermute | solution.py:18
  13.7 20.5 %collective-permute-start.2 = (bf16[128,1792]{1,0:T(8,128)(2,1)}, bf16[128,1792]{1,0:T(8,128)(2,1)S(1)}, u32[]{:S(2)}, u32[]{:S(2)}) collective-permute-start(bf16[128,1792]{1,0:T(8,128)(2,1)} %get-tuple-element.15), channel_id=1, source_target_pairs={{0,24},{8,16},{16,8},{24,0},{1,25},{9,17},{17,9},{25,1},{2,26},{10... | collective-permute-start | bytes 1376264 | tf_op jit(solution)/shard_map/ppermute | solution.py:18
  14.5 103.3 %reduce-scatter.2.cloned.1.call-start = ((), (), s32[]{:S(2)}) async-start(), calls=%async_computation.1 | async-start | bytes 4718592 | tf_op jit(solution)/shard_map/reduce_scatter | solution.py:128
  34.3 3.6 %copy-start.3 = (bf16[512,1792]{1,0:T(8,128)(2,1)}, bf16[512,1792]{1,0:T(8,128)(2,1)S(1)}, u32[]{:S(2)}) copy-start(bf16[512,1792]{1,0:T(8,128)(2,1)S(1)} %constant_dynamic-update-slice_fusion.7.refs_0_) | copy-start | bytes 5505028
  34.3 13.6 %collective-permute-start.3 = (bf16[128,1792]{1,0:T(8,128)(2,1)S(1)}, bf16[128,1792]{1,0:T(8,128)(2,1)}, u32[]{:S(2)}, u32[]{:S(2)}) collective-permute-start(bf16[128,1792]{1,0:T(8,128)(2,1)S(1)} %get-tuple-element.6), channel_id=1, source_target_pairs={{0,8},{8,0},{16,24},{24,16},{1,9},{9,1},{17,25},{25,17},{2,10},{10... | collective-permute-start | bytes 1376264 | tf_op jit(solution)/shard_map/ppermute | solution.py:18
  35.5 21.0 %collective-permute-start.4 = (bf16[128,1792]{1,0:T(8,128)(2,1)S(1)}, bf16[128,1792]{1,0:T(8,128)(2,1)S(1)}, u32[]{:S(2)}, u32[]{:S(2)}) collective-permute-start(bf16[128,1792]{1,0:T(8,128)(2,1)S(1)} %get-tuple-element.6), channel_id=1, source_target_pairs={{0,16},{8,24},{16,0},{24,8},{1,17},{9,25},{17,1},{25,9},{2,18},{10... | collective-permute-start | bytes 1376264 | tf_op jit(solution)/shard_map/ppermute | solution.py:18
  36.4 20.2 %collective-permute-start.5 = (bf16[128,1792]{1,0:T(8,128)(2,1)S(1)}, bf16[128,1792]{1,0:T(8,128)(2,1)S(1)}, u32[]{:S(2)}, u32[]{:S(2)}) collective-permute-start(bf16[128,1792]{1,0:T(8,128)(2,1)S(1)} %get-tuple-element.6), channel_id=1, source_target_pairs={{0,24},{8,16},{16,8},{24,0},{1,25},{9,17},{17,9},{25,1},{2,26},{10... | collective-permute-start | bytes 1376264 | tf_op jit(solution)/shard_map/ppermute | solution.py:18
  56.6 1.3 %copy-start = (bf16[512,1792]{1,0:T(8,128)(2,1)}, bf16[512,1792]{1,0:T(8,128)(2,1)S(1)}, u32[]{:S(2)}) copy-start(bf16[512,1792]{1,0:T(8,128)(2,1)S(1)} %constant_dynamic-update-slice_fusion.3.refs_0_) | copy-start | bytes 5505028
  67.8 1.5 %copy-start.1 = (bf16[512,1792]{1,0:T(8,128)(2,1)S(1)}, bf16[512,1792]{1,0:T(8,128)(2,1)}, u32[]{:S(2)}) copy-start(bf16[512,1792]{1,0:T(8,128)(2,1)} %copy-done) | copy-start | bytes 5505028
  75.6 15.2 %collective-permute-start.6 = (bf16[64,32,128]{2,1,0:T(8,128)(2,1)}, bf16[64,32,128]{2,1,0:T(8,128)(2,1)}, u32[]{:S(2)}, u32[]{:S(2)}) collective-permute-start(bf16[64,32,128]{2,1,0:T(8,128)(2,1)} %get-tuple-element.14), channel_id=1, source_target_pairs={{0,8},{8,0},{16,24},{24,16},{1,9},{9,1},{17,25},{25,17},{2,10},{10... | collective-permute-start | bytes 1572872 | tf_op jit(solution)/shard_map/ppermute | solution.py:137
  75.9 21.6 %collective-permute-start.7 = (bf16[64,32,128]{2,1,0:T(8,128)(2,1)S(1)}, bf16[64,32,128]{2,1,0:T(8,128)(2,1)}, u32[]{:S(2)}, u32[]{:S(2)}) collective-permute-start(bf16[64,32,128]{2,1,0:T(8,128)(2,1)S(1)} %get-tuple-element.13), channel_id=1, source_target_pairs={{0,16},{8,24},{16,0},{24,8},{1,17},{9,25},{17,1},{25,9},{2,18},{10... | collective-permute-start | bytes 1572872 | tf_op jit(solution)/shard_map/ppermute | solution.py:137
  77.0 21.6 %collective-permute-start.8 = (bf16[64,32,128]{2,1,0:T(8,128)(2,1)S(1)}, bf16[64,32,128]{2,1,0:T(8,128)(2,1)}, u32[]{:S(2)}, u32[]{:S(2)}) collective-permute-start(bf16[64,32,128]{2,1,0:T(8,128)(2,1)S(1)} %get-tuple-element.12), channel_id=1, source_target_pairs={{0,24},{8,16},{16,8},{24,0},{1,25},{9,17},{17,9},{25,1},{2,26},{10... | collective-permute-start | bytes 1572872 | tf_op jit(solution)/shard_map/ppermute | solution.py:137
  99.8 1.4 %copy-start.2 = (bf16[64,32,512]{2,1,0:T(8,128)(2,1)}, bf16[64,32,512]{2,1,0:T(8,128)(2,1)S(1)}, u32[]{:S(2)}) copy-start(bf16[64,32,512]{2,1,0:T(8,128)(2,1)S(1)} %constant_dynamic-update-slice_fusion.2.a_ref) | copy-start | bytes 6291460
Sparse Core Ops, SparseCore 0:
  14.7 30.8 all-gather.1
  68.0 49.8 reduce-scatter.1

commit v8 on v7

--- a/solution.py
+++ b/solution.py
@@ -66,38 +66,38 @@
 
 def matmul_kernel(*refs):
     if len(refs) == 4:
-        g_ref, w_ref, acc_ref, o_ref = refs
+        w_ref, g_ref, acc_ref, o_ref = refs
     else:
-        (g_ref, w_ref, o_ref), acc_ref = refs, None
-    out = lax.dot_general(
-        g_ref[...], w_ref[...], (((1,), (1,)), ((), ())), preferred_element_type=jnp.float32
-    )
+        (w_ref, g_ref, o_ref), acc_ref = refs, None
+    out = jnp.dot(w_ref[...], g_ref[...], preferred_element_type=jnp.float32)
     if acc_ref is not None:
         out = out + acc_ref[...]
     o_ref[...] = out
 
 
-def matmul_nt(g, w, acc):
-    rows, depth = g.shape
-    cols = w.shape[0]
-    tile = min(cols, 512)
+def matmul_wg(w, g_t, k, acc):
+    depth, tokens = g_t.shape
+    rows = w.shape[0]
+    tile = min(rows, 512)
     in_specs = [
-        pl.BlockSpec((rows, depth), lambda j: (0, 0)),
-        pl.BlockSpec((tile, depth), lambda j: (j, 0)),
+        pl.BlockSpec((tile, depth), lambda j: (j, k)),
+        pl.BlockSpec((depth, tokens), lambda j: (0, 0)),
     ]
-    args = [g, w]
+    args = [w, g_t]
     if acc is not None:
-        in_specs.append(pl.BlockSpec((rows, tile), lambda j: (0, j)))
+        in_specs.append(pl.BlockSpec((tile, tokens), lambda j: (j, 0)))
         args.append(acc)
     return pl.pallas_call(
         matmul_kernel,
-        grid=(cols // tile,),
+        grid=(rows // tile,),
         in_specs=in_specs,
-        out_specs=pl.BlockSpec((rows, tile), lambda j: (0, j)),
-        out_shape=jax.ShapeDtypeStruct((rows, cols), jnp.float32),
+        out_specs=pl.BlockSpec((tile, tokens), lambda j: (j, 0)),
+        out_shape=jax.ShapeDtypeStruct((rows, tokens), jnp.float32),
         cost_estimate=pl.CostEstimate(
-            flops=2 * rows * depth * cols,
-            bytes_accessed=g.size * 2 + w.size * 2 + rows * cols * 4 * (2 if acc is not None else 1),
+            flops=2 * rows * depth * tokens,
+            bytes_accessed=rows * depth * 2
+            + g_t.size * 2
+            + rows * tokens * 4 * (2 if acc is not None else 1),
             transcendentals=0,
         ),
     )(*args)
@@ -114,18 +114,16 @@
 
     f_chunk = grad_out.shape[1] // F_CHUNKS
     gathered = []
-    partial_sums = None
     for k in range(F_CHUNKS):
-        cols = slice(k * f_chunk, (k + 1) * f_chunk)
-        piece = grad_out[:, cols]
+        piece = grad_out[:, k * f_chunk : (k + 1) * f_chunk]
         if gathered:
             piece, gathered[-1] = lax.optimization_barrier((piece, gathered[-1]))
         gathered.append(place_rows(xor_exchange(piece, "tok", n_tok), me))
+    partial_t = None
     for k in range(F_CHUNKS):
-        cols = slice(k * f_chunk, (k + 1) * f_chunk)
-        partial_sums = matmul_nt(gathered[k], weight[:, cols], partial_sums)
+        partial_t = matmul_wg(weight, gathered[k].T, k, partial_t)
     gout = jnp.concatenate(gathered, axis=1)
-    grad_in = lax.psum_scatter(partial_sums, "feat", scatter_dimension=0, tiled=True).astype(
+    grad_in = lax.psum_scatter(partial_t, "feat", scatter_dimension=1, tiled=True).T.astype(
         jnp.bfloat16
     )
 

time: 127 us -> 137 us (1.079)
  waiting for transfers between devices: 37.8 us -> 45.5 us
  local copies, waits for them, and re-layouts: 27.5 us -> 32.2 us
  other arithmetic: 5.32 us -> 3.54 us
    slice x2 -> x1, local copies, waits for them, and re-layouts: 11.3 us -> 0.86 us  [per_device(): piece = grad_out[:, k * f_chunk:(k + 1) * f_chunk]]
    unnamed x2 -> x3, waiting for transfers between devices: 0.03 us -> 7.5 us
    ppermute x6, waiting for transfers between devices: 17 us -> 23.3 us  [xor_exchange(): out.append(lax.ppermute(x, axis_name, perm=[(a, a ^ m) for a in range(n)]))]
    transpose x0 -> x2, local copies, waits for them, and re-layouts: none -> 6.17 us  [per_device(): partial_t = matmul_wg(weight, gathered[k].T, k, partial_t)]
    reduce_scatter x1 -> x0, waiting for transfers between devices: 5.7 us -> none  [per_device(): lax.psum_scatter(partial_sums, 'feat', scatter_dimension=0, tiled=True)]
    unnamed x13 -> x8, local copies, waits for them, and re-layouts: 5.94 us -> 10.9 us
    dynamic_update_slice x11, local copies, waits for them, and re-layouts: 6.99 us -> 10.1 us  [place_rows(): out = lax.dynamic_update_slice_in_dim(out, piece, (me ^ m) * rows, axis)]
    convert_element_type x1 -> x0, other arithmetic: 1.77 us -> none  [per_device(): lax.psum_scatter(partial_sums, 'feat', scatter_dimension=0, tiled=True)]
  transfers between devices with their start and end apart: 11 -> 11, of which waited for: 6 -> 6; matrix products, arithmetic and copies ran while one was open for 20% -> 22% of each run, Pallas kernels for 23% -> 21%
where the time goes in v8:
time: 137 us; the launch traced here: 136 us
  waiting for transfers between devices  45.5 us (33%)
  local copies, waits for them, and re-layouts  32.2 us (24%)
  Pallas kernels  28.6 us (21%)
  between operations  14.8 us (11%)
  starting transfers between devices  11.6 us (8%)
  other arithmetic  3.54 us (3%)
    ppermute x6, waiting for transfers between devices, xor_exchange(): out.append(lax.ppermute(x, axis_name, perm=[(a, a ^ m) for a in range(n)]))  23.3 us
    pallas_call x2, Pallas kernels, matmul_wg(): pl.pallas_call(matmul_kernel, grid=(rows // tile,), in_specs=in_specs, ou...  17.6 us
    ppermute x3, waiting for transfers between devices, per_device(): part = lax.ppermute(part, 'tok', perm=[(a, a ^ m) for a in range(n_tok)])  14.6 us
    pallas_call x1, Pallas kernels, block_tiles(): pl.pallas_call(block_kernel, grid_spec=grid_spec, out_shape=jax.ShapeDtyp...  11 us
    unnamed x8, local copies, waits for them, and re-layouts  10.9 us
    dynamic_update_slice x11, local copies, waits for them, and re-layouts, place_rows(): out = lax.dynamic_update_slice_in_dim(out, piece, (me ^ m) * rows, axis)  10.1 us
    ppermute x6, starting transfers between devices, xor_exchange(): out.append(lax.ppermute(x, axis_name, perm=[(a, a ^ m) for a in range(n)]))  8.01 us
    unnamed x3, waiting for transfers between devices  7.5 us
  transfers between devices with their start and end apart: 11, of which 6 were waited for; matrix products, arithmetic and copies ran while one was open for 22% of the time, Pallas kernels for 21%

profile of v8, /device:TPU:0, one launch (start us, length us, event | category | flops | bytes accessed | tf_op | source)
XLA Modules:
  0.0 136.3 jit_solution(11955068931465098308)
XLA Ops:
  7.2 0.0 all-gather.2.cloned.1.call-start
  7.2 1.9 %copy.18 = bf16[128,1024]{0,1:T(8,128)(2,1)} copy(bf16[128,1024]{1,0:T(8,128)(2,1)} %param.6) | data formatting | bytes 524288 | tf_op args[0]
  9.1 0.0 all-gather.2.cloned.1.call-update
  9.1 0.0 reduce-scatter.4.cloned.1.call-start
  9.2 0.1 broadcast.3.clone
  9.3 0.9 fusion
  10.2 2.9 %collective-permute-start = (bf16[128,1792]{1,0:T(8,128)(2,1)}, bf16[128,1792]{1,0:T(8,128)(2,1)}, u32[]{:S(2)}, u32[]{:S(2)}) collective-permute-start(bf16[128,1792]{1,0:T(8,128)(2,1)} %get-tuple-element.19), channel_id=1, source_target_pairs={{0,8},{8,0},{16,24},{24,16},{1,9},{9,1},{17,25},{25,17},{2,10},{10... | collective-permute-start | bytes 1376264 | tf_op jit(solution)/shard_map/ppermute | solution.py:18
  13.1 1.5 %collective-permute-start.1 = (bf16[128,1792]{1,0:T(8,128)(2,1)}, bf16[128,1792]{1,0:T(8,128)(2,1)S(1)}, u32[]{:S(2)}, u32[]{:S(2)}) collective-permute-start(bf16[128,1792]{1,0:T(8,128)(2,1)} %get-tuple-element.19), channel_id=1, source_target_pairs={{0,16},{8,24},{16,0},{24,8},{1,17},{9,25},{17,1},{25,9},{2,18},{10... | collective-permute-start | bytes 1376264 | tf_op jit(solution)/shard_map/ppermute | solution.py:18
  14.6 0.0 collective-permute-start.2
  14.6 10.1 %collective-permute-done = bf16[128,1792]{1,0:T(8,128)(2,1)} collective-permute-done((bf16[128,1792]{1,0:T(8,128)(2,1)}, bf16[128,1792]{1,0:T(8,128)(2,1)}, u32[]{:S(2)}, u32[]{:S(2)}) %collective-permute-start) | collective-permute-done | bytes 458784 | tf_op jit(solution)/shard_map/ppermute | solution.py:18
  24.8 1.1 constant_dynamic-update-slice_fusion.9
  25.8 9.3 %collective-permute-done.1 = bf16[128,1792]{1,0:T(8,128)(2,1)S(1)} collective-permute-done((bf16[128,1792]{1,0:T(8,128)(2,1)}, bf16[128,1792]{1,0:T(8,128)(2,1)S(1)}, u32[]{:S(2)}, u32[]{:S(2)}) %collective-permute-start.1) | collective-permute-done | bytes 458784 | tf_op jit(solution)/shard_map/ppermute | solution.py:18
  35.2 0.0 collective-permute-done.2
  35.2 1.2 collective-permute-start.3
  36.5 0.9 collective-permute-start.4
  37.3 1.4 %collective-permute-start.5 = (bf16[128,1792]{1,0:T(8,128)(2,1)S(1)}, bf16[128,1792]{1,0:T(8,128)(2,1)S(1)}, u32[]{:S(2)}, u32[]{:S(2)}) collective-permute-start(bf16[128,1792]{1,0:T(8,128)(2,1)S(1)} %get-tuple-element.6), channel_id=1, source_target_pairs={{0,24},{8,16},{16,8},{24,0},{1,25},{9,17},{17,9},{25,1},{2,26},{10... | collective-permute-start | bytes 1376264 | tf_op jit(solution)/shard_map/ppermute | solution.py:18
  38.8 2.3 %copy.16.refs_1_ = bf16[1792,512]{1,0:T(8,128)(2,1)} copy(bf16[1792,512]{0,1:T(8,128)(2,1)S(1)} %bitcast.19) | data formatting | bytes 3670016 | tf_op jit(solution)/shard_map/transpose | solution.py:124
  41.1 8.4 %shard_map.77.refs_2_ = f32[2048,512]{1,0:T(8,128)} custom-call(bf16[2048,3584]{1,0:T(8,128)(2,1)} %refs_0_.3, bf16[1792,512]{1,0:T(8,128)(2,1)} %copy.16.refs_1_), custom_call_target="tpu_custom_call" | custom-call | flops 3758096384 | bytes 13369344 | tf_op jit(solution)/shard_map/pallas_call | solution.py:90
  49.5 1.4 %broadcast.3 = bf16[512,1792]{1,0:T(8,128)(2,1)} broadcast(bf16[]{:T(256)} %constant.10.clone.1), dimensions={} | broadcast | bytes 1835010 | tf_op jit(solution)/shard_map/broadcast.1
  50.9 0.8 constant_dynamic-update-slice_fusion.6
  51.7 0.0 collective-permute-done.3
  51.7 1.9 %constant_dynamic-update-slice_fusion.5 = bf16[512,1792]{1,0:T(8,128)(2,1)} fusion(bf16[512,1792]{1,0:T(8,128)(2,1)} %constant_dynamic-update-slice_fusion.6, bf16[128,1792]{1,0:T(8,128)(2,1)} %collective-permute-done.3, s32[]{:T(128)S(6)} %select_n.34), kind=kLoop, calls=%fused_computation.11 | loop fusion | bytes 917508 | tf_op jit(solution)/shard_map/dynamic_update_slice | solution.py:28
  53.6 3.9 %collective-permute-done.4 = bf16[128,1792]{1,0:T(8,128)(2,1)S(1)} collective-permute-done((bf16[128,1792]{1,0:T(8,128)(2,1)S(1)}, bf16[128,1792]{1,0:T(8,128)(2,1)S(1)}, u32[]{:S(2)}, u32[]{:S(2)}) %collective-permute-start.4) | collective-permute-done | bytes 458784 | tf_op jit(solution)/shard_map/ppermute | solution.py:18
  57.5 0.8 constant_dynamic-update-slice_fusion.4
  58.3 0.0 collective-permute-done.5
  58.3 0.8 constant_dynamic-update-slice_fusion.3
  59.1 3.8 %copy.17.refs_1_ = bf16[1792,512]{1,0:T(8,128)(2,1)} copy(bf16[1792,512]{0,1:T(8,128)(2,1)} %bitcast.2) | data formatting | bytes 3670016 | tf_op jit(solution)/shard_map/transpose | solution.py:124
  63.0 9.2 %shard_map.78 = f32[2048,512]{1,0:T(8,128)} custom-call(bf16[2048,3584]{1,0:T(8,128)(2,1)} %refs_0_.3, bf16[1792,512]{1,0:T(8,128)(2,1)} %copy.17.refs_1_, f32[2048,512]{1,0:T(8,128)} %shard_map.77.refs_2_), custom_call_target="tpu_custom_call" | custom-call | flops 3758096384 | bytes 17563648 | tf_op jit(solution)/shard_map/pallas_call | solution.py:90
  72.2 5.4 %copy.20 = f32[2048,512]{0,1:T(8,128)} copy(f32[2048,512]{1,0:T(8,128)} %shard_map.78) | data formatting | bytes 8388608
  77.6 0.0 reduce-scatter.4.cloned.1.call-update
  77.6 3.5 %pad_maximum_fusion.g_ref = bf16[512,3584]{1,0:T(8,128)(2,1)} fusion(bf16[512,1792]{1,0:T(8,128)(2,1)} %constant_dynamic-update-slice_fusion.3, bf16[512,1792]{1,0:T(8,128)(2,1)S(1)} %constant_dynamic-update-slice_fusion.7), kind=kLoop, calls=%fused_computation | loop fusion | flops 7340032 | bytes 7340032 | tf_op jit(solution)/shard_map/concatenate | solution.py:125
  81.2 2.4 %dynamic-slice_bitcast_fusion = (bf16[64,32,128]{2,1,0:T(8,128)(2,1)S(1)}, bf16[64,32,128]{2,1,0:T(8,128)(2,1)S(1)}, bf16[64,32,128]{2,1,0:T(8,128)(2,1)}) fusion(bf16[4,64,32,128]{3,2,0,1:T(8,128)(2,1)} %bitcast.20, s32[]{:T(128)S(6)} %select_n.40, s32[]{:T(128)S(6)} %select_n.39, s32[]{:T(128)S(6)} %select_n.38), kind=kLoop, calls=%fused_computation.2 | loop fusion | bytes 3145740 | tf_op jit(solution)/shard_map/jit(dynamic_index_in_dim)/squeeze | solution.py:133
  83.6 0.6 collective-permute-start.6
  84.2 0.4 collective-permute-start.7
  84.6 2.5 %collective-permute-start.8 = (bf16[64,32,128]{2,1,0:T(8,128)(2,1)S(1)}, bf16[64,32,128]{2,1,0:T(8,128)(2,1)}, u32[]{:S(2)}, u32[]{:S(2)}) collective-permute-start(bf16[64,32,128]{2,1,0:T(8,128)(2,1)S(1)} %get-tuple-element.16), channel_id=1, source_target_pairs={{0,24},{8,16},{16,8},{24,0},{1,25},{9,17},{17,9},{25,1},{2,26},{10... | collective-permute-start | bytes 1572872 | tf_op jit(solution)/shard_map/ppermute | solution.py:135
  87.8 0.2 broadcast_in_dim.3
  88.0 1.2 bitcast_dynamic-update-slice_fusion
  89.2 9.6 %collective-permute-done.6 = bf16[64,32,128]{2,1,0:T(8,128)(2,1)} collective-permute-done((bf16[64,32,128]{2,1,0:T(8,128)(2,1)}, bf16[64,32,128]{2,1,0:T(8,128)(2,1)}, u32[]{:S(2)}, u32[]{:S(2)}) %collective-permute-start.6) | collective-permute-done | bytes 524320 | tf_op jit(solution)/shard_map/ppermute | solution.py:135
  98.8 1.2 constant_dynamic-update-slice_fusion.1
  100.0 5.0 %collective-permute-done.7 = bf16[64,32,128]{2,1,0:T(8,128)(2,1)} collective-permute-done((bf16[64,32,128]{2,1,0:T(8,128)(2,1)S(1)}, bf16[64,32,128]{2,1,0:T(8,128)(2,1)}, u32[]{:S(2)}, u32[]{:S(2)}) %collective-permute-start.7) | collective-permute-done | bytes 524320 | tf_op jit(solution)/shard_map/ppermute | solution.py:135
  105.0 1.2 constant_dynamic-update-slice_fusion
  106.2 0.0 collective-permute-done.8
  106.2 1.2 constant_dynamic-update-slice_fusion.2.a_ref
  107.4 1.4 %copy-done = bf16[64,32,512]{2,1,0:T(8,128)(2,1)} copy-done((bf16[64,32,512]{2,1,0:T(8,128)(2,1)}, bf16[64,32,512]{2,1,0:T(8,128)(2,1)S(1)}, u32[]{:S(2)}) %copy-start) | copy-done | bytes 2097176
  108.8 11.0 %shard_map.79 = bf16[128,32,128]{2,1,0:T(8,128)(2,1)} custom-call(s32[128]{0:T(128)} %rows_ref.1, s32[128]{0:T(128)} %cols_ref.1, s32[1]{0:T(128)S(6)} %copy.34.cnt_ref, bf16[64,32,512]{2,1,0:T(8,128)(2,1)} %copy-done, bf16[512,3584]{1,0:T(8,128)(2,1)} %pad_maximum_fusion.g_ref), custom_call_target="tpu_custom_call" | custom-call | flops 536870912 | bytes 6815744 | tf_op jit(solution)/shard_map/pallas_call | solution.py:55
  119.7 7.5 %reduce-scatter.4.cloned.1.call-done = f32[64,2048]{1,0:T(8,128)} async-done(((f32[512,2048]{1,0:T(8,128)}), f32[64,2048]{1,0:T(8,128)}) %reduce-scatter.4.cloned.1.call-update) | async-done | bytes 524304
  127.2 1.3 copy.21
  128.5 0.9 copy.19
  (6 shorter events, 0.1 us)
Async XLA Ops:
  7.2 2.1 %copy-start.1 = (bf16[128,3584]{1,0:T(8,128)(2,1)S(1)}, bf16[128,3584]{1,0:T(8,128)(2,1)}, u32[]{:S(2)}) copy-start(bf16[128,3584]{1,0:T(8,128)(2,1)} %param.7) | copy-start | bytes 2752516
  7.2 74.0 %all-gather.2.cloned.1.call-start = ((), (), s32[]{:S(2)}) async-start(), calls=%async_computation.1 | async-start | bytes 2359296 | tf_op jit(solution)/shard_map/all_gather | solution.py:111
  9.1 118.1 %reduce-scatter.4.cloned.1.call-start = ((), (), s32[]{:S(2)}) async-start(), calls=%async_computation.2 | async-start | bytes 4718592
  10.2 14.6 %collective-permute-start = (bf16[128,1792]{1,0:T(8,128)(2,1)}, bf16[128,1792]{1,0:T(8,128)(2,1)}, u32[]{:S(2)}, u32[]{:S(2)}) collective-permute-start(bf16[128,1792]{1,0:T(8,128)(2,1)} %get-tuple-element.19), channel_id=1, source_target_pairs={{0,8},{8,0},{16,24},{24,16},{1,9},{9,1},{17,25},{25,17},{2,10},{10... | collective-permute-start | bytes 1376264 | tf_op jit(solution)/shard_map/ppermute | solution.py:18
  13.1 22.0 %collective-permute-start.1 = (bf16[128,1792]{1,0:T(8,128)(2,1)}, bf16[128,1792]{1,0:T(8,128)(2,1)S(1)}, u32[]{:S(2)}, u32[]{:S(2)}) collective-permute-start(bf16[128,1792]{1,0:T(8,128)(2,1)} %get-tuple-element.19), channel_id=1, source_target_pairs={{0,16},{8,24},{16,0},{24,8},{1,17},{9,25},{17,1},{25,9},{2,18},{10... | collective-permute-start | bytes 1376264 | tf_op jit(solution)/shard_map/ppermute | solution.py:18
  14.6 20.5 %collective-permute-start.2 = (bf16[128,1792]{1,0:T(8,128)(2,1)}, bf16[128,1792]{1,0:T(8,128)(2,1)S(1)}, u32[]{:S(2)}, u32[]{:S(2)}) collective-permute-start(bf16[128,1792]{1,0:T(8,128)(2,1)} %get-tuple-element.19), channel_id=1, source_target_pairs={{0,24},{8,16},{16,8},{24,0},{1,25},{9,17},{17,9},{25,1},{2,26},{10... | collective-permute-start | bytes 1376264 | tf_op jit(solution)/shard_map/ppermute | solution.py:18
  35.2 16.5 %collective-permute-start.3 = (bf16[128,1792]{1,0:T(8,128)(2,1)S(1)}, bf16[128,1792]{1,0:T(8,128)(2,1)}, u32[]{:S(2)}, u32[]{:S(2)}) collective-permute-start(bf16[128,1792]{1,0:T(8,128)(2,1)S(1)} %get-tuple-element.6), channel_id=1, source_target_pairs={{0,8},{8,0},{16,24},{24,16},{1,9},{9,1},{17,25},{25,17},{2,10},{10... | collective-permute-start | bytes 1376264 | tf_op jit(solution)/shard_map/ppermute | solution.py:18
  36.5 21.0 %collective-permute-start.4 = (bf16[128,1792]{1,0:T(8,128)(2,1)S(1)}, bf16[128,1792]{1,0:T(8,128)(2,1)S(1)}, u32[]{:S(2)}, u32[]{:S(2)}) collective-permute-start(bf16[128,1792]{1,0:T(8,128)(2,1)S(1)} %get-tuple-element.6), channel_id=1, source_target_pairs={{0,16},{8,24},{16,0},{24,8},{1,17},{9,25},{17,1},{25,9},{2,18},{10... | collective-permute-start | bytes 1376264 | tf_op jit(solution)/shard_map/ppermute | solution.py:18
  37.3 21.0 %collective-permute-start.5 = (bf16[128,1792]{1,0:T(8,128)(2,1)S(1)}, bf16[128,1792]{1,0:T(8,128)(2,1)S(1)}, u32[]{:S(2)}, u32[]{:S(2)}) collective-permute-start(bf16[128,1792]{1,0:T(8,128)(2,1)S(1)} %get-tuple-element.6), channel_id=1, source_target_pairs={{0,24},{8,16},{16,8},{24,0},{1,25},{9,17},{17,9},{25,1},{2,26},{10... | collective-permute-start | bytes 1376264 | tf_op jit(solution)/shard_map/ppermute | solution.py:18
  83.6 15.2 %collective-permute-start.6 = (bf16[64,32,128]{2,1,0:T(8,128)(2,1)}, bf16[64,32,128]{2,1,0:T(8,128)(2,1)}, u32[]{:S(2)}, u32[]{:S(2)}) collective-permute-start(bf16[64,32,128]{2,1,0:T(8,128)(2,1)} %get-tuple-element.18), channel_id=1, source_target_pairs={{0,8},{8,0},{16,24},{24,16},{1,9},{9,1},{17,25},{25,17},{2,10},{10... | collective-permute-start | bytes 1572872 | tf_op jit(solution)/shard_map/ppermute | solution.py:135
  84.2 20.8 %collective-permute-start.7 = (bf16[64,32,128]{2,1,0:T(8,128)(2,1)S(1)}, bf16[64,32,128]{2,1,0:T(8,128)(2,1)}, u32[]{:S(2)}, u32[]{:S(2)}) collective-permute-start(bf16[64,32,128]{2,1,0:T(8,128)(2,1)S(1)} %get-tuple-element.17), channel_id=1, source_target_pairs={{0,16},{8,24},{16,0},{24,8},{1,17},{9,25},{17,1},{25,9},{2,18},{10... | collective-permute-start | bytes 1572872 | tf_op jit(solution)/shard_map/ppermute | solution.py:135
  84.6 21.6 %collective-permute-start.8 = (bf16[64,32,128]{2,1,0:T(8,128)(2,1)S(1)}, bf16[64,32,128]{2,1,0:T(8,128)(2,1)}, u32[]{:S(2)}, u32[]{:S(2)}) collective-permute-start(bf16[64,32,128]{2,1,0:T(8,128)(2,1)S(1)} %get-tuple-element.16), channel_id=1, source_target_pairs={{0,24},{8,16},{16,8},{24,0},{1,25},{9,17},{17,9},{25,1},{2,26},{10... | collective-permute-start | bytes 1572872 | tf_op jit(solution)/shard_map/ppermute | solution.py:135
  107.4 1.4 %copy-start = (bf16[64,32,512]{2,1,0:T(8,128)(2,1)}, bf16[64,32,512]{2,1,0:T(8,128)(2,1)S(1)}, u32[]{:S(2)}) copy-start(bf16[64,32,512]{2,1,0:T(8,128)(2,1)S(1)} %constant_dynamic-update-slice_fusion.2.a_ref) | copy-start | bytes 6291460
Sparse Core Ops, SparseCore 0:
  10.2 31.7 all-gather.1
  77.7 49.4 reduce-scatter.3

commit v9 on v7

--- a/solution.py
+++ b/solution.py
@@ -77,13 +77,13 @@
     o_ref[...] = out
 
 
-def matmul_nt(g, w, acc):
+def matmul_nt(g, w, k, acc):
     rows, depth = g.shape
     cols = w.shape[0]
     tile = min(cols, 512)
     in_specs = [
         pl.BlockSpec((rows, depth), lambda j: (0, 0)),
-        pl.BlockSpec((tile, depth), lambda j: (j, 0)),
+        pl.BlockSpec((tile, depth), lambda j: (j, k)),
     ]
     args = [g, w]
     if acc is not None:
@@ -97,7 +97,7 @@
         out_shape=jax.ShapeDtypeStruct((rows, cols), jnp.float32),
         cost_estimate=pl.CostEstimate(
             flops=2 * rows * depth * cols,
-            bytes_accessed=g.size * 2 + w.size * 2 + rows * cols * 4 * (2 if acc is not None else 1),
+            bytes_accessed=g.size * 2 + cols * depth * 2 + rows * cols * 4 * (2 if acc is not None else 1),
             transcendentals=0,
         ),
     )(*args)
@@ -121,9 +121,12 @@
         if gathered:
             piece, gathered[-1] = lax.optimization_barrier((piece, gathered[-1]))
         gathered.append(place_rows(xor_exchange(piece, "tok", n_tok), me))
-    for k in range(F_CHUNKS):
-        cols = slice(k * f_chunk, (k + 1) * f_chunk)
-        partial_sums = matmul_nt(gathered[k], weight[:, cols], partial_sums)
+    for k in range(F_CHUNKS - 1):
+        partial_sums = matmul_nt(gathered[k], weight, k, partial_sums)
+    last = slice((F_CHUNKS - 1) * f_chunk, F_CHUNKS * f_chunk)
+    partial_sums = partial_sums + lax.dot_general(
+        gathered[-1], weight[:, last], (((1,), (1,)), ((), ())), preferred_element_type=jnp.float32
+    )
     gout = jnp.concatenate(gathered, axis=1)
     grad_in = lax.psum_scatter(partial_sums, "feat", scatter_dimension=0, tiled=True).astype(
         jnp.bfloat16

time: 127 us -> 127 us (level)
  local copies, waits for them, and re-layouts: 27.5 us -> 15.8 us
  waiting for transfers between devices: 37.8 us -> 49.2 us
  Pallas kernels: 29.4 us -> 19.6 us
  matrix products: 0 us -> 6.95 us
  other arithmetic: 5.32 us -> 8.01 us
    ppermute x6, waiting for transfers between devices: 17 us -> 28.4 us  [xor_exchange(): out.append(lax.ppermute(x, axis_name, perm=[(a, a ^ m) for a in range(n)]))]
    slice x1 -> x0, local copies, waits for them, and re-layouts: 10.5 us -> none  [per_device(): partial_sums = matmul_nt(gathered[k], weight[:, cols], partial_sums)]
    pallas_call x2 -> x1, Pallas kernels: 18.4 us -> 8.59 us  [matmul_nt(): pl.pallas_call(matmul_kernel, grid=(cols // tile,), in_specs=in_specs, ou...]
    dot_general x0 -> x1, matrix products: none -> 6.95 us  [per_device(): lax.dot_general(gathered[-1], weight[:, last], (((1,), (1,)), ((), ())),...]
    add x0 -> x1, other arithmetic: none -> 2.71 us  [per_device(): partial_sums + lax.dot_general(gathered[-1], weight[:, last], (((1,), (1,...]
  transfers between devices with their start and end apart: 11 -> 11, of which waited for: 6 -> 7; matrix products, arithmetic and copies ran while one was open for 20% -> 19% of each run, Pallas kernels for 23% -> 16%
where the time goes in v9:
time: 127 us; the launch traced here: 126 us
  waiting for transfers between devices  49.2 us (39%)
  Pallas kernels  19.6 us (15%)
  local copies, waits for them, and re-layouts  15.8 us (12%)
  between operations  14.9 us (12%)
  starting transfers between devices  11.6 us (9%)
  other arithmetic  8.01 us (6%)
  matrix products  6.95 us (5%)
    ppermute x6, waiting for transfers between devices, xor_exchange(): out.append(lax.ppermute(x, axis_name, perm=[(a, a ^ m) for a in range(n)]))  28.4 us
    ppermute x3, waiting for transfers between devices, per_device(): part = lax.ppermute(part, 'tok', perm=[(a, a ^ m) for a in range(n_tok)])  15.1 us
    pallas_call x1, Pallas kernels, block_tiles(): pl.pallas_call(block_kernel, grid_spec=grid_spec, out_shape=jax.ShapeDtyp...  11 us
    pallas_call x1, Pallas kernels, matmul_nt(): pl.pallas_call(matmul_kernel, grid=(cols // tile,), in_specs=in_specs, ou...  8.59 us
    ppermute x6, starting transfers between devices, xor_exchange(): out.append(lax.ppermute(x, axis_name, perm=[(a, a ^ m) for a in range(n)]))  8.01 us
    dynamic_update_slice x11, local copies, waits for them, and re-layouts, place_rows(): out = lax.dynamic_update_slice_in_dim(out, piece, (me ^ m) * rows, axis)  7 us
    dot_general x1, matrix products, per_device(): lax.dot_general(gathered[-1], weight[:, last], (((1,), (1,)), ((), ())),...  6.95 us
    reduce_scatter x1, waiting for transfers between devices, per_device(): lax.psum_scatter(partial_sums, 'feat', scatter_dimension=0, tiled=True)  5.76 us
  transfers between devices with their start and end apart: 11, of which 7 were waited for; matrix products, arithmetic and copies ran while one was open for 19% of the time, Pallas kernels for 16%

profile of v9, /device:TPU:0, one launch (start us, length us, event | category | flops | bytes accessed | tf_op | source)
XLA Modules:
  0.0 126.0 jit_solution(17053707916394808789)
XLA Ops:
  7.2 0.0 copy-start.5
  7.2 0.0 all-gather.2.cloned.1.call-start
  7.2 1.9 %copy.9 = bf16[128,1024]{0,1:T(8,128)(2,1)} copy(bf16[128,1024]{1,0:T(8,128)(2,1)} %param.6) | data formatting | bytes 524288 | tf_op args[0]
  9.1 0.0 all-gather.2.cloned.1.call-update
  9.1 0.0 reduce-scatter.2.cloned.1.call-start
  9.2 0.1 broadcast.3.clone
  9.3 0.0 copy-done.5
  9.3 0.9 fusion.2
  10.2 2.9 %collective-permute-start = (bf16[128,1792]{1,0:T(8,128)(2,1)}, bf16[128,1792]{1,0:T(8,128)(2,1)}, u32[]{:S(2)}, u32[]{:S(2)}) collective-permute-start(bf16[128,1792]{1,0:T(8,128)(2,1)} %get-tuple-element.13), channel_id=1, source_target_pairs={{0,8},{8,0},{16,24},{24,16},{1,9},{9,1},{17,25},{25,17},{2,10},{10... | collective-permute-start | bytes 1376264 | tf_op jit(solution)/shard_map/ppermute | solution.py:18
  13.1 1.5 %collective-permute-start.1 = (bf16[128,1792]{1,0:T(8,128)(2,1)}, bf16[128,1792]{1,0:T(8,128)(2,1)S(1)}, u32[]{:S(2)}, u32[]{:S(2)}) collective-permute-start(bf16[128,1792]{1,0:T(8,128)(2,1)} %get-tuple-element.13), channel_id=1, source_target_pairs={{0,16},{8,24},{16,0},{24,8},{1,17},{9,25},{17,1},{25,9},{2,18},{10... | collective-permute-start | bytes 1376264 | tf_op jit(solution)/shard_map/ppermute | solution.py:18
  14.6 0.0 collective-permute-start.2
  14.6 10.1 %collective-permute-done = bf16[128,1792]{1,0:T(8,128)(2,1)} collective-permute-done((bf16[128,1792]{1,0:T(8,128)(2,1)}, bf16[128,1792]{1,0:T(8,128)(2,1)}, u32[]{:S(2)}, u32[]{:S(2)}) %collective-permute-start) | collective-permute-done | bytes 458784 | tf_op jit(solution)/shard_map/ppermute | solution.py:18
  24.8 1.1 constant_dynamic-update-slice_fusion.9
  25.8 9.3 %collective-permute-done.1 = bf16[128,1792]{1,0:T(8,128)(2,1)S(1)} collective-permute-done((bf16[128,1792]{1,0:T(8,128)(2,1)}, bf16[128,1792]{1,0:T(8,128)(2,1)S(1)}, u32[]{:S(2)}, u32[]{:S(2)}) %collective-permute-start.1) | collective-permute-done | bytes 458784 | tf_op jit(solution)/shard_map/ppermute | solution.py:18
  35.2 0.0 collective-permute-done.2
  35.2 0.0 copy-start.1
  35.2 1.2 collective-permute-start.3
  36.5 0.9 collective-permute-start.4
  37.3 1.4 %collective-permute-start.5 = (bf16[128,1792]{1,0:T(8,128)(2,1)S(1)}, bf16[128,1792]{1,0:T(8,128)(2,1)S(1)}, u32[]{:S(2)}, u32[]{:S(2)}) collective-permute-start(bf16[128,1792]{1,0:T(8,128)(2,1)S(1)} %get-tuple-element.7), channel_id=1, source_target_pairs={{0,24},{8,16},{16,8},{24,0},{1,25},{9,17},{17,9},{25,1},{2,26},{10... | collective-permute-start | bytes 1376264 | tf_op jit(solution)/shard_map/ppermute | solution.py:18
  38.8 0.0 copy-done.1
  38.8 8.6 %shard_map.77 = f32[512,2048]{1,0:T(8,128)} custom-call(bf16[512,1792]{1,0:T(8,128)(2,1)} %copy-done.1, bf16[2048,3584]{1,0:T(8,128)(2,1)} %refs_1_.1), custom_call_target="tpu_custom_call" | custom-call | flops 3758096384 | bytes 13369344 | tf_op jit(solution)/shard_map/pallas_call | solution.py:92
  47.4 0.1 broadcast.3
  47.6 1.3 %collective-permute-done.3 = bf16[128,1792]{1,0:T(8,128)(2,1)} collective-permute-done((bf16[128,1792]{1,0:T(8,128)(2,1)S(1)}, bf16[128,1792]{1,0:T(8,128)(2,1)}, u32[]{:S(2)}, u32[]{:S(2)}) %collective-permute-start.3) | collective-permute-done | bytes 458784 | tf_op jit(solution)/shard_map/ppermute | solution.py:18
  48.9 1.0 constant_dynamic-update-slice_fusion.5
  49.9 7.6 %collective-permute-done.4 = bf16[128,1792]{1,0:T(8,128)(2,1)S(1)} collective-permute-done((bf16[128,1792]{1,0:T(8,128)(2,1)S(1)}, bf16[128,1792]{1,0:T(8,128)(2,1)S(1)}, u32[]{:S(2)}, u32[]{:S(2)}) %collective-permute-start.4) | collective-permute-done | bytes 458784 | tf_op jit(solution)/shard_map/ppermute | solution.py:18
  57.6 0.0 collective-permute-done.5
  57.6 7.0 %fusion = f32[512,2048]{1,0:T(8,128)S(1)} fusion(bf16[512,1792]{1,0:T(8,128)(2,1)S(1)} %constant_dynamic-update-slice_fusion.3, bf16[2048,3584]{1,0:T(8,128)(2,1)} %refs_1_.1), kind=kOutput, calls=%fused_computation | convolution fusion | flops 3758096384 | bytes 13369344 | tf_op jit(solution)/shard_map/dot_general | solution.py:127
  64.6 2.7 %add.42 = f32[512,2048]{1,0:T(8,128)} add(f32[512,2048]{1,0:T(8,128)S(1)} %copy-done, f32[512,2048]{1,0:T(8,128)S(1)} %fusion) | non-fusion elementwise | flops 1048576 | bytes 12582912 | tf_op jit(solution)/shard_map/add | solution.py:127
  67.3 0.0 reduce-scatter.2.cloned.1.call-update
  67.4 1.4 %copy-done.2 = bf16[512,1792]{1,0:T(8,128)(2,1)S(1)} copy-done((bf16[512,1792]{1,0:T(8,128)(2,1)S(1)}, bf16[512,1792]{1,0:T(8,128)(2,1)}, u32[]{:S(2)}) %copy-start.2) | copy-done | bytes 1835032
  68.8 3.5 %pad_maximum_fusion.g_ref = bf16[512,3584]{1,0:T(8,128)(2,1)} fusion(bf16[512,1792]{1,0:T(8,128)(2,1)} %copy-done.4, bf16[512,1792]{1,0:T(8,128)(2,1)S(1)} %copy-done.2), kind=kLoop, calls=%fused_computation.2 | loop fusion | flops 7340032 | bytes 7340032 | tf_op jit(solution)/shard_map/concatenate | solution.py:130
  72.4 2.7 %dynamic-slice_bitcast_fusion = (bf16[64,32,128]{2,1,0:T(8,128)(2,1)S(1)}, bf16[64,32,128]{2,1,0:T(8,128)(2,1)S(1)}, bf16[64,32,128]{2,1,0:T(8,128)(2,1)}) fusion(bf16[4,64,32,128]{3,2,0,1:T(8,128)(2,1)} %bitcast.12, s32[]{:T(128)S(6)} %select_n.40, s32[]{:T(128)S(6)} %select_n.39, s32[]{:T(128)S(6)} %select_n.38), kind=kLoop, calls=%fused_computation.4 | loop fusion | bytes 3145740 | tf_op jit(solution)/shard_map/jit(dynamic_index_in_dim)/squeeze | solution.py:138
  75.1 0.3 collective-permute-start.6
  75.4 1.1 collective-permute-start.7
  76.5 2.1 %collective-permute-start.8 = (bf16[64,32,128]{2,1,0:T(8,128)(2,1)S(1)}, bf16[64,32,128]{2,1,0:T(8,128)(2,1)}, u32[]{:S(2)}, u32[]{:S(2)}) collective-permute-start(bf16[64,32,128]{2,1,0:T(8,128)(2,1)S(1)} %get-tuple-element.10), channel_id=1, source_target_pairs={{0,24},{8,16},{16,8},{24,0},{1,25},{9,17},{17,9},{25,1},{2,26},{10... | collective-permute-start | bytes 1572872 | tf_op jit(solution)/shard_map/ppermute | solution.py:140
  79.2 0.2 broadcast_in_dim.3
  79.5 1.2 bitcast_dynamic-update-slice_fusion
  80.7 9.6 %collective-permute-done.6 = bf16[64,32,128]{2,1,0:T(8,128)(2,1)} collective-permute-done((bf16[64,32,128]{2,1,0:T(8,128)(2,1)}, bf16[64,32,128]{2,1,0:T(8,128)(2,1)}, u32[]{:S(2)}, u32[]{:S(2)}) %collective-permute-start.6) | collective-permute-done | bytes 524320 | tf_op jit(solution)/shard_map/ppermute | solution.py:140
  90.3 1.2 constant_dynamic-update-slice_fusion.1
  91.4 5.5 %collective-permute-done.7 = bf16[64,32,128]{2,1,0:T(8,128)(2,1)} collective-permute-done((bf16[64,32,128]{2,1,0:T(8,128)(2,1)S(1)}, bf16[64,32,128]{2,1,0:T(8,128)(2,1)}, u32[]{:S(2)}, u32[]{:S(2)}) %collective-permute-start.7) | collective-permute-done | bytes 524320 | tf_op jit(solution)/shard_map/ppermute | solution.py:140
  96.9 1.2 constant_dynamic-update-slice_fusion
  98.1 0.0 collective-permute-done.8
  98.1 1.2 constant_dynamic-update-slice_fusion.2.a_ref
  99.3 0.0 copy-start.3
  99.3 1.4 %copy-done.3 = bf16[64,32,512]{2,1,0:T(8,128)(2,1)} copy-done((bf16[64,32,512]{2,1,0:T(8,128)(2,1)}, bf16[64,32,512]{2,1,0:T(8,128)(2,1)S(1)}, u32[]{:S(2)}) %copy-start.3) | copy-done | bytes 2097176
  100.7 11.0 %shard_map.78 = bf16[128,32,128]{2,1,0:T(8,128)(2,1)} custom-call(s32[128]{0:T(128)} %rows_ref.1, s32[128]{0:T(128)} %cols_ref.1, s32[1]{0:T(128)S(6)} %copy.22.cnt_ref, bf16[64,32,512]{2,1,0:T(8,128)(2,1)} %copy-done.3, bf16[512,3584]{1,0:T(8,128)(2,1)} %pad_maximum_fusion.g_ref), custom_call_target="tpu_custom_call" | custom-call | flops 536870912 | bytes 6815744 | tf_op jit(solution)/shard_map/pallas_call | solution.py:55
  111.7 5.8 %reduce-scatter.2.cloned.1.call-done = f32[64,2048]{1,0:T(8,128)} async-done(((f32[512,2048]{1,0:T(8,128)}), f32[64,2048]{1,0:T(8,128)}) %reduce-scatter.2.cloned.1.call-update) | async-done | bytes 524304 | tf_op jit(solution)/shard_map/reduce_scatter | solution.py:131
  117.4 1.8 %convert_element_type.3 = bf16[64,2048]{1,0:T(8,128)(2,1)} convert(f32[64,2048]{1,0:T(8,128)} %reduce-scatter.2.cloned.1.call-done) | non-fusion elementwise | flops 131072 | bytes 786432 | tf_op jit(solution)/shard_map/convert_element_type | solution.py:131
  (11 shorter events, 0.2 us)
Async XLA Ops:
  7.2 2.1 %copy-start.5 = (bf16[128,3584]{1,0:T(8,128)(2,1)S(1)}, bf16[128,3584]{1,0:T(8,128)(2,1)}, u32[]{:S(2)}) copy-start(bf16[128,3584]{1,0:T(8,128)(2,1)} %param.7) | copy-start | bytes 2752516
  7.2 65.2 %all-gather.2.cloned.1.call-start = ((), (), s32[]{:S(2)}) async-start(), calls=%async_computation.2 | async-start | bytes 2359296 | tf_op jit(solution)/shard_map/all_gather | solution.py:111
  9.1 108.3 %reduce-scatter.2.cloned.1.call-start = ((), (), s32[]{:S(2)}) async-start(), calls=%async_computation.1 | async-start | bytes 4718592 | tf_op jit(solution)/shard_map/reduce_scatter | solution.py:131
  10.2 14.6 %collective-permute-start = (bf16[128,1792]{1,0:T(8,128)(2,1)}, bf16[128,1792]{1,0:T(8,128)(2,1)}, u32[]{:S(2)}, u32[]{:S(2)}) collective-permute-start(bf16[128,1792]{1,0:T(8,128)(2,1)} %get-tuple-element.13), channel_id=1, source_target_pairs={{0,8},{8,0},{16,24},{24,16},{1,9},{9,1},{17,25},{25,17},{2,10},{10... | collective-permute-start | bytes 1376264 | tf_op jit(solution)/shard_map/ppermute | solution.py:18
  13.1 22.0 %collective-permute-start.1 = (bf16[128,1792]{1,0:T(8,128)(2,1)}, bf16[128,1792]{1,0:T(8,128)(2,1)S(1)}, u32[]{:S(2)}, u32[]{:S(2)}) collective-permute-start(bf16[128,1792]{1,0:T(8,128)(2,1)} %get-tuple-element.13), channel_id=1, source_target_pairs={{0,16},{8,24},{16,0},{24,8},{1,17},{9,25},{17,1},{25,9},{2,18},{10... | collective-permute-start | bytes 1376264 | tf_op jit(solution)/shard_map/ppermute | solution.py:18
  14.6 20.5 %collective-permute-start.2 = (bf16[128,1792]{1,0:T(8,128)(2,1)}, bf16[128,1792]{1,0:T(8,128)(2,1)S(1)}, u32[]{:S(2)}, u32[]{:S(2)}) collective-permute-start(bf16[128,1792]{1,0:T(8,128)(2,1)} %get-tuple-element.13), channel_id=1, source_target_pairs={{0,24},{8,16},{16,8},{24,0},{1,25},{9,17},{17,9},{25,1},{2,26},{10... | collective-permute-start | bytes 1376264 | tf_op jit(solution)/shard_map/ppermute | solution.py:18
  35.2 3.6 %copy-start.1 = (bf16[512,1792]{1,0:T(8,128)(2,1)}, bf16[512,1792]{1,0:T(8,128)(2,1)S(1)}, u32[]{:S(2)}) copy-start(bf16[512,1792]{1,0:T(8,128)(2,1)S(1)} %constant_dynamic-update-slice_fusion.7.refs_0_) | copy-start | bytes 5505028
  35.2 13.6 %collective-permute-start.3 = (bf16[128,1792]{1,0:T(8,128)(2,1)S(1)}, bf16[128,1792]{1,0:T(8,128)(2,1)}, u32[]{:S(2)}, u32[]{:S(2)}) collective-permute-start(bf16[128,1792]{1,0:T(8,128)(2,1)S(1)} %get-tuple-element.7), channel_id=1, source_target_pairs={{0,8},{8,0},{16,24},{24,16},{1,9},{9,1},{17,25},{25,17},{2,10},{10... | collective-permute-start | bytes 1376264 | tf_op jit(solution)/shard_map/ppermute | solution.py:18
  36.5 21.0 %collective-permute-start.4 = (bf16[128,1792]{1,0:T(8,128)(2,1)S(1)}, bf16[128,1792]{1,0:T(8,128)(2,1)S(1)}, u32[]{:S(2)}, u32[]{:S(2)}) collective-permute-start(bf16[128,1792]{1,0:T(8,128)(2,1)S(1)} %get-tuple-element.7), channel_id=1, source_target_pairs={{0,16},{8,24},{16,0},{24,8},{1,17},{9,25},{17,1},{25,9},{2,18},{10... | collective-permute-start | bytes 1376264 | tf_op jit(solution)/shard_map/ppermute | solution.py:18
  37.3 20.2 %collective-permute-start.5 = (bf16[128,1792]{1,0:T(8,128)(2,1)S(1)}, bf16[128,1792]{1,0:T(8,128)(2,1)S(1)}, u32[]{:S(2)}, u32[]{:S(2)}) collective-permute-start(bf16[128,1792]{1,0:T(8,128)(2,1)S(1)} %get-tuple-element.7), channel_id=1, source_target_pairs={{0,24},{8,16},{16,8},{24,0},{1,25},{9,17},{17,9},{25,1},{2,26},{10... | collective-permute-start | bytes 1376264 | tf_op jit(solution)/shard_map/ppermute | solution.py:18
  57.6 7.0 %copy-start.4 = (bf16[512,1792]{1,0:T(8,128)(2,1)}, bf16[512,1792]{1,0:T(8,128)(2,1)S(1)}, u32[]{:S(2)}) copy-start(bf16[512,1792]{1,0:T(8,128)(2,1)S(1)} %constant_dynamic-update-slice_fusion.3) | copy-start | bytes 5505028
  57.6 7.0 %copy-start = (f32[512,2048]{1,0:T(8,128)S(1)}, f32[512,2048]{1,0:T(8,128)}, u32[]{:S(2)}) copy-start(f32[512,2048]{1,0:T(8,128)} %shard_map.77) | copy-start | bytes 12582916
  67.3 1.5 %copy-start.2 = (bf16[512,1792]{1,0:T(8,128)(2,1)S(1)}, bf16[512,1792]{1,0:T(8,128)(2,1)}, u32[]{:S(2)}) copy-start(bf16[512,1792]{1,0:T(8,128)(2,1)} %copy-done.1) | copy-start | bytes 5505028
  75.1 15.2 %collective-permute-start.6 = (bf16[64,32,128]{2,1,0:T(8,128)(2,1)}, bf16[64,32,128]{2,1,0:T(8,128)(2,1)}, u32[]{:S(2)}, u32[]{:S(2)}) collective-permute-start(bf16[64,32,128]{2,1,0:T(8,128)(2,1)} %get-tuple-element.12), channel_id=1, source_target_pairs={{0,8},{8,0},{16,24},{24,16},{1,9},{9,1},{17,25},{25,17},{2,10},{10... | collective-permute-start | bytes 1572872 | tf_op jit(solution)/shard_map/ppermute | solution.py:140
  75.4 21.6 %collective-permute-start.7 = (bf16[64,32,128]{2,1,0:T(8,128)(2,1)S(1)}, bf16[64,32,128]{2,1,0:T(8,128)(2,1)}, u32[]{:S(2)}, u32[]{:S(2)}) collective-permute-start(bf16[64,32,128]{2,1,0:T(8,128)(2,1)S(1)} %get-tuple-element.11), channel_id=1, source_target_pairs={{0,16},{8,24},{16,0},{24,8},{1,17},{9,25},{17,1},{25,9},{2,18},{10... | collective-permute-start | bytes 1572872 | tf_op jit(solution)/shard_map/ppermute | solution.py:140
  76.5 21.6 %collective-permute-start.8 = (bf16[64,32,128]{2,1,0:T(8,128)(2,1)S(1)}, bf16[64,32,128]{2,1,0:T(8,128)(2,1)}, u32[]{:S(2)}, u32[]{:S(2)}) collective-permute-start(bf16[64,32,128]{2,1,0:T(8,128)(2,1)S(1)} %get-tuple-element.10), channel_id=1, source_target_pairs={{0,24},{8,16},{16,8},{24,0},{1,25},{9,17},{17,9},{25,1},{2,26},{10... | collective-permute-start | bytes 1572872 | tf_op jit(solution)/shard_map/ppermute | solution.py:140
  99.3 1.4 %copy-start.3 = (bf16[64,32,512]{2,1,0:T(8,128)(2,1)}, bf16[64,32,512]{2,1,0:T(8,128)(2,1)S(1)}, u32[]{:S(2)}) copy-start(bf16[64,32,512]{2,1,0:T(8,128)(2,1)S(1)} %constant_dynamic-update-slice_fusion.2.a_ref) | copy-start | bytes 6291460
Sparse Core Ops, SparseCore 0:
  10.2 31.7 all-gather.1
  67.5 49.9 reduce-scatter.1

commit v10 on v6

--- a/solution.py
+++ b/solution.py
@@ -75,13 +75,16 @@
     return jnp.transpose(both, (2, 0, 1, 3)).reshape(x.shape[0], -1)
 
 
-def feat_reduce_scatter(h, n_feat, me_feat):
+def chip_sum(h, n_feat, me_feat):
     core = me_feat % 2
-    z = me_feat // 2
     h = h.reshape((n_feat // 2, 2, h.shape[0] // n_feat) + h.shape[1:])
     send = lax.dynamic_index_in_dim(h, 1 - core, axis=1, keepdims=False)
     keep = lax.dynamic_index_in_dim(h, core, axis=1, keepdims=False)
-    chip = keep + lax.ppermute(send, "feat", perm=[(a, a ^ 1) for a in range(n_feat)])
+    return keep + lax.ppermute(send, "feat", perm=[(a, a ^ 1) for a in range(n_feat)])
+
+
+def z_reduce(chip, n_feat, me_feat):
+    z = me_feat // 2
     total = lax.dynamic_index_in_dim(chip, z, axis=0, keepdims=False)
     for m in range(1, n_feat // 2):
         part = lax.dynamic_index_in_dim(chip, z ^ m, axis=0, keepdims=False)
@@ -100,7 +103,17 @@
     acts_pieces = jnp.transpose(full_acts.reshape(tok_dev, row_blocks, n_tok, sub), (2, 1, 3, 0))
 
     gout = place_rows(xor_exchange(grad_out, "tok", n_tok), me)
-    halves = []
+
+    acts_pieces, gout = lax.optimization_barrier((acts_pieces, gout))
+    got = []
+    for m in range(n_tok):
+        part = lax.dynamic_index_in_dim(acts_pieces, me ^ m, axis=0, keepdims=False)
+        if m:
+            part = lax.ppermute(part, "tok", perm=[(a, a ^ m) for a in range(n_tok)])
+        got.append(part)
+    acts_t = place_rows(got, me, axis=2)
+
+    chips = []
     d_half = weight.shape[0] // 2
     for k in range(2):
         partial_sums = lax.dot_general(
@@ -109,18 +122,12 @@
             (((1,), (1,)), ((), ())),
             preferred_element_type=jnp.float32,
         )
-        halves.append(feat_reduce_scatter(partial_sums, n_feat, me_feat))
+        chips.append(chip_sum(partial_sums, n_feat, me_feat))
+    halves = [z_reduce(chip, n_feat, me_feat) for chip in chips]
+    grad_in = jnp.concatenate(halves, axis=1).astype(jnp.bfloat16)
 
-    acts_pieces, gout, halves[0] = lax.optimization_barrier((acts_pieces, gout, halves[0]))
-    grad_in = jnp.concatenate(halves, axis=1).astype(jnp.bfloat16)
-    got = []
-    for m in range(n_tok):
-        part = lax.dynamic_index_in_dim(acts_pieces, me ^ m, axis=0, keepdims=False)
-        if m:
-            part = lax.ppermute(part, "tok", perm=[(a, a ^ m) for a in range(n_tok)])
-        got.append(part)
-    acts_t = place_rows(got, me, axis=2)
-    block_grads = block_tiles(block_rows, block_cols, block_count, acts_t, gout)
+    acts_t, gout_b, _ = lax.optimization_barrier((acts_t, gout, chips[1]))
+    block_grads = block_tiles(block_rows, block_cols, block_count, acts_t, gout_b)
     return (grad_in, block_grads)
 
 

time: 134 us -> 148 us (1.10); the launches traced: 134 us -> 145 us
  waiting for transfers between devices: 58 us -> 66.7 us
  other arithmetic: 3.58 us -> 6.52 us
  local copies, waits for them, and re-layouts: 17.7 us -> 20.1 us
  matrix products: 14 us -> 12 us
    ppermute x3, waiting for transfers between devices: 6.5 us -> 20.2 us  [per_device(): part = lax.ppermute(part, 'tok', perm=[(a, a ^ m) for a in range(n_tok)])]
    ppermute x8, waiting for transfers between devices: 26.3 us -> 16.9 us  [the longest x6 16.9 us: z_reduce(): lax.ppermute(part, 'feat', perm=[(a, a ^ 2 * m) for a in range(n_feat)])]
    ppermute x3, waiting for transfers between devices: 15.4 us -> 21.2 us  [xor_exchange(): out.append(lax.ppermute(x, axis_name, perm=[(a, a ^ m) for a in range(n)]))]
    another operation x1 -> x2, other arithmetic: 0.06 us -> 2.25 us
    dynamic_update_slice x14, local copies, waits for them, and re-layouts: 9.58 us -> 11.7 us  [place_rows(): out = lax.dynamic_update_slice_in_dim(out, piece, (me ^ m) * rows, axis)]
    dot_general x2, matrix products: 14 us -> 12 us  [per_device(): lax.dot_general(gout, weight[k * d_half:(k + 1) * d_half], (((1,), (1,)),...]
    ppermute x3, starting transfers between devices: 7.33 us -> 5.68 us  [feat_all_gather(): lax.ppermute(x, 'feat', perm=[(a, a ^ m) for a in range(n_feat)])]
    add x3 -> x2, other arithmetic: 2.79 us -> 3.54 us  [chip_sum(): keep + lax.ppermute(send, 'feat', perm=[(a, a ^ 1) for a in range(n_feat)])]
  transfers between devices with their start and end apart: 18 -> 18, of which waited for: 10 -> 9; matrix products, arithmetic and copies ran while one was open for 25% -> 23% of each run, Pallas kernels for 0% -> 8%
where the time goes in v10:
time: 148 us; the launch traced here: 145 us
  waiting for transfers between devices  66.7 us (45%)
  starting transfers between devices  27.3 us (18%)
  local copies, waits for them, and re-layouts  20.1 us (14%)
  matrix products  12 us (8%)
  Pallas kernels  10.9 us (7%)
  other arithmetic  6.52 us (4%)
  between operations  1.59 us (1%)
    ppermute x3, waiting for transfers between devices, xor_exchange(): out.append(lax.ppermute(x, axis_name, perm=[(a, a ^ m) for a in range(n)]))  21.2 us
    ppermute x3, waiting for transfers between devices, per_device(): part = lax.ppermute(part, 'tok', perm=[(a, a ^ m) for a in range(n_tok)])  20.2 us
    ppermute x6, waiting for transfers between devices, z_reduce(): lax.ppermute(part, 'feat', perm=[(a, a ^ 2 * m) for a in range(n_feat)])  16.9 us
    ppermute x6, starting transfers between devices, z_reduce(): lax.ppermute(part, 'feat', perm=[(a, a ^ 2 * m) for a in range(n_feat)])  12.1 us
    dot_general x2, matrix products, per_device(): lax.dot_general(gout, weight[k * d_half:(k + 1) * d_half], (((1,), (1,)),...  12 us
    dynamic_update_slice x14, local copies, waits for them, and re-layouts, place_rows(): out = lax.dynamic_update_slice_in_dim(out, piece, (me ^ m) * rows, axis)  11.7 us
    pallas_call x1, Pallas kernels, block_tiles(): pl.pallas_call(block_kernel, grid_spec=grid_spec, out_shape=jax.ShapeDtyp...  10.9 us
    ppermute x3, waiting for transfers between devices, feat_all_gather(): lax.ppermute(x, 'feat', perm=[(a, a ^ m) for a in range(n_feat)])  8.42 us
  transfers between devices with their start and end apart: 18, of which 9 were waited for; matrix products, arithmetic and copies ran while one was open for 23% of the time, Pallas kernels for 8%

profile of v10, /device:TPU:0, one launch (start us, length us, event | category | flops | bytes accessed | tf_op | source)
XLA Modules:
  0.0 145.1 jit_solution(3487910548809584003)
XLA Ops:
  0.6 1.1 copy.8
  1.8 3.1 %collective-permute-start = (bf16[128,1024]{0,1:T(8,128)(2,1)S(1)}, bf16[128,1024]{0,1:T(8,128)(2,1)S(1)}, u32[]{:S(2)}, u32[]{:S(2)}) collective-permute-start(bf16[128,1024]{0,1:T(8,128)(2,1)S(1)} %copy.8), channel_id=1, source_target_pairs={{0,2},{1,3},{2,0},{3,1},{4,6},{5,7},{6,4},{7,5},{8,10},{9,11},{10,... | collective-permute-start | bytes 786440 | tf_op jit(solution)/shard_map/ppermute | solution.py:69
  4.8 2.6 %collective-permute-start.1 = (bf16[128,1024]{0,1:T(8,128)(2,1)S(1)}, bf16[128,1024]{0,1:T(8,128)(2,1)S(1)}, u32[]{:S(2)}, u32[]{:S(2)}) collective-permute-start(bf16[128,1024]{0,1:T(8,128)(2,1)S(1)} %copy.8), channel_id=1, source_target_pairs={{0,4},{1,5},{2,6},{3,7},{4,0},{5,1},{6,2},{7,3},{8,12},{9,13},{10,... | collective-permute-start | bytes 786440 | tf_op jit(solution)/shard_map/ppermute | solution.py:69
  7.4 1.7 %collective-permute-start.4 = (bf16[128,3584]{1,0:T(8,128)(2,1)}, bf16[128,3584]{1,0:T(8,128)(2,1)}, u32[]{:S(2)}, u32[]{:S(2)}) collective-permute-start(bf16[128,3584]{1,0:T(8,128)(2,1)} %param.7), channel_id=1, source_target_pairs={{0,8},{8,0},{16,24},{24,16},{1,9},{9,1},{17,25},{25,17},{2,10},{10... | collective-permute-start | bytes 2752520 | tf_op jit(solution)/shard_map/ppermute | solution.py:17
  9.1 1.5 %collective-permute-start.5 = (bf16[128,3584]{1,0:T(8,128)(2,1)}, bf16[128,3584]{1,0:T(8,128)(2,1)}, u32[]{:S(2)}, u32[]{:S(2)}) collective-permute-start(bf16[128,3584]{1,0:T(8,128)(2,1)} %param.7), channel_id=1, source_target_pairs={{0,16},{8,24},{16,0},{24,8},{1,17},{9,25},{17,1},{25,9},{2,18},{10... | collective-permute-start | bytes 2752520 | tf_op jit(solution)/shard_map/ppermute | solution.py:17
  10.7 2.0 %broadcast_in_dim.38 = bf16[512,3584]{1,0:T(8,128)(2,1)} broadcast(bf16[]{:T(256)} %constant.83.clone.1), dimensions={} | broadcast | bytes 3670018 | tf_op jit(solution)/shard_map/broadcast_in_dim | solution.py:25
  12.7 2.2 %constant_dynamic-update-slice_fusion.6 = bf16[512,3584]{1,0:T(8,128)(2,1)} fusion(bf16[512,3584]{1,0:T(8,128)(2,1)} %broadcast_in_dim.38, bf16[128,3584]{1,0:T(8,128)(2,1)} %param.7, s32[]{:T(128)S(6)} %select_n.88), kind=kLoop, calls=%fused_computation.39 | loop fusion | bytes 1835012 | tf_op jit(solution)/shard_map/dynamic_update_slice | solution.py:27
  14.9 0.1 broadcast_in_dim.31
  15.1 0.9 collective-permute-done
  16.0 2.6 %collective-permute-start.6 = (bf16[128,3584]{1,0:T(8,128)(2,1)}, bf16[128,3584]{1,0:T(8,128)(2,1)S(1)}, u32[]{:S(2)}, u32[]{:S(2)}) collective-permute-start(bf16[128,3584]{1,0:T(8,128)(2,1)} %param.7), channel_id=1, source_target_pairs={{0,24},{8,16},{16,8},{24,0},{1,25},{9,17},{17,9},{25,1},{2,26},{10... | collective-permute-start | bytes 2752520 | tf_op jit(solution)/shard_map/ppermute | solution.py:17
  18.6 7.6 %collective-permute-done.1 = bf16[128,1024]{0,1:T(8,128)(2,1)S(1)} collective-permute-done((bf16[128,1024]{0,1:T(8,128)(2,1)S(1)}, bf16[128,1024]{0,1:T(8,128)(2,1)S(1)}, u32[]{:S(2)}, u32[]{:S(2)}) %collective-permute-start.1) | collective-permute-done | bytes 262176 | tf_op jit(solution)/shard_map/ppermute | solution.py:69
  26.4 0.3 broadcast_in_dim.30
  26.7 0.1 bitcast_dynamic-update-slice_fusion
  26.8 4.2 %collective-permute-done.4 = bf16[128,3584]{1,0:T(8,128)(2,1)} collective-permute-done((bf16[128,3584]{1,0:T(8,128)(2,1)}, bf16[128,3584]{1,0:T(8,128)(2,1)}, u32[]{:S(2)}, u32[]{:S(2)}) %collective-permute-start.4) | collective-permute-done | bytes 917536 | tf_op jit(solution)/shard_map/ppermute | solution.py:17
  31.0 2.2 %constant_dynamic-update-slice_fusion.5 = bf16[512,3584]{1,0:T(8,128)(2,1)} fusion(bf16[512,3584]{1,0:T(8,128)(2,1)} %constant_dynamic-update-slice_fusion.6, bf16[128,3584]{1,0:T(8,128)(2,1)} %collective-permute-done.4, s32[]{:T(128)S(6)} %select_n.89), kind=kLoop, calls=%fused_computation.38 | loop fusion | bytes 1835012 | tf_op jit(solution)/shard_map/dynamic_update_slice | solution.py:27
  33.2 16.9 %collective-permute-done.5 = bf16[128,3584]{1,0:T(8,128)(2,1)} collective-permute-done((bf16[128,3584]{1,0:T(8,128)(2,1)}, bf16[128,3584]{1,0:T(8,128)(2,1)}, u32[]{:S(2)}, u32[]{:S(2)}) %collective-permute-start.5) | collective-permute-done | bytes 917536 | tf_op jit(solution)/shard_map/ppermute | solution.py:17
  50.2 2.2 %constant_dynamic-update-slice_fusion.4 = bf16[512,3584]{1,0:T(8,128)(2,1)} fusion(bf16[512,3584]{1,0:T(8,128)(2,1)} %constant_dynamic-update-slice_fusion.5, bf16[128,3584]{1,0:T(8,128)(2,1)} %collective-permute-done.5, s32[]{:T(128)S(6)} %select_n.90), kind=kLoop, calls=%fused_computation.37 | loop fusion | bytes 1835012 | tf_op jit(solution)/shard_map/dynamic_update_slice | solution.py:27
  52.3 1.0 constant_dynamic-update-slice_fusion.3.g_ref
  53.5 1.3 dynamic-slice_bitcast_fusion.2
  54.8 6.0 %fusion.2 = f32[512,1024]{1,0:T(8,128)S(1)} fusion(bf16[512,3584]{1,0:T(8,128)(2,1)} %constant_dynamic-update-slice_fusion.3.g_ref, bf16[2048,3584]{1,0:T(8,128)(2,1)S(1)} %copy-done.7), kind=kOutput, calls=%fused_computation.2 | convolution fusion | flops 3758096384 | bytes 13107200 | tf_op jit(solution)/shard_map/dot_general | solution.py:119
  60.8 1.2 dynamic-slice_bitcast_fusion.1
  62.0 0.5 copy-done.3
  62.5 6.0 %fusion = f32[512,1024]{1,0:T(8,128)S(1)} fusion(bf16[512,3584]{1,0:T(8,128)(2,1)} %constant_dynamic-update-slice_fusion.3.g_ref, bf16[2048,3584]{1,0:T(8,128)(2,1)S(1)} %copy-done.7), kind=kOutput, calls=%fused_computation | convolution fusion | flops 3758096384 | bytes 13107200 | tf_op jit(solution)/shard_map/dot_general | solution.py:119
  68.5 2.1 %collective-permute-start.16 = (bf16[64,32,128]{2,1,0:T(8,128)(2,1)}, bf16[64,32,128]{2,1,0:T(8,128)(2,1)}, u32[]{:S(2)}, u32[]{:S(2)}) collective-permute-start(bf16[64,32,128]{2,1,0:T(8,128)(2,1)} %get-tuple-element.11), channel_id=1, source_target_pairs={{0,16},{8,24},{16,0},{24,8},{1,17},{9,25},{17,1},{25,9},{2,18},{10... | collective-permute-start | bytes 1572872 | tf_op jit(solution)/shard_map/ppermute | solution.py:112
  70.6 1.4 collective-permute-start.17
  72.8 0.2 broadcast_in_dim.39
  73.1 0.1 bitcast_dynamic-update-slice_fusion.2
  73.3 1.3 constant_dynamic-update-slice_fusion.1
  74.6 20.2 %collective-permute-done.16 = bf16[64,32,128]{2,1,0:T(8,128)(2,1)} collective-permute-done((bf16[64,32,128]{2,1,0:T(8,128)(2,1)}, bf16[64,32,128]{2,1,0:T(8,128)(2,1)}, u32[]{:S(2)}, u32[]{:S(2)}) %collective-permute-start.16) | collective-permute-done | bytes 524320 | tf_op jit(solution)/shard_map/ppermute | solution.py:112
  94.8 1.2 constant_dynamic-update-slice_fusion
  95.9 1.2 constant_dynamic-update-slice_fusion.2.a_ref
  97.2 2.2 %bitcast_add_fusion.1 = f32[4,64,1024]{2,1,0:T(8,128)S(1)} fusion(f32[4,64,1024]{2,1,0:T(8,128)} %collective-permute-done.7, f32[4,2,64,1024]{3,2,1,0:T(8,128)S(1)} %bitcast.72, s32[]{:T(128)S(6)} %select_n.86), kind=kLoop, calls=%fused_computation.6 | loop fusion | flops 262144 | bytes 3145732 | tf_op jit(solution)/shard_map/add | solution.py:83
  99.3 0.8 dynamic-slice_bitcast_fusion.10
  100.1 3.5 %collective-permute-start.10 = (f32[64,1024]{1,0:T(8,128)S(1)}, f32[64,1024]{1,0:T(8,128)S(1)}, u32[]{:S(2)}, u32[]{:S(2)}) collective-permute-start(f32[64,1024]{1,0:T(8,128)S(1)} %get-tuple-element.14), channel_id=1, source_target_pairs={{0,6},{1,7},{2,4},{3,5},{4,2},{5,3},{6,0},{7,1},{8,14},{9,15},{10,... | collective-permute-start | bytes 786440 | tf_op jit(solution)/shard_map/ppermute | solution.py:91
  103.7 0.8 collective-permute-start.9
  104.5 1.4 bitcast_add_fusion
  106.0 1.3 collective-permute-start.12
  107.2 2.9 %collective-permute-start.13 = (f32[64,1024]{1,0:T(8,128)S(1)}, f32[64,1024]{1,0:T(8,128)}, u32[]{:S(2)}, u32[]{:S(2)}) collective-permute-start(f32[64,1024]{1,0:T(8,128)S(1)} %get-tuple-element.18), channel_id=1, source_target_pairs={{0,4},{1,5},{2,6},{3,7},{4,0},{5,1},{6,2},{7,3},{8,12},{9,13},{10,... | collective-permute-start | bytes 786440 | tf_op jit(solution)/shard_map/ppermute | solution.py:91
  110.1 1.0 collective-permute-done.10
  111.2 0.7 copy-done.5
  111.8 3.5 %collective-permute-start.14 = (f32[64,1024]{1,0:T(8,128)S(1)}, f32[64,1024]{1,0:T(8,128)}, u32[]{:S(2)}, u32[]{:S(2)}) collective-permute-start(f32[64,1024]{1,0:T(8,128)S(1)} %get-tuple-element.17), channel_id=1, source_target_pairs={{0,6},{1,7},{2,4},{3,5},{4,2},{5,3},{6,0},{7,1},{8,14},{9,15},{10,... | collective-permute-start | bytes 786440 | tf_op jit(solution)/shard_map/ppermute | solution.py:91
  115.3 10.9 %shard_map.77 = bf16[128,32,128]{2,1,0:T(8,128)(2,1)} custom-call(s32[128]{0:T(128)} %rows_ref.1, s32[128]{0:T(128)} %cols_ref.1, s32[1]{0:T(128)S(6)} %copy.27.cnt_ref, bf16[64,32,512]{2,1,0:T(8,128)(2,1)} %copy-done, bf16[512,3584]{1,0:T(8,128)(2,1)} %constant_dynamic-update-slice_fusion.3.g_ref), custom_call_target="tpu_custom_call" | custom-call | flops 536870912 | bytes 6815744 | tf_op jit(solution)/shard_map/pallas_call | solution.py:54
  126.2 0.3 collective-permute-done.9
  126.6 1.1 fusion.9
  127.7 1.4 collective-permute-done.12
  129.1 14.2 %collective-permute-done.13 = f32[64,1024]{1,0:T(8,128)} collective-permute-done((f32[64,1024]{1,0:T(8,128)S(1)}, f32[64,1024]{1,0:T(8,128)}, u32[]{:S(2)}, u32[]{:S(2)}) %collective-permute-start.13) | collective-permute-done | bytes 262176 | tf_op jit(solution)/shard_map/ppermute | solution.py:91
  143.2 1.2 fusion.6
  144.4 0.7 pad_maximum_fusion
  (36 shorter events, 0.6 us)
Async XLA Ops:
  1.8 14.2 %collective-permute-start = (bf16[128,1024]{0,1:T(8,128)(2,1)S(1)}, bf16[128,1024]{0,1:T(8,128)(2,1)S(1)}, u32[]{:S(2)}, u32[]{:S(2)}) collective-permute-start(bf16[128,1024]{0,1:T(8,128)(2,1)S(1)} %copy.8), channel_id=1, source_target_pairs={{0,2},{1,3},{2,0},{3,1},{4,6},{5,7},{6,4},{7,5},{8,10},{9,11},{10,... | collective-permute-start | bytes 786440 | tf_op jit(solution)/shard_map/ppermute | solution.py:69
  4.8 21.4 %collective-permute-start.1 = (bf16[128,1024]{0,1:T(8,128)(2,1)S(1)}, bf16[128,1024]{0,1:T(8,128)(2,1)S(1)}, u32[]{:S(2)}, u32[]{:S(2)}) collective-permute-start(bf16[128,1024]{0,1:T(8,128)(2,1)S(1)} %copy.8), channel_id=1, source_target_pairs={{0,4},{1,5},{2,6},{3,7},{4,0},{5,1},{6,2},{7,3},{8,12},{9,13},{10,... | collective-permute-start | bytes 786440 | tf_op jit(solution)/shard_map/ppermute | solution.py:69
  7.4 18.8 %collective-permute-start.2 = (bf16[128,1024]{0,1:T(8,128)(2,1)S(1)}, bf16[128,1024]{0,1:T(8,128)(2,1)S(1)}, u32[]{:S(2)}, u32[]{:S(2)}) collective-permute-start(bf16[128,1024]{0,1:T(8,128)(2,1)S(1)} %copy.8), channel_id=1, source_target_pairs={{0,6},{1,7},{2,4},{3,5},{4,2},{5,3},{6,0},{7,1},{8,14},{9,15},{10,... | collective-permute-start | bytes 786440 | tf_op jit(solution)/shard_map/ppermute | solution.py:69
  7.4 23.6 %collective-permute-start.4 = (bf16[128,3584]{1,0:T(8,128)(2,1)}, bf16[128,3584]{1,0:T(8,128)(2,1)}, u32[]{:S(2)}, u32[]{:S(2)}) collective-permute-start(bf16[128,3584]{1,0:T(8,128)(2,1)} %param.7), channel_id=1, source_target_pairs={{0,8},{8,0},{16,24},{24,16},{1,9},{9,1},{17,25},{25,17},{2,10},{10... | collective-permute-start | bytes 2752520 | tf_op jit(solution)/shard_map/ppermute | solution.py:17
  9.1 41.0 %collective-permute-start.5 = (bf16[128,3584]{1,0:T(8,128)(2,1)}, bf16[128,3584]{1,0:T(8,128)(2,1)}, u32[]{:S(2)}, u32[]{:S(2)}) collective-permute-start(bf16[128,3584]{1,0:T(8,128)(2,1)} %param.7), channel_id=1, source_target_pairs={{0,16},{8,24},{16,0},{24,8},{1,17},{9,25},{17,1},{25,9},{2,18},{10... | collective-permute-start | bytes 2752520 | tf_op jit(solution)/shard_map/ppermute | solution.py:17
  16.0 36.3 %collective-permute-start.6 = (bf16[128,3584]{1,0:T(8,128)(2,1)}, bf16[128,3584]{1,0:T(8,128)(2,1)S(1)}, u32[]{:S(2)}, u32[]{:S(2)}) collective-permute-start(bf16[128,3584]{1,0:T(8,128)(2,1)} %param.7), channel_id=1, source_target_pairs={{0,24},{8,16},{16,8},{24,0},{1,25},{9,17},{17,9},{25,1},{2,26},{10... | collective-permute-start | bytes 2752520 | tf_op jit(solution)/shard_map/ppermute | solution.py:17
  26.3 27.0 %collective-permute-start.3 = (bf16[4,128,1024]{1,2,0:T(8,128)(2,1)S(1)}, bf16[4,128,1024]{1,2,0:T(8,128)(2,1)S(1)}, u32[]{:S(2)}, u32[]{:S(2)}) collective-permute-start(bf16[4,128,1024]{1,2,0:T(8,128)(2,1)S(1)} %bitcast_dynamic-update-slice_fusion.3), channel_id=1, source_target_pairs={{0,1},{1,0},{2,3},{3,2},{4,5},{5,4},{6,7},{7,6},{8,9},{9,8},{10,11... | collective-permute-start | bytes 3145736 | tf_op jit(solution)/shard_map/ppermute | solution.py:73
  26.4 28.4 %copy-start.7 = (bf16[2048,3584]{1,0:T(8,128)(2,1)S(1)}, bf16[2048,3584]{1,0:T(8,128)(2,1)}, u32[]{:S(2)}) copy-start(bf16[2048,3584]{1,0:T(8,128)(2,1)} %param.8) | copy-start | bytes 44040196
  54.8 18.5 %collective-permute-start.15 = (bf16[64,32,128]{2,1,0:T(8,128)(2,1)}, bf16[64,32,128]{2,1,0:T(8,128)(2,1)}, u32[]{:S(2)}, u32[]{:S(2)}) collective-permute-start(bf16[64,32,128]{2,1,0:T(8,128)(2,1)} %get-tuple-element.12), channel_id=1, source_target_pairs={{0,8},{8,0},{16,24},{24,16},{1,9},{9,1},{17,25},{25,17},{2,10},{10... | collective-permute-start | bytes 1572872 | tf_op jit(solution)/shard_map/ppermute | solution.py:112
  60.8 1.7 %copy-start.3 = (f32[512,1024]{1,0:T(8,128)}, f32[512,1024]{1,0:T(8,128)S(1)}, u32[]{:S(2)}) copy-start(f32[512,1024]{1,0:T(8,128)S(1)} %fusion.2) | copy-start | bytes 6291460
  62.5 34.7 %collective-permute-start.7 = (f32[4,64,1024]{2,1,0:T(8,128)}, f32[4,64,1024]{2,1,0:T(8,128)}, u32[]{:S(2)}, u32[]{:S(2)}) collective-permute-start(f32[4,64,1024]{2,1,0:T(8,128)} %dynamic-slice_bitcast_fusion.1), channel_id=1, source_target_pairs={{0,1},{1,0},{2,3},{3,2},{4,5},{5,4},{6,7},{7,6},{8,9},{9,8},{10,11... | collective-permute-start | bytes 3145736 | tf_op jit(solution)/shard_map/ppermute | solution.py:83
  68.5 3.6 %copy-start.1 = (f32[512,1024]{1,0:T(8,128)}, f32[512,1024]{1,0:T(8,128)S(1)}, u32[]{:S(2)}) copy-start(f32[512,1024]{1,0:T(8,128)S(1)} %fusion) | copy-start | bytes 6291460
  68.5 26.3 %collective-permute-start.16 = (bf16[64,32,128]{2,1,0:T(8,128)(2,1)}, bf16[64,32,128]{2,1,0:T(8,128)(2,1)}, u32[]{:S(2)}, u32[]{:S(2)}) collective-permute-start(bf16[64,32,128]{2,1,0:T(8,128)(2,1)} %get-tuple-element.11), channel_id=1, source_target_pairs={{0,16},{8,24},{16,0},{24,8},{1,17},{9,25},{17,1},{25,9},{2,18},{10... | collective-permute-start | bytes 1572872 | tf_op jit(solution)/shard_map/ppermute | solution.py:112
  70.6 25.3 %collective-permute-start.17 = (bf16[64,32,128]{2,1,0:T(8,128)(2,1)}, bf16[64,32,128]{2,1,0:T(8,128)(2,1)}, u32[]{:S(2)}, u32[]{:S(2)}) collective-permute-start(bf16[64,32,128]{2,1,0:T(8,128)(2,1)} %get-tuple-element.10), channel_id=1, source_target_pairs={{0,24},{8,16},{16,8},{24,0},{1,25},{9,17},{17,9},{25,1},{2,26},{10... | collective-permute-start | bytes 1572872 | tf_op jit(solution)/shard_map/ppermute | solution.py:112
  72.1 32.4 %collective-permute-start.11 = (f32[4,64,1024]{2,1,0:T(8,128)S(1)}, f32[4,64,1024]{2,1,0:T(8,128)}, u32[]{:S(2)}, u32[]{:S(2)}) collective-permute-start(f32[4,64,1024]{2,1,0:T(8,128)S(1)} %dynamic-slice_bitcast_fusion), channel_id=1, source_target_pairs={{0,1},{1,0},{2,3},{3,2},{4,5},{5,4},{6,7},{7,6},{8,9},{9,8},{10,11... | collective-permute-start | bytes 3145736 | tf_op jit(solution)/shard_map/ppermute | solution.py:83
  73.1 24.1 %copy-start.4 = (f32[512,1024]{1,0:T(8,128)S(1)}, f32[512,1024]{1,0:T(8,128)}, u32[]{:S(2)}) copy-start(f32[512,1024]{1,0:T(8,128)} %copy-done.3) | copy-start | bytes 6291460
  97.1 3.0 %copy-start = (bf16[64,32,512]{2,1,0:T(8,128)(2,1)}, bf16[64,32,512]{2,1,0:T(8,128)(2,1)S(1)}, u32[]{:S(2)}) copy-start(bf16[64,32,512]{2,1,0:T(8,128)(2,1)S(1)} %constant_dynamic-update-slice_fusion.2.a_ref) | copy-start | bytes 6291460
  97.1 7.4 %copy-start.2 = (f32[512,1024]{1,0:T(8,128)S(1)}, f32[512,1024]{1,0:T(8,128)}, u32[]{:S(2)}) copy-start(f32[512,1024]{1,0:T(8,128)} %copy-done.1) | copy-start | bytes 6291460
  100.1 11.0 %collective-permute-start.10 = (f32[64,1024]{1,0:T(8,128)S(1)}, f32[64,1024]{1,0:T(8,128)S(1)}, u32[]{:S(2)}, u32[]{:S(2)}) collective-permute-start(f32[64,1024]{1,0:T(8,128)S(1)} %get-tuple-element.14), channel_id=1, source_target_pairs={{0,6},{1,7},{2,4},{3,5},{4,2},{5,3},{6,0},{7,1},{8,14},{9,15},{10,... | collective-permute-start | bytes 786440 | tf_op jit(solution)/shard_map/ppermute | solution.py:91
  103.7 22.6 %collective-permute-start.8 = (f32[64,1024]{1,0:T(8,128)}, f32[64,1024]{1,0:T(8,128)}, u32[]{:S(2)}, u32[]{:S(2)}) collective-permute-start(f32[64,1024]{1,0:T(8,128)} %get-tuple-element.13), channel_id=1, source_target_pairs={{0,2},{1,3},{2,0},{3,1},{4,6},{5,7},{6,4},{7,5},{8,10},{9,11},{10,... | collective-permute-start | bytes 786440 | tf_op jit(solution)/shard_map/ppermute | solution.py:91
  103.7 22.9 %collective-permute-start.9 = (f32[64,1024]{1,0:T(8,128)S(1)}, f32[64,1024]{1,0:T(8,128)}, u32[]{:S(2)}, u32[]{:S(2)}) collective-permute-start(f32[64,1024]{1,0:T(8,128)S(1)} %get-tuple-element.15), channel_id=1, source_target_pairs={{0,4},{1,5},{2,6},{3,7},{4,0},{5,1},{6,2},{7,3},{8,12},{9,13},{10,... | collective-permute-start | bytes 786440 | tf_op jit(solution)/shard_map/ppermute | solution.py:91
  106.0 23.1 %collective-permute-start.12 = (f32[64,1024]{1,0:T(8,128)S(1)}, f32[64,1024]{1,0:T(8,128)}, u32[]{:S(2)}, u32[]{:S(2)}) collective-permute-start(f32[64,1024]{1,0:T(8,128)S(1)} %get-tuple-element.16), channel_id=1, source_target_pairs={{0,2},{1,3},{2,0},{3,1},{4,6},{5,7},{6,4},{7,5},{8,10},{9,11},{10,... | collective-permute-start | bytes 786440 | tf_op jit(solution)/shard_map/ppermute | solution.py:91
  107.2 36.0 %collective-permute-start.13 = (f32[64,1024]{1,0:T(8,128)S(1)}, f32[64,1024]{1,0:T(8,128)}, u32[]{:S(2)}, u32[]{:S(2)}) collective-permute-start(f32[64,1024]{1,0:T(8,128)S(1)} %get-tuple-element.18), channel_id=1, source_target_pairs={{0,4},{1,5},{2,6},{3,7},{4,0},{5,1},{6,2},{7,3},{8,12},{9,13},{10,... | collective-permute-start | bytes 786440 | tf_op jit(solution)/shard_map/ppermute | solution.py:91
  111.2 0.7 copy-start.5
  111.8 14.7 %copy-start.6 = (f32[64,1024]{1,0:T(8,128)S(1)}, f32[64,1024]{1,0:T(8,128)}, u32[]{:S(2)}) copy-start(f32[64,1024]{1,0:T(8,128)} %copy-done.5) | copy-start | bytes 786436
  111.8 31.4 %collective-permute-start.14 = (f32[64,1024]{1,0:T(8,128)S(1)}, f32[64,1024]{1,0:T(8,128)}, u32[]{:S(2)}, u32[]{:S(2)}) collective-permute-start(f32[64,1024]{1,0:T(8,128)S(1)} %get-tuple-element.17), channel_id=1, source_target_pairs={{0,6},{1,7},{2,4},{3,5},{4,2},{5,3},{6,0},{7,1},{8,14},{9,15},{10,... | collective-permute-start | bytes 786440 | tf_op jit(solution)/shard_map/ppermute | solution.py:91

commit v11 on v9

--- a/solution.py
+++ b/solution.py
@@ -9,7 +9,6 @@
 
 BLK = 128
 SLOTS_PER_STEP = 8
-F_CHUNKS = 2
 
 
 def xor_exchange(x, axis_name, n):
@@ -112,21 +111,22 @@
     row_blocks = full_acts.shape[1] // BLK
     acts_pieces = jnp.transpose(full_acts.reshape(tok_dev, row_blocks, n_tok, sub), (2, 1, 3, 0))
 
-    f_chunk = grad_out.shape[1] // F_CHUNKS
+    units = grad_out.shape[1] // BLK
+    last = units // 7
+    sizes = [(units - 3 * last) * BLK, 2 * last * BLK, last * BLK]
     gathered = []
-    partial_sums = None
-    for k in range(F_CHUNKS):
-        cols = slice(k * f_chunk, (k + 1) * f_chunk)
-        piece = grad_out[:, cols]
+    start = 0
+    for size in sizes:
+        piece = grad_out[:, start : start + size]
         if gathered:
             piece, gathered[-1] = lax.optimization_barrier((piece, gathered[-1]))
         gathered.append(place_rows(xor_exchange(piece, "tok", n_tok), me))
-    for k in range(F_CHUNKS - 1):
-        partial_sums = matmul_nt(gathered[k], weight, k, partial_sums)
-    last = slice((F_CHUNKS - 1) * f_chunk, F_CHUNKS * f_chunk)
-    partial_sums = partial_sums + lax.dot_general(
-        gathered[-1], weight[:, last], (((1,), (1,)), ((), ())), preferred_element_type=jnp.float32
-    )
+        start += size
+    partial_sums = None
+    start = 0
+    for size, g in zip(sizes, gathered):
+        partial_sums = matmul_nt(g, weight, start // size, partial_sums)
+        start += size
     gout = jnp.concatenate(gathered, axis=1)
     grad_in = lax.psum_scatter(partial_sums, "feat", scatter_dimension=0, tiled=True).astype(
         jnp.bfloat16

time: 127 us -> 132 us (1.039)
  Pallas kernels: 19.6 us -> 34.5 us
  matrix products: 6.95 us -> 0 us
  waiting for transfers between devices: 49.2 us -> 44.4 us
  starting transfers between devices: 11.6 us -> 15.1 us
  other arithmetic: 8.01 us -> 4.64 us
  local copies, waits for them, and re-layouts: 15.8 us -> 18 us
    pallas_call x1 -> x3, Pallas kernels: 8.59 us -> 23.5 us  [matmul_nt(): pl.pallas_call(matmul_kernel, grid=(cols // tile,), in_specs=in_specs, ou...]
    dot_general x1 -> x0, matrix products: 6.95 us -> none  [per_device(): lax.dot_general(gathered[-1], weight[:, last], (((1,), (1,)), ((), ())),...]
    ppermute x6 -> x9, waiting for transfers between devices: 28.4 us -> 22.3 us  [xor_exchange(): out.append(lax.ppermute(x, axis_name, perm=[(a, a ^ m) for a in range(n)]))]
    ppermute x6 -> x9, starting transfers between devices: 8.01 us -> 11.6 us  [xor_exchange(): out.append(lax.ppermute(x, axis_name, perm=[(a, a ^ m) for a in range(n)]))]
    add x1 -> x0, other arithmetic: 2.71 us -> none  [per_device(): partial_sums + lax.dot_general(gathered[-1], weight[:, last], (((1,), (1,...]
    dynamic_update_slice x11 -> x15, local copies, waits for them, and re-layouts: 7 us -> 8.13 us  [place_rows(): out = lax.dynamic_update_slice_in_dim(out, piece, (me ^ m) * rows, axis)]
    unnamed x13 -> x15, local copies, waits for them, and re-layouts: 4.72 us -> 5.84 us
  transfers between devices with their start and end apart: 11 -> 14, of which waited for: 7 -> 5; matrix products, arithmetic and copies ran while one was open for 19% -> 11% of each run, Pallas kernels for 16% -> 26%
where the time goes in v11:
time: 132 us
  waiting for transfers between devices  44.4 us (34%)
  Pallas kernels  34.5 us (26%)
  local copies, waits for them, and re-layouts  18 us (14%)
  starting transfers between devices  15.1 us (11%)
  between operations  15 us (11%)
  other arithmetic  4.64 us (4%)
    pallas_call x3, Pallas kernels, matmul_nt(): pl.pallas_call(matmul_kernel, grid=(cols // tile,), in_specs=in_specs, ou...  23.5 us
    ppermute x9, waiting for transfers between devices, xor_exchange(): out.append(lax.ppermute(x, axis_name, perm=[(a, a ^ m) for a in range(n)]))  22.3 us
    ppermute x3, waiting for transfers between devices, per_device(): part = lax.ppermute(part, 'tok', perm=[(a, a ^ m) for a in range(n_tok)])  15.5 us
    ppermute x9, starting transfers between devices, xor_exchange(): out.append(lax.ppermute(x, axis_name, perm=[(a, a ^ m) for a in range(n)]))  11.6 us
    pallas_call x1, Pallas kernels, block_tiles(): pl.pallas_call(block_kernel, grid_spec=grid_spec, out_shape=jax.ShapeDtyp...  11 us
    dynamic_update_slice x15, local copies, waits for them, and re-layouts, place_rows(): out = lax.dynamic_update_slice_in_dim(out, piece, (me ^ m) * rows, axis)  8.13 us
    reduce_scatter x1, waiting for transfers between devices, per_device(): lax.psum_scatter(partial_sums, 'feat', scatter_dimension=0, tiled=True)  6.58 us
    unnamed x15, local copies, waits for them, and re-layouts  5.84 us
  transfers between devices with their start and end apart: 14, of which 5 were waited for; matrix products, arithmetic and copies ran while one was open for 11% of the time, Pallas kernels for 26%

profile of v11, /device:TPU:0, one launch (start us, length us, event | category | flops | bytes accessed | tf_op | source)
XLA Modules:
  0.0 131.7 jit_solution(16293645988762438898)
XLA Ops:
  7.2 0.0 all-gather.2.cloned.1.call-start
  7.2 1.9 %copy.9 = bf16[128,1024]{0,1:T(8,128)(2,1)} copy(bf16[128,1024]{1,0:T(8,128)(2,1)} %param.6) | data formatting | bytes 524288 | tf_op args[0]
  9.1 0.0 all-gather.2.cloned.1.call-update
  9.1 0.0 reduce-scatter.2.cloned.1.call-start
  9.2 0.2 broadcast_in_dim.14
  9.4 0.9 fusion
  10.3 2.9 %collective-permute-start = (bf16[128,2048]{1,0:T(8,128)(2,1)}, bf16[128,2048]{1,0:T(8,128)(2,1)}, u32[]{:S(2)}, u32[]{:S(2)}) collective-permute-start(bf16[128,2048]{1,0:T(8,128)(2,1)} %get-tuple-element.17), channel_id=1, source_target_pairs={{0,8},{8,0},{16,24},{24,16},{1,9},{9,1},{17,25},{25,17},{2,10},{10... | collective-permute-start | bytes 1572872 | tf_op jit(solution)/shard_map/ppermute | solution.py:17
  13.3 1.5 %collective-permute-start.1 = (bf16[128,2048]{1,0:T(8,128)(2,1)}, bf16[128,2048]{1,0:T(8,128)(2,1)}, u32[]{:S(2)}, u32[]{:S(2)}) collective-permute-start(bf16[128,2048]{1,0:T(8,128)(2,1)} %get-tuple-element.17), channel_id=1, source_target_pairs={{0,16},{8,24},{16,0},{24,8},{1,17},{9,25},{17,1},{25,9},{2,18},{10... | collective-permute-start | bytes 1572872 | tf_op jit(solution)/shard_map/ppermute | solution.py:17
  14.8 0.0 collective-permute-start.2
  14.9 11.5 %collective-permute-done = bf16[128,2048]{1,0:T(8,128)(2,1)} collective-permute-done((bf16[128,2048]{1,0:T(8,128)(2,1)}, bf16[128,2048]{1,0:T(8,128)(2,1)}, u32[]{:S(2)}, u32[]{:S(2)}) %collective-permute-start) | collective-permute-done | bytes 524320 | tf_op jit(solution)/shard_map/ppermute | solution.py:17
  26.4 1.1 constant_dynamic-update-slice_fusion.13
  27.4 10.8 %collective-permute-done.1 = bf16[128,2048]{1,0:T(8,128)(2,1)} collective-permute-done((bf16[128,2048]{1,0:T(8,128)(2,1)}, bf16[128,2048]{1,0:T(8,128)(2,1)}, u32[]{:S(2)}, u32[]{:S(2)}) %collective-permute-start.1) | collective-permute-done | bytes 524320 | tf_op jit(solution)/shard_map/ppermute | solution.py:17
  38.2 1.1 constant_dynamic-update-slice_fusion.12
  39.3 1.1 constant_dynamic-update-slice_fusion.11.refs_0_
  40.4 0.2 collective-permute-start.3
  40.6 1.9 %collective-permute-start.4 = (bf16[128,1024]{1,0:T(8,128)(2,1)S(1)}, bf16[128,1024]{1,0:T(8,128)(2,1)S(1)}, u32[]{:S(2)}, u32[]{:S(2)}) collective-permute-start(bf16[128,1024]{1,0:T(8,128)(2,1)S(1)} %slice.10), channel_id=1, source_target_pairs={{0,16},{8,24},{16,0},{24,8},{1,17},{9,25},{17,1},{25,9},{2,18},{10... | collective-permute-start | bytes 786440 | tf_op jit(solution)/shard_map/ppermute | solution.py:17
  42.6 1.4 %collective-permute-start.5 = (bf16[128,1024]{1,0:T(8,128)(2,1)S(1)}, bf16[128,1024]{1,0:T(8,128)(2,1)S(1)}, u32[]{:S(2)}, u32[]{:S(2)}) collective-permute-start(bf16[128,1024]{1,0:T(8,128)(2,1)S(1)} %slice.10), channel_id=1, source_target_pairs={{0,24},{8,16},{16,8},{24,0},{1,25},{9,17},{17,9},{25,1},{2,26},{10... | collective-permute-start | bytes 786440 | tf_op jit(solution)/shard_map/ppermute | solution.py:17
  44.0 9.3 %shard_map.77.refs_2_ = f32[512,2048]{1,0:T(8,128)} custom-call(bf16[512,2048]{1,0:T(8,128)(2,1)} %copy-done, bf16[2048,3584]{1,0:T(8,128)(2,1)} %refs_1_.5), custom_call_target="tpu_custom_call" | custom-call | flops 4294967296 | bytes 14680064 | tf_op jit(solution)/shard_map/pallas_call | solution.py:91
  53.2 0.1 broadcast_in_dim.13
  53.4 0.0 collective-permute-done.3
  53.4 0.0 collective-permute-done.4
  53.5 0.0 copy-start.2
  53.5 0.3 collective-permute-start.6
  53.9 2.1 %collective-permute-start.7 = (bf16[128,512]{1,0:T(8,128)(2,1)S(1)}, bf16[128,512]{1,0:T(8,128)(2,1)S(1)}, u32[]{:S(2)}, u32[]{:S(2)}) collective-permute-start(bf16[128,512]{1,0:T(8,128)(2,1)S(1)} %slice.9), channel_id=1, source_target_pairs={{0,16},{8,24},{16,0},{24,8},{1,17},{9,25},{17,1},{25,9},{2,18},{10... | collective-permute-start | bytes 393224 | tf_op jit(solution)/shard_map/ppermute | solution.py:17
  56.0 1.1 collective-permute-start.8
  57.1 7.9 %shard_map.78.refs_2_ = f32[512,2048]{1,0:T(8,128)} custom-call(bf16[512,1024]{1,0:T(8,128)(2,1)} %copy-done.2, bf16[2048,3584]{1,0:T(8,128)(2,1)} %refs_1_.5, f32[512,2048]{1,0:T(8,128)} %shard_map.77.refs_2_), custom_call_target="tpu_custom_call" | custom-call | flops 2147483648 | bytes 13631488 | tf_op jit(solution)/shard_map/pallas_call | solution.py:91
  65.2 0.8 copy-done.5
  65.9 6.4 %shard_map.79 = f32[512,2048]{1,0:T(8,128)} custom-call(bf16[512,512]{1,0:T(8,128)(2,1)} %copy-done.5, bf16[2048,3584]{1,0:T(8,128)(2,1)} %refs_1_.5, f32[512,2048]{1,0:T(8,128)} %shard_map.78.refs_2_), custom_call_target="tpu_custom_call" | custom-call | flops 1073741824 | bytes 11010048 | tf_op jit(solution)/shard_map/pallas_call | solution.py:91
  72.3 0.0 reduce-scatter.2.cloned.1.call-update
  72.4 1.5 %copy-done.1 = bf16[512,2048]{1,0:T(8,128)(2,1)S(1)} copy-done((bf16[512,2048]{1,0:T(8,128)(2,1)S(1)}, bf16[512,2048]{1,0:T(8,128)(2,1)}, u32[]{:S(2)}) %copy-start.1) | copy-done | bytes 2097176
  73.9 0.3 copy-done.3
  74.2 2.9 %pad_maximum_fusion.g_ref = bf16[512,3584]{1,0:T(8,128)(2,1)} fusion(bf16[512,512]{1,0:T(8,128)(2,1)} %copy-done.5, bf16[512,1024]{1,0:T(8,128)(2,1)S(1)} %copy-done.3, bf16[512,2048]{1,0:T(8,128)(2,1)S(1)} %copy-done.1), kind=kLoop, calls=%fused_computation | loop fusion | flops 11010048 | bytes 7340032 | tf_op jit(solution)/shard_map/concatenate | solution.py:130
  77.1 2.4 %dynamic-slice_bitcast_fusion = (bf16[64,32,128]{2,1,0:T(8,128)(2,1)S(1)}, bf16[64,32,128]{2,1,0:T(8,128)(2,1)S(1)}, bf16[64,32,128]{2,1,0:T(8,128)(2,1)}) fusion(bf16[4,64,32,128]{3,2,0,1:T(8,128)(2,1)} %bitcast.11, s32[]{:T(128)S(6)} %select_n.44, s32[]{:T(128)S(6)} %select_n.43, s32[]{:T(128)S(6)} %select_n.42), kind=kLoop, calls=%fused_computation.2 | loop fusion | bytes 3145740 | tf_op jit(solution)/shard_map/jit(dynamic_index_in_dim)/squeeze | solution.py:138
  79.5 0.3 collective-permute-start.9
  79.8 2.0 %collective-permute-start.10 = (bf16[64,32,128]{2,1,0:T(8,128)(2,1)S(1)}, bf16[64,32,128]{2,1,0:T(8,128)(2,1)}, u32[]{:S(2)}, u32[]{:S(2)}) collective-permute-start(bf16[64,32,128]{2,1,0:T(8,128)(2,1)S(1)} %get-tuple-element.15), channel_id=1, source_target_pairs={{0,16},{8,24},{16,0},{24,8},{1,17},{9,25},{17,1},{25,9},{2,18},{10... | collective-permute-start | bytes 1572872 | tf_op jit(solution)/shard_map/ppermute | solution.py:140
  81.8 1.1 collective-permute-start.11
  83.6 0.2 broadcast_in_dim.15
  83.9 1.2 bitcast_dynamic-update-slice_fusion
  85.1 9.6 %collective-permute-done.9 = bf16[64,32,128]{2,1,0:T(8,128)(2,1)} collective-permute-done((bf16[64,32,128]{2,1,0:T(8,128)(2,1)}, bf16[64,32,128]{2,1,0:T(8,128)(2,1)}, u32[]{:S(2)}, u32[]{:S(2)}) %collective-permute-start.9) | collective-permute-done | bytes 524320 | tf_op jit(solution)/shard_map/ppermute | solution.py:140
  94.7 1.2 constant_dynamic-update-slice_fusion.1
  95.8 6.0 %collective-permute-done.10 = bf16[64,32,128]{2,1,0:T(8,128)(2,1)} collective-permute-done((bf16[64,32,128]{2,1,0:T(8,128)(2,1)S(1)}, bf16[64,32,128]{2,1,0:T(8,128)(2,1)}, u32[]{:S(2)}, u32[]{:S(2)}) %collective-permute-start.10) | collective-permute-done | bytes 524320 | tf_op jit(solution)/shard_map/ppermute | solution.py:140
  101.8 1.2 constant_dynamic-update-slice_fusion
  103.0 0.0 collective-permute-done.11
  103.0 1.2 constant_dynamic-update-slice_fusion.2.a_ref
  104.2 1.4 %copy-done.4 = bf16[64,32,512]{2,1,0:T(8,128)(2,1)} copy-done((bf16[64,32,512]{2,1,0:T(8,128)(2,1)}, bf16[64,32,512]{2,1,0:T(8,128)(2,1)S(1)}, u32[]{:S(2)}) %copy-start.4) | copy-done | bytes 2097176
  105.6 11.0 %shard_map.80 = bf16[128,32,128]{2,1,0:T(8,128)(2,1)} custom-call(s32[128]{0:T(128)} %rows_ref.1, s32[128]{0:T(128)} %cols_ref.1, s32[1]{0:T(128)S(6)} %copy.26.cnt_ref, bf16[64,32,512]{2,1,0:T(8,128)(2,1)} %copy-done.4, bf16[512,3584]{1,0:T(8,128)(2,1)} %pad_maximum_fusion.g_ref), custom_call_target="tpu_custom_call" | custom-call | flops 536870912 | bytes 6815744 | tf_op jit(solution)/shard_map/pallas_call | solution.py:54
  116.5 6.6 %reduce-scatter.2.cloned.1.call-done = f32[64,2048]{1,0:T(8,128)} async-done(((f32[512,2048]{1,0:T(8,128)}), f32[64,2048]{1,0:T(8,128)}) %reduce-scatter.2.cloned.1.call-update) | async-done | bytes 524304 | tf_op jit(solution)/shard_map/reduce_scatter | solution.py:131
  123.1 1.8 %convert_element_type.3 = bf16[64,2048]{1,0:T(8,128)(2,1)} convert(f32[64,2048]{1,0:T(8,128)} %reduce-scatter.2.cloned.1.call-done) | non-fusion elementwise | flops 131072 | bytes 786432 | tf_op jit(solution)/shard_map/convert_element_type | solution.py:131
  (26 shorter events, 0.3 us)
Async XLA Ops:
  7.2 2.3 %copy-start.6 = (bf16[128,3584]{1,0:T(8,128)(2,1)S(1)}, bf16[128,3584]{1,0:T(8,128)(2,1)}, u32[]{:S(2)}) copy-start(bf16[128,3584]{1,0:T(8,128)(2,1)} %param.7) | copy-start | bytes 2752516
  7.2 69.9 %all-gather.2.cloned.1.call-start = ((), (), s32[]{:S(2)}) async-start(), calls=%async_computation.2 | async-start | bytes 2359296 | tf_op jit(solution)/shard_map/all_gather | solution.py:110
  9.1 114.0 %reduce-scatter.2.cloned.1.call-start = ((), (), s32[]{:S(2)}) async-start(), calls=%async_computation.1 | async-start | bytes 4718592 | tf_op jit(solution)/shard_map/reduce_scatter | solution.py:131
  10.3 16.0 %collective-permute-start = (bf16[128,2048]{1,0:T(8,128)(2,1)}, bf16[128,2048]{1,0:T(8,128)(2,1)}, u32[]{:S(2)}, u32[]{:S(2)}) collective-permute-start(bf16[128,2048]{1,0:T(8,128)(2,1)} %get-tuple-element.17), channel_id=1, source_target_pairs={{0,8},{8,0},{16,24},{24,16},{1,9},{9,1},{17,25},{25,17},{2,10},{10... | collective-permute-start | bytes 1572872 | tf_op jit(solution)/shard_map/ppermute | solution.py:17
  13.3 24.9 %collective-permute-start.1 = (bf16[128,2048]{1,0:T(8,128)(2,1)}, bf16[128,2048]{1,0:T(8,128)(2,1)}, u32[]{:S(2)}, u32[]{:S(2)}) collective-permute-start(bf16[128,2048]{1,0:T(8,128)(2,1)} %get-tuple-element.17), channel_id=1, source_target_pairs={{0,16},{8,24},{16,0},{24,8},{1,17},{9,25},{17,1},{25,9},{2,18},{10... | collective-permute-start | bytes 1572872 | tf_op jit(solution)/shard_map/ppermute | solution.py:17
  14.8 24.5 %collective-permute-start.2 = (bf16[128,2048]{1,0:T(8,128)(2,1)}, bf16[128,2048]{1,0:T(8,128)(2,1)}, u32[]{:S(2)}, u32[]{:S(2)}) collective-permute-start(bf16[128,2048]{1,0:T(8,128)(2,1)} %get-tuple-element.17), channel_id=1, source_target_pairs={{0,24},{8,16},{16,8},{24,0},{1,25},{9,17},{17,9},{25,1},{2,26},{10... | collective-permute-start | bytes 1572872 | tf_op jit(solution)/shard_map/ppermute | solution.py:17
  40.4 3.6 %copy-start = (bf16[512,2048]{1,0:T(8,128)(2,1)}, bf16[512,2048]{1,0:T(8,128)(2,1)S(1)}, u32[]{:S(2)}) copy-start(bf16[512,2048]{1,0:T(8,128)(2,1)S(1)} %constant_dynamic-update-slice_fusion.11.refs_0_) | copy-start | bytes 6291460
  40.4 13.0 %collective-permute-start.3 = (bf16[128,1024]{1,0:T(8,128)(2,1)S(1)}, bf16[128,1024]{1,0:T(8,128)(2,1)S(1)}, u32[]{:S(2)}, u32[]{:S(2)}) collective-permute-start(bf16[128,1024]{1,0:T(8,128)(2,1)S(1)} %slice.10), channel_id=1, source_target_pairs={{0,8},{8,0},{16,24},{24,16},{1,9},{9,1},{17,25},{25,17},{2,10},{10... | collective-permute-start | bytes 786440 | tf_op jit(solution)/shard_map/ppermute | solution.py:17
  40.6 12.8 %collective-permute-start.4 = (bf16[128,1024]{1,0:T(8,128)(2,1)S(1)}, bf16[128,1024]{1,0:T(8,128)(2,1)S(1)}, u32[]{:S(2)}, u32[]{:S(2)}) collective-permute-start(bf16[128,1024]{1,0:T(8,128)(2,1)S(1)} %slice.10), channel_id=1, source_target_pairs={{0,16},{8,24},{16,0},{24,8},{1,17},{9,25},{17,1},{25,9},{2,18},{10... | collective-permute-start | bytes 786440 | tf_op jit(solution)/shard_map/ppermute | solution.py:17
  42.6 10.9 %collective-permute-start.5 = (bf16[128,1024]{1,0:T(8,128)(2,1)S(1)}, bf16[128,1024]{1,0:T(8,128)(2,1)S(1)}, u32[]{:S(2)}, u32[]{:S(2)}) collective-permute-start(bf16[128,1024]{1,0:T(8,128)(2,1)S(1)} %slice.10), channel_id=1, source_target_pairs={{0,24},{8,16},{16,8},{24,0},{1,25},{9,17},{17,9},{25,1},{2,26},{10... | collective-permute-start | bytes 786440 | tf_op jit(solution)/shard_map/ppermute | solution.py:17
  53.5 3.6 %copy-start.2 = (bf16[512,1024]{1,0:T(8,128)(2,1)}, bf16[512,1024]{1,0:T(8,128)(2,1)S(1)}, u32[]{:S(2)}) copy-start(bf16[512,1024]{1,0:T(8,128)(2,1)S(1)} %constant_dynamic-update-slice_fusion.7.refs_0_) | copy-start | bytes 3145732
  53.5 11.5 %collective-permute-start.6 = (bf16[128,512]{1,0:T(8,128)(2,1)S(1)}, bf16[128,512]{1,0:T(8,128)(2,1)S(1)}, u32[]{:S(2)}, u32[]{:S(2)}) collective-permute-start(bf16[128,512]{1,0:T(8,128)(2,1)S(1)} %slice.9), channel_id=1, source_target_pairs={{0,8},{8,0},{16,24},{24,16},{1,9},{9,1},{17,25},{25,17},{2,10},{10... | collective-permute-start | bytes 393224 | tf_op jit(solution)/shard_map/ppermute | solution.py:17
  53.9 11.2 %collective-permute-start.7 = (bf16[128,512]{1,0:T(8,128)(2,1)S(1)}, bf16[128,512]{1,0:T(8,128)(2,1)S(1)}, u32[]{:S(2)}, u32[]{:S(2)}) collective-permute-start(bf16[128,512]{1,0:T(8,128)(2,1)S(1)} %slice.9), channel_id=1, source_target_pairs={{0,16},{8,24},{16,0},{24,8},{1,17},{9,25},{17,1},{25,9},{2,18},{10... | collective-permute-start | bytes 393224 | tf_op jit(solution)/shard_map/ppermute | solution.py:17
  56.0 9.2 %collective-permute-start.8 = (bf16[128,512]{1,0:T(8,128)(2,1)S(1)}, bf16[128,512]{1,0:T(8,128)(2,1)S(1)}, u32[]{:S(2)}, u32[]{:S(2)}) collective-permute-start(bf16[128,512]{1,0:T(8,128)(2,1)S(1)} %slice.9), channel_id=1, source_target_pairs={{0,24},{8,16},{16,8},{24,0},{1,25},{9,17},{17,9},{25,1},{2,26},{10... | collective-permute-start | bytes 393224 | tf_op jit(solution)/shard_map/ppermute | solution.py:17
  65.1 0.8 copy-start.5
  72.3 1.6 %copy-start.1 = (bf16[512,2048]{1,0:T(8,128)(2,1)S(1)}, bf16[512,2048]{1,0:T(8,128)(2,1)}, u32[]{:S(2)}) copy-start(bf16[512,2048]{1,0:T(8,128)(2,1)} %copy-done) | copy-start | bytes 6291460
  72.3 1.9 %copy-start.3 = (bf16[512,1024]{1,0:T(8,128)(2,1)S(1)}, bf16[512,1024]{1,0:T(8,128)(2,1)}, u32[]{:S(2)}) copy-start(bf16[512,1024]{1,0:T(8,128)(2,1)} %copy-done.2) | copy-start | bytes 3145732
  79.5 15.2 %collective-permute-start.9 = (bf16[64,32,128]{2,1,0:T(8,128)(2,1)}, bf16[64,32,128]{2,1,0:T(8,128)(2,1)}, u32[]{:S(2)}, u32[]{:S(2)}) collective-permute-start(bf16[64,32,128]{2,1,0:T(8,128)(2,1)} %get-tuple-element.16), channel_id=1, source_target_pairs={{0,8},{8,0},{16,24},{24,16},{1,9},{9,1},{17,25},{25,17},{2,10},{10... | collective-permute-start | bytes 1572872 | tf_op jit(solution)/shard_map/ppermute | solution.py:140
  79.8 22.0 %collective-permute-start.10 = (bf16[64,32,128]{2,1,0:T(8,128)(2,1)S(1)}, bf16[64,32,128]{2,1,0:T(8,128)(2,1)}, u32[]{:S(2)}, u32[]{:S(2)}) collective-permute-start(bf16[64,32,128]{2,1,0:T(8,128)(2,1)S(1)} %get-tuple-element.15), channel_id=1, source_target_pairs={{0,16},{8,24},{16,0},{24,8},{1,17},{9,25},{17,1},{25,9},{2,18},{10... | collective-permute-start | bytes 1572872 | tf_op jit(solution)/shard_map/ppermute | solution.py:140
  81.8 21.1 %collective-permute-start.11 = (bf16[64,32,128]{2,1,0:T(8,128)(2,1)S(1)}, bf16[64,32,128]{2,1,0:T(8,128)(2,1)}, u32[]{:S(2)}, u32[]{:S(2)}) collective-permute-start(bf16[64,32,128]{2,1,0:T(8,128)(2,1)S(1)} %get-tuple-element.14), channel_id=1, source_target_pairs={{0,24},{8,16},{16,8},{24,0},{1,25},{9,17},{17,9},{25,1},{2,26},{10... | collective-permute-start | bytes 1572872 | tf_op jit(solution)/shard_map/ppermute | solution.py:140
  104.2 1.4 %copy-start.4 = (bf16[64,32,512]{2,1,0:T(8,128)(2,1)}, bf16[64,32,512]{2,1,0:T(8,128)(2,1)S(1)}, u32[]{:S(2)}) copy-start(bf16[64,32,512]{2,1,0:T(8,128)(2,1)S(1)} %constant_dynamic-update-slice_fusion.2.a_ref) | copy-start | bytes 6291460
Sparse Core Ops, SparseCore 0:
  10.2 31.7 all-gather.1
  72.5 50.5 reduce-scatter.1

commit v12 on v4

--- a/solution.py
+++ b/solution.py
@@ -72,10 +72,15 @@
     row_blocks = full_acts.shape[1] // BLK
     acts_pieces = jnp.transpose(full_acts.reshape(tok_dev, row_blocks, n_tok, sub), (2, 1, 3, 0))
 
-    gout = place_rows(xor_exchange(grad_out, "tok", n_tok), me)
-    partial_sums = lax.dot_general(
-        gout, weight, (((1,), (1,)), ((), ())), preferred_element_type=jnp.float32
-    )
+    pieces = xor_exchange(grad_out, "tok", n_tok)
+    gout = place_rows(pieces, me)
+
+    def nt(x):
+        return lax.dot_general(x, weight, (((1,), (1,)), ((), ())), preferred_element_type=jnp.float32)
+
+    own = nt(grad_out)
+    rest = nt(jnp.concatenate(pieces[1:], axis=0)).reshape(n_tok - 1, tok_dev, -1)
+    partial_sums = place_rows([own] + [rest[m] for m in range(n_tok - 1)], me)
     grad_in = lax.psum_scatter(partial_sums, "feat", scatter_dimension=0, tiled=True).astype(
         jnp.bfloat16
     )

time: 126 us -> 124 us (0.984)
  waiting for transfers between devices: 63.2 us -> 44.2 us
  local copies, waits for them, and re-layouts: 14.1 us -> 23.5 us
  matrix products: 12.4 us -> 20.2 us
    ppermute x3, waiting for transfers between devices: 36.6 us -> 24.9 us  [xor_exchange(): out.append(lax.ppermute(x, axis_name, perm=[(a, a ^ m) for a in range(n)]))]
    dot_general x1 -> x2, matrix products: 12.4 us -> 20.2 us  [nt(): lax.dot_general(x, weight, (((1,), (1,)), ((), ())), preferred_element_ty...]
    reduce_scatter x1, waiting for transfers between devices: 8.25 us -> 0.57 us  [per_device(): lax.psum_scatter(partial_sums, 'feat', scatter_dimension=0, tiled=True)]
    dynamic_update_slice x8 -> x11, local copies, waits for them, and re-layouts: 6.24 us -> 13.1 us  [place_rows(): out = lax.dynamic_update_slice_in_dim(out, piece, (me ^ m) * rows, axis)]
    broadcast_in_dim x2 -> x3, local copies, waits for them, and re-layouts: 0.49 us -> 4.75 us  [place_rows(): out = jnp.zeros(shape, pieces[0].dtype)]
    unnamed x7 -> x5, local copies, waits for them, and re-layouts: 4.96 us -> 3.15 us
  transfers between devices with their start and end apart: 8 -> 8, of which waited for: 5 -> 5; matrix products, arithmetic and copies ran while one was open for 19% -> 34% of each run, Pallas kernels for 9% -> 9%
where the time goes in v12:
time: 124 us
  waiting for transfers between devices  44.2 us (36%)
  local copies, waits for them, and re-layouts  23.5 us (19%)
  matrix products  20.2 us (16%)
  between operations  14.8 us (12%)
  Pallas kernels  11 us (9%)
  starting transfers between devices  8.11 us (7%)
  other arithmetic  1.77 us (1%)
    ppermute x3, waiting for transfers between devices, xor_exchange(): out.append(lax.ppermute(x, axis_name, perm=[(a, a ^ m) for a in range(n)]))  24.9 us
    dot_general x2, matrix products, nt(): lax.dot_general(x, weight, (((1,), (1,)), ((), ())), preferred_element_ty...  20.2 us
    ppermute x3, waiting for transfers between devices, per_device(): part = lax.ppermute(part, 'tok', perm=[(a, a ^ m) for a in range(n_tok)])  18.7 us
    dynamic_update_slice x11, local copies, waits for them, and re-layouts, place_rows(): out = lax.dynamic_update_slice_in_dim(out, piece, (me ^ m) * rows, axis)  13.1 us
    pallas_call x1, Pallas kernels, block_tiles(): pl.pallas_call(block_kernel, grid_spec=grid_spec, out_shape=jax.ShapeDtyp...  11 us
    broadcast_in_dim x3, local copies, waits for them, and re-layouts, place_rows(): out = jnp.zeros(shape, pieces[0].dtype)  4.75 us
    ppermute x3, starting transfers between devices, xor_exchange(): out.append(lax.ppermute(x, axis_name, perm=[(a, a ^ m) for a in range(n)]))  4.54 us
    ppermute x3, starting transfers between devices, per_device(): part = lax.ppermute(part, 'tok', perm=[(a, a ^ m) for a in range(n_tok)])  3.49 us
  transfers between devices with their start and end apart: 8, of which 5 were waited for; matrix products, arithmetic and copies ran while one was open for 34% of the time, Pallas kernels for 9%

profile of v12, /device:TPU:0, one launch (start us, length us, event | category | flops | bytes accessed | tf_op | source)
XLA Modules:
  0.0 123.6 jit_solution(13344036380206695984)
XLA Ops:
  7.2 0.0 copy-start.1
  7.2 0.0 all-gather.2.cloned.1.call-start
  7.2 3.0 %collective-permute-start = (bf16[128,3584]{1,0:T(8,128)(2,1)}, bf16[128,3584]{1,0:T(8,128)(2,1)S(1)}, u32[]{:S(2)}, u32[]{:S(2)}) collective-permute-start(bf16[128,3584]{1,0:T(8,128)(2,1)} %param.7), channel_id=1, source_target_pairs={{0,8},{8,0},{16,24},{24,16},{1,9},{9,1},{17,25},{25,17},{2,10},{10... | collective-permute-start | bytes 2752520 | tf_op jit(solution)/shard_map/ppermute | solution.py:17
  10.2 1.5 %collective-permute-start.1 = (bf16[128,3584]{1,0:T(8,128)(2,1)}, bf16[128,3584]{1,0:T(8,128)(2,1)S(1)}, u32[]{:S(2)}, u32[]{:S(2)}) collective-permute-start(bf16[128,3584]{1,0:T(8,128)(2,1)} %param.7), channel_id=1, source_target_pairs={{0,16},{8,24},{16,0},{24,8},{1,17},{9,25},{17,1},{25,9},{2,18},{10... | collective-permute-start | bytes 2752520 | tf_op jit(solution)/shard_map/ppermute | solution.py:17
  11.7 0.0 collective-permute-start.2
  11.8 1.8 %copy.9 = bf16[128,1024]{0,1:T(8,128)(2,1)} copy(bf16[128,1024]{1,0:T(8,128)(2,1)} %param.6) | data formatting | bytes 524288 | tf_op args[0]
  13.6 0.0 all-gather.2.cloned.1.call-update
  13.6 0.0 reduce-scatter.2.cloned.1.call-start
  13.7 2.5 %broadcast_in_dim.9 = f32[512,2048]{1,0:T(8,128)} broadcast(f32[]{:T(128)} %constant.10.clone.1), dimensions={} | broadcast | bytes 4194308 | tf_op jit(solution)/shard_map/broadcast_in_dim | solution.py:25
  16.1 0.0 copy-done.1
  16.1 10.9 %convolution_dynamic-update-slice_fusion = f32[512,2048]{1,0:T(8,128)} fusion(f32[512,2048]{1,0:T(8,128)} %broadcast_in_dim.9, s32[]{:T(128)S(6)} %select_n.33, bf16[128,3584]{1,0:T(8,128)(2,1)S(1)} %copy-done.1, bf16[2048,3584]{1,0:T(8,128)(2,1)} %param.8), kind=kOutput, calls=%fused_computation.6 | convolution fusion | flops 1879048192 | bytes 16646148 | tf_op jit(solution)/shard_map/dot_general | solution.py:79
  27.0 4.6 %collective-permute-done = bf16[128,3584]{1,0:T(8,128)(2,1)S(1)} collective-permute-done((bf16[128,3584]{1,0:T(8,128)(2,1)}, bf16[128,3584]{1,0:T(8,128)(2,1)S(1)}, u32[]{:S(2)}, u32[]{:S(2)}) %collective-permute-start) | collective-permute-done | bytes 917536 | tf_op jit(solution)/shard_map/ppermute | solution.py:17
  31.6 20.3 %collective-permute-done.1 = bf16[128,3584]{1,0:T(8,128)(2,1)S(1)} collective-permute-done((bf16[128,3584]{1,0:T(8,128)(2,1)}, bf16[128,3584]{1,0:T(8,128)(2,1)S(1)}, u32[]{:S(2)}, u32[]{:S(2)}) %collective-permute-start.1) | collective-permute-done | bytes 917536 | tf_op jit(solution)/shard_map/ppermute | solution.py:17
  51.9 0.0 collective-permute-done.2
  51.9 9.4 %fusion = f32[384,2048]{1,0:T(8,128)S(1)} fusion(bf16[2048,3584]{1,0:T(8,128)(2,1)} %param.8, bf16[128,3584]{1,0:T(8,128)(2,1)} %collective-permute-done.2, bf16[128,3584]{1,0:T(8,128)(2,1)S(1)} %collective-permute-done.1, bf16[128,3584]{1,0:T(8,128)(2,1)S(1)} %collective-permute-done), kind=kOutput, calls=%fused_computation | convolution fusion | flops 5645402112 | bytes 20578304 | tf_op jit(solution)/shard_map/dot_general | solution.py:79
  61.3 1.1 slice_dynamic-update-slice_fusion.2
  62.4 1.1 slice_dynamic-update-slice_fusion.1
  63.4 1.1 slice_dynamic-update-slice_fusion
  64.5 0.0 reduce-scatter.2.cloned.1.call-update
  64.6 2.0 %broadcast_in_dim.11 = bf16[512,3584]{1,0:T(8,128)(2,1)} broadcast(bf16[]{:T(256)} %constant.31.clone.1), dimensions={} | broadcast | bytes 3670018 | tf_op jit(solution)/shard_map/broadcast_in_dim | solution.py:25
  66.6 1.0 constant_dynamic-update-slice_fusion.6
  67.6 1.0 constant_dynamic-update-slice_fusion.5
  68.7 1.0 constant_dynamic-update-slice_fusion.4
  69.6 2.2 %constant_dynamic-update-slice_fusion.3.g_ref = bf16[512,3584]{1,0:T(8,128)(2,1)} fusion(bf16[512,3584]{1,0:T(8,128)(2,1)} %constant_dynamic-update-slice_fusion.4, bf16[128,3584]{1,0:T(8,128)(2,1)} %collective-permute-done.2, s32[]{:T(128)S(6)} %select_n.36), kind=kLoop, calls=%fused_computation.17 | loop fusion | bytes 1835012 | tf_op jit(solution)/shard_map/dynamic_update_slice | solution.py:27
  71.8 0.0 all-gather.2.cloned.1.call-done
  71.8 2.5 %dynamic-slice_bitcast_fusion = (bf16[64,32,128]{2,1,0:T(8,128)(2,1)S(1)}, bf16[64,32,128]{2,1,0:T(8,128)(2,1)S(1)}, bf16[64,32,128]{2,1,0:T(8,128)(2,1)}) fusion(bf16[4,64,32,128]{3,2,0,1:T(8,128)(2,1)} %bitcast.14, s32[]{:T(128)S(6)} %select_n.40, s32[]{:T(128)S(6)} %select_n.39, s32[]{:T(128)S(6)} %select_n.38), kind=kLoop, calls=%fused_computation.11 | loop fusion | bytes 3145740 | tf_op jit(solution)/shard_map/jit(dynamic_index_in_dim)/squeeze | solution.py:91
  74.3 1.3 %collective-permute-start.3 = (bf16[64,32,128]{2,1,0:T(8,128)(2,1)}, bf16[64,32,128]{2,1,0:T(8,128)(2,1)}, u32[]{:S(2)}, u32[]{:S(2)}) collective-permute-start(bf16[64,32,128]{2,1,0:T(8,128)(2,1)} %get-tuple-element.8), channel_id=1, source_target_pairs={{0,8},{8,0},{16,24},{24,16},{1,9},{9,1},{17,25},{25,17},{2,10},{10... | collective-permute-start | bytes 1572872 | tf_op jit(solution)/shard_map/ppermute | solution.py:93
  75.6 0.8 collective-permute-start.4
  76.5 1.3 %collective-permute-start.5 = (bf16[64,32,128]{2,1,0:T(8,128)(2,1)S(1)}, bf16[64,32,128]{2,1,0:T(8,128)(2,1)}, u32[]{:S(2)}, u32[]{:S(2)}) collective-permute-start(bf16[64,32,128]{2,1,0:T(8,128)(2,1)S(1)} %get-tuple-element.6), channel_id=1, source_target_pairs={{0,24},{8,16},{16,8},{24,0},{1,25},{9,17},{17,9},{25,1},{2,26},{10... | collective-permute-start | bytes 1572872 | tf_op jit(solution)/shard_map/ppermute | solution.py:93
  78.5 0.2 broadcast_in_dim.10
  78.7 1.2 bitcast_dynamic-update-slice_fusion
  79.9 9.6 %collective-permute-done.3 = bf16[64,32,128]{2,1,0:T(8,128)(2,1)} collective-permute-done((bf16[64,32,128]{2,1,0:T(8,128)(2,1)}, bf16[64,32,128]{2,1,0:T(8,128)(2,1)}, u32[]{:S(2)}, u32[]{:S(2)}) %collective-permute-start.3) | collective-permute-done | bytes 524320 | tf_op jit(solution)/shard_map/ppermute | solution.py:93
  89.5 1.2 constant_dynamic-update-slice_fusion.1
  90.7 9.1 %collective-permute-done.4 = bf16[64,32,128]{2,1,0:T(8,128)(2,1)} collective-permute-done((bf16[64,32,128]{2,1,0:T(8,128)(2,1)S(1)}, bf16[64,32,128]{2,1,0:T(8,128)(2,1)}, u32[]{:S(2)}, u32[]{:S(2)}) %collective-permute-start.4) | collective-permute-done | bytes 524320 | tf_op jit(solution)/shard_map/ppermute | solution.py:93
  99.8 1.2 constant_dynamic-update-slice_fusion
  100.9 0.0 collective-permute-done.5
  100.9 1.2 constant_dynamic-update-slice_fusion.2.a_ref
  102.1 0.0 copy-start
  102.1 1.4 %copy-done = bf16[64,32,512]{2,1,0:T(8,128)(2,1)} copy-done((bf16[64,32,512]{2,1,0:T(8,128)(2,1)}, bf16[64,32,512]{2,1,0:T(8,128)(2,1)S(1)}, u32[]{:S(2)}) %copy-start) | copy-done | bytes 2097176
  103.5 11.0 %shard_map.77 = bf16[128,32,128]{2,1,0:T(8,128)(2,1)} custom-call(s32[128]{0:T(128)} %rows_ref.1, s32[128]{0:T(128)} %cols_ref.1, s32[1]{0:T(128)S(6)} %copy.22.cnt_ref, bf16[64,32,512]{2,1,0:T(8,128)(2,1)} %copy-done, bf16[512,3584]{1,0:T(8,128)(2,1)} %constant_dynamic-update-slice_fusion.3.g_ref), custom_call_target="tpu_custom_call" | custom-call | flops 536870912 | bytes 6815744 | tf_op jit(solution)/shard_map/pallas_call | solution.py:54
  114.4 0.6 reduce-scatter.2.cloned.1.call-done
  115.0 1.8 %convert_element_type.3 = bf16[64,2048]{1,0:T(8,128)(2,1)} convert(f32[64,2048]{1,0:T(8,128)} %reduce-scatter.2.cloned.1.call-done) | non-fusion elementwise | flops 131072 | bytes 786432 | tf_op jit(solution)/shard_map/convert_element_type | solution.py:84
Async XLA Ops:
  7.2 9.0 %copy-start.1 = (bf16[128,3584]{1,0:T(8,128)(2,1)S(1)}, bf16[128,3584]{1,0:T(8,128)(2,1)}, u32[]{:S(2)}) copy-start(bf16[128,3584]{1,0:T(8,128)(2,1)} %param.7) | copy-start | bytes 2752516
  7.2 64.6 %all-gather.2.cloned.1.call-start = ((), (), s32[]{:S(2)}) async-start(), calls=%async_computation.2 | async-start | bytes 2359296 | tf_op jit(solution)/shard_map/all_gather | solution.py:71
  7.2 24.4 %collective-permute-start = (bf16[128,3584]{1,0:T(8,128)(2,1)}, bf16[128,3584]{1,0:T(8,128)(2,1)S(1)}, u32[]{:S(2)}, u32[]{:S(2)}) collective-permute-start(bf16[128,3584]{1,0:T(8,128)(2,1)} %param.7), channel_id=1, source_target_pairs={{0,8},{8,0},{16,24},{24,16},{1,9},{9,1},{17,25},{25,17},{2,10},{10... | collective-permute-start | bytes 2752520 | tf_op jit(solution)/shard_map/ppermute | solution.py:17
  10.2 41.7 %collective-permute-start.1 = (bf16[128,3584]{1,0:T(8,128)(2,1)}, bf16[128,3584]{1,0:T(8,128)(2,1)S(1)}, u32[]{:S(2)}, u32[]{:S(2)}) collective-permute-start(bf16[128,3584]{1,0:T(8,128)(2,1)} %param.7), channel_id=1, source_target_pairs={{0,16},{8,24},{16,0},{24,8},{1,17},{9,25},{17,1},{25,9},{2,18},{10... | collective-permute-start | bytes 2752520 | tf_op jit(solution)/shard_map/ppermute | solution.py:17
  11.7 40.2 %collective-permute-start.2 = (bf16[128,3584]{1,0:T(8,128)(2,1)}, bf16[128,3584]{1,0:T(8,128)(2,1)}, u32[]{:S(2)}, u32[]{:S(2)}) collective-permute-start(bf16[128,3584]{1,0:T(8,128)(2,1)} %param.7), channel_id=1, source_target_pairs={{0,24},{8,16},{16,8},{24,0},{1,25},{9,17},{17,9},{25,1},{2,26},{10... | collective-permute-start | bytes 2752520 | tf_op jit(solution)/shard_map/ppermute | solution.py:17
  13.6 101.4 %reduce-scatter.2.cloned.1.call-start = ((), (), s32[]{:S(2)}) async-start(), calls=%async_computation.1 | async-start | bytes 4718592 | tf_op jit(solution)/shard_map/reduce_scatter | solution.py:84
  74.3 15.2 %collective-permute-start.3 = (bf16[64,32,128]{2,1,0:T(8,128)(2,1)}, bf16[64,32,128]{2,1,0:T(8,128)(2,1)}, u32[]{:S(2)}, u32[]{:S(2)}) collective-permute-start(bf16[64,32,128]{2,1,0:T(8,128)(2,1)} %get-tuple-element.8), channel_id=1, source_target_pairs={{0,8},{8,0},{16,24},{24,16},{1,9},{9,1},{17,25},{25,17},{2,10},{10... | collective-permute-start | bytes 1572872 | tf_op jit(solution)/shard_map/ppermute | solution.py:93
  75.6 24.1 %collective-permute-start.4 = (bf16[64,32,128]{2,1,0:T(8,128)(2,1)S(1)}, bf16[64,32,128]{2,1,0:T(8,128)(2,1)}, u32[]{:S(2)}, u32[]{:S(2)}) collective-permute-start(bf16[64,32,128]{2,1,0:T(8,128)(2,1)S(1)} %get-tuple-element.7), channel_id=1, source_target_pairs={{0,16},{8,24},{16,0},{24,8},{1,17},{9,25},{17,1},{25,9},{2,18},{10... | collective-permute-start | bytes 1572872 | tf_op jit(solution)/shard_map/ppermute | solution.py:93
  76.5 24.5 %collective-permute-start.5 = (bf16[64,32,128]{2,1,0:T(8,128)(2,1)S(1)}, bf16[64,32,128]{2,1,0:T(8,128)(2,1)}, u32[]{:S(2)}, u32[]{:S(2)}) collective-permute-start(bf16[64,32,128]{2,1,0:T(8,128)(2,1)S(1)} %get-tuple-element.6), channel_id=1, source_target_pairs={{0,24},{8,16},{16,8},{24,0},{1,25},{9,17},{17,9},{25,1},{2,26},{10... | collective-permute-start | bytes 1572872 | tf_op jit(solution)/shard_map/ppermute | solution.py:93
  102.1 1.4 %copy-start = (bf16[64,32,512]{2,1,0:T(8,128)(2,1)}, bf16[64,32,512]{2,1,0:T(8,128)(2,1)S(1)}, u32[]{:S(2)}) copy-start(bf16[64,32,512]{2,1,0:T(8,128)(2,1)S(1)} %constant_dynamic-update-slice_fusion.2.a_ref) | copy-start | bytes 6291460
Sparse Core Ops, SparseCore 0:
  13.7 30.7 all-gather.1
  64.7 50.3 reduce-scatter.1

commit v13 on v12

--- a/solution.py
+++ b/solution.py
@@ -79,8 +79,9 @@
         return lax.dot_general(x, weight, (((1,), (1,)), ((), ())), preferred_element_type=jnp.float32)
 
     own = nt(grad_out)
-    rest = nt(jnp.concatenate(pieces[1:], axis=0)).reshape(n_tok - 1, tok_dev, -1)
-    partial_sums = place_rows([own] + [rest[m] for m in range(n_tok - 1)], me)
+    first = nt(pieces[1])
+    rest = nt(jnp.concatenate(pieces[2:], axis=0)).reshape(n_tok - 2, tok_dev, -1)
+    partial_sums = place_rows([own, first] + [rest[m] for m in range(n_tok - 2)], me)
     grad_in = lax.psum_scatter(partial_sums, "feat", scatter_dimension=0, tiled=True).astype(
         jnp.bfloat16
     )

time: 124 us -> 121 us (0.976)
  waiting for transfers between devices: 44.2 us -> 33.2 us
  matrix products: 20.2 us -> 29.5 us
    ppermute x3, waiting for transfers between devices: 24.9 us -> 13.9 us  [xor_exchange(): out.append(lax.ppermute(x, axis_name, perm=[(a, a ^ m) for a in range(n)]))]
    dot_general x2 -> x3, matrix products: 20.2 us -> 29.5 us  [nt(): lax.dot_general(x, weight, (((1,), (1,)), ((), ())), preferred_element_ty...]
    dynamic_update_slice x11 -> x10, local copies, waits for them, and re-layouts: 13.1 us -> 12 us  [place_rows(): out = lax.dynamic_update_slice_in_dim(out, piece, (me ^ m) * rows, axis)]
  transfers between devices with their start and end apart: 8 -> 8, of which waited for: 5 -> 5; matrix products, arithmetic and copies ran while one was open for 34% -> 42% of each run, Pallas kernels for 9% -> 9%
where the time goes in v13:
time: 121 us
  waiting for transfers between devices  33.2 us (27%)
  matrix products  29.5 us (24%)
  local copies, waits for them, and re-layouts  22.4 us (19%)
  between operations  14.8 us (12%)
  Pallas kernels  11 us (9%)
  starting transfers between devices  8.11 us (7%)
  other arithmetic  1.77 us (1%)
    dot_general x3, matrix products, nt(): lax.dot_general(x, weight, (((1,), (1,)), ((), ())), preferred_element_ty...  29.5 us
    ppermute x3, waiting for transfers between devices, per_device(): part = lax.ppermute(part, 'tok', perm=[(a, a ^ m) for a in range(n_tok)])  18.7 us
    ppermute x3, waiting for transfers between devices, xor_exchange(): out.append(lax.ppermute(x, axis_name, perm=[(a, a ^ m) for a in range(n)]))  13.9 us
    dynamic_update_slice x10, local copies, waits for them, and re-layouts, place_rows(): out = lax.dynamic_update_slice_in_dim(out, piece, (me ^ m) * rows, axis)  12 us
    pallas_call x1, Pallas kernels, block_tiles(): pl.pallas_call(block_kernel, grid_spec=grid_spec, out_shape=jax.ShapeDtyp...  11 us
    broadcast_in_dim x3, local copies, waits for them, and re-layouts, place_rows(): out = jnp.zeros(shape, pieces[0].dtype)  4.75 us
    ppermute x3, starting transfers between devices, xor_exchange(): out.append(lax.ppermute(x, axis_name, perm=[(a, a ^ m) for a in range(n)]))  4.54 us
    ppermute x3, starting transfers between devices, per_device(): part = lax.ppermute(part, 'tok', perm=[(a, a ^ m) for a in range(n_tok)])  3.49 us
  transfers between devices with their start and end apart: 8, of which 5 were waited for; matrix products, arithmetic and copies ran while one was open for 42% of the time, Pallas kernels for 9%

profile of v13, /device:TPU:0, one launch (start us, length us, event | category | flops | bytes accessed | tf_op | source)
XLA Modules:
  0.0 120.7 jit_solution(9662472971611877067)
XLA Ops:
  7.2 0.0 copy-start.1
  7.2 0.0 all-gather.2.cloned.1.call-start
  7.2 3.0 %collective-permute-start = (bf16[128,3584]{1,0:T(8,128)(2,1)}, bf16[128,3584]{1,0:T(8,128)(2,1)S(1)}, u32[]{:S(2)}, u32[]{:S(2)}) collective-permute-start(bf16[128,3584]{1,0:T(8,128)(2,1)} %param.7), channel_id=1, source_target_pairs={{0,8},{8,0},{16,24},{24,16},{1,9},{9,1},{17,25},{25,17},{2,10},{10... | collective-permute-start | bytes 2752520 | tf_op jit(solution)/shard_map/ppermute | solution.py:17
  10.2 1.5 %collective-permute-start.1 = (bf16[128,3584]{1,0:T(8,128)(2,1)}, bf16[128,3584]{1,0:T(8,128)(2,1)S(1)}, u32[]{:S(2)}, u32[]{:S(2)}) collective-permute-start(bf16[128,3584]{1,0:T(8,128)(2,1)} %param.7), channel_id=1, source_target_pairs={{0,16},{8,24},{16,0},{24,8},{1,17},{9,25},{17,1},{25,9},{2,18},{10... | collective-permute-start | bytes 2752520 | tf_op jit(solution)/shard_map/ppermute | solution.py:17
  11.7 0.0 collective-permute-start.2
  11.8 1.8 %copy.9 = bf16[128,1024]{0,1:T(8,128)(2,1)} copy(bf16[128,1024]{1,0:T(8,128)(2,1)} %param.6) | data formatting | bytes 524288 | tf_op args[0]
  13.6 0.0 all-gather.2.cloned.1.call-update
  13.6 0.0 reduce-scatter.2.cloned.1.call-start
  13.6 2.5 %broadcast_in_dim.9 = f32[512,2048]{1,0:T(8,128)} broadcast(f32[]{:T(128)} %constant.10.clone.1), dimensions={} | broadcast | bytes 4194308 | tf_op jit(solution)/shard_map/broadcast_in_dim | solution.py:25
  16.1 0.0 copy-done.1
  16.1 10.9 %convolution_dynamic-update-slice_fusion.1 = f32[512,2048]{1,0:T(8,128)} fusion(f32[512,2048]{1,0:T(8,128)} %broadcast_in_dim.9, s32[]{:T(128)S(6)} %select_n.33, bf16[128,3584]{1,0:T(8,128)(2,1)S(1)} %copy-done.1, bf16[2048,3584]{1,0:T(8,128)(2,1)} %param.8), kind=kOutput, calls=%fused_computation.1 | convolution fusion | flops 1879048192 | bytes 16646148 | tf_op jit(solution)/shard_map/dot_general | solution.py:79
  27.0 4.6 %collective-permute-done = bf16[128,3584]{1,0:T(8,128)(2,1)S(1)} collective-permute-done((bf16[128,3584]{1,0:T(8,128)(2,1)}, bf16[128,3584]{1,0:T(8,128)(2,1)S(1)}, u32[]{:S(2)}, u32[]{:S(2)}) %collective-permute-start) | collective-permute-done | bytes 917536 | tf_op jit(solution)/shard_map/ppermute | solution.py:17
  31.6 11.0 %convolution_dynamic-update-slice_fusion = f32[512,2048]{1,0:T(8,128)} fusion(f32[512,2048]{1,0:T(8,128)} %convolution_dynamic-update-slice_fusion.1, s32[]{:T(128)S(6)} %select_n.34, bf16[128,3584]{1,0:T(8,128)(2,1)S(1)} %collective-permute-done, bf16[2048,3584]{1,0:T(8,128)(2,1)} %param.8), kind=kOutput, calls=%fused_computation | convolution fusion | flops 1879048192 | bytes 16646148 | tf_op jit(solution)/shard_map/dot_general | solution.py:79
  42.7 9.3 %collective-permute-done.1 = bf16[128,3584]{1,0:T(8,128)(2,1)S(1)} collective-permute-done((bf16[128,3584]{1,0:T(8,128)(2,1)}, bf16[128,3584]{1,0:T(8,128)(2,1)S(1)}, u32[]{:S(2)}, u32[]{:S(2)}) %collective-permute-start.1) | collective-permute-done | bytes 917536 | tf_op jit(solution)/shard_map/ppermute | solution.py:17
  51.9 0.0 collective-permute-done.2
  51.9 7.5 %fusion = f32[256,2048]{1,0:T(8,128)S(1)} fusion(bf16[2048,3584]{1,0:T(8,128)(2,1)} %param.8, bf16[128,3584]{1,0:T(8,128)(2,1)} %collective-permute-done.2, bf16[128,3584]{1,0:T(8,128)(2,1)S(1)} %collective-permute-done.1), kind=kOutput, calls=%fused_computation.2 | convolution fusion | flops 3761766400 | bytes 18612224 | tf_op jit(solution)/shard_map/dot_general | solution.py:79
  59.5 1.1 slice_dynamic-update-slice_fusion.1
  60.5 1.1 slice_dynamic-update-slice_fusion
  61.6 0.0 reduce-scatter.2.cloned.1.call-update
  61.6 2.0 %broadcast_in_dim.11 = bf16[512,3584]{1,0:T(8,128)(2,1)} broadcast(bf16[]{:T(256)} %constant.31.clone.1), dimensions={} | broadcast | bytes 3670018 | tf_op jit(solution)/shard_map/broadcast_in_dim | solution.py:25
  63.7 1.0 constant_dynamic-update-slice_fusion.6
  64.7 1.0 constant_dynamic-update-slice_fusion.5
  65.7 1.0 constant_dynamic-update-slice_fusion.4
  66.7 2.2 %constant_dynamic-update-slice_fusion.3.g_ref = bf16[512,3584]{1,0:T(8,128)(2,1)} fusion(bf16[512,3584]{1,0:T(8,128)(2,1)} %constant_dynamic-update-slice_fusion.4, bf16[128,3584]{1,0:T(8,128)(2,1)} %collective-permute-done.2, s32[]{:T(128)S(6)} %select_n.36), kind=kLoop, calls=%fused_computation.15 | loop fusion | bytes 1835012 | tf_op jit(solution)/shard_map/dynamic_update_slice | solution.py:27
  68.9 0.0 all-gather.2.cloned.1.call-done
  68.9 2.4 %dynamic-slice_bitcast_fusion = (bf16[64,32,128]{2,1,0:T(8,128)(2,1)S(1)}, bf16[64,32,128]{2,1,0:T(8,128)(2,1)S(1)}, bf16[64,32,128]{2,1,0:T(8,128)(2,1)}) fusion(bf16[4,64,32,128]{3,2,0,1:T(8,128)(2,1)} %bitcast.16, s32[]{:T(128)S(6)} %select_n.40, s32[]{:T(128)S(6)} %select_n.39, s32[]{:T(128)S(6)} %select_n.38), kind=kLoop, calls=%fused_computation.9 | loop fusion | bytes 3145740 | tf_op jit(solution)/shard_map/jit(dynamic_index_in_dim)/squeeze | solution.py:92
  71.3 1.4 %collective-permute-start.3 = (bf16[64,32,128]{2,1,0:T(8,128)(2,1)}, bf16[64,32,128]{2,1,0:T(8,128)(2,1)}, u32[]{:S(2)}, u32[]{:S(2)}) collective-permute-start(bf16[64,32,128]{2,1,0:T(8,128)(2,1)} %get-tuple-element.8), channel_id=1, source_target_pairs={{0,8},{8,0},{16,24},{24,16},{1,9},{9,1},{17,25},{25,17},{2,10},{10... | collective-permute-start | bytes 1572872 | tf_op jit(solution)/shard_map/ppermute | solution.py:94
  72.7 0.8 collective-permute-start.4
  73.5 1.3 %collective-permute-start.5 = (bf16[64,32,128]{2,1,0:T(8,128)(2,1)S(1)}, bf16[64,32,128]{2,1,0:T(8,128)(2,1)}, u32[]{:S(2)}, u32[]{:S(2)}) collective-permute-start(bf16[64,32,128]{2,1,0:T(8,128)(2,1)S(1)} %get-tuple-element.6), channel_id=1, source_target_pairs={{0,24},{8,16},{16,8},{24,0},{1,25},{9,17},{17,9},{25,1},{2,26},{10... | collective-permute-start | bytes 1572872 | tf_op jit(solution)/shard_map/ppermute | solution.py:94
  75.5 0.2 broadcast_in_dim.10
  75.7 1.2 bitcast_dynamic-update-slice_fusion
  76.9 9.6 %collective-permute-done.3 = bf16[64,32,128]{2,1,0:T(8,128)(2,1)} collective-permute-done((bf16[64,32,128]{2,1,0:T(8,128)(2,1)}, bf16[64,32,128]{2,1,0:T(8,128)(2,1)}, u32[]{:S(2)}, u32[]{:S(2)}) %collective-permute-start.3) | collective-permute-done | bytes 524320 | tf_op jit(solution)/shard_map/ppermute | solution.py:94
  86.5 1.2 constant_dynamic-update-slice_fusion.1
  87.7 9.1 %collective-permute-done.4 = bf16[64,32,128]{2,1,0:T(8,128)(2,1)} collective-permute-done((bf16[64,32,128]{2,1,0:T(8,128)(2,1)S(1)}, bf16[64,32,128]{2,1,0:T(8,128)(2,1)}, u32[]{:S(2)}, u32[]{:S(2)}) %collective-permute-start.4) | collective-permute-done | bytes 524320 | tf_op jit(solution)/shard_map/ppermute | solution.py:94
  96.8 1.2 constant_dynamic-update-slice_fusion
  98.0 0.0 collective-permute-done.5
  98.0 1.2 constant_dynamic-update-slice_fusion.2.a_ref
  99.2 0.0 copy-start
  99.2 1.4 %copy-done = bf16[64,32,512]{2,1,0:T(8,128)(2,1)} copy-done((bf16[64,32,512]{2,1,0:T(8,128)(2,1)}, bf16[64,32,512]{2,1,0:T(8,128)(2,1)S(1)}, u32[]{:S(2)}) %copy-start) | copy-done | bytes 2097176
  100.5 11.0 %shard_map.77 = bf16[128,32,128]{2,1,0:T(8,128)(2,1)} custom-call(s32[128]{0:T(128)} %rows_ref.1, s32[128]{0:T(128)} %cols_ref.1, s32[1]{0:T(128)S(6)} %copy.22.cnt_ref, bf16[64,32,512]{2,1,0:T(8,128)(2,1)} %copy-done, bf16[512,3584]{1,0:T(8,128)(2,1)} %constant_dynamic-update-slice_fusion.3.g_ref), custom_call_target="tpu_custom_call" | custom-call | flops 536870912 | bytes 6815744 | tf_op jit(solution)/shard_map/pallas_call | solution.py:54
  111.5 0.6 reduce-scatter.2.cloned.1.call-done
  112.1 1.8 %convert_element_type.3 = bf16[64,2048]{1,0:T(8,128)(2,1)} convert(f32[64,2048]{1,0:T(8,128)} %reduce-scatter.2.cloned.1.call-done) | non-fusion elementwise | flops 131072 | bytes 786432 | tf_op jit(solution)/shard_map/convert_element_type | solution.py:85
Async XLA Ops:
  7.2 8.9 %copy-start.1 = (bf16[128,3584]{1,0:T(8,128)(2,1)S(1)}, bf16[128,3584]{1,0:T(8,128)(2,1)}, u32[]{:S(2)}) copy-start(bf16[128,3584]{1,0:T(8,128)(2,1)} %param.7) | copy-start | bytes 2752516
  7.2 61.7 %all-gather.2.cloned.1.call-start = ((), (), s32[]{:S(2)}) async-start(), calls=%async_computation.2 | async-start | bytes 2359296 | tf_op jit(solution)/shard_map/all_gather | solution.py:71
  7.2 24.4 %collective-permute-start = (bf16[128,3584]{1,0:T(8,128)(2,1)}, bf16[128,3584]{1,0:T(8,128)(2,1)S(1)}, u32[]{:S(2)}, u32[]{:S(2)}) collective-permute-start(bf16[128,3584]{1,0:T(8,128)(2,1)} %param.7), channel_id=1, source_target_pairs={{0,8},{8,0},{16,24},{24,16},{1,9},{9,1},{17,25},{25,17},{2,10},{10... | collective-permute-start | bytes 2752520 | tf_op jit(solution)/shard_map/ppermute | solution.py:17
  10.2 41.7 %collective-permute-start.1 = (bf16[128,3584]{1,0:T(8,128)(2,1)}, bf16[128,3584]{1,0:T(8,128)(2,1)S(1)}, u32[]{:S(2)}, u32[]{:S(2)}) collective-permute-start(bf16[128,3584]{1,0:T(8,128)(2,1)} %param.7), channel_id=1, source_target_pairs={{0,16},{8,24},{16,0},{24,8},{1,17},{9,25},{17,1},{25,9},{2,18},{10... | collective-permute-start | bytes 2752520 | tf_op jit(solution)/shard_map/ppermute | solution.py:17
  11.7 40.2 %collective-permute-start.2 = (bf16[128,3584]{1,0:T(8,128)(2,1)}, bf16[128,3584]{1,0:T(8,128)(2,1)}, u32[]{:S(2)}, u32[]{:S(2)}) collective-permute-start(bf16[128,3584]{1,0:T(8,128)(2,1)} %param.7), channel_id=1, source_target_pairs={{0,24},{8,16},{16,8},{24,0},{1,25},{9,17},{17,9},{25,1},{2,26},{10... | collective-permute-start | bytes 2752520 | tf_op jit(solution)/shard_map/ppermute | solution.py:17
  13.6 98.5 %reduce-scatter.2.cloned.1.call-start = ((), (), s32[]{:S(2)}) async-start(), calls=%async_computation.1 | async-start | bytes 4718592 | tf_op jit(solution)/shard_map/reduce_scatter | solution.py:85
  71.3 15.2 %collective-permute-start.3 = (bf16[64,32,128]{2,1,0:T(8,128)(2,1)}, bf16[64,32,128]{2,1,0:T(8,128)(2,1)}, u32[]{:S(2)}, u32[]{:S(2)}) collective-permute-start(bf16[64,32,128]{2,1,0:T(8,128)(2,1)} %get-tuple-element.8), channel_id=1, source_target_pairs={{0,8},{8,0},{16,24},{24,16},{1,9},{9,1},{17,25},{25,17},{2,10},{10... | collective-permute-start | bytes 1572872 | tf_op jit(solution)/shard_map/ppermute | solution.py:94
  72.7 24.1 %collective-permute-start.4 = (bf16[64,32,128]{2,1,0:T(8,128)(2,1)S(1)}, bf16[64,32,128]{2,1,0:T(8,128)(2,1)}, u32[]{:S(2)}, u32[]{:S(2)}) collective-permute-start(bf16[64,32,128]{2,1,0:T(8,128)(2,1)S(1)} %get-tuple-element.7), channel_id=1, source_target_pairs={{0,16},{8,24},{16,0},{24,8},{1,17},{9,25},{17,1},{25,9},{2,18},{10... | collective-permute-start | bytes 1572872 | tf_op jit(solution)/shard_map/ppermute | solution.py:94
  73.5 24.5 %collective-permute-start.5 = (bf16[64,32,128]{2,1,0:T(8,128)(2,1)S(1)}, bf16[64,32,128]{2,1,0:T(8,128)(2,1)}, u32[]{:S(2)}, u32[]{:S(2)}) collective-permute-start(bf16[64,32,128]{2,1,0:T(8,128)(2,1)S(1)} %get-tuple-element.6), channel_id=1, source_target_pairs={{0,24},{8,16},{16,8},{24,0},{1,25},{9,17},{17,9},{25,1},{2,26},{10... | collective-permute-start | bytes 1572872 | tf_op jit(solution)/shard_map/ppermute | solution.py:94
  99.2 1.4 %copy-start = (bf16[64,32,512]{2,1,0:T(8,128)(2,1)}, bf16[64,32,512]{2,1,0:T(8,128)(2,1)S(1)}, u32[]{:S(2)}) copy-start(bf16[64,32,512]{2,1,0:T(8,128)(2,1)S(1)} %constant_dynamic-update-slice_fusion.2.a_ref) | copy-start | bytes 6291460
Sparse Core Ops, SparseCore 0:
  13.7 30.8 all-gather.1
  61.7 50.3 reduce-scatter.1

commit v14 on v12

--- a/solution.py
+++ b/solution.py
@@ -78,9 +78,20 @@
     def nt(x):
         return lax.dot_general(x, weight, (((1,), (1,)), ((), ())), preferred_element_type=jnp.float32)
 
-    own = nt(grad_out)
-    rest = nt(jnp.concatenate(pieces[1:], axis=0)).reshape(n_tok - 1, tok_dev, -1)
-    partial_sums = place_rows([own] + [rest[m] for m in range(n_tok - 1)], me)
+    half = n_tok // 2
+    partial_sums = jnp.zeros((n_tok * tok_dev, weight.shape[0]), jnp.float32)
+    for m in range(half):
+        partial_sums = lax.dynamic_update_slice_in_dim(
+            partial_sums, nt(pieces[m]), (me ^ m) * tok_dev, 0
+        )
+    far_pieces, partial_sums = lax.optimization_barrier((pieces[half:], partial_sums))
+    far = nt(jnp.concatenate(far_pieces, axis=0))
+    for bit in range(half.bit_length() - 1):
+        step = 1 << bit
+        swapped = far.reshape(half // (2 * step), 2, step * tok_dev, -1)[:, ::-1].reshape(far.shape)
+        far = jnp.where((me >> bit) % 2 == 1, swapped, far)
+    base = ((me ^ half) // half) * half
+    partial_sums = lax.dynamic_update_slice_in_dim(partial_sums, far, base * tok_dev, 0)
     grad_in = lax.psum_scatter(partial_sums, "feat", scatter_dimension=0, tiled=True).astype(
         jnp.bfloat16
     )

time: 124 us -> 127 us (1.024)
  matrix products: 20.2 us -> 30.4 us
  waiting for transfers between devices: 44.2 us -> 34.4 us
  other arithmetic: 1.77 us -> 4.95 us
    dot_general x2 -> x3, matrix products: 20.2 us -> 30.4 us  [nt(): lax.dot_general(x, weight, (((1,), (1,)), ((), ())), preferred_element_ty...]
    ppermute x3, waiting for transfers between devices: 24.9 us -> 15.1 us  [xor_exchange(): out.append(lax.ppermute(x, axis_name, perm=[(a, a ^ m) for a in range(n)]))]
    dynamic_update_slice x11 -> x8, local copies, waits for them, and re-layouts: 13.1 us -> 9.88 us  [place_rows(): out = lax.dynamic_update_slice_in_dim(out, piece, (me ^ m) * rows, axis)]
    dynamic_update_slice x0 -> x1, other arithmetic: none -> 3.18 us  [per_device(): lax.dynamic_update_slice_in_dim(partial_sums, far, base * tok_dev, 0)]
    broadcast_in_dim x3 -> x2, local copies, waits for them, and re-layouts: 4.75 us -> 2.27 us  [place_rows(): out = jnp.zeros(shape, pieces[0].dtype)]
    broadcast_in_dim x0 -> x1, local copies, waits for them, and re-layouts: none -> 2.48 us  [per_device(): partial_sums = jnp.zeros((n_tok * tok_dev, weight.shape[0]), jnp.float32)]
    rev x0 -> x1, local copies, waits for them, and re-layouts: none -> 1.5 us  [per_device(): far.reshape(half // (2 * step), 2, step * tok_dev, -1)[:, ::-1]]
    unnamed x5 -> x13, local copies, waits for them, and re-layouts: 3.15 us -> 4.18 us
  transfers between devices with their start and end apart: 8 -> 8, of which waited for: 5 -> 5; matrix products, arithmetic and copies ran while one was open for 34% -> 41% of each run, Pallas kernels for 9% -> 9%
where the time goes in v14:
time: 127 us; the launch traced here: 126 us
  waiting for transfers between devices  34.4 us (27%)
  matrix products  30.4 us (24%)
  local copies, waits for them, and re-layouts  22.8 us (18%)
  between operations  14.8 us (12%)
  Pallas kernels  11 us (9%)
  starting transfers between devices  8.11 us (6%)
  other arithmetic  4.95 us (4%)
    dot_general x3, matrix products, nt(): lax.dot_general(x, weight, (((1,), (1,)), ((), ())), preferred_element_ty...  30.4 us
    ppermute x3, waiting for transfers between devices, per_device(): part = lax.ppermute(part, 'tok', perm=[(a, a ^ m) for a in range(n_tok)])  17.5 us
    ppermute x3, waiting for transfers between devices, xor_exchange(): out.append(lax.ppermute(x, axis_name, perm=[(a, a ^ m) for a in range(n)]))  15.1 us
    pallas_call x1, Pallas kernels, block_tiles(): pl.pallas_call(block_kernel, grid_spec=grid_spec, out_shape=jax.ShapeDtyp...  11 us
    dynamic_update_slice x8, local copies, waits for them, and re-layouts, place_rows(): out = lax.dynamic_update_slice_in_dim(out, piece, (me ^ m) * rows, axis)  9.88 us
    ppermute x3, starting transfers between devices, xor_exchange(): out.append(lax.ppermute(x, axis_name, perm=[(a, a ^ m) for a in range(n)]))  4.55 us
    unnamed x13, local copies, waits for them, and re-layouts  4.18 us
    ppermute x3, starting transfers between devices, per_device(): part = lax.ppermute(part, 'tok', perm=[(a, a ^ m) for a in range(n_tok)])  3.49 us
  transfers between devices with their start and end apart: 8, of which 5 were waited for; matrix products, arithmetic and copies ran while one was open for 41% of the time, Pallas kernels for 9%

profile of v14, /device:TPU:0, one launch (start us, length us, event | category | flops | bytes accessed | tf_op | source)
XLA Modules:
  0.0 126.4 jit_solution(14280367973851120648)
XLA Ops:
  7.2 0.0 copy-start.1
  7.2 0.0 all-gather.2.cloned.1.call-start
  7.2 1.9 %copy.9 = bf16[128,1024]{0,1:T(8,128)(2,1)} copy(bf16[128,1024]{1,0:T(8,128)(2,1)} %param.6) | data formatting | bytes 524288 | tf_op args[0]
  9.1 0.0 all-gather.2.cloned.1.call-update
  9.1 0.0 reduce-scatter.2.cloned.1.call-start
  9.2 3.0 %collective-permute-start.2 = (bf16[128,3584]{1,0:T(8,128)(2,1)}, bf16[128,3584]{1,0:T(8,128)(2,1)S(1)}, u32[]{:S(2)}, u32[]{:S(2)}) collective-permute-start(bf16[128,3584]{1,0:T(8,128)(2,1)} %param.7), channel_id=1, source_target_pairs={{0,8},{8,0},{16,24},{24,16},{1,9},{9,1},{17,25},{25,17},{2,10},{10... | collective-permute-start | bytes 2752520 | tf_op jit(solution)/shard_map/ppermute | solution.py:17
  12.2 1.5 %collective-permute-start = (bf16[128,3584]{1,0:T(8,128)(2,1)}, bf16[128,3584]{1,0:T(8,128)(2,1)S(1)}, u32[]{:S(2)}, u32[]{:S(2)}) collective-permute-start(bf16[128,3584]{1,0:T(8,128)(2,1)} %param.7), channel_id=1, source_target_pairs={{0,16},{8,24},{16,0},{24,8},{1,17},{9,25},{17,1},{25,9},{2,18},{10... | collective-permute-start | bytes 2752520 | tf_op jit(solution)/shard_map/ppermute | solution.py:17
  13.7 0.0 collective-permute-start.1
  13.7 2.5 %broadcast_in_dim.9 = f32[512,2048]{1,0:T(8,128)} broadcast(f32[]{:T(128)} %constant.43.clone.1), dimensions={} | broadcast | bytes 4194308 | tf_op jit(solution)/shard_map/broadcast_in_dim | solution.py:82
  16.2 0.0 copy-done.1
  16.2 11.2 %convolution_dynamic-update-slice_fusion.1 = f32[512,2048]{1,0:T(8,128)} fusion(f32[512,2048]{1,0:T(8,128)} %broadcast_in_dim.9, s32[]{:T(128)S(6)} %select_n.53, bf16[128,3584]{1,0:T(8,128)(2,1)S(1)} %copy-done.1, bf16[2048,3584]{1,0:T(8,128)(2,1)} %param.8), kind=kOutput, calls=%fused_computation.1 | convolution fusion | flops 1879048192 | bytes 16646148 | tf_op jit(solution)/shard_map/dot_general | solution.py:79
  27.4 6.1 %collective-permute-done.2 = bf16[128,3584]{1,0:T(8,128)(2,1)S(1)} collective-permute-done((bf16[128,3584]{1,0:T(8,128)(2,1)}, bf16[128,3584]{1,0:T(8,128)(2,1)S(1)}, u32[]{:S(2)}, u32[]{:S(2)}) %collective-permute-start.2) | collective-permute-done | bytes 917536 | tf_op jit(solution)/shard_map/ppermute | solution.py:17
  33.6 0.0 copy-start.2
  33.6 11.3 %convolution_dynamic-update-slice_fusion = f32[512,2048]{1,0:T(8,128)} fusion(f32[512,2048]{1,0:T(8,128)} %convolution_dynamic-update-slice_fusion.1, s32[]{:T(128)S(6)} %select_n.54, bf16[128,3584]{1,0:T(8,128)(2,1)S(1)} %collective-permute-done.2, bf16[2048,3584]{1,0:T(8,128)(2,1)} %param.8), kind=kOutput, calls=%fused_computation | convolution fusion | flops 1879048192 | bytes 16646148 | tf_op jit(solution)/shard_map/dot_general | solution.py:79
  44.9 0.0 copy-done.2
  44.9 9.0 %collective-permute-done = bf16[128,3584]{1,0:T(8,128)(2,1)S(1)} collective-permute-done((bf16[128,3584]{1,0:T(8,128)(2,1)}, bf16[128,3584]{1,0:T(8,128)(2,1)S(1)}, u32[]{:S(2)}, u32[]{:S(2)}) %collective-permute-start) | collective-permute-done | bytes 917536 | tf_op jit(solution)/shard_map/ppermute | solution.py:17
  53.8 0.9 copy-done.4
  54.8 0.0 collective-permute-done.1
  54.8 7.8 %fusion = f32[256,2048]{1,0:T(8,128)S(1)} fusion(bf16[2048,3584]{1,0:T(8,128)(2,1)} %param.8, bf16[128,3584]{1,0:T(8,128)(2,1)} %collective-permute-done.1, bf16[128,3584]{1,0:T(8,128)(2,1)} %copy-done.4), kind=kOutput, calls=%fused_computation.3 | convolution fusion | flops 3761766400 | bytes 18612224 | tf_op jit(solution)/shard_map/dot_general | solution.py:79
  62.6 1.5 %rev.3 = f32[1,2,128,2048]{3,2,1,0:T(8,128)} reverse(f32[1,2,128,2048]{3,2,1,0:T(8,128)S(1)} %bitcast.19), dimensions={1} | reverse | bytes 4194304 | tf_op jit(solution)/shard_map/rev | solution.py:91
  64.1 3.2 %constant_dynamic-update-slice_fusion.7 = f32[512,2048]{1,0:T(8,128)} fusion(f32[512,2048]{1,0:T(8,128)} %convolution_dynamic-update-slice_fusion, s32[]{:T(128)S(6)} %select_n.59, f32[256,2048]{1,0:T(8,128)S(1)} %fusion, f32[1,2,128,2048]{3,2,1,0:T(8,128)} %rev.3, pred[]{:T(512)S(6)} %eq.5), kind=kLoop, calls=%fused_computation.18 | loop fusion | flops 524288 | bytes 6291461 | tf_op jit(solution)/shard_map/dynamic_update_slice | solution.py:94
  67.3 0.0 reduce-scatter.2.cloned.1.call-update
  67.3 0.0 copy-start.3
  67.3 0.0 copy-start.5
  67.3 2.0 %broadcast_in_dim.11 = bf16[512,3584]{1,0:T(8,128)(2,1)} broadcast(bf16[]{:T(256)} %constant.52.clone.1), dimensions={} | broadcast | bytes 3670018 | tf_op jit(solution)/shard_map/broadcast_in_dim | solution.py:25
  69.4 1.0 constant_dynamic-update-slice_fusion.6
  70.3 0.0 copy-done.3
  70.3 1.0 constant_dynamic-update-slice_fusion.5
  71.4 0.0 copy-done.5
  71.4 1.0 constant_dynamic-update-slice_fusion.4
  72.4 2.2 %constant_dynamic-update-slice_fusion.3.g_ref = bf16[512,3584]{1,0:T(8,128)(2,1)} fusion(bf16[512,3584]{1,0:T(8,128)(2,1)} %constant_dynamic-update-slice_fusion.4, bf16[128,3584]{1,0:T(8,128)(2,1)} %collective-permute-done.1, s32[]{:T(128)S(6)} %select_n.61), kind=kLoop, calls=%fused_computation.14 | loop fusion | bytes 1835012 | tf_op jit(solution)/shard_map/dynamic_update_slice | solution.py:27
  74.6 2.5 %dynamic-slice_bitcast_fusion = (bf16[64,32,128]{2,1,0:T(8,128)(2,1)S(1)}, bf16[64,32,128]{2,1,0:T(8,128)(2,1)S(1)}, bf16[64,32,128]{2,1,0:T(8,128)(2,1)}) fusion(bf16[4,64,32,128]{3,2,0,1:T(8,128)(2,1)} %bitcast.20, s32[]{:T(128)S(6)} %select_n.65, s32[]{:T(128)S(6)} %select_n.64, s32[]{:T(128)S(6)} %select_n.63), kind=kLoop, calls=%fused_computation.8 | loop fusion | bytes 3145740 | tf_op jit(solution)/shard_map/jit(dynamic_index_in_dim)/squeeze | solution.py:102
  77.1 0.6 collective-permute-start.3
  77.6 1.6 %collective-permute-start.4 = (bf16[64,32,128]{2,1,0:T(8,128)(2,1)S(1)}, bf16[64,32,128]{2,1,0:T(8,128)(2,1)}, u32[]{:S(2)}, u32[]{:S(2)}) collective-permute-start(bf16[64,32,128]{2,1,0:T(8,128)(2,1)S(1)} %get-tuple-element.13), channel_id=1, source_target_pairs={{0,16},{8,24},{16,0},{24,8},{1,17},{9,25},{17,1},{25,9},{2,18},{10... | collective-permute-start | bytes 1572872 | tf_op jit(solution)/shard_map/ppermute | solution.py:104
  79.2 1.3 %collective-permute-start.5 = (bf16[64,32,128]{2,1,0:T(8,128)(2,1)S(1)}, bf16[64,32,128]{2,1,0:T(8,128)(2,1)}, u32[]{:S(2)}, u32[]{:S(2)}) collective-permute-start(bf16[64,32,128]{2,1,0:T(8,128)(2,1)S(1)} %get-tuple-element.12), channel_id=1, source_target_pairs={{0,24},{8,16},{16,8},{24,0},{1,25},{9,17},{17,9},{25,1},{2,26},{10... | collective-permute-start | bytes 1572872 | tf_op jit(solution)/shard_map/ppermute | solution.py:104
  81.2 0.2 broadcast_in_dim.10
  81.4 1.2 bitcast_dynamic-update-slice_fusion
  82.6 9.6 %collective-permute-done.3 = bf16[64,32,128]{2,1,0:T(8,128)(2,1)} collective-permute-done((bf16[64,32,128]{2,1,0:T(8,128)(2,1)}, bf16[64,32,128]{2,1,0:T(8,128)(2,1)}, u32[]{:S(2)}, u32[]{:S(2)}) %collective-permute-start.3) | collective-permute-done | bytes 524320 | tf_op jit(solution)/shard_map/ppermute | solution.py:104
  92.2 1.2 constant_dynamic-update-slice_fusion.1
  93.4 7.9 %collective-permute-done.4 = bf16[64,32,128]{2,1,0:T(8,128)(2,1)} collective-permute-done((bf16[64,32,128]{2,1,0:T(8,128)(2,1)S(1)}, bf16[64,32,128]{2,1,0:T(8,128)(2,1)}, u32[]{:S(2)}, u32[]{:S(2)}) %collective-permute-start.4) | collective-permute-done | bytes 524320 | tf_op jit(solution)/shard_map/ppermute | solution.py:104
  101.3 1.2 constant_dynamic-update-slice_fusion
  102.5 0.0 collective-permute-done.5
  102.5 1.2 constant_dynamic-update-slice_fusion.2.a_ref
  103.7 0.0 copy-start
  103.7 1.4 %copy-done = bf16[64,32,512]{2,1,0:T(8,128)(2,1)} copy-done((bf16[64,32,512]{2,1,0:T(8,128)(2,1)}, bf16[64,32,512]{2,1,0:T(8,128)(2,1)S(1)}, u32[]{:S(2)}) %copy-start) | copy-done | bytes 2097176
  105.1 11.0 %shard_map.77 = bf16[128,32,128]{2,1,0:T(8,128)(2,1)} custom-call(s32[128]{0:T(128)} %rows_ref.1, s32[128]{0:T(128)} %cols_ref.1, s32[1]{0:T(128)S(6)} %copy.21.cnt_ref, bf16[64,32,512]{2,1,0:T(8,128)(2,1)} %copy-done, bf16[512,3584]{1,0:T(8,128)(2,1)} %constant_dynamic-update-slice_fusion.3.g_ref), custom_call_target="tpu_custom_call" | custom-call | flops 536870912 | bytes 6815744 | tf_op jit(solution)/shard_map/pallas_call | solution.py:54
  116.0 1.7 %reduce-scatter.2.cloned.1.call-done = f32[64,2048]{1,0:T(8,128)} async-done(((f32[512,2048]{1,0:T(8,128)}), f32[64,2048]{1,0:T(8,128)}) %reduce-scatter.2.cloned.1.call-update) | async-done | bytes 524304 | tf_op jit(solution)/shard_map/reduce_scatter | solution.py:95
  117.8 1.8 %convert_element_type.3 = bf16[64,2048]{1,0:T(8,128)(2,1)} convert(f32[64,2048]{1,0:T(8,128)} %reduce-scatter.2.cloned.1.call-done) | non-fusion elementwise | flops 131072 | bytes 786432 | tf_op jit(solution)/shard_map/convert_element_type | solution.py:95
  (2 shorter events, 0.0 us)
Async XLA Ops:
  7.2 9.0 %copy-start.1 = (bf16[128,3584]{1,0:T(8,128)(2,1)S(1)}, bf16[128,3584]{1,0:T(8,128)(2,1)}, u32[]{:S(2)}) copy-start(bf16[128,3584]{1,0:T(8,128)(2,1)} %param.7) | copy-start | bytes 2752516
  7.2 67.4 %all-gather.2.cloned.1.call-start = ((), (), s32[]{:S(2)}) async-start(), calls=%async_computation.2 | async-start | bytes 2359296 | tf_op jit(solution)/shard_map/all_gather | solution.py:71
  9.1 108.6 %reduce-scatter.2.cloned.1.call-start = ((), (), s32[]{:S(2)}) async-start(), calls=%async_computation.1 | async-start | bytes 4718592 | tf_op jit(solution)/shard_map/reduce_scatter | solution.py:95
  9.2 24.4 %collective-permute-start.2 = (bf16[128,3584]{1,0:T(8,128)(2,1)}, bf16[128,3584]{1,0:T(8,128)(2,1)S(1)}, u32[]{:S(2)}, u32[]{:S(2)}) collective-permute-start(bf16[128,3584]{1,0:T(8,128)(2,1)} %param.7), channel_id=1, source_target_pairs={{0,8},{8,0},{16,24},{24,16},{1,9},{9,1},{17,25},{25,17},{2,10},{10... | collective-permute-start | bytes 2752520 | tf_op jit(solution)/shard_map/ppermute | solution.py:17
  12.2 41.7 %collective-permute-start = (bf16[128,3584]{1,0:T(8,128)(2,1)}, bf16[128,3584]{1,0:T(8,128)(2,1)S(1)}, u32[]{:S(2)}, u32[]{:S(2)}) collective-permute-start(bf16[128,3584]{1,0:T(8,128)(2,1)} %param.7), channel_id=1, source_target_pairs={{0,16},{8,24},{16,0},{24,8},{1,17},{9,25},{17,1},{25,9},{2,18},{10... | collective-permute-start | bytes 2752520 | tf_op jit(solution)/shard_map/ppermute | solution.py:17
  13.7 41.1 %collective-permute-start.1 = (bf16[128,3584]{1,0:T(8,128)(2,1)}, bf16[128,3584]{1,0:T(8,128)(2,1)}, u32[]{:S(2)}, u32[]{:S(2)}) collective-permute-start(bf16[128,3584]{1,0:T(8,128)(2,1)} %param.7), channel_id=1, source_target_pairs={{0,24},{8,16},{16,8},{24,0},{1,25},{9,17},{17,9},{25,1},{2,26},{10... | collective-permute-start | bytes 2752520 | tf_op jit(solution)/shard_map/ppermute | solution.py:17
  33.6 11.3 %copy-start.2 = (bf16[128,3584]{1,0:T(8,128)(2,1)}, bf16[128,3584]{1,0:T(8,128)(2,1)S(1)}, u32[]{:S(2)}) copy-start(bf16[128,3584]{1,0:T(8,128)(2,1)S(1)} %collective-permute-done.2) | copy-start | bytes 2752516
  53.8 0.9 copy-start.4
  67.3 3.1 %copy-start.3 = (bf16[128,3584]{1,0:T(8,128)(2,1)S(1)}, bf16[128,3584]{1,0:T(8,128)(2,1)}, u32[]{:S(2)}) copy-start(bf16[128,3584]{1,0:T(8,128)(2,1)} %copy-done.2) | copy-start | bytes 2752516
  67.3 4.1 %copy-start.5 = (bf16[128,3584]{1,0:T(8,128)(2,1)S(1)}, bf16[128,3584]{1,0:T(8,128)(2,1)}, u32[]{:S(2)}) copy-start(bf16[128,3584]{1,0:T(8,128)(2,1)} %copy-done.4) | copy-start | bytes 2752516
  77.1 15.2 %collective-permute-start.3 = (bf16[64,32,128]{2,1,0:T(8,128)(2,1)}, bf16[64,32,128]{2,1,0:T(8,128)(2,1)}, u32[]{:S(2)}, u32[]{:S(2)}) collective-permute-start(bf16[64,32,128]{2,1,0:T(8,128)(2,1)} %get-tuple-element.14), channel_id=1, source_target_pairs={{0,8},{8,0},{16,24},{24,16},{1,9},{9,1},{17,25},{25,17},{2,10},{10... | collective-permute-start | bytes 1572872 | tf_op jit(solution)/shard_map/ppermute | solution.py:104
  77.6 23.7 %collective-permute-start.4 = (bf16[64,32,128]{2,1,0:T(8,128)(2,1)S(1)}, bf16[64,32,128]{2,1,0:T(8,128)(2,1)}, u32[]{:S(2)}, u32[]{:S(2)}) collective-permute-start(bf16[64,32,128]{2,1,0:T(8,128)(2,1)S(1)} %get-tuple-element.13), channel_id=1, source_target_pairs={{0,16},{8,24},{16,0},{24,8},{1,17},{9,25},{17,1},{25,9},{2,18},{10... | collective-permute-start | bytes 1572872 | tf_op jit(solution)/shard_map/ppermute | solution.py:104
  79.2 23.3 %collective-permute-start.5 = (bf16[64,32,128]{2,1,0:T(8,128)(2,1)S(1)}, bf16[64,32,128]{2,1,0:T(8,128)(2,1)}, u32[]{:S(2)}, u32[]{:S(2)}) collective-permute-start(bf16[64,32,128]{2,1,0:T(8,128)(2,1)S(1)} %get-tuple-element.12), channel_id=1, source_target_pairs={{0,24},{8,16},{16,8},{24,0},{1,25},{9,17},{17,9},{25,1},{2,26},{10... | collective-permute-start | bytes 1572872 | tf_op jit(solution)/shard_map/ppermute | solution.py:104
  103.7 1.4 %copy-start = (bf16[64,32,512]{2,1,0:T(8,128)(2,1)}, bf16[64,32,512]{2,1,0:T(8,128)(2,1)S(1)}, u32[]{:S(2)}) copy-start(bf16[64,32,512]{2,1,0:T(8,128)(2,1)S(1)} %constant_dynamic-update-slice_fusion.2.a_ref) | copy-start | bytes 6291460
Sparse Core Ops, SparseCore 0:
  10.2 31.7 all-gather.1
  67.4 50.3 reduce-scatter.1

commit v15 on v13

--- a/solution.py
+++ b/solution.py
@@ -72,7 +72,11 @@
     row_blocks = full_acts.shape[1] // BLK
     acts_pieces = jnp.transpose(full_acts.reshape(tok_dev, row_blocks, n_tok, sub), (2, 1, 3, 0))
 
-    pieces = xor_exchange(grad_out, "tok", n_tok)
+    pieces = [grad_out] + [
+        lax.ppermute(grad_out, "tok", perm=[(a, a ^ m) for a in range(n_tok)]) for m in range(1, n_tok - 1)
+    ]
+    late, pieces[n_tok // 2] = lax.optimization_barrier((grad_out, pieces[n_tok // 2]))
+    pieces.append(lax.ppermute(late, "tok", perm=[(a, a ^ (n_tok - 1)) for a in range(n_tok)]))
     gout = place_rows(pieces, me)
 
     def nt(x):

time: 121 us -> 126 us (1.041)
  starting transfers between devices: 8.11 us -> 10.8 us
  waiting for transfers between devices: 33.2 us -> 35.5 us
    ppermute x3, waiting for transfers between devices: 13.9 us -> 17.2 us  [the longest x2 17.2 us: per_device(): lax.ppermute(grad_out, 'tok', perm=[(a, a ^ m) for a in range(n_tok)])]
    ppermute x3, starting transfers between devices: 4.54 us -> 7.19 us  [the longest x2 4.52 us: per_device(): lax.ppermute(grad_out, 'tok', perm=[(a, a ^ m) for a in range(n_tok)])]
    ppermute x3, waiting for transfers between devices: 18.7 us -> 16.5 us  [per_device(): part = lax.ppermute(part, 'tok', perm=[(a, a ^ m) for a in range(n_tok)])]
  transfers between devices with their start and end apart: 8 -> 8, of which waited for: 5 -> 4; matrix products, arithmetic and copies ran while one was open for 42% -> 40% of each run, Pallas kernels for 9% -> 9%
where the time goes in v15:
time: 126 us
  waiting for transfers between devices  35.5 us (28%)
  matrix products  29.4 us (23%)
  local copies, waits for them, and re-layouts  22.5 us (18%)
  between operations  14.8 us (12%)
  Pallas kernels  11 us (9%)
  starting transfers between devices  10.8 us (9%)
  other arithmetic  1.77 us (1%)
    dot_general x3, matrix products, nt(): lax.dot_general(x, weight, (((1,), (1,)), ((), ())), preferred_element_ty...  29.4 us
    ppermute x2, waiting for transfers between devices, per_device(): lax.ppermute(grad_out, 'tok', perm=[(a, a ^ m) for a in range(n_tok)])  17.2 us
    ppermute x3, waiting for transfers between devices, per_device(): part = lax.ppermute(part, 'tok', perm=[(a, a ^ m) for a in range(n_tok)])  16.5 us
    dynamic_update_slice x10, local copies, waits for them, and re-layouts, place_rows(): out = lax.dynamic_update_slice_in_dim(out, piece, (me ^ m) * rows, axis)  12.1 us
    pallas_call x1, Pallas kernels, block_tiles(): pl.pallas_call(block_kernel, grid_spec=grid_spec, out_shape=jax.ShapeDtyp...  11 us
    broadcast_in_dim x3, local copies, waits for them, and re-layouts, place_rows(): out = jnp.zeros(shape, pieces[0].dtype)  4.75 us
    ppermute x2, starting transfers between devices, per_device(): lax.ppermute(grad_out, 'tok', perm=[(a, a ^ m) for a in range(n_tok)])  4.52 us
    ppermute x3, starting transfers between devices, per_device(): part = lax.ppermute(part, 'tok', perm=[(a, a ^ m) for a in range(n_tok)])  3.49 us
  transfers between devices with their start and end apart: 8, of which 4 were waited for; matrix products, arithmetic and copies ran while one was open for 40% of the time, Pallas kernels for 9%

profile of v15, /device:TPU:0, one launch (start us, length us, event | category | flops | bytes accessed | tf_op | source)
XLA Modules:
  0.0 125.6 jit_solution(5974897108098184646)
XLA Ops:
  7.2 0.0 copy-start.1
  7.2 0.0 all-gather.2.cloned.1.call-start
  7.2 3.0 %collective-permute-start.1 = (bf16[128,3584]{1,0:T(8,128)(2,1)}, bf16[128,3584]{1,0:T(8,128)(2,1)S(1)}, u32[]{:S(2)}, u32[]{:S(2)}) collective-permute-start(bf16[128,3584]{1,0:T(8,128)(2,1)} %param.7), channel_id=1, source_target_pairs={{0,16},{8,24},{16,0},{24,8},{1,17},{9,25},{17,1},{25,9},{2,18},{10... | collective-permute-start | bytes 2752520 | tf_op jit(solution)/shard_map/ppermute | solution.py:76
  10.3 1.5 %collective-permute-start = (bf16[128,3584]{1,0:T(8,128)(2,1)}, bf16[128,3584]{1,0:T(8,128)(2,1)S(1)}, u32[]{:S(2)}, u32[]{:S(2)}) collective-permute-start(bf16[128,3584]{1,0:T(8,128)(2,1)} %param.7), channel_id=1, source_target_pairs={{0,8},{8,0},{16,24},{24,16},{1,9},{9,1},{17,25},{25,17},{2,10},{10... | collective-permute-start | bytes 2752520 | tf_op jit(solution)/shard_map/ppermute | solution.py:76
  11.7 1.8 %copy.9 = bf16[128,1024]{0,1:T(8,128)(2,1)} copy(bf16[128,1024]{1,0:T(8,128)(2,1)} %param.6) | data formatting | bytes 524288 | tf_op args[0]
  13.5 0.0 all-gather.2.cloned.1.call-update
  13.6 0.0 reduce-scatter.2.cloned.1.call-start
  13.6 17.2 %collective-permute-done.1 = bf16[128,3584]{1,0:T(8,128)(2,1)S(1)} collective-permute-done((bf16[128,3584]{1,0:T(8,128)(2,1)}, bf16[128,3584]{1,0:T(8,128)(2,1)S(1)}, u32[]{:S(2)}, u32[]{:S(2)}) %collective-permute-start.1) | collective-permute-done | bytes 917536 | tf_op jit(solution)/shard_map/ppermute | solution.py:76
  30.8 2.7 %collective-permute-start.2 = (bf16[128,3584]{1,0:T(8,128)(2,1)}, bf16[128,3584]{1,0:T(8,128)(2,1)}, u32[]{:S(2)}, u32[]{:S(2)}) collective-permute-start(bf16[128,3584]{1,0:T(8,128)(2,1)} %param.7), channel_id=1, source_target_pairs={{0,24},{8,16},{16,8},{24,0},{1,25},{9,17},{17,9},{25,1},{2,26},{10... | collective-permute-start | bytes 2752520 | tf_op jit(solution)/shard_map/ppermute | solution.py:79
  33.5 2.5 %broadcast_in_dim.9 = f32[512,2048]{1,0:T(8,128)} broadcast(f32[]{:T(128)} %constant.10.clone.1), dimensions={} | broadcast | bytes 4194308 | tf_op jit(solution)/shard_map/broadcast_in_dim | solution.py:25
  35.9 0.0 copy-done.1
  36.0 11.0 %convolution_dynamic-update-slice_fusion.1 = f32[512,2048]{1,0:T(8,128)} fusion(f32[512,2048]{1,0:T(8,128)} %broadcast_in_dim.9, s32[]{:T(128)S(6)} %select_n.33, bf16[128,3584]{1,0:T(8,128)(2,1)S(1)} %copy-done.1, bf16[2048,3584]{1,0:T(8,128)(2,1)} %param.8), kind=kOutput, calls=%fused_computation.1 | convolution fusion | flops 1879048192 | bytes 16646148 | tf_op jit(solution)/shard_map/dot_general | solution.py:83
  46.9 0.0 collective-permute-done
  46.9 10.9 %convolution_dynamic-update-slice_fusion = f32[512,2048]{1,0:T(8,128)} fusion(f32[512,2048]{1,0:T(8,128)} %convolution_dynamic-update-slice_fusion.1, s32[]{:T(128)S(6)} %select_n.34, bf16[128,3584]{1,0:T(8,128)(2,1)S(1)} %collective-permute-done, bf16[2048,3584]{1,0:T(8,128)(2,1)} %param.8), kind=kOutput, calls=%fused_computation | convolution fusion | flops 1879048192 | bytes 16646148 | tf_op jit(solution)/shard_map/dot_general | solution.py:83
  57.8 0.0 collective-permute-done.2
  57.8 7.5 %fusion = f32[256,2048]{1,0:T(8,128)S(1)} fusion(bf16[2048,3584]{1,0:T(8,128)(2,1)} %param.8, bf16[128,3584]{1,0:T(8,128)(2,1)} %collective-permute-done.2, bf16[128,3584]{1,0:T(8,128)(2,1)S(1)} %collective-permute-done.1), kind=kOutput, calls=%fused_computation.2 | convolution fusion | flops 3761766400 | bytes 18612224 | tf_op jit(solution)/shard_map/dot_general | solution.py:83
  65.4 1.1 slice_dynamic-update-slice_fusion.1
  66.4 1.1 slice_dynamic-update-slice_fusion
  67.5 0.0 reduce-scatter.2.cloned.1.call-update
  67.5 2.0 %broadcast_in_dim.11 = bf16[512,3584]{1,0:T(8,128)(2,1)} broadcast(bf16[]{:T(256)} %constant.31.clone.1), dimensions={} | broadcast | bytes 3670018 | tf_op jit(solution)/shard_map/broadcast_in_dim | solution.py:25
  69.6 1.0 constant_dynamic-update-slice_fusion.6
  70.6 1.0 constant_dynamic-update-slice_fusion.5
  71.6 1.0 constant_dynamic-update-slice_fusion.4
  72.6 2.3 %constant_dynamic-update-slice_fusion.3.g_ref = bf16[512,3584]{1,0:T(8,128)(2,1)} fusion(bf16[512,3584]{1,0:T(8,128)(2,1)} %constant_dynamic-update-slice_fusion.4, bf16[128,3584]{1,0:T(8,128)(2,1)} %collective-permute-done.2, s32[]{:T(128)S(6)} %select_n.36), kind=kLoop, calls=%fused_computation.15 | loop fusion | bytes 1835012 | tf_op jit(solution)/shard_map/dynamic_update_slice | solution.py:27
  74.9 0.0 all-gather.2.cloned.1.call-done
  74.9 2.4 %dynamic-slice_bitcast_fusion = (bf16[64,32,128]{2,1,0:T(8,128)(2,1)S(1)}, bf16[64,32,128]{2,1,0:T(8,128)(2,1)S(1)}, bf16[64,32,128]{2,1,0:T(8,128)(2,1)}) fusion(bf16[4,64,32,128]{3,2,0,1:T(8,128)(2,1)} %bitcast.16, s32[]{:T(128)S(6)} %select_n.40, s32[]{:T(128)S(6)} %select_n.39, s32[]{:T(128)S(6)} %select_n.38), kind=kLoop, calls=%fused_computation.9 | loop fusion | bytes 3145740 | tf_op jit(solution)/shard_map/jit(dynamic_index_in_dim)/squeeze | solution.py:96
  77.3 0.5 collective-permute-start.3
  77.8 0.4 collective-permute-start.4
  78.2 2.6 %collective-permute-start.5 = (bf16[64,32,128]{2,1,0:T(8,128)(2,1)S(1)}, bf16[64,32,128]{2,1,0:T(8,128)(2,1)}, u32[]{:S(2)}, u32[]{:S(2)}) collective-permute-start(bf16[64,32,128]{2,1,0:T(8,128)(2,1)S(1)} %get-tuple-element.10), channel_id=1, source_target_pairs={{0,24},{8,16},{16,8},{24,0},{1,25},{9,17},{17,9},{25,1},{2,26},{10... | collective-permute-start | bytes 1572872 | tf_op jit(solution)/shard_map/ppermute | solution.py:98
  81.4 0.2 broadcast_in_dim.10
  81.7 1.2 bitcast_dynamic-update-slice_fusion
  82.9 9.6 %collective-permute-done.3 = bf16[64,32,128]{2,1,0:T(8,128)(2,1)} collective-permute-done((bf16[64,32,128]{2,1,0:T(8,128)(2,1)}, bf16[64,32,128]{2,1,0:T(8,128)(2,1)}, u32[]{:S(2)}, u32[]{:S(2)}) %collective-permute-start.3) | collective-permute-done | bytes 524320 | tf_op jit(solution)/shard_map/ppermute | solution.py:98
  92.5 1.2 constant_dynamic-update-slice_fusion.1
  93.7 0.0 collective-permute-done.4
  93.7 1.2 constant_dynamic-update-slice_fusion
  94.8 6.9 %collective-permute-done.5 = bf16[64,32,128]{2,1,0:T(8,128)(2,1)} collective-permute-done((bf16[64,32,128]{2,1,0:T(8,128)(2,1)S(1)}, bf16[64,32,128]{2,1,0:T(8,128)(2,1)}, u32[]{:S(2)}, u32[]{:S(2)}) %collective-permute-start.5) | collective-permute-done | bytes 524320 | tf_op jit(solution)/shard_map/ppermute | solution.py:98
  101.8 1.2 constant_dynamic-update-slice_fusion.2.a_ref
  102.9 0.0 copy-start
  102.9 1.4 %copy-done = bf16[64,32,512]{2,1,0:T(8,128)(2,1)} copy-done((bf16[64,32,512]{2,1,0:T(8,128)(2,1)}, bf16[64,32,512]{2,1,0:T(8,128)(2,1)S(1)}, u32[]{:S(2)}) %copy-start) | copy-done | bytes 2097176
  104.3 11.0 %shard_map.77 = bf16[128,32,128]{2,1,0:T(8,128)(2,1)} custom-call(s32[128]{0:T(128)} %rows_ref.1, s32[128]{0:T(128)} %cols_ref.1, s32[1]{0:T(128)S(6)} %copy.22.cnt_ref, bf16[64,32,512]{2,1,0:T(8,128)(2,1)} %copy-done, bf16[512,3584]{1,0:T(8,128)(2,1)} %constant_dynamic-update-slice_fusion.3.g_ref), custom_call_target="tpu_custom_call" | custom-call | flops 536870912 | bytes 6815744 | tf_op jit(solution)/shard_map/pallas_call | solution.py:54
  115.3 1.7 %reduce-scatter.2.cloned.1.call-done = f32[64,2048]{1,0:T(8,128)} async-done(((f32[512,2048]{1,0:T(8,128)}), f32[64,2048]{1,0:T(8,128)}) %reduce-scatter.2.cloned.1.call-update) | async-done | bytes 524304 | tf_op jit(solution)/shard_map/reduce_scatter | solution.py:89
  117.0 1.8 %convert_element_type.3 = bf16[64,2048]{1,0:T(8,128)(2,1)} convert(f32[64,2048]{1,0:T(8,128)} %reduce-scatter.2.cloned.1.call-done) | non-fusion elementwise | flops 131072 | bytes 786432 | tf_op jit(solution)/shard_map/convert_element_type | solution.py:89
Async XLA Ops:
  7.2 28.8 %copy-start.1 = (bf16[128,3584]{1,0:T(8,128)(2,1)S(1)}, bf16[128,3584]{1,0:T(8,128)(2,1)}, u32[]{:S(2)}) copy-start(bf16[128,3584]{1,0:T(8,128)(2,1)} %param.7) | copy-start | bytes 2752516
  7.2 67.7 %all-gather.2.cloned.1.call-start = ((), (), s32[]{:S(2)}) async-start(), calls=%async_computation.2 | async-start | bytes 2359296 | tf_op jit(solution)/shard_map/all_gather | solution.py:71
  7.2 23.6 %collective-permute-start.1 = (bf16[128,3584]{1,0:T(8,128)(2,1)}, bf16[128,3584]{1,0:T(8,128)(2,1)S(1)}, u32[]{:S(2)}, u32[]{:S(2)}) collective-permute-start(bf16[128,3584]{1,0:T(8,128)(2,1)} %param.7), channel_id=1, source_target_pairs={{0,16},{8,24},{16,0},{24,8},{1,17},{9,25},{17,1},{25,9},{2,18},{10... | collective-permute-start | bytes 2752520 | tf_op jit(solution)/shard_map/ppermute | solution.py:76
  10.3 36.7 %collective-permute-start = (bf16[128,3584]{1,0:T(8,128)(2,1)}, bf16[128,3584]{1,0:T(8,128)(2,1)S(1)}, u32[]{:S(2)}, u32[]{:S(2)}) collective-permute-start(bf16[128,3584]{1,0:T(8,128)(2,1)} %param.7), channel_id=1, source_target_pairs={{0,8},{8,0},{16,24},{24,16},{1,9},{9,1},{17,25},{25,17},{2,10},{10... | collective-permute-start | bytes 2752520 | tf_op jit(solution)/shard_map/ppermute | solution.py:76
  13.6 103.5 %reduce-scatter.2.cloned.1.call-start = ((), (), s32[]{:S(2)}) async-start(), calls=%async_computation.1 | async-start | bytes 4718592 | tf_op jit(solution)/shard_map/reduce_scatter | solution.py:89
  30.8 27.0 %collective-permute-start.2 = (bf16[128,3584]{1,0:T(8,128)(2,1)}, bf16[128,3584]{1,0:T(8,128)(2,1)}, u32[]{:S(2)}, u32[]{:S(2)}) collective-permute-start(bf16[128,3584]{1,0:T(8,128)(2,1)} %param.7), channel_id=1, source_target_pairs={{0,24},{8,16},{16,8},{24,0},{1,25},{9,17},{17,9},{25,1},{2,26},{10... | collective-permute-start | bytes 2752520 | tf_op jit(solution)/shard_map/ppermute | solution.py:79
  77.3 15.2 %collective-permute-start.3 = (bf16[64,32,128]{2,1,0:T(8,128)(2,1)}, bf16[64,32,128]{2,1,0:T(8,128)(2,1)}, u32[]{:S(2)}, u32[]{:S(2)}) collective-permute-start(bf16[64,32,128]{2,1,0:T(8,128)(2,1)} %get-tuple-element.12), channel_id=1, source_target_pairs={{0,8},{8,0},{16,24},{24,16},{1,9},{9,1},{17,25},{25,17},{2,10},{10... | collective-permute-start | bytes 1572872 | tf_op jit(solution)/shard_map/ppermute | solution.py:98
  77.8 15.9 %collective-permute-start.4 = (bf16[64,32,128]{2,1,0:T(8,128)(2,1)S(1)}, bf16[64,32,128]{2,1,0:T(8,128)(2,1)}, u32[]{:S(2)}, u32[]{:S(2)}) collective-permute-start(bf16[64,32,128]{2,1,0:T(8,128)(2,1)S(1)} %get-tuple-element.11), channel_id=1, source_target_pairs={{0,16},{8,24},{16,0},{24,8},{1,17},{9,25},{17,1},{25,9},{2,18},{10... | collective-permute-start | bytes 1572872 | tf_op jit(solution)/shard_map/ppermute | solution.py:98
  78.2 23.5 %collective-permute-start.5 = (bf16[64,32,128]{2,1,0:T(8,128)(2,1)S(1)}, bf16[64,32,128]{2,1,0:T(8,128)(2,1)}, u32[]{:S(2)}, u32[]{:S(2)}) collective-permute-start(bf16[64,32,128]{2,1,0:T(8,128)(2,1)S(1)} %get-tuple-element.10), channel_id=1, source_target_pairs={{0,24},{8,16},{16,8},{24,0},{1,25},{9,17},{17,9},{25,1},{2,26},{10... | collective-permute-start | bytes 1572872 | tf_op jit(solution)/shard_map/ppermute | solution.py:98
  102.9 1.4 %copy-start = (bf16[64,32,512]{2,1,0:T(8,128)(2,1)}, bf16[64,32,512]{2,1,0:T(8,128)(2,1)S(1)}, u32[]{:S(2)}) copy-start(bf16[64,32,512]{2,1,0:T(8,128)(2,1)S(1)} %constant_dynamic-update-slice_fusion.2.a_ref) | copy-start | bytes 6291460
Sparse Core Ops, SparseCore 0:
  13.7 28.4 all-gather.1
  67.6 49.3 reduce-scatter.1

commit v16 on v14

--- a/solution.py
+++ b/solution.py
@@ -85,11 +85,10 @@
             partial_sums, nt(pieces[m]), (me ^ m) * tok_dev, 0
         )
     far_pieces, partial_sums = lax.optimization_barrier((pieces[half:], partial_sums))
-    far = nt(jnp.concatenate(far_pieces, axis=0))
-    for bit in range(half.bit_length() - 1):
-        step = 1 << bit
-        swapped = far.reshape(half // (2 * step), 2, step * tok_dev, -1)[:, ::-1].reshape(far.shape)
-        far = jnp.where((me >> bit) % 2 == 1, swapped, far)
+    far_in = jnp.zeros((half * tok_dev, grad_out.shape[1]), grad_out.dtype)
+    for k, piece in enumerate(far_pieces):
+        far_in = lax.dynamic_update_slice_in_dim(far_in, piece, ((me ^ (half + k)) % half) * tok_dev, 0)
+    far = nt(far_in)
     base = ((me ^ half) // half) * half
     partial_sums = lax.dynamic_update_slice_in_dim(partial_sums, far, base * tok_dev, 0)
     grad_in = lax.psum_scatter(partial_sums, "feat", scatter_dimension=0, tiled=True).astype(

time: 127 us -> 120 us (0.945)
  other arithmetic: 4.95 us -> 1.77 us
  local copies, waits for them, and re-layouts: 22.8 us -> 20.8 us
  waiting for transfers between devices: 34.4 us -> 32.7 us
    dynamic_update_slice x1 -> x0, other arithmetic: 3.18 us -> none  [per_device(): lax.dynamic_update_slice_in_dim(partial_sums, far, base * tok_dev, 0)]
    ppermute x3, waiting for transfers between devices: 15.1 us -> 13.6 us  [xor_exchange(): out.append(lax.ppermute(x, axis_name, perm=[(a, a ^ m) for a in range(n)]))]
    rev x1 -> x0, local copies, waits for them, and re-layouts: 1.5 us -> none  [per_device(): far.reshape(half // (2 * step), 2, step * tok_dev, -1)[:, ::-1]]
    unnamed x13 -> x5, local copies, waits for them, and re-layouts: 4.18 us -> 3.11 us
  transfers between devices with their start and end apart: 8 -> 8, of which waited for: 5 -> 5; matrix products, arithmetic and copies ran while one was open for 41% -> 42% of each run, Pallas kernels for 9% -> 9%
where the time goes in v16:
time: 120 us
  waiting for transfers between devices  32.7 us (27%)
  matrix products  30.8 us (26%)
  local copies, waits for them, and re-layouts  20.8 us (17%)
  between operations  14.8 us (12%)
  Pallas kernels  11 us (9%)
  starting transfers between devices  8.11 us (7%)
  other arithmetic  1.77 us (1%)
    dot_general x3, matrix products, nt(): lax.dot_general(x, weight, (((1,), (1,)), ((), ())), preferred_element_ty...  30.8 us
    ppermute x3, waiting for transfers between devices, per_device(): part = lax.ppermute(part, 'tok', perm=[(a, a ^ m) for a in range(n_tok)])  18.6 us
    ppermute x3, waiting for transfers between devices, xor_exchange(): out.append(lax.ppermute(x, axis_name, perm=[(a, a ^ m) for a in range(n)]))  13.6 us
    pallas_call x1, Pallas kernels, block_tiles(): pl.pallas_call(block_kernel, grid_spec=grid_spec, out_shape=jax.ShapeDtyp...  11 us
    dynamic_update_slice x8, local copies, waits for them, and re-layouts, place_rows(): out = lax.dynamic_update_slice_in_dim(out, piece, (me ^ m) * rows, axis)  10 us
    ppermute x3, starting transfers between devices, xor_exchange(): out.append(lax.ppermute(x, axis_name, perm=[(a, a ^ m) for a in range(n)]))  4.55 us
    ppermute x3, starting transfers between devices, per_device(): part = lax.ppermute(part, 'tok', perm=[(a, a ^ m) for a in range(n_tok)])  3.49 us
    unnamed x5, local copies, waits for them, and re-layouts  3.11 us
  transfers between devices with their start and end apart: 8, of which 5 were waited for; matrix products, arithmetic and copies ran while one was open for 42% of the time, Pallas kernels for 9%

profile of v16, /device:TPU:0, one launch (start us, length us, event | category | flops | bytes accessed | tf_op | source)
XLA Modules:
  0.0 120.0 jit_solution(4887518063159930782)
XLA Ops:
  7.2 0.0 copy-start.1
  7.2 0.0 all-gather.2.cloned.1.call-start
  7.2 3.0 %collective-permute-start.2 = (bf16[128,3584]{1,0:T(8,128)(2,1)}, bf16[128,3584]{1,0:T(8,128)(2,1)}, u32[]{:S(2)}, u32[]{:S(2)}) collective-permute-start(bf16[128,3584]{1,0:T(8,128)(2,1)} %param.7), channel_id=1, source_target_pairs={{0,8},{8,0},{16,24},{24,16},{1,9},{9,1},{17,25},{25,17},{2,10},{10... | collective-permute-start | bytes 2752520 | tf_op jit(solution)/shard_map/ppermute | solution.py:17
  10.2 1.5 %collective-permute-start = (bf16[128,3584]{1,0:T(8,128)(2,1)}, bf16[128,3584]{1,0:T(8,128)(2,1)S(1)}, u32[]{:S(2)}, u32[]{:S(2)}) collective-permute-start(bf16[128,3584]{1,0:T(8,128)(2,1)} %param.7), channel_id=1, source_target_pairs={{0,16},{8,24},{16,0},{24,8},{1,17},{9,25},{17,1},{25,9},{2,18},{10... | collective-permute-start | bytes 2752520 | tf_op jit(solution)/shard_map/ppermute | solution.py:17
  11.7 0.0 collective-permute-start.1
  11.8 1.8 %copy.9 = bf16[128,1024]{0,1:T(8,128)(2,1)} copy(bf16[128,1024]{1,0:T(8,128)(2,1)} %param.6) | data formatting | bytes 524288 | tf_op args[0]
  13.6 0.0 all-gather.2.cloned.1.call-update
  13.6 0.0 reduce-scatter.2.cloned.1.call-start
  13.6 2.5 %broadcast_in_dim.12 = f32[512,2048]{1,0:T(8,128)} broadcast(f32[]{:T(128)} %constant.49.clone.1), dimensions={} | broadcast | bytes 4194308 | tf_op jit(solution)/shard_map/broadcast_in_dim | solution.py:82
  16.1 0.0 copy-done.1
  16.1 10.9 %convolution_dynamic-update-slice_fusion.2 = f32[512,2048]{1,0:T(8,128)} fusion(f32[512,2048]{1,0:T(8,128)} %broadcast_in_dim.12, s32[]{:T(128)S(6)} %select_n.55, bf16[128,3584]{1,0:T(8,128)(2,1)S(1)} %copy-done.1, bf16[2048,3584]{1,0:T(8,128)(2,1)} %param.8), kind=kOutput, calls=%fused_computation.2 | convolution fusion | flops 1879048192 | bytes 16646148 | tf_op jit(solution)/shard_map/dot_general | solution.py:79
  27.0 4.7 %collective-permute-done.2 = bf16[128,3584]{1,0:T(8,128)(2,1)} collective-permute-done((bf16[128,3584]{1,0:T(8,128)(2,1)}, bf16[128,3584]{1,0:T(8,128)(2,1)}, u32[]{:S(2)}, u32[]{:S(2)}) %collective-permute-start.2) | collective-permute-done | bytes 917536 | tf_op jit(solution)/shard_map/ppermute | solution.py:17
  31.7 11.3 %convolution_dynamic-update-slice_fusion.1 = f32[512,2048]{1,0:T(8,128)} fusion(f32[512,2048]{1,0:T(8,128)} %convolution_dynamic-update-slice_fusion.2, s32[]{:T(128)S(6)} %select_n.56, bf16[128,3584]{1,0:T(8,128)(2,1)} %collective-permute-done.2, bf16[2048,3584]{1,0:T(8,128)(2,1)} %param.8), kind=kOutput, calls=%fused_computation.1 | convolution fusion | flops 1879048192 | bytes 16646148 | tf_op jit(solution)/shard_map/dot_general | solution.py:79
  43.1 8.8 %collective-permute-done = bf16[128,3584]{1,0:T(8,128)(2,1)S(1)} collective-permute-done((bf16[128,3584]{1,0:T(8,128)(2,1)}, bf16[128,3584]{1,0:T(8,128)(2,1)S(1)}, u32[]{:S(2)}, u32[]{:S(2)}) %collective-permute-start) | collective-permute-done | bytes 917536 | tf_op jit(solution)/shard_map/ppermute | solution.py:17
  51.9 0.0 collective-permute-done.1
  51.9 0.1 broadcast_in_dim.13
  52.0 0.1 constant_dynamic-update-slice_fusion.8
  52.1 0.1 constant_dynamic-update-slice_fusion.7
  52.2 8.6 %convolution_dynamic-update-slice_fusion = f32[512,2048]{1,0:T(8,128)} fusion(f32[512,2048]{1,0:T(8,128)} %convolution_dynamic-update-slice_fusion.1, s32[]{:T(128)S(6)} %select_n.62, bf16[256,3584]{1,0:T(8,128)(2,1)S(1)} %constant_dynamic-update-slice_fusion.7, bf16[2048,3584]{1,0:T(8,128)(2,1)} %param.8), kind=kOutput, calls=%fused_computation | convolution fusion | flops 3758096384 | bytes 18612228 | tf_op jit(solution)/shard_map/dot_general | solution.py:79
  60.8 0.0 reduce-scatter.2.cloned.1.call-update
  60.9 2.1 %broadcast_in_dim.15 = bf16[512,3584]{1,0:T(8,128)(2,1)} broadcast(bf16[]{:T(256)} %constant.55.clone.1), dimensions={} | broadcast | bytes 3670018 | tf_op jit(solution)/shard_map/broadcast_in_dim | solution.py:25
  63.0 1.0 constant_dynamic-update-slice_fusion.6
  64.0 2.3 %constant_dynamic-update-slice_fusion.5 = bf16[512,3584]{1,0:T(8,128)(2,1)} fusion(bf16[512,3584]{1,0:T(8,128)(2,1)} %constant_dynamic-update-slice_fusion.6, bf16[128,3584]{1,0:T(8,128)(2,1)} %collective-permute-done.2, s32[]{:T(128)S(6)} %select_n.56), kind=kLoop, calls=%fused_computation.12 | loop fusion | bytes 1835012 | tf_op jit(solution)/shard_map/dynamic_update_slice | solution.py:27
  66.3 1.1 constant_dynamic-update-slice_fusion.4
  67.4 1.0 constant_dynamic-update-slice_fusion.3.g_ref
  68.3 0.0 all-gather.2.cloned.1.call-done
  68.3 2.5 %dynamic-slice_bitcast_fusion = (bf16[64,32,128]{2,1,0:T(8,128)(2,1)S(1)}, bf16[64,32,128]{2,1,0:T(8,128)(2,1)S(1)}, bf16[64,32,128]{2,1,0:T(8,128)(2,1)}) fusion(bf16[4,64,32,128]{3,2,0,1:T(8,128)(2,1)} %bitcast.17, s32[]{:T(128)S(6)} %select_n.68, s32[]{:T(128)S(6)} %select_n.67, s32[]{:T(128)S(6)} %select_n.66), kind=kLoop, calls=%fused_computation.4 | loop fusion | bytes 3145740 | tf_op jit(solution)/shard_map/jit(dynamic_index_in_dim)/squeeze | solution.py:101
  70.8 1.3 %collective-permute-start.3 = (bf16[64,32,128]{2,1,0:T(8,128)(2,1)}, bf16[64,32,128]{2,1,0:T(8,128)(2,1)}, u32[]{:S(2)}, u32[]{:S(2)}) collective-permute-start(bf16[64,32,128]{2,1,0:T(8,128)(2,1)} %get-tuple-element.14), channel_id=1, source_target_pairs={{0,8},{8,0},{16,24},{24,16},{1,9},{9,1},{17,25},{25,17},{2,10},{10... | collective-permute-start | bytes 1572872 | tf_op jit(solution)/shard_map/ppermute | solution.py:103
  72.1 0.9 collective-permute-start.4
  73.0 1.4 %collective-permute-start.5 = (bf16[64,32,128]{2,1,0:T(8,128)(2,1)S(1)}, bf16[64,32,128]{2,1,0:T(8,128)(2,1)}, u32[]{:S(2)}, u32[]{:S(2)}) collective-permute-start(bf16[64,32,128]{2,1,0:T(8,128)(2,1)S(1)} %get-tuple-element.12), channel_id=1, source_target_pairs={{0,24},{8,16},{16,8},{24,0},{1,25},{9,17},{17,9},{25,1},{2,26},{10... | collective-permute-start | bytes 1572872 | tf_op jit(solution)/shard_map/ppermute | solution.py:103
  75.0 0.2 broadcast_in_dim.14
  75.2 1.2 bitcast_dynamic-update-slice_fusion
  76.4 9.6 %collective-permute-done.3 = bf16[64,32,128]{2,1,0:T(8,128)(2,1)} collective-permute-done((bf16[64,32,128]{2,1,0:T(8,128)(2,1)}, bf16[64,32,128]{2,1,0:T(8,128)(2,1)}, u32[]{:S(2)}, u32[]{:S(2)}) %collective-permute-start.3) | collective-permute-done | bytes 524320 | tf_op jit(solution)/shard_map/ppermute | solution.py:103
  86.0 1.2 constant_dynamic-update-slice_fusion.1
  87.2 9.0 %collective-permute-done.4 = bf16[64,32,128]{2,1,0:T(8,128)(2,1)} collective-permute-done((bf16[64,32,128]{2,1,0:T(8,128)(2,1)S(1)}, bf16[64,32,128]{2,1,0:T(8,128)(2,1)}, u32[]{:S(2)}, u32[]{:S(2)}) %collective-permute-start.4) | collective-permute-done | bytes 524320 | tf_op jit(solution)/shard_map/ppermute | solution.py:103
  96.2 1.2 constant_dynamic-update-slice_fusion
  97.4 0.0 collective-permute-done.5
  97.4 1.2 constant_dynamic-update-slice_fusion.2.a_ref
  98.6 0.0 copy-start
  98.6 1.3 %copy-done = bf16[64,32,512]{2,1,0:T(8,128)(2,1)} copy-done((bf16[64,32,512]{2,1,0:T(8,128)(2,1)}, bf16[64,32,512]{2,1,0:T(8,128)(2,1)S(1)}, u32[]{:S(2)}) %copy-start) | copy-done | bytes 2097176
  99.9 11.0 %shard_map.77 = bf16[128,32,128]{2,1,0:T(8,128)(2,1)} custom-call(s32[128]{0:T(128)} %rows_ref.1, s32[128]{0:T(128)} %cols_ref.1, s32[1]{0:T(128)S(6)} %copy.23.cnt_ref, bf16[64,32,512]{2,1,0:T(8,128)(2,1)} %copy-done, bf16[512,3584]{1,0:T(8,128)(2,1)} %constant_dynamic-update-slice_fusion.3.g_ref), custom_call_target="tpu_custom_call" | custom-call | flops 536870912 | bytes 6815744 | tf_op jit(solution)/shard_map/pallas_call | solution.py:54
  110.8 0.5 reduce-scatter.2.cloned.1.call-done
  111.4 1.8 %convert_element_type.3 = bf16[64,2048]{1,0:T(8,128)(2,1)} convert(f32[64,2048]{1,0:T(8,128)} %reduce-scatter.2.cloned.1.call-done) | non-fusion elementwise | flops 131072 | bytes 786432 | tf_op jit(solution)/shard_map/convert_element_type | solution.py:94
Async XLA Ops:
  7.2 8.9 %copy-start.1 = (bf16[128,3584]{1,0:T(8,128)(2,1)S(1)}, bf16[128,3584]{1,0:T(8,128)(2,1)}, u32[]{:S(2)}) copy-start(bf16[128,3584]{1,0:T(8,128)(2,1)} %param.7) | copy-start | bytes 2752516
  7.2 61.2 %all-gather.2.cloned.1.call-start = ((), (), s32[]{:S(2)}) async-start(), calls=%async_computation.2 | async-start | bytes 2359296 | tf_op jit(solution)/shard_map/all_gather | solution.py:71
  7.2 24.5 %collective-permute-start.2 = (bf16[128,3584]{1,0:T(8,128)(2,1)}, bf16[128,3584]{1,0:T(8,128)(2,1)}, u32[]{:S(2)}, u32[]{:S(2)}) collective-permute-start(bf16[128,3584]{1,0:T(8,128)(2,1)} %param.7), channel_id=1, source_target_pairs={{0,8},{8,0},{16,24},{24,16},{1,9},{9,1},{17,25},{25,17},{2,10},{10... | collective-permute-start | bytes 2752520 | tf_op jit(solution)/shard_map/ppermute | solution.py:17
  10.2 41.7 %collective-permute-start = (bf16[128,3584]{1,0:T(8,128)(2,1)}, bf16[128,3584]{1,0:T(8,128)(2,1)S(1)}, u32[]{:S(2)}, u32[]{:S(2)}) collective-permute-start(bf16[128,3584]{1,0:T(8,128)(2,1)} %param.7), channel_id=1, source_target_pairs={{0,16},{8,24},{16,0},{24,8},{1,17},{9,25},{17,1},{25,9},{2,18},{10... | collective-permute-start | bytes 2752520 | tf_op jit(solution)/shard_map/ppermute | solution.py:17
  11.7 40.2 %collective-permute-start.1 = (bf16[128,3584]{1,0:T(8,128)(2,1)}, bf16[128,3584]{1,0:T(8,128)(2,1)S(1)}, u32[]{:S(2)}, u32[]{:S(2)}) collective-permute-start(bf16[128,3584]{1,0:T(8,128)(2,1)} %param.7), channel_id=1, source_target_pairs={{0,24},{8,16},{16,8},{24,0},{1,25},{9,17},{17,9},{25,1},{2,26},{10... | collective-permute-start | bytes 2752520 | tf_op jit(solution)/shard_map/ppermute | solution.py:17
  13.6 97.8 %reduce-scatter.2.cloned.1.call-start = ((), (), s32[]{:S(2)}) async-start(), calls=%async_computation.1 | async-start | bytes 4718592 | tf_op jit(solution)/shard_map/reduce_scatter | solution.py:94
  70.8 15.2 %collective-permute-start.3 = (bf16[64,32,128]{2,1,0:T(8,128)(2,1)}, bf16[64,32,128]{2,1,0:T(8,128)(2,1)}, u32[]{:S(2)}, u32[]{:S(2)}) collective-permute-start(bf16[64,32,128]{2,1,0:T(8,128)(2,1)} %get-tuple-element.14), channel_id=1, source_target_pairs={{0,8},{8,0},{16,24},{24,16},{1,9},{9,1},{17,25},{25,17},{2,10},{10... | collective-permute-start | bytes 1572872 | tf_op jit(solution)/shard_map/ppermute | solution.py:103
  72.1 24.1 %collective-permute-start.4 = (bf16[64,32,128]{2,1,0:T(8,128)(2,1)S(1)}, bf16[64,32,128]{2,1,0:T(8,128)(2,1)}, u32[]{:S(2)}, u32[]{:S(2)}) collective-permute-start(bf16[64,32,128]{2,1,0:T(8,128)(2,1)S(1)} %get-tuple-element.13), channel_id=1, source_target_pairs={{0,16},{8,24},{16,0},{24,8},{1,17},{9,25},{17,1},{25,9},{2,18},{10... | collective-permute-start | bytes 1572872 | tf_op jit(solution)/shard_map/ppermute | solution.py:103
  73.0 24.4 %collective-permute-start.5 = (bf16[64,32,128]{2,1,0:T(8,128)(2,1)S(1)}, bf16[64,32,128]{2,1,0:T(8,128)(2,1)}, u32[]{:S(2)}, u32[]{:S(2)}) collective-permute-start(bf16[64,32,128]{2,1,0:T(8,128)(2,1)S(1)} %get-tuple-element.12), channel_id=1, source_target_pairs={{0,24},{8,16},{16,8},{24,0},{1,25},{9,17},{17,9},{25,1},{2,26},{10... | collective-permute-start | bytes 1572872 | tf_op jit(solution)/shard_map/ppermute | solution.py:103
  98.6 1.3 %copy-start = (bf16[64,32,512]{2,1,0:T(8,128)(2,1)}, bf16[64,32,512]{2,1,0:T(8,128)(2,1)S(1)}, u32[]{:S(2)}) copy-start(bf16[64,32,512]{2,1,0:T(8,128)(2,1)S(1)} %constant_dynamic-update-slice_fusion.2.a_ref) | copy-start | bytes 6291460
Sparse Core Ops, SparseCore 0:
  13.7 30.7 all-gather.1
  61.0 50.3 reduce-scatter.1
